TPU v7x, 32 devices: a whole 2x2x4 slice. The times are simulated.
32 devices in a mesh: win: 4 (over y, core), pair: 8 (over z, x).
Axes of the slice: x: 2, y: 2, z: 4, core: 2. Of those that a mesh axis runs over, the one named last changes fastest.
Arguments:
- strain: bfloat16 [4, 2048, 7680], P('win', 'pair'), may hold values from -40 to 40
- pair_list: int32 [32, 2], replicated, may hold values from 0 to 15, as said below
- tile_live: int32 [32], P('pair'), may hold values 0 or 1
Outputs:
- stack: float32 [128, 32, 16, 128], P('win', 'pair')
Inputs may be any that keep to these rules, and one draw needn't show every extreme that they name: `pair_list`: rows q * 4 to (q + 1) * 4 - 1 are the tiles of owner q; the 8 block numbers in them fall into distinct groups of 2 consecutive blocks.
All inputs are finite; a program needn't handle non-finite values. No bound on the sum of `tile_live` on one device may be relied on, other than what follows from the above.
Results may differ from a plain program's by a relative error of at most 0.02.
Values may be sent and summed in bfloat16 or wider, within the bound.
No kernel may reach another device: no remote copies, remote signals or barrier semaphores. Data moves between devices by JAX's collectives and lax.ppermute only.
A program may use at most 64 MiB of HBM per device.

v0:
```python
import math

import jax
import jax.numpy as jnp
from jax import lax
from jax.sharding import PartitionSpec as P

C = 128
F = 384
LAGS = 16
DECIM = 32
B_DEV = 2


def dft_piece(first_row, row_count, sample_count, bin_count):
    sample_index = first_row + lax.iota(jnp.int32, row_count)
    bin_index = lax.iota(jnp.int32, bin_count) + 1
    product = sample_index[:, None] * bin_index[None, :] % sample_count
    angle = 2.0 * math.pi / sample_count * product.astype(jnp.float32)
    return jnp.concatenate([jnp.cos(angle), -jnp.sin(angle)], axis=1).astype(jnp.bfloat16)


def lag_tables(sample_count, bin_count, lag_count, stride):
    bin_index = lax.iota(jnp.int32, bin_count) + 1
    lag_shift = (lax.iota(jnp.int32, lag_count) - lag_count // 2) * stride
    product = bin_index[:, None] * lag_shift[None, :] % sample_count
    angle = 2.0 * math.pi / sample_count * product.astype(jnp.float32)
    return (jnp.cos(angle), jnp.sin(angle))


def whiten_rows(strain_rows, bin_count):
    row_total, sample_count = strain_rows.shape
    piece_len = sample_count // 4
    spectrum = jnp.zeros((row_total, 2 * bin_count), jnp.float32)
    for piece_index in range(4):
        dft_table = dft_piece(piece_index * piece_len, piece_len, sample_count, bin_count)
        samples_part = strain_rows[:, piece_index * piece_len : (piece_index + 1) * piece_len]
        spectrum = spectrum + jnp.dot(samples_part, dft_table, preferred_element_type=jnp.float32)
    real_part = spectrum[:, :bin_count]
    imag_part = spectrum[:, bin_count:]
    amplitude = jnp.sqrt(real_part * real_part + imag_part * imag_part)
    level = 0.2 * jnp.mean(amplitude, axis=1, keepdims=True) + 1e-06
    divisor = jnp.maximum(amplitude, level)
    return jnp.concatenate([real_part / divisor, imag_part / divisor], axis=1).astype(jnp.bfloat16)


def shift_block(spectrum_block, cos_lag, sin_lag):
    bin_count = cos_lag.shape[0]
    real_part = spectrum_block[:, :bin_count].astype(jnp.float32).T
    imag_part = spectrum_block[:, bin_count:].astype(jnp.float32).T
    upper_half = (
        real_part[:, None, :] * cos_lag[:, :, None] + imag_part[:, None, :] * sin_lag[:, :, None]
    )
    lower_half = (
        imag_part[:, None, :] * cos_lag[:, :, None] - real_part[:, None, :] * sin_lag[:, :, None]
    )
    joined = jnp.concatenate([upper_half, lower_half], axis=0).astype(jnp.bfloat16)
    return joined.reshape(2 * bin_count, -1)


def body(strain, pair_list, tile_live):
    window_count, local_rows, sample_count = strain.shape
    slot_count = tile_live.shape[0]
    pair_here = lax.axis_index("pair")
    flat_rows = strain.reshape(window_count * local_rows, sample_count)
    whitened = whiten_rows(flat_rows, F).reshape(window_count, B_DEV, C, 2 * F)
    local_blocks = jnp.transpose(whitened, (1, 0, 2, 3))
    wanted = lax.dynamic_slice_in_dim(pair_list, pair_here * slot_count, slot_count, 0).reshape(
        2 * slot_count
    )
    blank_slots = jnp.zeros((2 * slot_count,) + local_blocks.shape[1:], jnp.bfloat16)
    shard_rows = lax.all_gather(local_blocks, "pair", axis=0, tiled=True)
    block_count = shard_rows.shape[0]
    inside = (wanted >= 0) & (wanted < block_count)
    picked = jnp.take(shard_rows, jnp.clip(wanted, 0, block_count - 1), axis=0)
    needed = jnp.where(inside[:, None, None, None], picked, blank_slots)
    cos_lag, sin_lag = lag_tables(sample_count, F, LAGS, DECIM)
    own_rows = C // lax.axis_size("win")
    results = []
    for slot_index in range(slot_count):
        shifted = shift_block(needed[2 * slot_index + 1, 0], cos_lag, sin_lag)
        left_rows = needed[2 * slot_index, 0]
        summed = jnp.dot(left_rows, shifted, preferred_element_type=jnp.float32)
        results.append(summed)
    stacked = lax.psum_scatter(
        jnp.stack(results, axis=1).astype(jnp.bfloat16), "win", scatter_dimension=0, tiled=True
    ).astype(jnp.float32)
    live_local = tile_live.astype(jnp.float32)
    output = (
        stacked * live_local[None, :, None] / math.sqrt(F * window_count * lax.axis_size("win"))
    )
    return output.reshape(own_rows, slot_count, LAGS, C)


def solution(mesh):
    in_specs = (P("win", "pair", None), P(), P("pair"))
    out_specs = P("win", "pair", None, None)
    return jax.shard_map(body, mesh=mesh, in_specs=in_specs, out_specs=out_specs, check_vma=False)
```

profile of v0, /device:TPU:0, one launch (start us, length us, event | category | flops | bytes accessed | tf_op | source)
XLA Modules:
  0.0 182.1 jit_solution(2870586868444226078)
XLA Ops:
  6.6 50.0 %cosine_convert_fusion = (bf16[1920,384]{1,0:T(8,128)(2,1)S(1)}, bf16[1920,384]{1,0:T(8,128)(2,1)S(1)}, bf16[1920,384]{1,0:T(8,128)(2,1)S(1)}, bf16[1920,384]{1,...) fusion(s32[1920]{0:T(1024)S(1)} %get-tuple-element.47, ...), kind=kLoop, calls=%fused_computation.54 | loop fusion | flops 35389440 | bytes 11821056 | tf_op jit(solution)/shard_map/convert.36
  56.6 1.0 fusion.24
  57.6 1.0 fusion.86
  58.6 1.0 fusion.83
  59.6 1.0 fusion.80
  60.6 0.2 fusion.109
  60.8 0.2 divide_convert_fusion.1
  61.0 0.8 pad_maximum_fusion.1
  61.8 0.2 reduce-scatter.2.cloned.1.call-start
  62.1 0.1 dynamic-slice_clamp_fusion
  62.1 0.1 copy.43
  62.2 0.1 min.18
  62.3 0.1 min.16
  62.5 0.1 copy.42
  62.6 0.1 and.81
  62.7 0.2 fusion.98
  62.9 0.1 copy.48
  63.0 0.1 copy.50
  63.2 61.9 %all-gather.2.cloned.1.call-done = bf16[16,1,128,768]{3,2,1,0:T(8,128)(2,1)} async-done(((bf16[2,1,128,768]{3,2,1,0:T(8,128)(2,1)}), bf16[16,1,128,768]{3,2,1,0:T(8,128)(2,1)}) %all-gather.2.cloned.1.call-update) | async-done | bytes 3145744 | tf_op jit(solution)/shard_map/all_gather | solution.py:72
  125.1 2.5 %gather_fusion = bf16[8,128,768]{2,1,0:T(8,128)(2,1)S(1)} fusion(bf16[16,128,768]{2,1,0:T(8,128)(2,1)} %bitcast.116, s32[1024]{0:T(1024)S(1)} %pad_clamp_fusion), kind=kCustom, calls=%fused_computation | custom fusion | bytes 3145760 | tf_op jit(solution)/shard_map/jit(_take)/gather | solution.py:75
  127.7 0.2 fusion.76
  128.0 0.1 copy.47
  128.1 0.1 copy.49
  128.3 0.1 copy.51
  128.4 0.1 copy.52
  128.6 0.1 copy.53
  128.7 0.1 copy.54
  128.9 0.7 convert_bitcast_fusion.1
  129.6 0.1 copy.55
  129.7 1.1 copy.56
  130.8 4.3 %add_convert_fusion.3 = (bf16[384,16,128]{2,1,0:T(8,128)(2,1)S(1)}, bf16[384,16,128]{2,1,0:T(8,128)(2,1)S(1)}, bf16[384,16,128]{2,1,0:T(8,128)(2,1)S(1)}, bf16[3...) fusion(f32[384,16]{1,0:T(8,128)S(1)} %copy.50, ...), kind=kLoop, calls=%fused_computation.28 | loop fusion | flops 25165824 | bytes 14204928 | tf_op jit(solution)/shard_map/convert.31
  135.0 0.4 copy.81
  135.5 0.4 copy.82
  135.9 0.4 copy.79
  136.3 0.4 copy.80
  136.7 0.4 copy.77
  137.1 0.4 copy.78
  137.5 0.4 copy.75
  138.0 0.4 copy.76
  138.4 0.6 fusion.64
  139.0 0.6 fusion.67
  139.6 0.6 fusion.70
  140.2 0.6 fusion.73
  140.9 1.6 pad_maximum_fusion
  142.5 30.2 %reduce-scatter.2.cloned.1.call-done = bf16[32,4,2048]{2,0,1:T(8,128)(2,1)} async-done(((bf16[128,4,2048]{2,0,1:T(8,128)(2,1)}), bf16[32,4,2048]{2,0,1:T(8,128)(2,1)}) %reduce-scatter.2.cloned.1.call-update) | async-done | bytes 524304 | tf_op jit(solution)/shard_map/reduce_scatter | solution.py:85
  172.7 1.2 multiply_multiply_fusion
  174.0 0.2 copy.66
  174.1 1.1 copy.57
  (23 shorter events, 0.3 us)
Async XLA Ops:
  6.5 118.6 %all-gather.2.cloned.1.call-start = ((), (), s32[]{:S(2)}) async-start(), calls=%async_computation.1 | async-start | bytes 3538944 | tf_op jit(solution)/shard_map/all_gather | solution.py:72
  6.6 50.1 %copy-start.1 = (bf16[1,256,7680]{2,1,0:T(8,128)(2,1)S(1)}, bf16[1,256,7680]{2,1,0:T(8,128)(2,1)}, u32[]{:S(2)}) copy-start(bf16[1,256,7680]{2,1,0:T(8,128)(2,1)} %param.3) | copy-start | bytes 11796484
  60.6 1.5 copy-start
  61.8 110.9 %reduce-scatter.2.cloned.1.call-start = ((), (), s32[]{:S(2)}) async-start(), calls=%async_computation.2 | async-start | bytes 2621440 | tf_op jit(solution)/shard_map/reduce_scatter | solution.py:85
  140.9 1.6 copy-start.2
Sparse Core Ops, SparseCore 0:
  61.9 63.1 all-gather.1
  142.6 30.0 reduce-scatter.1
where the time goes:
time: 182 us
  waiting for transfers between devices  92.1 us (51%)
  other arithmetic  59.8 us (33%)
  between operations  13.8 us (8%)
  local copies, waits for them, and re-layouts  9.81 us (5%)
  matrix products  6.39 us (4%)
    all_gather x1, waiting for transfers between devices, body(): shard_rows = lax.all_gather(local_blocks, 'pair', axis=0, tiled=True)  61.9 us
    another operation x3, other arithmetic  54.5 us
    reduce_scatter x1, waiting for transfers between devices, body(): lax.psum_scatter(jnp.stack(results, axis=1).astype(jnp.bfloat16), 'win',...  30.2 us
    dot_general x4, matrix products, whiten_rows(): jnp.dot(samples_part, dft_table, preferred_element_type=jnp.float32)  3.91 us
  transfers between devices with their start and end apart: 2, of which 2 were waited for; matrix products, arithmetic and copies ran while one was open for 1% of the time, Pallas kernels for 0%

commit v1 on v0

v1 whole, which is shorter than its diff:
```python
import math

import jax
import jax.numpy as jnp
from jax import lax
from jax.sharding import PartitionSpec as P

C = 128
F = 384
LAGS = 16
DECIM = 32
SPLIT = 128


def cos_sin(product, sample_count):
    angle = 2.0 * math.pi / sample_count * (product % sample_count).astype(jnp.float32)
    return jnp.cos(angle), jnp.sin(angle)


def dft_table(sample_count, bin_count):
    bin_index = lax.iota(jnp.int32, bin_count) + 1
    coarse = lax.iota(jnp.int32, sample_count // SPLIT) * SPLIT
    fine = lax.iota(jnp.int32, SPLIT)
    ca, sa = cos_sin(coarse[:, None] * bin_index[None, :], sample_count)
    cb, sb = cos_sin(fine[:, None] * bin_index[None, :], sample_count)
    cos_t = ca[:, None, :] * cb[None, :, :] - sa[:, None, :] * sb[None, :, :]
    sin_t = sa[:, None, :] * cb[None, :, :] + ca[:, None, :] * sb[None, :, :]
    table = jnp.concatenate([cos_t, -sin_t], axis=2).astype(jnp.bfloat16)
    return table.reshape(sample_count, 2 * bin_count)


def whiten_rows(strain_rows, bin_count):
    sample_count = strain_rows.shape[1]
    spectrum = jnp.dot(strain_rows, dft_table(sample_count, bin_count), preferred_element_type=jnp.float32)
    real_part = spectrum[:, :bin_count]
    imag_part = spectrum[:, bin_count:]
    amplitude = jnp.sqrt(real_part * real_part + imag_part * imag_part)
    level = 0.2 * jnp.mean(amplitude, axis=1, keepdims=True) + 1e-06
    divisor = jnp.maximum(amplitude, level)
    return jnp.concatenate([real_part / divisor, imag_part / divisor], axis=1).astype(jnp.bfloat16)


def rotate(block, cos_r, sin_r):
    re = block[..., :F].astype(jnp.float32)[None]
    im = block[..., F:].astype(jnp.float32)[None]
    shape = (cos_r.shape[0],) + (1,) * (block.ndim - 1) + (F,)
    c = cos_r.reshape(shape)
    s = sin_r.reshape(shape)
    return jnp.concatenate([re * c - im * s, re * s + im * c], axis=-1).astype(jnp.bfloat16)


def body(strain, pair_list, tile_live):
    window_count, local_rows, sample_count = strain.shape
    slot_count = tile_live.shape[0]
    n_pair = lax.axis_size("pair")
    n_win = lax.axis_size("win")
    pair_here = lax.axis_index("pair")
    win_here = lax.axis_index("win")
    b_dev = local_rows // C

    flat_rows = strain.reshape(window_count * local_rows, sample_count)
    whitened = whiten_rows(flat_rows, F).reshape(window_count, b_dev, C, 2 * F)

    lists = pair_list.reshape(n_pair, 2 * slot_count)
    mine = (lists // b_dev) == pair_here
    local_pick = jnp.sum(jnp.where(mine, lists % b_dev, 0), axis=1)
    outgoing = jnp.take(jnp.transpose(whitened, (1, 0, 2, 3)), local_pick, axis=0)
    incoming = lax.all_to_all(outgoing, "pair", 0, 0, tiled=True)
    wanted = lax.dynamic_slice_in_dim(pair_list, pair_here * slot_count, slot_count, 0)
    left = jnp.take(incoming, wanted[:, 0] // b_dev, axis=0)
    right = jnp.take(incoming, wanted[:, 1] // b_dev, axis=0)

    sub = 4
    bins = lax.iota(jnp.int32, F) + 1
    fine_lag = lax.iota(jnp.int32, sub) * DECIM
    coarse_lag = (lax.iota(jnp.int32, LAGS // sub) * sub - LAGS // 2) * DECIM
    cf, sf = cos_sin(fine_lag[:, None] * bins[None, :], sample_count)
    cc, sc = cos_sin(coarse_lag[:, None] * bins[None, :], sample_count)
    left_t = rotate(left, cc, sc)
    right_t = rotate(right, cf, -sf)
    corr = jnp.einsum("atwic,btwjc->tiawbj", left_t, right_t, preferred_element_type=jnp.float32)
    corr = jnp.sum(corr, axis=3)
    corr = corr.reshape(slot_count, C, LAGS * C).astype(jnp.bfloat16)

    own_rows = C // n_win
    n_y = n_win // 2
    core = win_here % 2
    y_here = win_here // 2
    parts = jnp.transpose(corr.reshape(slot_count, n_y, 2, own_rows, LAGS * C), (1, 2, 3, 0, 4))
    send = jnp.take(parts, 1 - core, axis=1)
    keep = jnp.take(parts, core, axis=1).astype(jnp.float32)
    got = lax.ppermute(send, "win", [(w, w ^ 1) for w in range(n_win)])
    half = keep + got.astype(jnp.float32)
    total = jnp.take(half, y_here, axis=0)
    for shift in range(1, n_y):
        dest = (y_here + shift) % n_y
        piece = jnp.take(half, dest, axis=0).astype(jnp.bfloat16)
        perm = [(w, ((w // 2 + shift) % n_y) * 2 + w % 2) for w in range(n_win)]
        total = total + lax.ppermute(piece, "win", perm).astype(jnp.float32)

    live_local = tile_live.astype(jnp.float32)
    output = total * live_local[None, :, None] / math.sqrt(F * window_count * n_win)
    return output.reshape(own_rows, slot_count, LAGS, C)


def solution(mesh):
    in_specs = (P("win", "pair", None), P(), P("pair"))
    out_specs = P("win", "pair", None, None)
    return jax.shard_map(body, mesh=mesh, in_specs=in_specs, out_specs=out_specs, check_vma=False)
```

time: 182 us -> 92.2 us (0.51)
  other arithmetic: 59.8 us -> 13.9 us
  waiting for transfers between devices: 92.1 us -> 52 us
  between operations: 13.8 us -> 0.24 us
  starting transfers between devices: 0.22 us -> 8.84 us
  local copies, waits for them, and re-layouts: 9.81 us -> 11.7 us
    all_gather x1 -> x0, waiting for transfers between devices: 61.9 us -> none  [body(): shard_rows = lax.all_gather(local_blocks, 'pair', axis=0, tiled=True)]
    another operation x4 -> x3, other arithmetic: 56.1 us -> 5.55 us
    all_to_all x0 -> x1, waiting for transfers between devices: none -> 36.7 us  [body(): incoming = lax.all_to_all(outgoing, 'pair', 0, 0, tiled=True)]
    reduce_scatter x1 -> x0, waiting for transfers between devices: 30.2 us -> none  [body(): lax.psum_scatter(jnp.stack(results, axis=1).astype(jnp.bfloat16), 'win',...]
    ppermute x0 -> x2, waiting for transfers between devices: none -> 15.3 us  [the longest x1 12.4 us: body(): total = total + lax.ppermute(piece, 'win', perm).astype(jnp.float32)]
    all_to_all x0 -> x1, starting transfers between devices: none -> 7.25 us  [body(): incoming = lax.all_to_all(outgoing, 'pair', 0, 0, tiled=True)]
    convert_element_type x0 -> x2, local copies, waits for them, and re-layouts: none -> 6.18 us  [body(): corr = corr.reshape(slot_count, C, LAGS * C).astype(jnp.bfloat16)]
    select_n x2 -> x5, other arithmetic: 0.24 us -> 2.72 us  [the longest x2 1.37 us: body(): jnp.take(jnp.transpose(whitened, (1, 0, 2, 3)), local_pick, axis=0)]
  transfers between devices with their start and end apart: 2 -> 3, of which waited for: 2 -> 3; matrix products, arithmetic and copies ran while one was open for 1% -> 0% of each run, Pallas kernels for 0% -> 0%
where the time goes in v1:
time: 92.2 us; the launch traced here: 91.9 us
  waiting for transfers between devices  52 us (56%)
  other arithmetic  13.9 us (15%)
  local copies, waits for them, and re-layouts  11.7 us (13%)
  starting transfers between devices  8.84 us (10%)
  matrix products  5.27 us (6%)
    all_to_all x1, waiting for transfers between devices, body(): incoming = lax.all_to_all(outgoing, 'pair', 0, 0, tiled=True)  36.7 us
    ppermute x1, waiting for transfers between devices, body(): total = total + lax.ppermute(piece, 'win', perm).astype(jnp.float32)  12.4 us
    all_to_all x1, starting transfers between devices, body(): incoming = lax.all_to_all(outgoing, 'pair', 0, 0, tiled=True)  7.25 us
    convert_element_type x2, local copies, waits for them, and re-layouts, body(): corr = corr.reshape(slot_count, C, LAGS * C).astype(jnp.bfloat16)  6.18 us
    another operation x3, other arithmetic  5.55 us
    dot_general x1, matrix products, whiten_rows(): jnp.dot(strain_rows, dft_table(sample_count, bin_count), preferred_elemen...  3.2 us
    ppermute x1, waiting for transfers between devices, body(): got = lax.ppermute(send, 'win', [(w, w ^ 1) for w in range(n_win)])  2.87 us
    unnamed x11, local copies, waits for them, and re-layouts  2.41 us
  transfers between devices with their start and end apart: 3, of which 3 were waited for; matrix products, arithmetic and copies ran while one was open for 0% of the time, Pallas kernels for 0%

profile of v1, /device:TPU:0, one launch (start us, length us, event | category | flops | bytes accessed | tf_op | source)
XLA Modules:
  0.0 91.9 jit_solution(819970427564556267)
XLA Ops:
  0.0 0.7 fusion.51
  0.7 0.1 reduce_sum.32
  0.8 0.1 reduce_sum.33
  0.9 0.8 fusion.29
  1.7 0.5 fusion.36
  2.2 0.0 copy-start.3
  2.2 3.5 %subtract_convert_fusion = (bf16[60,128,384]{2,1,0:T(8,128)(2,1)S(1)}, bf16[60,128,384]{2,1,0:T(8,128)(2,1)S(1)}) fusion(f32[128,384]{1,0:T(8,128)S(1)} %get-tuple-element.55, f32[60,384]{1,0:T(8,128)S(1)} %get-tuple-element.51, f32[128,384]{1,0:T(8,128)S(1)} %get-tuple-element.54, f32[60,384]{1,0:T(8,128)S(1)} %get-tuple-element.50), kind=kLoop, calls=%fused_computation.8 | loop fusion | flops 26542080 | bytes 12374016 | tf_op jit(solution)/shard_map/convert.15
  5.7 0.0 copy-done.3
  5.7 3.2 %fusion.10 = f32[256,768]{1,0:T(8,128)S(1)} fusion(bf16[7680,384]{1,0:T(8,128)(2,1)S(1)} %bitcast.131, bf16[7680,384]{1,0:T(8,128)(2,1)S(1)} %bitcast.130, bf16[1,256,7680]{2,1,0:T(8,128)(2,1)S(1)} %copy-done.3), kind=kOutput, calls=%fused_computation.24 | convolution fusion | flops 3043491840 | bytes 16515072 | tf_op jit(solution)/shard_map/dot_general | solution.py:34
  9.0 0.2 fusion.55
  9.2 0.2 divide_convert_fusion.1
  9.5 0.6 gather_fusion
  10.1 0.0 copy-start.2
  10.1 1.4 %bitcast_select_fusion = bf16[8,1,128,768]{3,2,1,0:T(8,128)(2,1)} fusion(bf16[8,128,768]{2,1,0:T(8,128)(2,1)S(1)} %gather_fusion, pred[8]{0:T(512)(128)(4,1)S(1)} %compare_and_fusion.2), kind=kLoop, calls=%fused_computation.23 | loop fusion | flops 786432 | bytes 3145736 | tf_op jit(solution)/shard_map/jit(_take)/select_n | solution.py:67
  11.5 7.3 %all-to-all-start = ((bf16[8,1,128,768]{3,2,1,0:T(8,128)(2,1)}), bf16[8,1,128,768]{3,2,1,0:T(8,128)(2,1)S(1)}, u32[]{:S(2)}, u32[]{:S(2)}) async-start(bf16[8,1,128,768]{3,2,1,0:T(8,128)(2,1)} %bitcast_select_fusion), calls=%async_computation | async-start | bytes 3145728 | tf_op jit(solution)/shard_map/all_to_all | solution.py:68
  18.8 0.0 copy-done.2
  18.8 0.1 constant_dynamic-slice_fusion
  18.9 0.2 fusion.50
  19.1 36.7 %all-to-all-done = bf16[8,1,128,768]{3,2,1,0:T(8,128)(2,1)S(1)} async-done(((bf16[8,1,128,768]{3,2,1,0:T(8,128)(2,1)}), bf16[8,1,128,768]{3,2,1,0:T(8,128)(2,1)S(1)}, u32[]{:S(2)}, u32[]{:S(2)}) %all-to-all-start) | async-done | bytes 1572896 | tf_op jit(solution)/shard_map/all_to_all | solution.py:68
  55.7 0.6 gather_fusion.1
  56.3 0.1 bitcast_select_fusion.4
  56.5 1.0 %fusion.23 = (f32[4,128,384]{2,1,0:T(8,128)S(1)}, f32[4,128,384]{2,1,0:T(8,128)}) fusion(bf16[4,1,128,768]{3,2,0,1:T(8,128)(2,1)S(1)} %bitcast_select_fusion.4), kind=kLoop, calls=%fused_computation.43 | loop fusion | flops 393216 | bytes 2359296 | tf_op jit(solution)/shard_map/mul | solution.py:49
  57.5 0.6 gather_fusion.2
  58.1 0.0 copy-start.1
  58.1 0.1 bitcast_select_fusion.3
  58.2 0.1 fusion.21
  58.4 0.9 copy-done.1
  59.2 1.9 %subtract_convert_fusion.1 = (bf16[4,4,128,384]{3,2,0,1:T(8,128)(2,1)S(1)}, bf16[4,4,128,384]{3,2,0,1:T(8,128)(2,1)S(1)}, bf16[4,4,128,384]{3,2,0,1:T(8,128)(2,1)S(1)}, bf16[4,4,128,384]{3,2,0,1:T(8,128)(2,1)S(1)}) fusion(f32[4,384]{1,0:T(4,128)S(1)} %get-tuple-element.52, f32[4,128,384]{2,1,0:T(8,128)S(1)} %get-tuple-element.43, ...), kind=kLoop, calls=%fused_computation.18 | loop fusion | flops 12582912 | bytes 9461760 | tf_op jit(solution)/shard_map/convert.4
  61.1 2.1 %convert_bitcast_fusion = bf16[4,128,4,1,4,128]{1,5,2,4,0,3:T(8,128)(2,1)S(1)} fusion(bf16[4,4,128,384]{3,2,0,1:T(8,128)(2,1)S(1)} %get-tuple-element.37, bf16[4,4,128,384]{3,2,0,1:T(8,128)(2,1)S(1)} %get-tuple-element.36, bf16[4,4,128,384]{3,2,0,1:T(8,128)(2,1)S(1)} %get-tuple-element.58, bf16[4,4,128,384]{3,2,0,1:T(8,128)(2,1)S(1)} %get-tuple-element.59), kind=kOutput, calls=%fused_computation.22 | convolution fusion | flops 1624244224 | bytes 8388608 | tf_op jit(solution)/shard_map/atwic,btwjc->tiawbj/dot_general | solution.py:81
  63.2 2.9 %copy.8 = bf16[4,128,4,1,4,128]{5,4,2,1,0,3:T(4,128)(2,1)} copy(bf16[4,128,4,1,4,128]{1,5,2,4,0,3:T(8,128)(2,1)S(1)} %convert_bitcast_fusion) | data formatting | bytes 4194304 | tf_op jit(solution)/shard_map/convert_element_type | solution.py:83
  66.0 3.3 %convert_element_type.113 = bf16[4,2,2,32,2048]{4,3,2,1,0:T(8,128)(2,1)S(1)} reshape(bf16[4,128,4,1,4,128]{5,4,2,1,0,3:T(4,128)(2,1)} %copy.8) | data formatting | bytes 4194304 | tf_op jit(solution)/shard_map/convert_element_type | solution.py:83
  69.3 1.1 %select_bitcast_fusion = bf16[2,32,4,2048]{3,1,0,2:T(8,128)(2,1)} fusion(bf16[2,2,32,4,2048]{4,2,1,0,3:T(8,128)(2,1)S(1)} %bitcast.126, s32[]{:T(128)S(6)} %select_n.198, pred[]{:T(512)S(6)} %and.136), kind=kLoop, calls=%fused_computation.33 | loop fusion | flops 524288 | bytes 2097157 | tf_op jit(solution)/shard_map/jit(_take)/select_n | solution.py:90
  70.4 0.0 copy-start.4
  70.4 0.0 collective-permute-start
  70.4 2.9 %collective-permute-done = bf16[2,32,4,2048]{3,1,0,2:T(8,128)(2,1)S(1)} collective-permute-done((bf16[2,32,4,2048]{3,1,0,2:T(8,128)(2,1)}, bf16[2,32,4,2048]{3,1,0,2:T(8,128)(2,1)S(1)}, u32[]{:S(2)}, u32[]{:S(2)}) %collective-permute-start) | collective-permute-done | bytes 1048608 | tf_op jit(solution)/shard_map/ppermute | solution.py:92
  73.3 0.4 convert_add_fusion
  73.7 0.0 copy-start
  73.7 1.3 %copy-done = f32[2,32,4,2048]{3,1,0,2:T(8,128)} copy-done((f32[2,32,4,2048]{3,1,0,2:T(8,128)}, f32[2,32,4,2048]{3,1,0,2:T(8,128)S(1)}, u32[]{:S(2)}) %copy-start) | copy-done | bytes 2097176
  75.0 0.1 bitcast_convert_fusion
  75.1 1.6 %collective-permute-start.1 = (bf16[32,4,2048]{2,0,1:T(8,128)(2,1)S(1)}, bf16[32,4,2048]{2,0,1:T(8,128)(2,1)S(1)}, u32[]{:S(2)}, u32[]{:S(2)}) collective-permute-start(bf16[32,4,2048]{2,0,1:T(8,128)(2,1)S(1)} %bitcast_convert_fusion), channel_id=1, source_target_pairs={{0,16},{8,24},{16,0},{24,8},{1,17},{9,25},{17,1},{25,9},{2,18},{10... | collective-permute-start | bytes 1572872 | tf_op jit(solution)/shard_map/ppermute | solution.py:99
  76.7 0.0 copy-done.4
  76.7 12.4 %collective-permute-done.1 = bf16[32,4,2048]{2,0,1:T(8,128)(2,1)S(1)} collective-permute-done((bf16[32,4,2048]{2,0,1:T(8,128)(2,1)S(1)}, bf16[32,4,2048]{2,0,1:T(8,128)(2,1)S(1)}, u32[]{:S(2)}, u32[]{:S(2)}) %collective-permute-start.1) | collective-permute-done | bytes 524320 | tf_op jit(solution)/shard_map/ppermute | solution.py:99
  89.1 1.4 %fusion.18 = f32[32,4,2048]{2,0,1:T(8,128)S(1)} fusion(f32[2,32,4,2048]{3,1,0,2:T(8,128)} %copy-done, s32[]{:T(128)S(6)} %select_n.200, bf16[32,4,2048]{2,0,1:T(8,128)(2,1)S(1)} %collective-permute-done.1, f32[4]{0:T(128)S(1)} %convert_element_type.118, pred[]{:T(512)S(6)} %and.137), kind=kLoop, calls=%fused_computation.29 | loop fusion | flops 1310720 | bytes 2621461 | tf_op jit(solution)/shard_map/div | solution.py:102
  90.6 0.2 copy.16
  90.8 1.1 %copy.11 = f32[32,4,16,128]{3,2,1,0:T(8,128)} copy(f32[32,4,16,128]{3,2,0,1:T(8,128)S(1)} %bitcast.133) | data formatting | bytes 2097152 | tf_op jit(solution)/shard_map/reshape | solution.py:103
  (13 shorter events, 0.1 us)
Async XLA Ops:
  2.2 3.5 %copy-start.3 = (bf16[1,256,7680]{2,1,0:T(8,128)(2,1)S(1)}, bf16[1,256,7680]{2,1,0:T(8,128)(2,1)}, u32[]{:S(2)}) copy-start(bf16[1,256,7680]{2,1,0:T(8,128)(2,1)} %param.9) | copy-start | bytes 11796484
  10.1 8.6 %copy-start.2 = (s32[32,2]{0,1:T(2,128)S(1)}, s32[32,2]{0,1:T(2,128)}, u32[]{:S(2)}) copy-start(s32[32,2]{0,1:T(2,128)} %param.10) | copy-start | bytes 772
  11.5 44.3 %all-to-all-start = ((bf16[8,1,128,768]{3,2,1,0:T(8,128)(2,1)}), bf16[8,1,128,768]{3,2,1,0:T(8,128)(2,1)S(1)}, u32[]{:S(2)}, u32[]{:S(2)}) async-start(bf16[8,1,128,768]{3,2,1,0:T(8,128)(2,1)} %bitcast_select_fusion), calls=%async_computation | async-start | bytes 3145728 | tf_op jit(solution)/shard_map/all_to_all | solution.py:68
  58.1 1.1 %copy-start.1 = (f32[4,128,384]{2,1,0:T(8,128)S(1)}, f32[4,128,384]{2,1,0:T(8,128)}, u32[]{:S(2)}) copy-start(f32[4,128,384]{2,1,0:T(8,128)} %get-tuple-element.41) | copy-start | bytes 2359300
  70.4 6.3 %copy-start.4 = (s32[4]{0:T(128)S(1)}, s32[4]{0:T(128)}, u32[]{:S(2)}) copy-start(s32[4]{0:T(128)} %param.11) | copy-start | bytes 52
  70.4 2.9 %collective-permute-start = (bf16[2,32,4,2048]{3,1,0,2:T(8,128)(2,1)}, bf16[2,32,4,2048]{3,1,0,2:T(8,128)(2,1)S(1)}, u32[]{:S(2)}, u32[]{:S(2)}) collective-permute-start(bf16[2,32,4,2048]{3,1,0,2:T(8,128)(2,1)} %select_bitcast_fusion), channel_id=1, source_target_pairs={{0,8},{8,0},{16,24},{24,16},{1,9},{9,1},{17,25},{25,17},{2,10},{10... | collective-permute-start | bytes 3145736 | tf_op jit(solution)/shard_map/ppermute | solution.py:92
  73.7 1.3 %copy-start = (f32[2,32,4,2048]{3,1,0,2:T(8,128)}, f32[2,32,4,2048]{3,1,0,2:T(8,128)S(1)}, u32[]{:S(2)}) copy-start(f32[2,32,4,2048]{3,1,0,2:T(8,128)S(1)} %convert_add_fusion) | copy-start | bytes 6291460
  75.1 14.0 %collective-permute-start.1 = (bf16[32,4,2048]{2,0,1:T(8,128)(2,1)S(1)}, bf16[32,4,2048]{2,0,1:T(8,128)(2,1)S(1)}, u32[]{:S(2)}, u32[]{:S(2)}) collective-permute-start(bf16[32,4,2048]{2,0,1:T(8,128)(2,1)S(1)} %bitcast_convert_fusion), channel_id=1, source_target_pairs={{0,16},{8,24},{16,0},{24,8},{1,17},{9,25},{17,1},{25,9},{2,18},{10... | collective-permute-start | bytes 1572872 | tf_op jit(solution)/shard_map/ppermute | solution.py:99

commit v2 on v1

--- a/solution.py
+++ b/solution.py
@@ -1,8 +1,11 @@
+import functools
 import math
 
 import jax
 import jax.numpy as jnp
 from jax import lax
+from jax.experimental import pallas as pl
+from jax.experimental.pallas import tpu as pltpu
 from jax.sharding import PartitionSpec as P
 
 C = 128
@@ -40,13 +43,49 @@
     return jnp.concatenate([real_part / divisor, imag_part / divisor], axis=1).astype(jnp.bfloat16)
 
 
-def rotate(block, cos_r, sin_r):
-    re = block[..., :F].astype(jnp.float32)[None]
-    im = block[..., F:].astype(jnp.float32)[None]
-    shape = (cos_r.shape[0],) + (1,) * (block.ndim - 1) + (F,)
-    c = cos_r.reshape(shape)
-    s = sin_r.reshape(shape)
-    return jnp.concatenate([re * c - im * s, re * s + im * c], axis=-1).astype(jnp.bfloat16)
+def correlation_kernel(sub, cc_ref, sc_ref, cf_ref, sf_ref, left_ref, right_ref, out_ref):
+    window_count = left_ref.shape[1]
+    acc = None
+    for w in range(window_count):
+        lre = left_ref[0, w, :, :F].astype(jnp.float32)
+        lim = left_ref[0, w, :, F:].astype(jnp.float32)
+        rre = right_ref[0, w, :, :F].astype(jnp.float32)
+        rim = right_ref[0, w, :, F:].astype(jnp.float32)
+        turned = []
+        for l1 in range(sub):
+            c = cf_ref[l1 : l1 + 1, :]
+            s = sf_ref[l1 : l1 + 1, :]
+            turned.append(jnp.concatenate([rre * c + rim * s, rim * c - rre * s], axis=1).astype(jnp.bfloat16))
+        right_all = jnp.concatenate(turned, axis=0)
+        parts = []
+        for l2 in range(LAGS // sub):
+            c = cc_ref[l2 : l2 + 1, :]
+            s = sc_ref[l2 : l2 + 1, :]
+            left_t = jnp.concatenate([lre * c - lim * s, lre * s + lim * c], axis=1).astype(jnp.bfloat16)
+            parts.append(
+                lax.dot_general(left_t, right_all, (((1,), (1,)), ((), ())), preferred_element_type=jnp.float32)
+            )
+        acc = parts if acc is None else [a + p for a, p in zip(acc, parts)]
+    for l2, res in enumerate(acc):
+        for l1 in range(sub):
+            out_ref[:, 0, l2 * sub + l1, :] = res[:, l1 * C : (l1 + 1) * C].astype(out_ref.dtype)
+
+
+def tile_correlation(cc, sc, cf, sf, left, right, sub):
+    slot_count, window_count = left.shape[:2]
+    table_spec = pl.BlockSpec(cc.shape, lambda t: (0, 0))
+    block_spec = pl.BlockSpec((1, window_count, C, 2 * F), lambda t: (t, 0, 0, 0))
+    flops = 2 * slot_count * window_count * C * 2 * F * LAGS * C
+    return pl.pallas_call(
+        functools.partial(correlation_kernel, sub),
+        grid=(slot_count,),
+        in_specs=[table_spec] * 4 + [block_spec] * 2,
+        out_specs=pl.BlockSpec((C, 1, LAGS, C), lambda t: (0, t, 0, 0)),
+        out_shape=jax.ShapeDtypeStruct((C, slot_count, LAGS, C), jnp.bfloat16),
+        cost_estimate=pl.CostEstimate(
+            flops=flops, transcendentals=0, bytes_accessed=slot_count * (4 * window_count * C * F * 2 + 2 * C * LAGS * C)
+        ),
+    )(cc, sc, cf, sf, left, right)
 
 
 def body(strain, pair_list, tile_live):
@@ -71,24 +110,22 @@
     right = jnp.take(incoming, wanted[:, 1] // b_dev, axis=0)
 
     sub = 4
+    own_rows = C // n_win
+    n_y = n_win // 2
     bins = lax.iota(jnp.int32, F) + 1
     fine_lag = lax.iota(jnp.int32, sub) * DECIM
     coarse_lag = (lax.iota(jnp.int32, LAGS // sub) * sub - LAGS // 2) * DECIM
     cf, sf = cos_sin(fine_lag[:, None] * bins[None, :], sample_count)
     cc, sc = cos_sin(coarse_lag[:, None] * bins[None, :], sample_count)
-    left_t = rotate(left, cc, sc)
-    right_t = rotate(right, cf, -sf)
-    corr = jnp.einsum("atwic,btwjc->tiawbj", left_t, right_t, preferred_element_type=jnp.float32)
-    corr = jnp.sum(corr, axis=3)
-    corr = corr.reshape(slot_count, C, LAGS * C).astype(jnp.bfloat16)
+    left = left.reshape(slot_count, window_count, n_y, 2, own_rows, 2 * F)
+    left = jnp.transpose(left, (0, 1, 3, 2, 4, 5)).reshape(slot_count, window_count, C, 2 * F)
+    corr = tile_correlation(cc, sc, cf, sf, left, right, sub)
 
-    own_rows = C // n_win
-    n_y = n_win // 2
     core = win_here % 2
     y_here = win_here // 2
-    parts = jnp.transpose(corr.reshape(slot_count, n_y, 2, own_rows, LAGS * C), (1, 2, 3, 0, 4))
-    send = jnp.take(parts, 1 - core, axis=1)
-    keep = jnp.take(parts, core, axis=1).astype(jnp.float32)
+    parts = corr.reshape(2, n_y, own_rows, slot_count, LAGS, C)
+    send = jnp.take(parts, 1 - core, axis=0)
+    keep = jnp.take(parts, core, axis=0).astype(jnp.float32)
     got = lax.ppermute(send, "win", [(w, w ^ 1) for w in range(n_win)])
     half = keep + got.astype(jnp.float32)
     total = jnp.take(half, y_here, axis=0)
@@ -99,8 +136,7 @@
         total = total + lax.ppermute(piece, "win", perm).astype(jnp.float32)
 
     live_local = tile_live.astype(jnp.float32)
-    output = total * live_local[None, :, None] / math.sqrt(F * window_count * n_win)
-    return output.reshape(own_rows, slot_count, LAGS, C)
+    return total * live_local[None, :, None, None] / math.sqrt(F * window_count * n_win)
 
 
 def solution(mesh):

time: 92.2 us -> 91.5 us (level)
  Pallas kernels: 0 us -> 11 us
  local copies, waits for them, and re-layouts: 11.7 us -> 2.95 us
  matrix products: 5.27 us -> 3.2 us
    pallas_call x0 -> x1, Pallas kernels: none -> 11 us  [tile_correlation(): pl.pallas_call(functools.partial(correlation_kernel, sub), grid=(slot_cou...]
    convert_element_type x2 -> x0, local copies, waits for them, and re-layouts: 6.18 us -> none  [body(): corr = corr.reshape(slot_count, C, LAGS * C).astype(jnp.bfloat16)]
    unnamed x11 -> x6, local copies, waits for them, and re-layouts: 2.41 us -> 0.01 us
    dot_general x1 -> x0, matrix products: 2.07 us -> none  [body(): jnp.einsum('atwic,btwjc->tiawbj', left_t, right_t, preferred_element_type...]
    another operation x3 -> x2, other arithmetic: 5.55 us -> 3.7 us
    add x1, other arithmetic: 0.39 us -> 1.63 us  [body(): half = keep + got.astype(jnp.float32)]
    reshape x1 -> x0, local copies, waits for them, and re-layouts: 1.11 us -> none  [body(): return output.reshape(own_rows, slot_count, LAGS, C)]
    mul x3 -> x0, other arithmetic: 1.1 us -> none  [the longest x2 1.1 us: rotate(): re * c - im * s]
  transfers between devices with their start and end apart: 3 -> 3, of which waited for: 3 -> 3; matrix products, arithmetic and copies ran while one was open for 0% -> 1% of each run, Pallas kernels for 0% -> 0%
where the time goes in v2:
time: 91.5 us; the launch traced here: 91.2 us
  waiting for transfers between devices  51.1 us (56%)
  other arithmetic  13.8 us (15%)
  Pallas kernels  11 us (12%)
  starting transfers between devices  8.91 us (10%)
  matrix products  3.2 us (3%)
  local copies, waits for them, and re-layouts  2.95 us (3%)
    all_to_all x1, waiting for transfers between devices, body(): incoming = lax.all_to_all(outgoing, 'pair', 0, 0, tiled=True)  36.1 us
    ppermute x1, waiting for transfers between devices, body(): total = total + lax.ppermute(piece, 'win', perm).astype(jnp.float32)  12.4 us
    pallas_call x1, Pallas kernels, tile_correlation(): pl.pallas_call(functools.partial(correlation_kernel, sub), grid=(slot_cou...  11 us
    all_to_all x1, starting transfers between devices, body(): incoming = lax.all_to_all(outgoing, 'pair', 0, 0, tiled=True)  7.25 us
    another operation x2, other arithmetic  3.7 us
    dot_general x1, matrix products, whiten_rows(): jnp.dot(strain_rows, dft_table(sample_count, bin_count), preferred_elemen...  3.2 us
    ppermute x1, waiting for transfers between devices, body(): got = lax.ppermute(send, 'win', [(w, w ^ 1) for w in range(n_win)])  2.59 us
  transfers between devices with their start and end apart: 3, of which 3 were waited for; matrix products, arithmetic and copies ran while one was open for 1% of the time, Pallas kernels for 0%

profile of v2, /device:TPU:0, one launch (start us, length us, event | category | flops | bytes accessed | tf_op | source)
XLA Modules:
  0.0 91.2 jit_solution(16299996922222421783)
XLA Ops:
  0.0 0.7 fusion.40
  0.7 0.1 reduce_sum.28
  0.8 0.1 reduce_sum.29
  0.9 0.8 fusion.17
  1.7 0.5 fusion.24
  2.2 0.0 copy-start.1
  2.2 3.5 %subtract_convert_fusion = (bf16[60,128,384]{2,1,0:T(8,128)(2,1)S(1)}, bf16[60,128,384]{2,1,0:T(8,128)(2,1)S(1)}) fusion(f32[128,384]{1,0:T(8,128)S(1)} %get-tuple-element.45, f32[60,384]{1,0:T(8,128)S(1)} %get-tuple-element.39, f32[128,384]{1,0:T(8,128)S(1)} %get-tuple-element.44, f32[60,384]{1,0:T(8,128)S(1)} %get-tuple-element.38), kind=kLoop, calls=%fused_computation.8 | loop fusion | flops 26542080 | bytes 12374016 | tf_op jit(solution)/shard_map/convert.7
  5.7 0.0 copy-done.1
  5.7 3.2 %fusion.5 = f32[256,768]{1,0:T(8,128)S(1)} fusion(bf16[7680,384]{1,0:T(8,128)(2,1)S(1)} %bitcast.67, bf16[7680,384]{1,0:T(8,128)(2,1)S(1)} %bitcast.66, bf16[1,256,7680]{2,1,0:T(8,128)(2,1)S(1)} %copy-done.1), kind=kOutput, calls=%fused_computation.12 | convolution fusion | flops 3043491840 | bytes 16515072 | tf_op jit(solution)/shard_map/dot_general | solution.py:37
  9.0 0.2 fusion.43
  9.2 0.0 copy-start
  9.2 0.2 divide_convert_fusion.1
  9.5 0.6 gather_fusion
  10.1 1.4 %bitcast_select_fusion = bf16[8,1,128,768]{3,2,1,0:T(8,128)(2,1)} fusion(bf16[8,128,768]{2,1,0:T(8,128)(2,1)S(1)} %gather_fusion, pred[8]{0:T(512)(128)(4,1)S(1)} %compare_and_fusion.2), kind=kLoop, calls=%fused_computation.11 | loop fusion | flops 786432 | bytes 3145736 | tf_op jit(solution)/shard_map/jit(_take)/select_n | solution.py:106
  11.5 7.3 %all-to-all-start = ((bf16[8,1,128,768]{3,2,1,0:T(8,128)(2,1)}), bf16[8,1,128,768]{3,2,1,0:T(8,128)(2,1)S(1)}, u32[]{:S(2)}, u32[]{:S(2)}) async-start(bf16[8,1,128,768]{3,2,1,0:T(8,128)(2,1)} %bitcast_select_fusion), calls=%async_computation | async-start | bytes 3145728 | tf_op jit(solution)/shard_map/all_to_all | solution.py:107
  18.8 0.0 copy-done
  18.8 0.1 constant_dynamic-slice_fusion
  18.9 0.8 fusion.36
  19.7 36.1 %all-to-all-done = bf16[8,1,128,768]{3,2,1,0:T(8,128)(2,1)S(1)} async-done(((bf16[8,1,128,768]{3,2,1,0:T(8,128)(2,1)}), bf16[8,1,128,768]{3,2,1,0:T(8,128)(2,1)S(1)}, u32[]{:S(2)}, u32[]{:S(2)}) %all-to-all-start) | async-done | bytes 1572896 | tf_op jit(solution)/shard_map/all_to_all | solution.py:107
  55.8 0.6 gather_fusion.1
  56.4 0.1 bitcast_select_fusion.2
  56.5 0.9 %copy.5 = bf16[4,1,2,2,32,768]{5,4,3,2,0,1:T(8,128)(2,1)} copy(bf16[4,1,2,2,32,768]{5,4,2,3,0,1:T(8,128)(2,1)S(1)} %bitcast.68) | data formatting | bytes 1572864 | tf_op jit(solution)/shard_map/transpose | solution.py:121
  57.4 0.6 gather_fusion.2
  58.0 1.0 %bitcast_select_fusion.1.right_ref = bf16[4,1,128,768]{3,2,1,0:T(8,128)(2,1)} fusion(bf16[4,128,768]{2,1,0:T(8,128)(2,1)S(1)} %gather_fusion.2, pred[4]{0:T(512)(128)(4,1)S(1)} %get-tuple-element.30), kind=kLoop, calls=%fused_computation.18 | loop fusion | flops 393216 | bytes 1572868 | tf_op jit(solution)/shard_map/jit(_take)/select_n | solution.py:110
  59.1 0.0 copy-start.2
  59.1 11.0 %shard_map.37 = bf16[128,4,16,128]{3,2,1,0:T(8,128)(2,1)} custom-call(f32[4,384]{1,0:T(4,128)} %get-tuple-element.46.cc_ref, f32[4,384]{1,0:T(4,128)} %get-tuple-element.47.sc_ref, f32[4,384]{1,0:T(4,128)} %get-tuple-element.41.cf_ref, f32[4,384]{1,0:T(4,128)} %get-tuple-element.40.sf_ref, bf16[4,1,128,768]{3,2,1,0:T(8,128)(2,1)} %bitcast.71, ...), custom_call_target="tpu_custom_call" | custom-call | flops 1610612736 | bytes 3670016 | tf_op jit(solution)/shard_map/pallas_call | solution.py:79
  70.1 1.3 %select_bitcast_fusion = bf16[2,32,4,16,128]{4,3,2,1,0:T(8,128)(2,1)S(1)} fusion(bf16[2,2,32,4,16,128]{5,4,3,2,1,0:T(8,128)(2,1)} %bitcast.69, s32[]{:T(128)S(6)} %select_n.174, pred[]{:T(512)S(6)} %and.114), kind=kLoop, calls=%fused_computation.17 | loop fusion | flops 524288 | bytes 2097157 | tf_op jit(solution)/shard_map/jit(_take)/select_n | solution.py:127
  71.4 0.1 collective-permute-start
  71.6 2.6 %collective-permute-done = bf16[2,32,4,16,128]{4,3,2,1,0:T(8,128)(2,1)S(1)} collective-permute-done((bf16[2,32,4,16,128]{4,3,2,1,0:T(8,128)(2,1)S(1)}, bf16[2,32,4,16,128]{4,3,2,1,0:T(8,128)(2,1)S(1)}, u32[]{:S(2)}, u32[]{:S(2)}) %collective-permute-start) | collective-permute-done | bytes 1048608 | tf_op jit(solution)/shard_map/ppermute | solution.py:129
  74.2 1.6 %convert_add_fusion = f32[2,32,4,16,128]{4,3,2,1,0:T(8,128)S(1)} fusion(bf16[2,32,4,16,128]{4,3,2,1,0:T(8,128)(2,1)S(1)} %collective-permute-done, bf16[2,2,32,4,16,128]{5,4,3,2,1,0:T(8,128)(2,1)} %bitcast.70, s32[]{:T(128)S(6)} %select_n.172, pred[]{:T(512)S(6)} %and.113), kind=kLoop, calls=%fused_computation.10 | loop fusion | flops 2097152 | bytes 4194309 | tf_op jit(solution)/shard_map/add | solution.py:130
  75.8 0.1 bitcast_convert_fusion
  75.9 1.6 %collective-permute-start.1 = (bf16[32,4,16,128]{3,2,1,0:T(8,128)(2,1)S(1)}, bf16[32,4,16,128]{3,2,1,0:T(8,128)(2,1)S(1)}, u32[]{:S(2)}, u32[]{:S(2)}) collective-permute-start(bf16[32,4,16,128]{3,2,1,0:T(8,128)(2,1)S(1)} %bitcast_convert_fusion), channel_id=1, source_target_pairs={{0,16},{8,24},{16,0},{24,8},{1,17},{9,25},{17,1},{25,9},{2,18},{10... | collective-permute-start | bytes 1572872 | tf_op jit(solution)/shard_map/ppermute | solution.py:136
  77.5 0.0 copy-done.2
  77.5 12.4 %collective-permute-done.1 = bf16[32,4,16,128]{3,2,1,0:T(8,128)(2,1)S(1)} collective-permute-done((bf16[32,4,16,128]{3,2,1,0:T(8,128)(2,1)S(1)}, bf16[32,4,16,128]{3,2,1,0:T(8,128)(2,1)S(1)}, u32[]{:S(2)}, u32[]{:S(2)}) %collective-permute-start.1) | collective-permute-done | bytes 524320 | tf_op jit(solution)/shard_map/ppermute | solution.py:136
  90.0 1.2 %fusion.11 = f32[32,4,16,128]{3,2,1,0:T(8,128)} fusion(f32[2,32,4,16,128]{4,3,2,1,0:T(8,128)S(1)} %convert_add_fusion, s32[]{:T(128)S(6)} %select_n.176, bf16[32,4,16,128]{3,2,1,0:T(8,128)(2,1)S(1)} %collective-permute-done.1, f32[4]{0:T(128)S(1)} %convert_element_type.67, pred[]{:T(512)S(6)} %and.115), kind=kLoop, calls=%fused_computation.16 | loop fusion | flops 1310720 | bytes 2621461 | tf_op jit(solution)/shard_map/div | solution.py:139
  (11 shorter events, 0.1 us)
Async XLA Ops:
  2.2 3.5 %copy-start.1 = (bf16[1,256,7680]{2,1,0:T(8,128)(2,1)S(1)}, bf16[1,256,7680]{2,1,0:T(8,128)(2,1)}, u32[]{:S(2)}) copy-start(bf16[1,256,7680]{2,1,0:T(8,128)(2,1)} %param.9) | copy-start | bytes 11796484
  9.2 9.6 %copy-start = (s32[32,2]{0,1:T(2,128)S(1)}, s32[32,2]{0,1:T(2,128)}, u32[]{:S(2)}) copy-start(s32[32,2]{0,1:T(2,128)} %param.10) | copy-start | bytes 772
  11.5 44.3 %all-to-all-start = ((bf16[8,1,128,768]{3,2,1,0:T(8,128)(2,1)}), bf16[8,1,128,768]{3,2,1,0:T(8,128)(2,1)S(1)}, u32[]{:S(2)}, u32[]{:S(2)}) async-start(bf16[8,1,128,768]{3,2,1,0:T(8,128)(2,1)} %bitcast_select_fusion), calls=%async_computation | async-start | bytes 3145728 | tf_op jit(solution)/shard_map/all_to_all | solution.py:107
  59.1 18.4 %copy-start.2 = (s32[4]{0:T(128)S(1)}, s32[4]{0:T(128)}, u32[]{:S(2)}) copy-start(s32[4]{0:T(128)} %param.11) | copy-start | bytes 52
  71.4 2.7 %collective-permute-start = (bf16[2,32,4,16,128]{4,3,2,1,0:T(8,128)(2,1)S(1)}, bf16[2,32,4,16,128]{4,3,2,1,0:T(8,128)(2,1)S(1)}, u32[]{:S(2)}, u32[]{:S(2)}) collective-permute-start(bf16[2,32,4,16,128]{4,3,2,1,0:T(8,128)(2,1)S(1)} %select_bitcast_fusion), channel_id=1, source_target_pairs={{0,8},{8,0},{16,24},{24,16},{1,9},{9,1},{17,25},{25,17},{2,10},{10... | collective-permute-start | bytes 3145736 | tf_op jit(solution)/shard_map/ppermute | solution.py:129
  75.9 14.0 %collective-permute-start.1 = (bf16[32,4,16,128]{3,2,1,0:T(8,128)(2,1)S(1)}, bf16[32,4,16,128]{3,2,1,0:T(8,128)(2,1)S(1)}, u32[]{:S(2)}, u32[]{:S(2)}) collective-permute-start(bf16[32,4,16,128]{3,2,1,0:T(8,128)(2,1)S(1)} %bitcast_convert_fusion), channel_id=1, source_target_pairs={{0,16},{8,24},{16,0},{24,8},{1,17},{9,25},{17,1},{25,9},{2,18},{10... | collective-permute-start | bytes 1572872 | tf_op jit(solution)/shard_map/ppermute | solution.py:136

commit v3 on v2

--- a/solution.py
+++ b/solution.py
@@ -49,21 +49,21 @@
     for w in range(window_count):
         lre = left_ref[0, w, :, :F].astype(jnp.float32)
         lim = left_ref[0, w, :, F:].astype(jnp.float32)
-        rre = right_ref[0, w, :, :F].astype(jnp.float32)
-        rim = right_ref[0, w, :, F:].astype(jnp.float32)
+        rre = right_ref[0, w, :F, :].astype(jnp.float32)
+        rim = right_ref[0, w, F:, :].astype(jnp.float32)
         turned = []
         for l1 in range(sub):
-            c = cf_ref[l1 : l1 + 1, :]
-            s = sf_ref[l1 : l1 + 1, :]
-            turned.append(jnp.concatenate([rre * c + rim * s, rim * c - rre * s], axis=1).astype(jnp.bfloat16))
-        right_all = jnp.concatenate(turned, axis=0)
+            c = cf_ref[:, l1 : l1 + 1]
+            s = sf_ref[:, l1 : l1 + 1]
+            turned.append(jnp.concatenate([rre * c + rim * s, rim * c - rre * s], axis=0).astype(jnp.bfloat16))
+        right_all = jnp.concatenate(turned, axis=1)
         parts = []
         for l2 in range(LAGS // sub):
             c = cc_ref[l2 : l2 + 1, :]
             s = sc_ref[l2 : l2 + 1, :]
             left_t = jnp.concatenate([lre * c - lim * s, lre * s + lim * c], axis=1).astype(jnp.bfloat16)
             parts.append(
-                lax.dot_general(left_t, right_all, (((1,), (1,)), ((), ())), preferred_element_type=jnp.float32)
+                jnp.dot(left_t, right_all, preferred_element_type=jnp.float32)
             )
         acc = parts if acc is None else [a + p for a, p in zip(acc, parts)]
     for l2, res in enumerate(acc):
@@ -74,12 +74,14 @@
 def tile_correlation(cc, sc, cf, sf, left, right, sub):
     slot_count, window_count = left.shape[:2]
     table_spec = pl.BlockSpec(cc.shape, lambda t: (0, 0))
+    column_spec = pl.BlockSpec(cf.shape, lambda t: (0, 0))
     block_spec = pl.BlockSpec((1, window_count, C, 2 * F), lambda t: (t, 0, 0, 0))
+    right_spec = pl.BlockSpec((1, window_count, 2 * F, C), lambda t: (t, 0, 0, 0))
     flops = 2 * slot_count * window_count * C * 2 * F * LAGS * C
     return pl.pallas_call(
         functools.partial(correlation_kernel, sub),
         grid=(slot_count,),
-        in_specs=[table_spec] * 4 + [block_spec] * 2,
+        in_specs=[table_spec] * 2 + [column_spec] * 2 + [block_spec, right_spec],
         out_specs=pl.BlockSpec((C, 1, LAGS, C), lambda t: (0, t, 0, 0)),
         out_shape=jax.ShapeDtypeStruct((C, slot_count, LAGS, C), jnp.bfloat16),
         cost_estimate=pl.CostEstimate(
@@ -103,11 +105,11 @@
     lists = pair_list.reshape(n_pair, 2 * slot_count)
     mine = (lists // b_dev) == pair_here
     local_pick = jnp.sum(jnp.where(mine, lists % b_dev, 0), axis=1)
-    outgoing = jnp.take(jnp.transpose(whitened, (1, 0, 2, 3)), local_pick, axis=0)
+    outgoing = jnp.take(jnp.transpose(whitened, (1, 0, 2, 3)), local_pick, axis=0, mode="clip")
     incoming = lax.all_to_all(outgoing, "pair", 0, 0, tiled=True)
     wanted = lax.dynamic_slice_in_dim(pair_list, pair_here * slot_count, slot_count, 0)
-    left = jnp.take(incoming, wanted[:, 0] // b_dev, axis=0)
-    right = jnp.take(incoming, wanted[:, 1] // b_dev, axis=0)
+    left = jnp.take(incoming, wanted[:, 0] // b_dev, axis=0, mode="clip")
+    right = jnp.take(incoming, wanted[:, 1] // b_dev, axis=0, mode="clip")
 
     sub = 4
     own_rows = C // n_win
@@ -119,19 +121,20 @@
     cc, sc = cos_sin(coarse_lag[:, None] * bins[None, :], sample_count)
     left = left.reshape(slot_count, window_count, n_y, 2, own_rows, 2 * F)
     left = jnp.transpose(left, (0, 1, 3, 2, 4, 5)).reshape(slot_count, window_count, C, 2 * F)
-    corr = tile_correlation(cc, sc, cf, sf, left, right, sub)
+    right = jnp.swapaxes(right, 2, 3)
+    corr = tile_correlation(cc, sc, cf.T, sf.T, left, right, sub)
 
     core = win_here % 2
     y_here = win_here // 2
     parts = corr.reshape(2, n_y, own_rows, slot_count, LAGS, C)
-    send = jnp.take(parts, 1 - core, axis=0)
-    keep = jnp.take(parts, core, axis=0).astype(jnp.float32)
+    send = jnp.take(parts, 1 - core, axis=0, mode="clip")
+    keep = jnp.take(parts, core, axis=0, mode="clip").astype(jnp.float32)
     got = lax.ppermute(send, "win", [(w, w ^ 1) for w in range(n_win)])
     half = keep + got.astype(jnp.float32)
-    total = jnp.take(half, y_here, axis=0)
+    total = jnp.take(half, y_here, axis=0, mode="clip")
     for shift in range(1, n_y):
         dest = (y_here + shift) % n_y
-        piece = jnp.take(half, dest, axis=0).astype(jnp.bfloat16)
+        piece = jnp.take(half, dest, axis=0, mode="clip").astype(jnp.bfloat16)
         perm = [(w, ((w // 2 + shift) % n_y) * 2 + w % 2) for w in range(n_win)]
         total = total + lax.ppermute(piece, "win", perm).astype(jnp.float32)
 

time: 91.5 us -> 91.3 us (level)
  local copies, waits for them, and re-layouts: 2.95 us -> 6.91 us
  other arithmetic: 13.8 us -> 10.6 us
  waiting for transfers between devices: 51.1 us -> 49.5 us
    select_n x5 -> x1, other arithmetic: 3.86 us -> 0.01 us  [body(): right = jnp.take(incoming, wanted[:, 1] // b_dev, axis=0, mode='clip')]
    gather x3 -> x5, local copies, waits for them, and re-layouts: 1.84 us -> 5.57 us  [the longest x1 1.8 us: body(): jnp.take(jnp.transpose(whitened, (1, 0, 2, 3)), local_pick, axis=0, mode=...]
    all_to_all x1, waiting for transfers between devices: 36.1 us -> 34.4 us  [body(): incoming = lax.all_to_all(outgoing, 'pair', 0, 0, tiled=True)]
    sin x1 -> x2, other arithmetic: 0.79 us -> 2.2 us  [cos_sin(): return (jnp.cos(angle), jnp.sin(angle))]
  transfers between devices with their start and end apart: 3 -> 3, of which waited for: 3 -> 3; matrix products, arithmetic and copies ran while one was open for 1% -> 3% of each run, Pallas kernels for 0% -> 0%
where the time goes in v3:
time: 91.3 us; the launch traced here: 91 us
  waiting for transfers between devices  49.5 us (54%)
  Pallas kernels  11.7 us (13%)
  other arithmetic  10.6 us (12%)
  starting transfers between devices  8.91 us (10%)
  local copies, waits for them, and re-layouts  6.91 us (8%)
  matrix products  3.2 us (4%)
    all_to_all x1, waiting for transfers between devices, body(): incoming = lax.all_to_all(outgoing, 'pair', 0, 0, tiled=True)  34.4 us
    ppermute x1, waiting for transfers between devices, body(): total = total + lax.ppermute(piece, 'win', perm).astype(jnp.float32)  12.4 us
    pallas_call x1, Pallas kernels, tile_correlation(): pl.pallas_call(functools.partial(correlation_kernel, sub), grid=(slot_cou...  11.7 us
    all_to_all x1, starting transfers between devices, body(): incoming = lax.all_to_all(outgoing, 'pair', 0, 0, tiled=True)  7.25 us
    another operation x2, other arithmetic  3.7 us
    dot_general x1, matrix products, whiten_rows(): jnp.dot(strain_rows, dft_table(sample_count, bin_count), preferred_elemen...  3.2 us
    ppermute x1, waiting for transfers between devices, body(): got = lax.ppermute(send, 'win', [(w, w ^ 1) for w in range(n_win)])  2.62 us
    sin x2, other arithmetic, cos_sin(): return (jnp.cos(angle), jnp.sin(angle))  2.2 us
  transfers between devices with their start and end apart: 3, of which 3 were waited for; matrix products, arithmetic and copies ran while one was open for 3% of the time, Pallas kernels for 0%

profile of v3, /device:TPU:0, one launch (start us, length us, event | category | flops | bytes accessed | tf_op | source)
XLA Modules:
  0.0 91.0 jit_solution(10766166520522156660)
XLA Ops:
  0.0 0.8 fusion.18
  0.8 0.5 fusion.25
  1.3 0.0 copy-start.1
  1.3 3.5 %subtract_convert_fusion = (bf16[60,128,384]{2,1,0:T(8,128)(2,1)S(1)}, bf16[60,128,384]{2,1,0:T(8,128)(2,1)S(1)}) fusion(f32[128,384]{1,0:T(8,128)S(1)} %get-tuple-element.60, f32[60,384]{1,0:T(8,128)S(1)} %get-tuple-element.56, f32[128,384]{1,0:T(8,128)S(1)} %get-tuple-element.59, f32[60,384]{1,0:T(8,128)S(1)} %get-tuple-element.55), kind=kLoop, calls=%fused_computation.8 | loop fusion | flops 26542080 | bytes 12374016 | tf_op jit(solution)/shard_map/convert.7
  4.8 0.0 copy-done.1
  4.8 0.0 copy-start
  4.8 3.2 %fusion.5 = f32[256,768]{1,0:T(8,128)S(1)} fusion(bf16[7680,384]{1,0:T(8,128)(2,1)S(1)} %bitcast.43, bf16[7680,384]{1,0:T(8,128)(2,1)S(1)} %bitcast.42, bf16[1,256,7680]{2,1,0:T(8,128)(2,1)S(1)} %copy-done.1), kind=kOutput, calls=%fused_computation.11 | convolution fusion | flops 3043491840 | bytes 16515072 | tf_op jit(solution)/shard_map/dot_general | solution.py:37
  8.0 0.2 fusion.42
  8.3 0.2 divide_convert_fusion.1
  8.5 0.0 copy-done
  8.5 0.1 reduce_sum.27
  8.6 0.1 reduce_sum.28
  8.8 1.8 %gather_fusion = bf16[8,128,768]{2,1,0:T(8,128)(2,1)} fusion(bf16[2,128,768]{2,1,0:T(8,128)(2,1)S(1)} %maximum_bitcast_fusion, s32[1024]{0:T(1024)S(1)} %pad_clamp_fusion.2), kind=kCustom, calls=%fused_computation | custom fusion | bytes 3145760 | tf_op jit(solution)/shard_map/jit(_take)/gather | solution.py:108
  10.6 7.3 %all-to-all-start = ((bf16[8,1,128,768]{3,2,1,0:T(8,128)(2,1)}), bf16[8,1,128,768]{3,2,1,0:T(8,128)(2,1)S(1)}, u32[]{:S(2)}, u32[]{:S(2)}) async-start(bf16[8,1,128,768]{3,2,1,0:T(8,128)(2,1)} %bitcast.7), calls=%async_computation | async-start | bytes 3145728 | tf_op jit(solution)/shard_map/all_to_all | solution.py:109
  17.8 0.1 fusion.29
  17.9 0.1 copy.8
  18.1 0.1 constant_dynamic-slice_fusion
  18.2 0.7 fusion.36
  18.9 1.5 %multiply_sine_fusion = (f32[384,4]{1,0:T(8,128)}, f32[384,4]{1,0:T(8,128)}) fusion(f32[384,4]{1,0:T(8,128)S(1)} %copy.8), kind=kLoop, calls=%fused_computation.31 | loop fusion | flops 1536 | bytes 18432 | tf_op jit(solution)/shard_map/sin | solution.py:20
  20.4 34.4 %all-to-all-done = bf16[8,1,128,768]{3,2,1,0:T(8,128)(2,1)S(1)} async-done(((bf16[8,1,128,768]{3,2,1,0:T(8,128)(2,1)}), bf16[8,1,128,768]{3,2,1,0:T(8,128)(2,1)S(1)}, u32[]{:S(2)}, u32[]{:S(2)}) %all-to-all-start) | async-done | bytes 1572896 | tf_op jit(solution)/shard_map/all_to_all | solution.py:109
  54.8 0.6 gather_fusion.2
  55.4 1.2 %copy.10 = bf16[4,128,768]{1,2,0:T(8,128)(2,1)} copy(bf16[4,128,768]{2,1,0:T(8,128)(2,1)S(1)} %gather_fusion.2) | data formatting | bytes 1572864 | tf_op jit(solution)/shard_map/jit(_take)/gather | solution.py:112
  56.6 0.6 gather_fusion.1
  57.2 0.9 %copy.9 = bf16[4,1,2,2,32,768]{5,4,3,2,0,1:T(8,128)(2,1)} copy(bf16[4,1,2,2,32,768]{5,4,2,3,0,1:T(8,128)(2,1)S(1)} %bitcast.44) | data formatting | bytes 1572864 | tf_op jit(solution)/shard_map/transpose | solution.py:123
  58.1 0.0 copy-start.2
  58.1 11.7 %shard_map.37 = bf16[128,4,16,128]{3,2,1,0:T(8,128)(2,1)} custom-call(f32[4,384]{1,0:T(4,128)} %get-tuple-element.58.cc_ref, f32[4,384]{1,0:T(4,128)} %get-tuple-element.57.sc_ref, f32[384,4]{1,0:T(8,128)} %get-tuple-element.54.cf_ref, f32[384,4]{1,0:T(8,128)} %get-tuple-element.53.sf_ref, bf16[4,1,128,768]{3,2,1,0:T(8,128)(2,1)} %bitcast.48, ...), custom_call_target="tpu_custom_call" | custom-call | flops 1610612736 | bytes 3670016 | tf_op jit(solution)/shard_map/pallas_call | solution.py:81
  69.8 1.4 %dynamic-slice_bitcast_fusion = bf16[2,32,4,16,128]{4,3,2,1,0:T(8,128)(2,1)S(1)} fusion(bf16[2,2,32,4,16,128]{5,4,3,2,1,0:T(8,128)(2,1)} %bitcast.45, s32[]{:T(128)S(6)} %sub.38), kind=kLoop, calls=%fused_computation.16 | loop fusion | bytes 2097156 | tf_op jit(solution)/shard_map/jit(_take)/gather | solution.py:130
  71.2 0.1 collective-permute-start
  71.3 2.6 %collective-permute-done = bf16[2,32,4,16,128]{4,3,2,1,0:T(8,128)(2,1)S(1)} collective-permute-done((bf16[2,32,4,16,128]{4,3,2,1,0:T(8,128)(2,1)S(1)}, bf16[2,32,4,16,128]{4,3,2,1,0:T(8,128)(2,1)S(1)}, u32[]{:S(2)}, u32[]{:S(2)}) %collective-permute-start) | collective-permute-done | bytes 1048608 | tf_op jit(solution)/shard_map/ppermute | solution.py:132
  74.0 1.6 %convert_add_fusion = f32[2,32,4,16,128]{4,3,2,1,0:T(8,128)S(1)} fusion(bf16[2,32,4,16,128]{4,3,2,1,0:T(8,128)(2,1)S(1)} %collective-permute-done, bf16[2,2,32,4,16,128]{5,4,3,2,1,0:T(8,128)(2,1)} %bitcast.46, s32[]{:T(128)S(6)} %select_n.102), kind=kLoop, calls=%fused_computation.10 | loop fusion | flops 1572864 | bytes 4194308 | tf_op jit(solution)/shard_map/add | solution.py:133
  75.6 0.1 fusion.12
  75.7 1.6 %collective-permute-start.1 = (bf16[32,4,16,128]{3,2,1,0:T(8,128)(2,1)S(1)}, bf16[32,4,16,128]{3,2,1,0:T(8,128)(2,1)S(1)}, u32[]{:S(2)}, u32[]{:S(2)}) collective-permute-start(bf16[32,4,16,128]{3,2,1,0:T(8,128)(2,1)S(1)} %fusion.12), channel_id=1, source_target_pairs={{0,16},{8,24},{16,0},{24,8},{1,17},{9,25},{17,1},{25,9},{2,18},{10... | collective-permute-start | bytes 1572872 | tf_op jit(solution)/shard_map/ppermute | solution.py:139
  77.3 0.0 copy-done.2
  77.3 12.4 %collective-permute-done.1 = bf16[32,4,16,128]{3,2,1,0:T(8,128)(2,1)S(1)} collective-permute-done((bf16[32,4,16,128]{3,2,1,0:T(8,128)(2,1)S(1)}, bf16[32,4,16,128]{3,2,1,0:T(8,128)(2,1)S(1)}, u32[]{:S(2)}, u32[]{:S(2)}) %collective-permute-start.1) | collective-permute-done | bytes 524320 | tf_op jit(solution)/shard_map/ppermute | solution.py:139
  89.7 1.3 %fusion.11 = f32[32,4,16,128]{3,2,1,0:T(8,128)} fusion(f32[2,32,4,16,128]{4,3,2,1,0:T(8,128)S(1)} %convert_add_fusion, s32[]{:T(128)S(6)} %select_n.103, bf16[32,4,16,128]{3,2,1,0:T(8,128)(2,1)S(1)} %collective-permute-done.1, f32[4]{0:T(128)S(1)} %convert_element_type.69), kind=kLoop, calls=%fused_computation.14 | loop fusion | flops 1048576 | bytes 2621460 | tf_op jit(solution)/shard_map/div | solution.py:142
  (11 shorter events, 0.1 us)
Async XLA Ops:
  1.3 3.5 %copy-start.1 = (bf16[1,256,7680]{2,1,0:T(8,128)(2,1)S(1)}, bf16[1,256,7680]{2,1,0:T(8,128)(2,1)}, u32[]{:S(2)}) copy-start(bf16[1,256,7680]{2,1,0:T(8,128)(2,1)} %param.3) | copy-start | bytes 11796484
  4.8 3.7 %copy-start = (s32[32,2]{0,1:T(2,128)S(1)}, s32[32,2]{0,1:T(2,128)}, u32[]{:S(2)}) copy-start(s32[32,2]{0,1:T(2,128)} %param.4) | copy-start | bytes 772
  10.6 44.3 %all-to-all-start = ((bf16[8,1,128,768]{3,2,1,0:T(8,128)(2,1)}), bf16[8,1,128,768]{3,2,1,0:T(8,128)(2,1)S(1)}, u32[]{:S(2)}, u32[]{:S(2)}) async-start(bf16[8,1,128,768]{3,2,1,0:T(8,128)(2,1)} %bitcast.7), calls=%async_computation | async-start | bytes 3145728 | tf_op jit(solution)/shard_map/all_to_all | solution.py:109
  58.1 19.1 %copy-start.2 = (s32[4]{0:T(128)S(1)}, s32[4]{0:T(128)}, u32[]{:S(2)}) copy-start(s32[4]{0:T(128)} %param.5) | copy-start | bytes 52
  71.2 2.7 %collective-permute-start = (bf16[2,32,4,16,128]{4,3,2,1,0:T(8,128)(2,1)S(1)}, bf16[2,32,4,16,128]{4,3,2,1,0:T(8,128)(2,1)S(1)}, u32[]{:S(2)}, u32[]{:S(2)}) collective-permute-start(bf16[2,32,4,16,128]{4,3,2,1,0:T(8,128)(2,1)S(1)} %dynamic-slice_bitcast_fusion), channel_id=1, source_target_pairs={{0,8},{8,0},{16,24},{24,16},{1,9},{9,1},{17,25},{25,17},{2,10},{10... | collective-permute-start | bytes 3145736 | tf_op jit(solution)/shard_map/ppermute | solution.py:132
  75.7 14.0 %collective-permute-start.1 = (bf16[32,4,16,128]{3,2,1,0:T(8,128)(2,1)S(1)}, bf16[32,4,16,128]{3,2,1,0:T(8,128)(2,1)S(1)}, u32[]{:S(2)}, u32[]{:S(2)}) collective-permute-start(bf16[32,4,16,128]{3,2,1,0:T(8,128)(2,1)S(1)} %fusion.12), channel_id=1, source_target_pairs={{0,16},{8,24},{16,0},{24,8},{1,17},{9,25},{17,1},{25,9},{2,18},{10... | collective-permute-start | bytes 1572872 | tf_op jit(solution)/shard_map/ppermute | solution.py:139

commit v4 on v3

--- a/solution.py
+++ b/solution.py
@@ -53,15 +53,21 @@
         rim = right_ref[0, w, F:, :].astype(jnp.float32)
         turned = []
         for l1 in range(sub):
+            if l1 == 0:
+                turned.append(right_ref[0, w])
+                continue
             c = cf_ref[:, l1 : l1 + 1]
             s = sf_ref[:, l1 : l1 + 1]
             turned.append(jnp.concatenate([rre * c + rim * s, rim * c - rre * s], axis=0).astype(jnp.bfloat16))
         right_all = jnp.concatenate(turned, axis=1)
         parts = []
         for l2 in range(LAGS // sub):
-            c = cc_ref[l2 : l2 + 1, :]
-            s = sc_ref[l2 : l2 + 1, :]
-            left_t = jnp.concatenate([lre * c - lim * s, lre * s + lim * c], axis=1).astype(jnp.bfloat16)
+            if l2 * sub == LAGS // 2:
+                left_t = left_ref[0, w]
+            else:
+                c = cc_ref[l2 : l2 + 1, :]
+                s = sc_ref[l2 : l2 + 1, :]
+                left_t = jnp.concatenate([lre * c - lim * s, lre * s + lim * c], axis=1).astype(jnp.bfloat16)
             parts.append(
                 jnp.dot(left_t, right_all, preferred_element_type=jnp.float32)
             )
@@ -88,6 +94,22 @@
             flops=flops, transcendentals=0, bytes_accessed=slot_count * (4 * window_count * C * F * 2 + 2 * C * LAGS * C)
         ),
     )(cc, sc, cf, sf, left, right)
+
+
+def window_sum(corr, core, y_here, n_win, own_rows):
+    n_y = n_win // 2
+    parts = corr.reshape((2, n_y, own_rows) + corr.shape[1:])
+    send = jnp.take(parts, 1 - core, axis=0, mode="clip")
+    keep = jnp.take(parts, core, axis=0, mode="clip").astype(jnp.float32)
+    got = lax.ppermute(send, "win", [(w, w ^ 1) for w in range(n_win)])
+    half = keep + got.astype(jnp.float32)
+    total = jnp.take(half, y_here, axis=0, mode="clip")
+    for shift in range(1, n_y):
+        dest = (y_here + shift) % n_y
+        piece = jnp.take(half, dest, axis=0, mode="clip").astype(jnp.bfloat16)
+        perm = [(w, ((w // 2 + shift) % n_y) * 2 + w % 2) for w in range(n_win)]
+        total = total + lax.ppermute(piece, "win", perm).astype(jnp.float32)
+    return total
 
 
 def body(strain, pair_list, tile_live):
@@ -122,21 +144,13 @@
     left = left.reshape(slot_count, window_count, n_y, 2, own_rows, 2 * F)
     left = jnp.transpose(left, (0, 1, 3, 2, 4, 5)).reshape(slot_count, window_count, C, 2 * F)
     right = jnp.swapaxes(right, 2, 3)
-    corr = tile_correlation(cc, sc, cf.T, sf.T, left, right, sub)
-
     core = win_here % 2
     y_here = win_here // 2
-    parts = corr.reshape(2, n_y, own_rows, slot_count, LAGS, C)
-    send = jnp.take(parts, 1 - core, axis=0, mode="clip")
-    keep = jnp.take(parts, core, axis=0, mode="clip").astype(jnp.float32)
-    got = lax.ppermute(send, "win", [(w, w ^ 1) for w in range(n_win)])
-    half = keep + got.astype(jnp.float32)
-    total = jnp.take(half, y_here, axis=0, mode="clip")
-    for shift in range(1, n_y):
-        dest = (y_here + shift) % n_y
-        piece = jnp.take(half, dest, axis=0, mode="clip").astype(jnp.bfloat16)
-        perm = [(w, ((w // 2 + shift) % n_y) * 2 + w % 2) for w in range(n_win)]
-        total = total + lax.ppermute(piece, "win", perm).astype(jnp.float32)
+    totals = []
+    for t in range(slot_count):
+        corr = tile_correlation(cc, sc, cf.T, sf.T, left[t : t + 1], right[t : t + 1], sub)
+        totals.append(window_sum(corr, core, y_here, n_win, own_rows))
+    total = jnp.concatenate(totals, axis=1)
 
     live_local = tile_live.astype(jnp.float32)
     return total * live_local[None, :, None, None] / math.sqrt(F * window_count * n_win)

time: 91.3 us -> 98.2 us (1.076)
  waiting for transfers between devices: 49.5 us -> 41.8 us
  Pallas kernels: 11.7 us -> 17 us
  local copies, waits for them, and re-layouts: 6.91 us -> 11.4 us
  starting transfers between devices: 8.91 us -> 12.8 us
    ppermute x2 -> x8, waiting for transfers between devices: 15.1 us -> 7.33 us  [the longest x4 7.32 us: window_sum(): total = total + lax.ppermute(piece, 'win', perm).astype(jnp.float32)]
    pallas_call x1 -> x4, Pallas kernels: 11.7 us -> 17 us  [tile_correlation(): pl.pallas_call(functools.partial(correlation_kernel, sub), grid=(slot_cou...]
    ppermute x2 -> x8, starting transfers between devices: 1.65 us -> 5.59 us  [the longest x4 4.31 us: window_sum(): total = total + lax.ppermute(piece, 'win', perm).astype(jnp.float32)]
    slice x0 -> x6, local copies, waits for them, and re-layouts: none -> 3.72 us  [the longest x5 2.81 us: body(): left[t:t + 1]]
    gather x1 -> x4, local copies, waits for them, and re-layouts: 1.41 us -> 4.01 us  [window_sum(): send = jnp.take(parts, 1 - core, axis=0, mode='clip')]
    add x1 -> x8, other arithmetic: 1.61 us -> 2.23 us  [the longest x4 2.13 us: window_sum(): half = keep + got.astype(jnp.float32)]
  transfers between devices with their start and end apart: 3 -> 9, of which waited for: 3 -> 4; matrix products, arithmetic and copies ran while one was open for 3% -> 10% of each run, Pallas kernels for 0% -> 13%
where the time goes in v4:
time: 98.2 us; the launch traced here: 97.7 us
  waiting for transfers between devices  41.8 us (43%)
  Pallas kernels  17 us (17%)
  starting transfers between devices  12.8 us (13%)
  local copies, waits for them, and re-layouts  11.4 us (12%)
  other arithmetic  11.3 us (12%)
  matrix products  3.2 us (3%)
    all_to_all x1, waiting for transfers between devices, body(): incoming = lax.all_to_all(outgoing, 'pair', 0, 0, tiled=True)  34.4 us
    pallas_call x4, Pallas kernels, tile_correlation(): pl.pallas_call(functools.partial(correlation_kernel, sub), grid=(slot_cou...  17 us
    ppermute x4, waiting for transfers between devices, window_sum(): total = total + lax.ppermute(piece, 'win', perm).astype(jnp.float32)  7.32 us
    all_to_all x1, starting transfers between devices, body(): incoming = lax.all_to_all(outgoing, 'pair', 0, 0, tiled=True)  7.25 us
    ppermute x4, starting transfers between devices, window_sum(): total = total + lax.ppermute(piece, 'win', perm).astype(jnp.float32)  4.31 us
    gather x4, local copies, waits for them, and re-layouts, window_sum(): send = jnp.take(parts, 1 - core, axis=0, mode='clip')  4.01 us
    another operation x2, other arithmetic  3.7 us
    dot_general x1, matrix products, whiten_rows(): jnp.dot(strain_rows, dft_table(sample_count, bin_count), preferred_elemen...  3.2 us
  transfers between devices with their start and end apart: 9, of which 4 were waited for; matrix products, arithmetic and copies ran while one was open for 10% of the time, Pallas kernels for 13%

profile of v4, /device:TPU:0, one launch (start us, length us, event | category | flops | bytes accessed | tf_op | source)
XLA Modules:
  0.0 97.7 jit_solution(7596225583127347530)
XLA Ops:
  0.0 0.8 fusion.18
  0.8 0.5 fusion.34
  1.3 0.0 copy-start.3
  1.3 3.5 %subtract_convert_fusion = (bf16[60,128,384]{2,1,0:T(8,128)(2,1)S(1)}, bf16[60,128,384]{2,1,0:T(8,128)(2,1)S(1)}) fusion(f32[128,384]{1,0:T(8,128)S(1)} %get-tuple-element.200, f32[60,384]{1,0:T(8,128)S(1)} %get-tuple-element.194, f32[128,384]{1,0:T(8,128)S(1)} %get-tuple-element.199, f32[60,384]{1,0:T(8,128)S(1)} %get-tuple-element.193), kind=kLoop, calls=%fused_computation.8 | loop fusion | flops 26542080 | bytes 12374016 | tf_op jit(solution)/shard_map/convert.7
  4.8 3.2 %fusion.5 = f32[256,768]{1,0:T(8,128)S(1)} fusion(bf16[7680,384]{1,0:T(8,128)(2,1)S(1)} %bitcast.80, bf16[7680,384]{1,0:T(8,128)(2,1)S(1)} %bitcast.79, bf16[1,256,7680]{2,1,0:T(8,128)(2,1)S(1)} %copy-done.3), kind=kOutput, calls=%fused_computation.10 | convolution fusion | flops 3043491840 | bytes 16515072 | tf_op jit(solution)/shard_map/dot_general | solution.py:37
  8.1 0.2 fusion.47
  8.3 0.2 divide_convert_fusion.1
  8.5 0.1 reduce_sum.27
  8.6 0.1 reduce_sum.28
  8.8 1.8 %gather_fusion = bf16[8,128,768]{2,1,0:T(8,128)(2,1)} fusion(bf16[2,128,768]{2,1,0:T(8,128)(2,1)S(1)} %maximum_bitcast_fusion, s32[1024]{0:T(1024)S(1)} %pad_clamp_fusion.2), kind=kCustom, calls=%fused_computation | custom fusion | bytes 3145760 | tf_op jit(solution)/shard_map/jit(_take)/gather | solution.py:130
  10.6 7.3 %all-to-all-start = ((bf16[8,1,128,768]{3,2,1,0:T(8,128)(2,1)}), bf16[8,1,128,768]{3,2,1,0:T(8,128)(2,1)S(1)}, u32[]{:S(2)}, u32[]{:S(2)}) async-start(bf16[8,1,128,768]{3,2,1,0:T(8,128)(2,1)} %bitcast.7), calls=%async_computation | async-start | bytes 3145728 | tf_op jit(solution)/shard_map/all_to_all | solution.py:131
  17.9 0.1 constant_dynamic-slice_fusion
  18.0 0.7 fusion.41
  18.8 1.7 %fusion.21 = (f32[384,4]{1,0:T(8,128)}, f32[384,4]{1,0:T(8,128)}) fusion(s32[4]{0:T(128)S(1)} %iota_multiply_fusion.1, s32[384]{0:T(512)S(1)} %iota_add_fusion), kind=kLoop, calls=%fused_computation.47 | loop fusion | flops 13824 | bytes 13840 | tf_op jit(solution)/shard_map/sin | solution.py:20
  20.4 34.4 %all-to-all-done = bf16[8,1,128,768]{3,2,1,0:T(8,128)(2,1)S(1)} async-done(((bf16[8,1,128,768]{3,2,1,0:T(8,128)(2,1)}), bf16[8,1,128,768]{3,2,1,0:T(8,128)(2,1)S(1)}, u32[]{:S(2)}, u32[]{:S(2)}) %all-to-all-start) | async-done | bytes 1572896 | tf_op jit(solution)/shard_map/all_to_all | solution.py:131
  54.9 0.6 gather_fusion.2
  55.5 0.4 copy.28
  55.9 0.9 fusion.48
  56.8 0.6 gather_fusion.1
  57.4 0.1 fusion.49
  57.4 0.7 copy.27
  58.1 4.2 %shard_map.37 = bf16[128,1,16,128]{3,2,1,0:T(8,128)(2,1)} custom-call(f32[4,384]{1,0:T(4,128)} %get-tuple-element.198.cc_ref, f32[4,384]{1,0:T(4,128)} %get-tuple-element.197.sc_ref, f32[384,4]{1,0:T(8,128)} %get-tuple-element.196.cf_ref, f32[384,4]{1,0:T(8,128)} %get-tuple-element.195.sf_ref, bf16[1,1,128,768]{3,2,1,0:T(8,128)(2,1)} %bitcast.94, ...), custom_call_target="tpu_custom_call" | custom-call | flops 402653184 | bytes 917504 | tf_op jit(solution)/shard_map/pallas_call | solution.py:87
  62.3 1.0 %dynamic-slice_bitcast_fusion.3 = bf16[2,32,1,16,128]{4,3,1,2,0:T(8,128)(2,1)S(1)} fusion(bf16[2,2,32,1,16,128]{5,4,2,1,0,3:T(8,128)(2,1)} %bitcast.91, s32[]{:T(128)S(6)} %sub.53), kind=kLoop, calls=%fused_computation.34 | loop fusion | bytes 524292 | tf_op jit(solution)/shard_map/jit(_take)/gather | solution.py:102
  63.4 0.1 collective-permute-start
  63.5 0.7 copy.30
  64.2 4.2 %shard_map.38 = bf16[128,1,16,128]{3,2,1,0:T(8,128)(2,1)} custom-call(f32[4,384]{1,0:T(4,128)} %get-tuple-element.198.cc_ref, f32[4,384]{1,0:T(4,128)} %get-tuple-element.197.sc_ref, f32[384,4]{1,0:T(8,128)} %get-tuple-element.196.cf_ref, f32[384,4]{1,0:T(8,128)} %get-tuple-element.195.sf_ref, bf16[1,1,128,768]{3,2,1,0:T(8,128)(2,1)} %bitcast.95, ...), custom_call_target="tpu_custom_call" | custom-call | flops 402653184 | bytes 917504 | tf_op jit(solution)/shard_map/pallas_call | solution.py:87
  68.4 1.0 %dynamic-slice_bitcast_fusion.2 = bf16[2,32,1,16,128]{4,3,1,2,0:T(8,128)(2,1)S(1)} fusion(bf16[2,2,32,1,16,128]{5,4,2,1,0,3:T(8,128)(2,1)} %bitcast.89, s32[]{:T(128)S(6)} %sub.53), kind=kLoop, calls=%fused_computation.32 | loop fusion | bytes 524292 | tf_op jit(solution)/shard_map/jit(_take)/gather | solution.py:102
  69.5 0.6 collective-permute-start.2
  70.0 0.7 copy.32
  70.7 4.3 %shard_map.39 = bf16[128,1,16,128]{3,2,1,0:T(8,128)(2,1)} custom-call(f32[4,384]{1,0:T(4,128)} %get-tuple-element.198.cc_ref, f32[4,384]{1,0:T(4,128)} %get-tuple-element.197.sc_ref, f32[384,4]{1,0:T(8,128)} %get-tuple-element.196.cf_ref, f32[384,4]{1,0:T(8,128)} %get-tuple-element.195.sf_ref, bf16[1,1,128,768]{3,2,1,0:T(8,128)(2,1)} %bitcast.96, ...), custom_call_target="tpu_custom_call" | custom-call | flops 402653184 | bytes 917504 | tf_op jit(solution)/shard_map/pallas_call | solution.py:87
  75.0 1.0 dynamic-slice_bitcast_fusion.1
  76.0 0.1 collective-permute-start.4
  76.0 0.7 copy.34
  76.7 4.2 %shard_map.40 = bf16[128,1,16,128]{3,2,1,0:T(8,128)(2,1)} custom-call(f32[4,384]{1,0:T(4,128)} %get-tuple-element.198.cc_ref, f32[4,384]{1,0:T(4,128)} %get-tuple-element.197.sc_ref, f32[384,4]{1,0:T(8,128)} %get-tuple-element.196.cf_ref, f32[384,4]{1,0:T(8,128)} %get-tuple-element.195.sf_ref, bf16[1,1,128,768]{3,2,1,0:T(8,128)(2,1)} %bitcast.93, ...), custom_call_target="tpu_custom_call" | custom-call | flops 402653184 | bytes 917504 | tf_op jit(solution)/shard_map/pallas_call | solution.py:87
  81.0 1.0 dynamic-slice_bitcast_fusion
  81.9 0.6 collective-permute-start.6
  82.5 0.1 convert_add_fusion.3
  82.6 1.6 %collective-permute-start.1 = (bf16[32,1,16,128]{3,2,1,0:T(8,128)(2,1)S(1)}, bf16[32,1,16,128]{3,2,1,0:T(8,128)(2,1)S(1)}, u32[]{:S(2)}, u32[]{:S(2)}) collective-permute-start(bf16[32,1,16,128]{3,2,1,0:T(8,128)(2,1)S(1)} %fusion.25), channel_id=1, source_target_pairs={{0,16},{8,24},{16,0},{24,8},{1,17},{9,25},{17,1},{25,9},{2,18},{10... | collective-permute-start | bytes 393224 | tf_op jit(solution)/shard_map/ppermute | solution.py:111
  84.2 0.1 convert_add_fusion.2
  84.3 0.6 collective-permute-start.3
  84.9 1.0 %convert_add_fusion.1 = f32[2,32,1,16,128]{4,3,1,2,0:T(8,128)S(1)} fusion(bf16[2,32,1,16,128]{4,3,1,2,0:T(8,128)(2,1)S(1)} %collective-permute-done.4, bf16[2,2,32,1,16,128]{5,4,2,1,3,0:T(8,128)(2,1)} %bitcast.88, s32[]{:T(128)S(6)} %select_n.132), kind=kLoop, calls=%fused_computation.14 | loop fusion | flops 393216 | bytes 1048580 | tf_op jit(solution)/shard_map/add | solution.py:105
  85.9 1.6 %collective-permute-start.5 = (bf16[32,1,16,128]{3,2,1,0:T(8,128)(2,1)S(1)}, bf16[32,1,16,128]{3,2,1,0:T(8,128)(2,1)S(1)}, u32[]{:S(2)}, u32[]{:S(2)}) collective-permute-start(bf16[32,1,16,128]{3,2,1,0:T(8,128)(2,1)S(1)} %fusion.27), channel_id=1, source_target_pairs={{0,16},{8,24},{16,0},{24,8},{1,17},{9,25},{17,1},{25,9},{2,18},{10... | collective-permute-start | bytes 393224 | tf_op jit(solution)/shard_map/ppermute | solution.py:111
  87.5 1.0 %convert_add_fusion = f32[2,32,1,16,128]{4,3,1,2,0:T(8,128)S(1)} fusion(bf16[2,32,1,16,128]{4,3,1,2,0:T(8,128)(2,1)S(1)} %collective-permute-done.6, bf16[2,2,32,1,16,128]{5,4,2,1,3,0:T(8,128)(2,1)} %bitcast.86, s32[]{:T(128)S(6)} %select_n.132), kind=kLoop, calls=%fused_computation.13 | loop fusion | flops 393216 | bytes 1048580 | tf_op jit(solution)/shard_map/add | solution.py:105
  88.5 0.6 collective-permute-start.7
  89.2 2.7 %collective-permute-done.3 = bf16[32,1,16,128]{3,2,1,0:T(8,128)(2,1)S(1)} collective-permute-done((bf16[32,1,16,128]{3,2,1,0:T(8,128)(2,1)S(1)}, bf16[32,1,16,128]{3,2,1,0:T(8,128)(2,1)S(1)}, u32[]{:S(2)}, u32[]{:S(2)}) %collective-permute-start.3) | collective-permute-done | bytes 131104 | tf_op jit(solution)/shard_map/ppermute | solution.py:111
  91.9 2.8 %collective-permute-done.5 = bf16[32,1,16,128]{3,2,1,0:T(8,128)(2,1)S(1)} collective-permute-done((bf16[32,1,16,128]{3,2,1,0:T(8,128)(2,1)S(1)}, bf16[32,1,16,128]{3,2,1,0:T(8,128)(2,1)S(1)}, u32[]{:S(2)}, u32[]{:S(2)}) %collective-permute-start.5) | collective-permute-done | bytes 131104 | tf_op jit(solution)/shard_map/ppermute | solution.py:111
  94.7 1.9 %collective-permute-done.7 = bf16[32,1,16,128]{3,2,1,0:T(8,128)(2,1)S(1)} collective-permute-done((bf16[32,1,16,128]{3,2,1,0:T(8,128)(2,1)S(1)}, bf16[32,1,16,128]{3,2,1,0:T(8,128)(2,1)S(1)}, u32[]{:S(2)}, u32[]{:S(2)}) %collective-permute-start.7) | collective-permute-done | bytes 131104 | tf_op jit(solution)/shard_map/ppermute | solution.py:111
  96.6 1.2 %fusion.10 = f32[32,4,16,128]{3,2,1,0:T(8,128)} fusion(f32[32,1,16,128]{3,2,1,0:T(8,128)S(1)} %bitcast_add_fusion, f32[32,1,16,128]{3,2,1,0:T(8,128)S(1)} %bitcast_add_fusion.1, f32[32,1,16,128]{3,2,1,0:T(8,128)S(1)} %bitcast_add_fusion.2, f32[32,1,16,128]{3,2,1,0:T(8,128)S(1)} %bitcast_add_fusion.3, f32[4]{0:T(128)S(1)} %convert_element_type.205), kind=kLoop, calls=%fused_computation.12 | loop fusion | flops 1310720 | bytes 2097168 | tf_op jit(solution)/shard_map/div | solution.py:156
  (33 shorter events, 0.4 us)
Async XLA Ops:
  1.3 3.5 %copy-start.3 = (bf16[1,256,7680]{2,1,0:T(8,128)(2,1)S(1)}, bf16[1,256,7680]{2,1,0:T(8,128)(2,1)}, u32[]{:S(2)}) copy-start(bf16[1,256,7680]{2,1,0:T(8,128)(2,1)} %param.3) | copy-start | bytes 11796484
  4.8 3.7 %copy-start.2 = (s32[32,2]{0,1:T(2,128)S(1)}, s32[32,2]{0,1:T(2,128)}, u32[]{:S(2)}) copy-start(s32[32,2]{0,1:T(2,128)} %param.4) | copy-start | bytes 772
  8.0 9.8 %copy-start.4 = (s32[4]{0:T(128)S(1)}, s32[4]{0:T(128)}, u32[]{:S(2)}) copy-start(s32[4]{0:T(128)} %param.5) | copy-start | bytes 52
  10.6 44.3 %all-to-all-start = ((bf16[8,1,128,768]{3,2,1,0:T(8,128)(2,1)}), bf16[8,1,128,768]{3,2,1,0:T(8,128)(2,1)S(1)}, u32[]{:S(2)}, u32[]{:S(2)}) async-start(bf16[8,1,128,768]{3,2,1,0:T(8,128)(2,1)} %bitcast.7), calls=%async_computation | async-start | bytes 3145728 | tf_op jit(solution)/shard_map/all_to_all | solution.py:131
  62.3 20.2 %copy-start.1 = (bf16[128,1,16,128]{3,2,1,0:T(8,128)(2,1)S(1)}, bf16[128,1,16,128]{3,2,1,0:T(8,128)(2,1)}, u32[]{:S(2)}) copy-start(bf16[128,1,16,128]{3,2,1,0:T(8,128)(2,1)} %shard_map.37) | copy-start | bytes 1572868
  63.4 19.1 %collective-permute-start = (bf16[2,32,1,16,128]{4,3,1,2,0:T(8,128)(2,1)S(1)}, bf16[2,32,1,16,128]{4,3,1,2,0:T(8,128)(2,1)S(1)}, u32[]{:S(2)}, u32[]{:S(2)}) collective-permute-start(bf16[2,32,1,16,128]{4,3,1,2,0:T(8,128)(2,1)S(1)} %dynamic-slice_bitcast_fusion.3), channel_id=1, source_target_pairs={{0,8},{8,0},{16,24},{24,16},{1,9},{9,1},{17,25},{25,17},{2,10},{10... | collective-permute-start | bytes 786440 | tf_op jit(solution)/shard_map/ppermute | solution.py:104
  68.4 15.8 %copy-start = (bf16[128,1,16,128]{3,2,1,0:T(8,128)(2,1)S(1)}, bf16[128,1,16,128]{3,2,1,0:T(8,128)(2,1)}, u32[]{:S(2)}) copy-start(bf16[128,1,16,128]{3,2,1,0:T(8,128)(2,1)} %shard_map.38) | copy-start | bytes 1572868
  69.5 14.7 %collective-permute-start.2 = (bf16[2,32,1,16,128]{4,3,1,2,0:T(8,128)(2,1)S(1)}, bf16[2,32,1,16,128]{4,3,1,2,0:T(8,128)(2,1)S(1)}, u32[]{:S(2)}, u32[]{:S(2)}) collective-permute-start(bf16[2,32,1,16,128]{4,3,1,2,0:T(8,128)(2,1)S(1)} %dynamic-slice_bitcast_fusion.2), channel_id=1, source_target_pairs={{0,8},{8,0},{16,24},{24,16},{1,9},{9,1},{17,25},{25,17},{2,10},{10... | collective-permute-start | bytes 786440 | tf_op jit(solution)/shard_map/ppermute | solution.py:104
  76.0 8.9 %collective-permute-start.4 = (bf16[2,32,1,16,128]{4,3,1,2,0:T(8,128)(2,1)S(1)}, bf16[2,32,1,16,128]{4,3,1,2,0:T(8,128)(2,1)S(1)}, u32[]{:S(2)}, u32[]{:S(2)}) collective-permute-start(bf16[2,32,1,16,128]{4,3,1,2,0:T(8,128)(2,1)S(1)} %dynamic-slice_bitcast_fusion.1), channel_id=1, source_target_pairs={{0,8},{8,0},{16,24},{24,16},{1,9},{9,1},{17,25},{25,17},{2,10},{10... | collective-permute-start | bytes 786440 | tf_op jit(solution)/shard_map/ppermute | solution.py:104
  81.9 5.6 %collective-permute-start.6 = (bf16[2,32,1,16,128]{4,3,1,2,0:T(8,128)(2,1)S(1)}, bf16[2,32,1,16,128]{4,3,1,2,0:T(8,128)(2,1)S(1)}, u32[]{:S(2)}, u32[]{:S(2)}) collective-permute-start(bf16[2,32,1,16,128]{4,3,1,2,0:T(8,128)(2,1)S(1)} %dynamic-slice_bitcast_fusion), channel_id=1, source_target_pairs={{0,8},{8,0},{16,24},{24,16},{1,9},{9,1},{17,25},{25,17},{2,10},{10... | collective-permute-start | bytes 786440 | tf_op jit(solution)/shard_map/ppermute | solution.py:104
  82.6 6.5 %collective-permute-start.1 = (bf16[32,1,16,128]{3,2,1,0:T(8,128)(2,1)S(1)}, bf16[32,1,16,128]{3,2,1,0:T(8,128)(2,1)S(1)}, u32[]{:S(2)}, u32[]{:S(2)}) collective-permute-start(bf16[32,1,16,128]{3,2,1,0:T(8,128)(2,1)S(1)} %fusion.25), channel_id=1, source_target_pairs={{0,16},{8,24},{16,0},{24,8},{1,17},{9,25},{17,1},{25,9},{2,18},{10... | collective-permute-start | bytes 393224 | tf_op jit(solution)/shard_map/ppermute | solution.py:111
  84.3 7.5 %collective-permute-start.3 = (bf16[32,1,16,128]{3,2,1,0:T(8,128)(2,1)S(1)}, bf16[32,1,16,128]{3,2,1,0:T(8,128)(2,1)S(1)}, u32[]{:S(2)}, u32[]{:S(2)}) collective-permute-start(bf16[32,1,16,128]{3,2,1,0:T(8,128)(2,1)S(1)} %fusion.26), channel_id=1, source_target_pairs={{0,16},{8,24},{16,0},{24,8},{1,17},{9,25},{17,1},{25,9},{2,18},{10... | collective-permute-start | bytes 393224 | tf_op jit(solution)/shard_map/ppermute | solution.py:111
  85.9 8.7 %collective-permute-start.5 = (bf16[32,1,16,128]{3,2,1,0:T(8,128)(2,1)S(1)}, bf16[32,1,16,128]{3,2,1,0:T(8,128)(2,1)S(1)}, u32[]{:S(2)}, u32[]{:S(2)}) collective-permute-start(bf16[32,1,16,128]{3,2,1,0:T(8,128)(2,1)S(1)} %fusion.27), channel_id=1, source_target_pairs={{0,16},{8,24},{16,0},{24,8},{1,17},{9,25},{17,1},{25,9},{2,18},{10... | collective-permute-start | bytes 393224 | tf_op jit(solution)/shard_map/ppermute | solution.py:111
  88.5 8.0 %collective-permute-start.7 = (bf16[32,1,16,128]{3,2,1,0:T(8,128)(2,1)S(1)}, bf16[32,1,16,128]{3,2,1,0:T(8,128)(2,1)S(1)}, u32[]{:S(2)}, u32[]{:S(2)}) collective-permute-start(bf16[32,1,16,128]{3,2,1,0:T(8,128)(2,1)S(1)} %fusion.28), channel_id=1, source_target_pairs={{0,16},{8,24},{16,0},{24,8},{1,17},{9,25},{17,1},{25,9},{2,18},{10... | collective-permute-start | bytes 393224 | tf_op jit(solution)/shard_map/ppermute | solution.py:111

commit v5 on v3

--- a/solution.py
+++ b/solution.py
@@ -53,22 +53,32 @@
         rim = right_ref[0, w, F:, :].astype(jnp.float32)
         turned = []
         for l1 in range(sub):
+            if l1 == 0:
+                turned.append(right_ref[0, w])
+                continue
             c = cf_ref[:, l1 : l1 + 1]
             s = sf_ref[:, l1 : l1 + 1]
             turned.append(jnp.concatenate([rre * c + rim * s, rim * c - rre * s], axis=0).astype(jnp.bfloat16))
         right_all = jnp.concatenate(turned, axis=1)
         parts = []
         for l2 in range(LAGS // sub):
-            c = cc_ref[l2 : l2 + 1, :]
-            s = sc_ref[l2 : l2 + 1, :]
-            left_t = jnp.concatenate([lre * c - lim * s, lre * s + lim * c], axis=1).astype(jnp.bfloat16)
+            if l2 * sub == LAGS // 2:
+                left_t = left_ref[0, w]
+            else:
+                c = cc_ref[l2 : l2 + 1, :]
+                s = sc_ref[l2 : l2 + 1, :]
+                left_t = jnp.concatenate([lre * c - lim * s, lre * s + lim * c], axis=1).astype(jnp.bfloat16)
             parts.append(
                 jnp.dot(left_t, right_all, preferred_element_type=jnp.float32)
             )
         acc = parts if acc is None else [a + p for a, p in zip(acc, parts)]
+    half_rows = C // 2
     for l2, res in enumerate(acc):
         for l1 in range(sub):
-            out_ref[:, 0, l2 * sub + l1, :] = res[:, l1 * C : (l1 + 1) * C].astype(out_ref.dtype)
+            for part in range(2):
+                out_ref[part, l2 * sub + l1] = res[part * half_rows : (part + 1) * half_rows, l1 * C : (l1 + 1) * C].astype(
+                    out_ref.dtype
+                )
 
 
 def tile_correlation(cc, sc, cf, sf, left, right, sub):
@@ -82,8 +92,8 @@
         functools.partial(correlation_kernel, sub),
         grid=(slot_count,),
         in_specs=[table_spec] * 2 + [column_spec] * 2 + [block_spec, right_spec],
-        out_specs=pl.BlockSpec((C, 1, LAGS, C), lambda t: (0, t, 0, 0)),
-        out_shape=jax.ShapeDtypeStruct((C, slot_count, LAGS, C), jnp.bfloat16),
+        out_specs=pl.BlockSpec((2, LAGS, C // 2, C), lambda t: (0, 0, 0, t)),
+        out_shape=jax.ShapeDtypeStruct((2, LAGS, C // 2, slot_count * C), jnp.bfloat16),
         cost_estimate=pl.CostEstimate(
             flops=flops, transcendentals=0, bytes_accessed=slot_count * (4 * window_count * C * F * 2 + 2 * C * LAGS * C)
         ),
@@ -126,17 +136,18 @@
 
     core = win_here % 2
     y_here = win_here // 2
-    parts = corr.reshape(2, n_y, own_rows, slot_count, LAGS, C)
-    send = jnp.take(parts, 1 - core, axis=0, mode="clip")
-    keep = jnp.take(parts, core, axis=0, mode="clip").astype(jnp.float32)
+    send = jnp.take(corr, 1 - core, axis=0, mode="clip")
+    keep = jnp.take(corr, core, axis=0, mode="clip").astype(jnp.float32)
     got = lax.ppermute(send, "win", [(w, w ^ 1) for w in range(n_win)])
-    half = keep + got.astype(jnp.float32)
+    half = (keep + got.astype(jnp.float32)).reshape(LAGS, n_y, own_rows, slot_count * C)
+    half = jnp.transpose(half, (1, 0, 2, 3))
     total = jnp.take(half, y_here, axis=0, mode="clip")
     for shift in range(1, n_y):
         dest = (y_here + shift) % n_y
         piece = jnp.take(half, dest, axis=0, mode="clip").astype(jnp.bfloat16)
         perm = [(w, ((w // 2 + shift) % n_y) * 2 + w % 2) for w in range(n_win)]
         total = total + lax.ppermute(piece, "win", perm).astype(jnp.float32)
+    total = jnp.transpose(total.reshape(LAGS, own_rows, slot_count, C), (1, 2, 0, 3))
 
     live_local = tile_live.astype(jnp.float32)
     return total * live_local[None, :, None, None] / math.sqrt(F * window_count * n_win)

time: 91.3 us -> 87.2 us (0.955)
  Pallas kernels: 11.7 us -> 6.49 us
  local copies, waits for them, and re-layouts: 6.91 us -> 8.74 us
    pallas_call x1, Pallas kernels: 11.7 us -> 6.49 us  [tile_correlation(): pl.pallas_call(functools.partial(correlation_kernel, sub), grid=(slot_cou...]
    div x0 -> x1, local copies, waits for them, and re-layouts: none -> 1.58 us  [body(): total * live_local[None, :, None, None]]
where the time goes in v5:
time: 87.2 us; the launch traced here: 86.9 us
  waiting for transfers between devices  49.5 us (57%)
  other arithmetic  9.82 us (11%)
  starting transfers between devices  8.91 us (10%)
  local copies, waits for them, and re-layouts  8.74 us (10%)
  Pallas kernels  6.49 us (7%)
  matrix products  3.2 us (4%)
    all_to_all x1, waiting for transfers between devices, body(): incoming = lax.all_to_all(outgoing, 'pair', 0, 0, tiled=True)  34.4 us
    ppermute x1, waiting for transfers between devices, body(): total = total + lax.ppermute(piece, 'win', perm).astype(jnp.float32)  12.4 us
    all_to_all x1, starting transfers between devices, body(): incoming = lax.all_to_all(outgoing, 'pair', 0, 0, tiled=True)  7.25 us
    pallas_call x1, Pallas kernels, tile_correlation(): pl.pallas_call(functools.partial(correlation_kernel, sub), grid=(slot_cou...  6.49 us
    another operation x2, other arithmetic  3.7 us
    dot_general x1, matrix products, whiten_rows(): jnp.dot(strain_rows, dft_table(sample_count, bin_count), preferred_elemen...  3.2 us
    ppermute x1, waiting for transfers between devices, body(): got = lax.ppermute(send, 'win', [(w, w ^ 1) for w in range(n_win)])  2.62 us
    sin x2, other arithmetic, cos_sin(): return (jnp.cos(angle), jnp.sin(angle))  2.2 us
  transfers between devices with their start and end apart: 3, of which 3 were waited for; matrix products, arithmetic and copies ran while one was open for 3% of the time, Pallas kernels for 0%

profile of v5, /device:TPU:0, one launch (start us, length us, event | category | flops | bytes accessed | tf_op | source)
XLA Modules:
  0.0 86.9 jit_solution(5041685931538305179)
XLA Ops:
  0.0 0.8 fusion.16
  0.8 0.5 fusion.23
  1.3 0.0 copy-start.1
  1.3 3.5 %subtract_convert_fusion = (bf16[60,128,384]{2,1,0:T(8,128)(2,1)S(1)}, bf16[60,128,384]{2,1,0:T(8,128)(2,1)S(1)}) fusion(f32[128,384]{1,0:T(8,128)S(1)} %get-tuple-element.60, f32[60,384]{1,0:T(8,128)S(1)} %get-tuple-element.56, f32[128,384]{1,0:T(8,128)S(1)} %get-tuple-element.59, f32[60,384]{1,0:T(8,128)S(1)} %get-tuple-element.55), kind=kLoop, calls=%fused_computation.8 | loop fusion | flops 26542080 | bytes 12374016 | tf_op jit(solution)/shard_map/convert.7
  4.8 0.0 copy-done.1
  4.8 0.0 copy-start
  4.8 3.2 %fusion.5 = f32[256,768]{1,0:T(8,128)S(1)} fusion(bf16[7680,384]{1,0:T(8,128)(2,1)S(1)} %bitcast.47, bf16[7680,384]{1,0:T(8,128)(2,1)S(1)} %bitcast.46, bf16[1,256,7680]{2,1,0:T(8,128)(2,1)S(1)} %copy-done.1), kind=kOutput, calls=%fused_computation.11 | convolution fusion | flops 3043491840 | bytes 16515072 | tf_op jit(solution)/shard_map/dot_general | solution.py:37
  8.0 0.2 fusion.40
  8.3 0.2 divide_convert_fusion.1
  8.5 0.0 copy-done
  8.5 0.1 reduce_sum.27
  8.6 0.1 reduce_sum.28
  8.8 1.8 %gather_fusion = bf16[8,128,768]{2,1,0:T(8,128)(2,1)} fusion(bf16[2,128,768]{2,1,0:T(8,128)(2,1)S(1)} %maximum_bitcast_fusion, s32[1024]{0:T(1024)S(1)} %pad_clamp_fusion.2), kind=kCustom, calls=%fused_computation | custom fusion | bytes 3145760 | tf_op jit(solution)/shard_map/jit(_take)/gather | solution.py:118
  10.6 7.3 %all-to-all-start = ((bf16[8,1,128,768]{3,2,1,0:T(8,128)(2,1)}), bf16[8,1,128,768]{3,2,1,0:T(8,128)(2,1)S(1)}, u32[]{:S(2)}, u32[]{:S(2)}) async-start(bf16[8,1,128,768]{3,2,1,0:T(8,128)(2,1)} %bitcast.7), calls=%async_computation | async-start | bytes 3145728 | tf_op jit(solution)/shard_map/all_to_all | solution.py:119
  17.8 0.1 fusion.27
  17.9 0.1 copy.12
  18.1 0.1 constant_dynamic-slice_fusion
  18.2 0.7 fusion.34
  18.9 1.5 %multiply_sine_fusion = (f32[384,4]{1,0:T(8,128)}, f32[384,4]{1,0:T(8,128)}) fusion(f32[384,4]{1,0:T(8,128)S(1)} %copy.12), kind=kLoop, calls=%fused_computation.30 | loop fusion | flops 1536 | bytes 18432 | tf_op jit(solution)/shard_map/sin | solution.py:20
  20.4 34.4 %all-to-all-done = bf16[8,1,128,768]{3,2,1,0:T(8,128)(2,1)S(1)} async-done(((bf16[8,1,128,768]{3,2,1,0:T(8,128)(2,1)}), bf16[8,1,128,768]{3,2,1,0:T(8,128)(2,1)S(1)}, u32[]{:S(2)}, u32[]{:S(2)}) %all-to-all-start) | async-done | bytes 1572896 | tf_op jit(solution)/shard_map/all_to_all | solution.py:119
  54.8 0.6 gather_fusion.2
  55.4 1.2 %copy.14 = bf16[4,128,768]{1,2,0:T(8,128)(2,1)} copy(bf16[4,128,768]{2,1,0:T(8,128)(2,1)S(1)} %gather_fusion.2) | data formatting | bytes 1572864 | tf_op jit(solution)/shard_map/jit(_take)/gather | solution.py:122
  56.6 0.6 gather_fusion.1
  57.2 0.9 %copy.13 = bf16[4,1,2,2,32,768]{5,4,3,2,0,1:T(8,128)(2,1)} copy(bf16[4,1,2,2,32,768]{5,4,2,3,0,1:T(8,128)(2,1)S(1)} %bitcast.48) | data formatting | bytes 1572864 | tf_op jit(solution)/shard_map/transpose | solution.py:133
  58.1 0.0 copy-start.2
  58.1 6.5 %shard_map.37 = bf16[2,16,64,512]{3,2,1,0:T(8,128)(2,1)} custom-call(f32[4,384]{1,0:T(4,128)} %get-tuple-element.58.cc_ref, f32[4,384]{1,0:T(4,128)} %get-tuple-element.57.sc_ref, f32[384,4]{1,0:T(8,128)} %get-tuple-element.54.cf_ref, f32[384,4]{1,0:T(8,128)} %get-tuple-element.53.sf_ref, bf16[4,1,128,768]{3,2,1,0:T(8,128)(2,1)} %bitcast.50, ...), custom_call_target="tpu_custom_call" | custom-call | flops 1610612736 | bytes 3670016 | tf_op jit(solution)/shard_map/pallas_call | solution.py:91
  64.6 1.3 %dynamic-slice_bitcast_fusion = bf16[16,64,512]{2,1,0:T(8,128)(2,1)S(1)} fusion(bf16[2,16,64,512]{3,2,1,0:T(8,128)(2,1)} %shard_map.37, s32[]{:T(128)S(6)} %sub.38), kind=kLoop, calls=%fused_computation.14 | loop fusion | bytes 2097156 | tf_op jit(solution)/shard_map/jit(_take)/gather | solution.py:139
  66.0 0.1 collective-permute-start
  66.1 2.6 %collective-permute-done = bf16[16,64,512]{2,1,0:T(8,128)(2,1)S(1)} collective-permute-done((bf16[16,64,512]{2,1,0:T(8,128)(2,1)S(1)}, bf16[16,64,512]{2,1,0:T(8,128)(2,1)S(1)}, u32[]{:S(2)}, u32[]{:S(2)}) %collective-permute-start) | collective-permute-done | bytes 1048608 | tf_op jit(solution)/shard_map/ppermute | solution.py:141
  68.7 1.5 %convert_add_fusion = f32[16,64,512]{2,1,0:T(8,128)S(1)} fusion(bf16[16,64,512]{2,1,0:T(8,128)(2,1)S(1)} %collective-permute-done, bf16[2,16,64,512]{3,2,1,0:T(8,128)(2,1)} %shard_map.37, s32[]{:T(128)S(6)} %select_n.102), kind=kLoop, calls=%fused_computation.10 | loop fusion | flops 1572864 | bytes 4194308 | tf_op jit(solution)/shard_map/add | solution.py:142
  70.2 0.1 fusion.10
  70.3 1.6 %collective-permute-start.1 = (bf16[16,32,512]{2,1,0:T(8,128)(2,1)S(1)}, bf16[16,32,512]{2,1,0:T(8,128)(2,1)S(1)}, u32[]{:S(2)}, u32[]{:S(2)}) collective-permute-start(bf16[16,32,512]{2,1,0:T(8,128)(2,1)S(1)} %fusion.10), channel_id=1, source_target_pairs={{0,16},{8,24},{16,0},{24,8},{1,17},{9,25},{17,1},{25,9},{2,18},{10... | collective-permute-start | bytes 1572872 | tf_op jit(solution)/shard_map/ppermute | solution.py:149
  71.9 0.0 copy-done.2
  71.9 12.4 %collective-permute-done.1 = bf16[16,32,512]{2,1,0:T(8,128)(2,1)S(1)} collective-permute-done((bf16[16,32,512]{2,1,0:T(8,128)(2,1)S(1)}, bf16[16,32,512]{2,1,0:T(8,128)(2,1)S(1)}, u32[]{:S(2)}, u32[]{:S(2)}) %collective-permute-start.1) | collective-permute-done | bytes 524320 | tf_op jit(solution)/shard_map/ppermute | solution.py:149
  84.3 0.2 bitcast_add_fusion
  84.5 0.4 reshape.200
  84.9 0.4 multiply_bitcast_fusion
  85.3 1.6 %copy.16 = f32[32,4,16,128]{3,2,1,0:T(8,128)} copy(f32[32,4,16,128]{3,1,0,2:T(4,128)S(1)} %multiply_bitcast_fusion) | data formatting | bytes 2097152 | tf_op jit(solution)/shard_map/div | solution.py:153
  (11 shorter events, 0.1 us)
Async XLA Ops:
  1.3 3.5 %copy-start.1 = (bf16[1,256,7680]{2,1,0:T(8,128)(2,1)S(1)}, bf16[1,256,7680]{2,1,0:T(8,128)(2,1)}, u32[]{:S(2)}) copy-start(bf16[1,256,7680]{2,1,0:T(8,128)(2,1)} %param.3) | copy-start | bytes 11796484
  4.8 3.7 %copy-start = (s32[32,2]{0,1:T(2,128)S(1)}, s32[32,2]{0,1:T(2,128)}, u32[]{:S(2)}) copy-start(s32[32,2]{0,1:T(2,128)} %param.4) | copy-start | bytes 772
  10.6 44.3 %all-to-all-start = ((bf16[8,1,128,768]{3,2,1,0:T(8,128)(2,1)}), bf16[8,1,128,768]{3,2,1,0:T(8,128)(2,1)S(1)}, u32[]{:S(2)}, u32[]{:S(2)}) async-start(bf16[8,1,128,768]{3,2,1,0:T(8,128)(2,1)} %bitcast.7), calls=%async_computation | async-start | bytes 3145728 | tf_op jit(solution)/shard_map/all_to_all | solution.py:119
  58.1 13.8 %copy-start.2 = (s32[4]{0:T(128)S(1)}, s32[4]{0:T(128)}, u32[]{:S(2)}) copy-start(s32[4]{0:T(128)} %param.5) | copy-start | bytes 52
  66.0 2.7 %collective-permute-start = (bf16[16,64,512]{2,1,0:T(8,128)(2,1)S(1)}, bf16[16,64,512]{2,1,0:T(8,128)(2,1)S(1)}, u32[]{:S(2)}, u32[]{:S(2)}) collective-permute-start(bf16[16,64,512]{2,1,0:T(8,128)(2,1)S(1)} %dynamic-slice_bitcast_fusion), channel_id=1, source_target_pairs={{0,8},{8,0},{16,24},{24,16},{1,9},{9,1},{17,25},{25,17},{2,10},{10... | collective-permute-start | bytes 3145736 | tf_op jit(solution)/shard_map/ppermute | solution.py:141
  70.3 14.0 %collective-permute-start.1 = (bf16[16,32,512]{2,1,0:T(8,128)(2,1)S(1)}, bf16[16,32,512]{2,1,0:T(8,128)(2,1)S(1)}, u32[]{:S(2)}, u32[]{:S(2)}) collective-permute-start(bf16[16,32,512]{2,1,0:T(8,128)(2,1)S(1)} %fusion.10), channel_id=1, source_target_pairs={{0,16},{8,24},{16,0},{24,8},{1,17},{9,25},{17,1},{25,9},{2,18},{10... | collective-permute-start | bytes 1572872 | tf_op jit(solution)/shard_map/ppermute | solution.py:149

commit v6 on v5

--- a/solution.py
+++ b/solution.py
@@ -12,7 +12,7 @@
 F = 384
 LAGS = 16
 DECIM = 32
-SPLIT = 128
+SPLIT = 256
 
 
 def cos_sin(product, sample_count):
@@ -20,27 +20,56 @@
     return jnp.cos(angle), jnp.sin(angle)
 
 
-def dft_table(sample_count, bin_count):
-    bin_index = lax.iota(jnp.int32, bin_count) + 1
-    coarse = lax.iota(jnp.int32, sample_count // SPLIT) * SPLIT
-    fine = lax.iota(jnp.int32, SPLIT)
-    ca, sa = cos_sin(coarse[:, None] * bin_index[None, :], sample_count)
-    cb, sb = cos_sin(fine[:, None] * bin_index[None, :], sample_count)
-    cos_t = ca[:, None, :] * cb[None, :, :] - sa[:, None, :] * sb[None, :, :]
-    sin_t = sa[:, None, :] * cb[None, :, :] + ca[:, None, :] * sb[None, :, :]
-    table = jnp.concatenate([cos_t, -sin_t], axis=2).astype(jnp.bfloat16)
-    return table.reshape(sample_count, 2 * bin_count)
+def dft_kernel(group, bin_count, ca_ref, sa_ref, cb_ref, sb_ref, x_ref, out_ref, acc_ref):
+    k = pl.program_id(0)
+
+    @pl.when(k == 0)
+    def _():
+        acc_ref[...] = jnp.zeros_like(acc_ref)
+
+    cb = cb_ref[...]
+    sb = sb_ref[...]
+    for g in range(group):
+        a = k * group + g
+        ca = ca_ref[pl.ds(a, 1), :]
+        sa = sa_ref[pl.ds(a, 1), :]
+        table = jnp.concatenate([ca * cb - sa * sb, -(sa * cb + ca * sb)], axis=1).astype(jnp.bfloat16)
+        acc_ref[...] += jnp.dot(x_ref[:, g * SPLIT : (g + 1) * SPLIT], table, preferred_element_type=jnp.float32)
+
+    @pl.when(k == pl.num_programs(0) - 1)
+    def _():
+        spectrum = acc_ref[...]
+        real_part = spectrum[:, :bin_count]
+        imag_part = spectrum[:, bin_count:]
+        amplitude = jnp.sqrt(real_part * real_part + imag_part * imag_part)
+        level = 0.2 * jnp.mean(amplitude, axis=1, keepdims=True) + 1e-06
+        divisor = jnp.maximum(amplitude, level)
+        out_ref[...] = jnp.concatenate([real_part / divisor, imag_part / divisor], axis=1).astype(out_ref.dtype)
 
 
 def whiten_rows(strain_rows, bin_count):
-    sample_count = strain_rows.shape[1]
-    spectrum = jnp.dot(strain_rows, dft_table(sample_count, bin_count), preferred_element_type=jnp.float32)
-    real_part = spectrum[:, :bin_count]
-    imag_part = spectrum[:, bin_count:]
-    amplitude = jnp.sqrt(real_part * real_part + imag_part * imag_part)
-    level = 0.2 * jnp.mean(amplitude, axis=1, keepdims=True) + 1e-06
-    divisor = jnp.maximum(amplitude, level)
-    return jnp.concatenate([real_part / divisor, imag_part / divisor], axis=1).astype(jnp.bfloat16)
+    row_count, sample_count = strain_rows.shape
+    bin_index = lax.iota(jnp.int32, bin_count) + 1
+    coarse_count = sample_count // SPLIT
+    ca, sa = cos_sin((lax.iota(jnp.int32, coarse_count) * SPLIT)[:, None] * bin_index[None, :], sample_count)
+    cb, sb = cos_sin(lax.iota(jnp.int32, SPLIT)[:, None] * bin_index[None, :], sample_count)
+    group = max(g for g in range(1, 7) if coarse_count % g == 0)
+    steps = coarse_count // group
+    full = lambda shape: pl.BlockSpec(shape, lambda k: (0, 0))
+    return pl.pallas_call(
+        functools.partial(dft_kernel, group, bin_count),
+        grid=(steps,),
+        in_specs=[full(ca.shape), full(sa.shape), full(cb.shape), full(sb.shape)]
+        + [pl.BlockSpec((row_count, group * SPLIT), lambda k: (0, k))],
+        out_specs=pl.BlockSpec((row_count, 2 * bin_count), lambda k: (0, 0)),
+        out_shape=jax.ShapeDtypeStruct((row_count, 2 * bin_count), jnp.bfloat16),
+        scratch_shapes=[pltpu.VMEM((row_count, 2 * bin_count), jnp.float32)],
+        cost_estimate=pl.CostEstimate(
+            flops=2 * row_count * sample_count * 2 * bin_count,
+            transcendentals=0,
+            bytes_accessed=row_count * sample_count * 2 + row_count * 2 * bin_count * 2,
+        ),
+    )(ca, sa, cb, sb, strain_rows)
 
 
 def correlation_kernel(sub, cc_ref, sc_ref, cf_ref, sf_ref, left_ref, right_ref, out_ref):

time: 87.2 us -> 91.5 us (1.049)
  Pallas kernels: 6.49 us -> 13.9 us
  matrix products: 3.2 us -> 0 us
  other arithmetic: 9.82 us -> 7.54 us
  local copies, waits for them, and re-layouts: 8.74 us -> 10.8 us
    pallas_call x0 -> x1, Pallas kernels: none -> 7.42 us  [whiten_rows(): pl.pallas_call(functools.partial(dft_kernel, group, bin_count), grid=(ste...]
    another operation x2 -> x0, other arithmetic: 3.7 us -> none
    sin x2 -> x4, other arithmetic: 2.2 us -> 5.69 us  [cos_sin(): return (jnp.cos(angle), jnp.sin(angle))]
    dot_general x1 -> x0, matrix products: 3.2 us -> none  [whiten_rows(): jnp.dot(strain_rows, dft_table(sample_count, bin_count), preferred_elemen...]
    cos x2 -> x0, other arithmetic: 1.28 us -> none  [cos_sin(): return (jnp.cos(angle), jnp.sin(angle))]
    add x1, other arithmetic: 1.54 us -> 0.34 us  [body(): keep + got.astype(jnp.float32)]
    gather x1, local copies, waits for them, and re-layouts: 1.31 us -> 2.44 us  [body(): send = jnp.take(corr, 1 - core, axis=0, mode='clip')]
    gather x1, local copies, waits for them, and re-layouts: 1.8 us -> 2.79 us  [body(): jnp.take(jnp.transpose(whitened, (1, 0, 2, 3)), local_pick, axis=0, mode=...]
where the time goes in v6:
time: 91.5 us; the launch traced here: 91.1 us
  waiting for transfers between devices  49.7 us (54%)
  Pallas kernels  13.9 us (15%)
  local copies, waits for them, and re-layouts  10.8 us (12%)
  starting transfers between devices  8.96 us (10%)
  other arithmetic  7.54 us (8%)
    all_to_all x1, waiting for transfers between devices, body(): incoming = lax.all_to_all(outgoing, 'pair', 0, 0, tiled=True)  34.4 us
    ppermute x1, waiting for transfers between devices, body(): total = total + lax.ppermute(piece, 'win', perm).astype(jnp.float32)  12.4 us
    pallas_call x1, Pallas kernels, whiten_rows(): pl.pallas_call(functools.partial(dft_kernel, group, bin_count), grid=(ste...  7.42 us
    all_to_all x1, starting transfers between devices, body(): incoming = lax.all_to_all(outgoing, 'pair', 0, 0, tiled=True)  7.38 us
    pallas_call x1, Pallas kernels, tile_correlation(): pl.pallas_call(functools.partial(correlation_kernel, sub), grid=(slot_cou...  6.47 us
    sin x4, other arithmetic, cos_sin(): return (jnp.cos(angle), jnp.sin(angle))  5.69 us
    ppermute x1, waiting for transfers between devices, body(): got = lax.ppermute(send, 'win', [(w, w ^ 1) for w in range(n_win)])  2.87 us
    gather x1, local copies, waits for them, and re-layouts, body(): jnp.take(jnp.transpose(whitened, (1, 0, 2, 3)), local_pick, axis=0, mode=...  2.79 us
  transfers between devices with their start and end apart: 3, of which 3 were waited for; matrix products, arithmetic and copies ran while one was open for 3% of the time, Pallas kernels for 0%

profile of v6, /device:TPU:0, one launch (start us, length us, event | category | flops | bytes accessed | tf_op | source)
XLA Modules:
  0.0 91.1 jit_solution(15569232806533726139)
XLA Ops:
  0.0 0.7 fusion.26
  0.7 0.1 reduce_sum.14
  0.8 0.1 reduce_sum.18
  0.9 2.5 %fusion.5 = (f32[256,384]{1,0:T(8,128)}, f32[256,384]{1,0:T(8,128)}) fusion(s32[384]{0:T(512)S(1)} %iota_add_fusion), kind=kLoop, calls=%fused_computation.15 | loop fusion | flops 884736 | bytes 787968 | tf_op jit(solution)/shard_map/sin | solution.py:20
  3.5 0.9 %fusion.12 = (f32[30,384]{1,0:T(8,128)}, f32[30,384]{1,0:T(8,128)}) fusion(s32[384]{0:T(512)S(1)} %iota_add_fusion, s32[30]{0:T(128)S(1)} %iota_multiply_fusion), kind=kLoop, calls=%fused_computation.26 | loop fusion | flops 103680 | bytes 93816 | tf_op jit(solution)/shard_map/sin | solution.py:20
  4.4 7.4 %shard_map.37 = bf16[256,768]{1,0:T(8,128)(2,1)} custom-call(f32[30,384]{1,0:T(8,128)} %get-tuple-element.52.ca_ref, f32[30,384]{1,0:T(8,128)} %get-tuple-element.51.sa_ref, f32[256,384]{1,0:T(8,128)} %get-tuple-element.56.cb_ref, f32[256,384]{1,0:T(8,128)} %get-tuple-element.55.sb_ref, bf16[256,7680]{1,0:T(8,128)(2,1)} %bitcast.39), custom_call_target="tpu_custom_call" | custom-call | flops 3019898880 | bytes 4325376 | tf_op jit(solution)/shard_map/pallas_call | solution.py:59
  11.8 2.8 %gather_fusion = bf16[8,128,768]{2,1,0:T(8,128)(2,1)} fusion(bf16[2,128,768]{2,1,0:T(8,128)(2,1)} %bitcast.35, s32[1024]{0:T(1024)S(1)} %pad_clamp_fusion.2), kind=kCustom, calls=%fused_computation | custom fusion | bytes 3145760 | tf_op jit(solution)/shard_map/jit(_take)/gather | solution.py:147
  14.6 0.0 copy-start.1
  14.6 7.4 %all-to-all-start = ((bf16[8,1,128,768]{3,2,1,0:T(8,128)(2,1)}), bf16[8,1,128,768]{3,2,1,0:T(8,128)(2,1)S(1)}, u32[]{:S(2)}, u32[]{:S(2)}) async-start(bf16[8,1,128,768]{3,2,1,0:T(8,128)(2,1)} %bitcast.2), calls=%async_computation | async-start | bytes 3145728 | tf_op jit(solution)/shard_map/all_to_all | solution.py:148
  22.0 0.1 fusion.17
  22.1 0.1 copy.12
  22.2 0.0 copy-done.1
  22.2 0.1 constant_dynamic-slice_fusion
  22.3 0.7 fusion.24
  23.1 1.5 %multiply_sine_fusion = (f32[384,4]{1,0:T(8,128)}, f32[384,4]{1,0:T(8,128)}) fusion(f32[384,4]{1,0:T(8,128)S(1)} %copy.12), kind=kLoop, calls=%fused_computation.18 | loop fusion | flops 1536 | bytes 18432 | tf_op jit(solution)/shard_map/sin | solution.py:20
  24.6 34.4 %all-to-all-done = bf16[8,1,128,768]{3,2,1,0:T(8,128)(2,1)S(1)} async-done(((bf16[8,1,128,768]{3,2,1,0:T(8,128)(2,1)}), bf16[8,1,128,768]{3,2,1,0:T(8,128)(2,1)S(1)}, u32[]{:S(2)}, u32[]{:S(2)}) %all-to-all-start) | async-done | bytes 1572896 | tf_op jit(solution)/shard_map/all_to_all | solution.py:148
  59.0 0.6 gather_fusion.2
  59.6 0.6 gather_fusion.1
  60.2 0.9 %copy.13 = bf16[4,1,2,2,32,768]{5,4,3,2,0,1:T(8,128)(2,1)} copy(bf16[4,1,2,2,32,768]{5,4,2,3,0,1:T(8,128)(2,1)S(1)} %bitcast.36) | data formatting | bytes 1572864 | tf_op jit(solution)/shard_map/transpose | solution.py:162
  61.1 1.1 %copy.14 = bf16[4,128,768]{1,2,0:T(8,128)(2,1)} copy(bf16[4,128,768]{2,1,0:T(8,128)(2,1)S(1)} %gather_fusion.2) | data formatting | bytes 1572864 | tf_op jit(solution)/shard_map/jit(_take)/gather | solution.py:151
  62.3 6.5 %shard_map.38 = bf16[2,16,64,512]{3,2,1,0:T(8,128)(2,1)} custom-call(f32[4,384]{1,0:T(4,128)} %get-tuple-element.54.cc_ref, f32[4,384]{1,0:T(4,128)} %get-tuple-element.53.sc_ref, f32[384,4]{1,0:T(8,128)} %get-tuple-element.50.cf_ref, f32[384,4]{1,0:T(8,128)} %get-tuple-element.49.sf_ref, bf16[4,1,128,768]{3,2,1,0:T(8,128)(2,1)} %bitcast.37, ...), custom_call_target="tpu_custom_call" | custom-call | flops 1610612736 | bytes 3670016 | tf_op jit(solution)/shard_map/pallas_call | solution.py:120
  68.8 0.0 copy-start
  68.8 2.4 %dynamic-slice_bitcast_fusion = bf16[16,64,512]{2,1,0:T(8,128)(2,1)} fusion(bf16[2,16,64,512]{3,2,1,0:T(8,128)(2,1)} %shard_map.38, s32[]{:T(128)S(6)} %sub.29), kind=kLoop, calls=%fused_computation.6 | loop fusion | bytes 2097156 | tf_op jit(solution)/shard_map/jit(_take)/gather | solution.py:168
  71.2 0.0 collective-permute-start
  71.2 0.0 copy-start.2
  71.2 2.9 %collective-permute-done = bf16[16,64,512]{2,1,0:T(8,128)(2,1)S(1)} collective-permute-done((bf16[16,64,512]{2,1,0:T(8,128)(2,1)}, bf16[16,64,512]{2,1,0:T(8,128)(2,1)S(1)}, u32[]{:S(2)}, u32[]{:S(2)}) %collective-permute-start) | collective-permute-done | bytes 1048608 | tf_op jit(solution)/shard_map/ppermute | solution.py:170
  74.1 0.0 copy-done
  74.1 0.3 convert_add_fusion
  74.4 0.1 fusion
  74.5 1.6 %collective-permute-start.1 = (bf16[16,32,512]{2,1,0:T(8,128)(2,1)S(1)}, bf16[16,32,512]{2,1,0:T(8,128)(2,1)S(1)}, u32[]{:S(2)}, u32[]{:S(2)}) collective-permute-start(bf16[16,32,512]{2,1,0:T(8,128)(2,1)S(1)} %fusion), channel_id=1, source_target_pairs={{0,16},{8,24},{16,0},{24,8},{1,17},{9,25},{17,1},{25,9},{2,18},{10... | collective-permute-start | bytes 1572872 | tf_op jit(solution)/shard_map/ppermute | solution.py:178
  76.1 0.0 copy-done.2
  76.1 12.4 %collective-permute-done.1 = bf16[16,32,512]{2,1,0:T(8,128)(2,1)S(1)} collective-permute-done((bf16[16,32,512]{2,1,0:T(8,128)(2,1)S(1)}, bf16[16,32,512]{2,1,0:T(8,128)(2,1)S(1)}, u32[]{:S(2)}, u32[]{:S(2)}) %collective-permute-start.1) | collective-permute-done | bytes 524320 | tf_op jit(solution)/shard_map/ppermute | solution.py:178
  88.5 0.2 bitcast_add_fusion
  88.7 0.4 reshape.40
  89.1 0.4 multiply_bitcast_fusion
  89.5 1.6 %copy.16 = f32[32,4,16,128]{3,2,1,0:T(8,128)} copy(f32[32,4,16,128]{3,1,0,2:T(4,128)S(1)} %multiply_bitcast_fusion) | data formatting | bytes 2097152 | tf_op jit(solution)/shard_map/div | solution.py:182
  (8 shorter events, 0.0 us)
Async XLA Ops:
  14.6 7.6 %copy-start.1 = (s32[32,2]{0,1:T(2,128)S(1)}, s32[32,2]{0,1:T(2,128)}, u32[]{:S(2)}) copy-start(s32[32,2]{0,1:T(2,128)} %param.4) | copy-start | bytes 772
  14.6 44.4 %all-to-all-start = ((bf16[8,1,128,768]{3,2,1,0:T(8,128)(2,1)}), bf16[8,1,128,768]{3,2,1,0:T(8,128)(2,1)S(1)}, u32[]{:S(2)}, u32[]{:S(2)}) async-start(bf16[8,1,128,768]{3,2,1,0:T(8,128)(2,1)} %bitcast.2), calls=%async_computation | async-start | bytes 3145728 | tf_op jit(solution)/shard_map/all_to_all | solution.py:148
  68.8 5.3 %copy-start = (bf16[2,16,64,512]{3,2,1,0:T(8,128)(2,1)S(1)}, bf16[2,16,64,512]{3,2,1,0:T(8,128)(2,1)}, u32[]{:S(2)}) copy-start(bf16[2,16,64,512]{3,2,1,0:T(8,128)(2,1)} %shard_map.38) | copy-start | bytes 6291460
  71.2 2.9 %collective-permute-start = (bf16[16,64,512]{2,1,0:T(8,128)(2,1)}, bf16[16,64,512]{2,1,0:T(8,128)(2,1)S(1)}, u32[]{:S(2)}, u32[]{:S(2)}) collective-permute-start(bf16[16,64,512]{2,1,0:T(8,128)(2,1)} %dynamic-slice_bitcast_fusion), channel_id=1, source_target_pairs={{0,8},{8,0},{16,24},{24,16},{1,9},{9,1},{17,25},{25,17},{2,10},{10... | collective-permute-start | bytes 3145736 | tf_op jit(solution)/shard_map/ppermute | solution.py:170
  71.2 4.9 %copy-start.2 = (s32[4]{0:T(128)S(1)}, s32[4]{0:T(128)}, u32[]{:S(2)}) copy-start(s32[4]{0:T(128)} %param.5) | copy-start | bytes 52
  74.5 14.0 %collective-permute-start.1 = (bf16[16,32,512]{2,1,0:T(8,128)(2,1)S(1)}, bf16[16,32,512]{2,1,0:T(8,128)(2,1)S(1)}, u32[]{:S(2)}, u32[]{:S(2)}) collective-permute-start(bf16[16,32,512]{2,1,0:T(8,128)(2,1)S(1)} %fusion), channel_id=1, source_target_pairs={{0,16},{8,24},{16,0},{24,8},{1,17},{9,25},{17,1},{25,9},{2,18},{10... | collective-permute-start | bytes 1572872 | tf_op jit(solution)/shard_map/ppermute | solution.py:178

commit v7 on v5

--- a/solution.py
+++ b/solution.py
@@ -43,33 +43,36 @@
     return jnp.concatenate([real_part / divisor, imag_part / divisor], axis=1).astype(jnp.bfloat16)
 
 
-def correlation_kernel(sub, cc_ref, sc_ref, cf_ref, sf_ref, left_ref, right_ref, out_ref):
+def correlation_kernel(sub, n_y, own_rows, index_ref, cc_ref, sc_ref, cf_ref, sf_ref, left_ref, right_ref, out_ref):
     window_count = left_ref.shape[1]
+    order = [(y * 2 + c) * own_rows for c in range(2) for y in range(n_y)]
     acc = None
     for w in range(window_count):
-        lre = left_ref[0, w, :, :F].astype(jnp.float32)
-        lim = left_ref[0, w, :, F:].astype(jnp.float32)
-        rre = right_ref[0, w, :F, :].astype(jnp.float32)
-        rim = right_ref[0, w, F:, :].astype(jnp.float32)
+        left = left_ref[0, w].astype(jnp.float32)
+        left = jnp.concatenate([left[r : r + own_rows] for r in order], axis=0)
+        lre = left[:, :F]
+        lim = left[:, F:]
+        rre = right_ref[0, w, :, :F].astype(jnp.float32)
+        rim = right_ref[0, w, :, F:].astype(jnp.float32)
         turned = []
         for l1 in range(sub):
             if l1 == 0:
                 turned.append(right_ref[0, w])
                 continue
-            c = cf_ref[:, l1 : l1 + 1]
-            s = sf_ref[:, l1 : l1 + 1]
-            turned.append(jnp.concatenate([rre * c + rim * s, rim * c - rre * s], axis=0).astype(jnp.bfloat16))
-        right_all = jnp.concatenate(turned, axis=1)
+            c = cf_ref[l1 : l1 + 1, :]
+            s = sf_ref[l1 : l1 + 1, :]
+            turned.append(jnp.concatenate([rre * c + rim * s, rim * c - rre * s], axis=1).astype(jnp.bfloat16))
+        right_all = jnp.concatenate(turned, axis=0)
         parts = []
         for l2 in range(LAGS // sub):
             if l2 * sub == LAGS // 2:
-                left_t = left_ref[0, w]
+                left_t = left.astype(jnp.bfloat16)
             else:
                 c = cc_ref[l2 : l2 + 1, :]
                 s = sc_ref[l2 : l2 + 1, :]
                 left_t = jnp.concatenate([lre * c - lim * s, lre * s + lim * c], axis=1).astype(jnp.bfloat16)
             parts.append(
-                jnp.dot(left_t, right_all, preferred_element_type=jnp.float32)
+                lax.dot_general(left_t, right_all, (((1,), (1,)), ((), ())), preferred_element_type=jnp.float32)
             )
         acc = parts if acc is None else [a + p for a, p in zip(acc, parts)]
     half_rows = C // 2
@@ -81,23 +84,27 @@
                 )
 
 
-def tile_correlation(cc, sc, cf, sf, left, right, sub):
-    slot_count, window_count = left.shape[:2]
-    table_spec = pl.BlockSpec(cc.shape, lambda t: (0, 0))
-    column_spec = pl.BlockSpec(cf.shape, lambda t: (0, 0))
-    block_spec = pl.BlockSpec((1, window_count, C, 2 * F), lambda t: (t, 0, 0, 0))
-    right_spec = pl.BlockSpec((1, window_count, 2 * F, C), lambda t: (t, 0, 0, 0))
+def tile_correlation(cc, sc, cf, sf, incoming, slots, sub, n_y, own_rows):
+    window_count = incoming.shape[1]
+    slot_count = slots.shape[0] // 2
+    table_spec = pl.BlockSpec(cc.shape, lambda t, idx: (0, 0))
+    left_spec = pl.BlockSpec((1, window_count, C, 2 * F), lambda t, idx: (idx[2 * t], 0, 0, 0))
+    right_spec = pl.BlockSpec((1, window_count, C, 2 * F), lambda t, idx: (idx[2 * t + 1], 0, 0, 0))
     flops = 2 * slot_count * window_count * C * 2 * F * LAGS * C
+    grid_spec = pltpu.PrefetchScalarGridSpec(
+        num_scalar_prefetch=1,
+        grid=(slot_count,),
+        in_specs=[table_spec] * 4 + [left_spec, right_spec],
+        out_specs=pl.BlockSpec((2, LAGS, C // 2, C), lambda t, idx: (0, 0, 0, t)),
+    )
     return pl.pallas_call(
-        functools.partial(correlation_kernel, sub),
-        grid=(slot_count,),
-        in_specs=[table_spec] * 2 + [column_spec] * 2 + [block_spec, right_spec],
-        out_specs=pl.BlockSpec((2, LAGS, C // 2, C), lambda t: (0, 0, 0, t)),
+        functools.partial(correlation_kernel, sub, n_y, own_rows),
+        grid_spec=grid_spec,
         out_shape=jax.ShapeDtypeStruct((2, LAGS, C // 2, slot_count * C), jnp.bfloat16),
         cost_estimate=pl.CostEstimate(
             flops=flops, transcendentals=0, bytes_accessed=slot_count * (4 * window_count * C * F * 2 + 2 * C * LAGS * C)
         ),
-    )(cc, sc, cf, sf, left, right)
+    )(slots, cc, sc, cf, sf, incoming, incoming)
 
 
 def body(strain, pair_list, tile_live):
@@ -115,11 +122,13 @@
     lists = pair_list.reshape(n_pair, 2 * slot_count)
     mine = (lists // b_dev) == pair_here
     local_pick = jnp.sum(jnp.where(mine, lists % b_dev, 0), axis=1)
-    outgoing = jnp.take(jnp.transpose(whitened, (1, 0, 2, 3)), local_pick, axis=0, mode="clip")
+    pick = local_pick[:, None, None, None]
+    outgoing = jnp.broadcast_to(whitened[:, 0][None], (n_pair,) + whitened[:, 0].shape)
+    for k in range(1, b_dev):
+        outgoing = jnp.where(pick == k, whitened[:, k][None], outgoing)
     incoming = lax.all_to_all(outgoing, "pair", 0, 0, tiled=True)
     wanted = lax.dynamic_slice_in_dim(pair_list, pair_here * slot_count, slot_count, 0)
-    left = jnp.take(incoming, wanted[:, 0] // b_dev, axis=0, mode="clip")
-    right = jnp.take(incoming, wanted[:, 1] // b_dev, axis=0, mode="clip")
+    slots = jnp.clip(wanted.reshape(2 * slot_count) // b_dev, 0, n_pair - 1)
 
     sub = 4
     own_rows = C // n_win
@@ -129,10 +138,7 @@
     coarse_lag = (lax.iota(jnp.int32, LAGS // sub) * sub - LAGS // 2) * DECIM
     cf, sf = cos_sin(fine_lag[:, None] * bins[None, :], sample_count)
     cc, sc = cos_sin(coarse_lag[:, None] * bins[None, :], sample_count)
-    left = left.reshape(slot_count, window_count, n_y, 2, own_rows, 2 * F)
-    left = jnp.transpose(left, (0, 1, 3, 2, 4, 5)).reshape(slot_count, window_count, C, 2 * F)
-    right = jnp.swapaxes(right, 2, 3)
-    corr = tile_correlation(cc, sc, cf.T, sf.T, left, right, sub)
+    corr = tile_correlation(cc, sc, cf, sf, incoming, slots, sub, n_y, own_rows)
 
     core = win_here % 2
     y_here = win_here // 2

time: 87.2 us -> 85.5 us (0.981)
  local copies, waits for them, and re-layouts: 8.74 us -> 4.84 us
  waiting for transfers between devices: 49.5 us -> 50.4 us
    gather x4 -> x0, local copies, waits for them, and re-layouts: 4.15 us -> none  [the longest x1 1.8 us: body(): jnp.take(jnp.transpose(whitened, (1, 0, 2, 3)), local_pick, axis=0, mode=...]
    sin x2 -> x1, other arithmetic: 2.2 us -> 0.78 us  [cos_sin(): return (jnp.cos(angle), jnp.sin(angle))]
    select_n x1, other arithmetic: 0.01 us -> 1.35 us  [body(): outgoing = jnp.where(pick == k, whitened[:, k][None], outgoing)]
    unnamed x6 -> x8, local copies, waits for them, and re-layouts: 0.02 us -> 1.17 us
    transpose x1 -> x0, local copies, waits for them, and re-layouts: 0.94 us -> none  [body(): jnp.transpose(left, (0, 1, 3, 2, 4, 5))]
    all_to_all x1, waiting for transfers between devices: 34.4 us -> 35.4 us  [body(): incoming = lax.all_to_all(outgoing, 'pair', 0, 0, tiled=True)]
  transfers between devices with their start and end apart: 3 -> 3, of which waited for: 3 -> 3; matrix products, arithmetic and copies ran while one was open for 3% -> 2% of each run, Pallas kernels for 0% -> 0%
where the time goes in v7:
time: 85.5 us; the launch traced here: 85.1 us
  waiting for transfers between devices  50.4 us (59%)
  other arithmetic  10.2 us (12%)
  starting transfers between devices  8.91 us (10%)
  Pallas kernels  7.35 us (9%)
  local copies, waits for them, and re-layouts  4.84 us (6%)
  matrix products  3.2 us (4%)
    all_to_all x1, waiting for transfers between devices, body(): incoming = lax.all_to_all(outgoing, 'pair', 0, 0, tiled=True)  35.4 us
    ppermute x1, waiting for transfers between devices, body(): total = total + lax.ppermute(piece, 'win', perm).astype(jnp.float32)  12.4 us
    pallas_call x1, Pallas kernels, tile_correlation(): pl.pallas_call(functools.partial(correlation_kernel, sub, n_y, own_rows),...  7.35 us
    all_to_all x1, starting transfers between devices, body(): incoming = lax.all_to_all(outgoing, 'pair', 0, 0, tiled=True)  7.25 us
    another operation x2, other arithmetic  3.7 us
    dot_general x1, matrix products, whiten_rows(): jnp.dot(strain_rows, dft_table(sample_count, bin_count), preferred_elemen...  3.2 us
    ppermute x1, waiting for transfers between devices, body(): got = lax.ppermute(send, 'win', [(w, w ^ 1) for w in range(n_win)])  2.62 us
  transfers between devices with their start and end apart: 3, of which 3 were waited for; matrix products, arithmetic and copies ran while one was open for 2% of the time, Pallas kernels for 0%

profile of v7, /device:TPU:0, one launch (start us, length us, event | category | flops | bytes accessed | tf_op | source)
XLA Modules:
  0.0 85.1 jit_solution(2424619558472203355)
XLA Ops:
  0.0 0.8 fusion.19
  0.8 0.5 fusion.26
  1.3 0.0 copy-start.2
  1.3 3.5 %subtract_convert_fusion = (bf16[60,128,384]{2,1,0:T(8,128)(2,1)S(1)}, bf16[60,128,384]{2,1,0:T(8,128)(2,1)S(1)}) fusion(f32[128,384]{1,0:T(8,128)S(1)} %get-tuple-element.62, f32[60,384]{1,0:T(8,128)S(1)} %get-tuple-element.56, f32[128,384]{1,0:T(8,128)S(1)} %get-tuple-element.61, f32[60,384]{1,0:T(8,128)S(1)} %get-tuple-element.55), kind=kLoop, calls=%fused_computation.5 | loop fusion | flops 26542080 | bytes 12374016 | tf_op jit(solution)/shard_map/convert.7
  4.8 0.0 copy-done.2
  4.8 0.0 copy-start.1
  4.8 3.2 %fusion.5 = f32[256,768]{1,0:T(8,128)S(1)} fusion(bf16[7680,384]{1,0:T(8,128)(2,1)S(1)} %bitcast.34, bf16[7680,384]{1,0:T(8,128)(2,1)S(1)} %bitcast.33, bf16[1,256,7680]{2,1,0:T(8,128)(2,1)S(1)} %copy-done.2), kind=kOutput, calls=%fused_computation.9 | convolution fusion | flops 3043491840 | bytes 16515072 | tf_op jit(solution)/shard_map/dot_general | solution.py:37
  8.0 0.2 fusion.45
  8.3 0.2 divide_convert_fusion.1
  8.5 0.0 copy-done.1
  8.5 0.1 reduce_sum.26
  8.6 0.1 reduce_sum.27
  8.8 1.4 %broadcast_select_fusion = bf16[8,1,128,768]{3,2,1,0:T(8,128)(2,1)} fusion(pred[8]{0:T(512)(128)(4,1)S(1)} %broadcast_compare_fusion, bf16[128,768]{1,0:T(8,128)(2,1)S(1)} %get-tuple-element.54, bf16[128,768]{1,0:T(8,128)(2,1)S(1)} %get-tuple-element.53), kind=kLoop, calls=%fused_computation.8 | loop fusion | flops 786432 | bytes 1966088 | tf_op jit(solution)/shard_map/jit(_where)/select_n | solution.py:128
  10.1 7.3 %all-to-all-start = ((bf16[8,1,128,768]{3,2,1,0:T(8,128)(2,1)}), bf16[8,1,128,768]{3,2,1,0:T(8,128)(2,1)S(1)}, u32[]{:S(2)}, u32[]{:S(2)}) async-start(bf16[8,1,128,768]{3,2,1,0:T(8,128)(2,1)} %broadcast_select_fusion), calls=%async_computation | async-start | bytes 3145728 | tf_op jit(solution)/shard_map/all_to_all | solution.py:129
  17.4 0.1 constant_dynamic-slice_fusion
  17.5 0.1 copy.5
  17.5 0.1 reshape.208
  17.6 0.6 fusion.43.index_ref
  18.2 0.8 fusion.38
  19.0 35.4 %all-to-all-done.left_ref.right_ref = bf16[8,1,128,768]{3,2,1,0:T(8,128)(2,1)S(1)} async-done(((bf16[8,1,128,768]{3,2,1,0:T(8,128)(2,1)}), bf16[8,1,128,768]{3,2,1,0:T(8,128)(2,1)S(1)}, u32[]{:S(2)}, u32[]{:S(2)}) %all-to-all-start) | async-done | bytes 1572896 | tf_op jit(solution)/shard_map/all_to_all | solution.py:129
  54.4 0.0 copy-start
  54.4 1.1 %copy-done = bf16[8,1,128,768]{3,2,1,0:T(8,128)(2,1)} copy-done((bf16[8,1,128,768]{3,2,1,0:T(8,128)(2,1)}, bf16[8,1,128,768]{3,2,1,0:T(8,128)(2,1)S(1)}, u32[]{:S(2)}) %copy-start) | copy-done | bytes 1572888
  55.5 0.0 copy-start.3
  55.5 7.3 %shard_map.37 = bf16[2,16,64,512]{3,2,1,0:T(8,128)(2,1)} custom-call(s32[8]{0:T(128)} %fusion.43.index_ref, f32[4,384]{1,0:T(4,128)} %get-tuple-element.63.cc_ref, f32[4,384]{1,0:T(4,128)} %get-tuple-element.64.sc_ref, f32[4,384]{1,0:T(4,128)} %get-tuple-element.58.cf_ref, f32[4,384]{1,0:T(4,128)} %get-tuple-element.57.sf_ref, ...), custom_call_target="tpu_custom_call" | custom-call | flops 1610612736 | bytes 3670016 | tf_op jit(solution)/shard_map/pallas_call | solution.py:100
  62.9 1.3 %dynamic-slice_bitcast_fusion = bf16[16,64,512]{2,1,0:T(8,128)(2,1)S(1)} fusion(bf16[2,16,64,512]{3,2,1,0:T(8,128)(2,1)} %shard_map.37, s32[]{:T(128)S(6)} %sub.34), kind=kLoop, calls=%fused_computation.12 | loop fusion | bytes 2097156 | tf_op jit(solution)/shard_map/jit(_take)/gather | solution.py:145
  64.2 0.1 collective-permute-start
  64.3 2.6 %collective-permute-done = bf16[16,64,512]{2,1,0:T(8,128)(2,1)S(1)} collective-permute-done((bf16[16,64,512]{2,1,0:T(8,128)(2,1)S(1)}, bf16[16,64,512]{2,1,0:T(8,128)(2,1)S(1)}, u32[]{:S(2)}, u32[]{:S(2)}) %collective-permute-start) | collective-permute-done | bytes 1048608 | tf_op jit(solution)/shard_map/ppermute | solution.py:147
  66.9 1.5 %convert_add_fusion = f32[16,64,512]{2,1,0:T(8,128)S(1)} fusion(bf16[16,64,512]{2,1,0:T(8,128)(2,1)S(1)} %collective-permute-done, bf16[2,16,64,512]{3,2,1,0:T(8,128)(2,1)} %shard_map.37, s32[]{:T(128)S(6)} %select_n.107), kind=kLoop, calls=%fused_computation.7 | loop fusion | flops 1572864 | bytes 4194308 | tf_op jit(solution)/shard_map/add | solution.py:148
  68.5 0.1 fusion.10
  68.6 1.6 %collective-permute-start.1 = (bf16[16,32,512]{2,1,0:T(8,128)(2,1)S(1)}, bf16[16,32,512]{2,1,0:T(8,128)(2,1)S(1)}, u32[]{:S(2)}, u32[]{:S(2)}) collective-permute-start(bf16[16,32,512]{2,1,0:T(8,128)(2,1)S(1)} %fusion.10), channel_id=1, source_target_pairs={{0,16},{8,24},{16,0},{24,8},{1,17},{9,25},{17,1},{25,9},{2,18},{10... | collective-permute-start | bytes 1572872 | tf_op jit(solution)/shard_map/ppermute | solution.py:155
  70.2 0.0 copy-done.3
  70.2 12.4 %collective-permute-done.1 = bf16[16,32,512]{2,1,0:T(8,128)(2,1)S(1)} collective-permute-done((bf16[16,32,512]{2,1,0:T(8,128)(2,1)S(1)}, bf16[16,32,512]{2,1,0:T(8,128)(2,1)S(1)}, u32[]{:S(2)}, u32[]{:S(2)}) %collective-permute-start.1) | collective-permute-done | bytes 524320 | tf_op jit(solution)/shard_map/ppermute | solution.py:155
  82.6 0.2 bitcast_add_fusion
  82.8 0.4 reshape.211
  83.2 0.4 multiply_bitcast_fusion
  83.5 1.6 %copy.7 = f32[32,4,16,128]{3,2,1,0:T(8,128)} copy(f32[32,4,16,128]{3,1,0,2:T(4,128)S(1)} %multiply_bitcast_fusion) | data formatting | bytes 2097152 | tf_op jit(solution)/shard_map/div | solution.py:159
  (8 shorter events, 0.1 us)
Async XLA Ops:
  1.3 3.5 %copy-start.2 = (bf16[1,256,7680]{2,1,0:T(8,128)(2,1)S(1)}, bf16[1,256,7680]{2,1,0:T(8,128)(2,1)}, u32[]{:S(2)}) copy-start(bf16[1,256,7680]{2,1,0:T(8,128)(2,1)} %param.3) | copy-start | bytes 11796484
  4.8 3.7 %copy-start.1 = (s32[32,2]{0,1:T(2,128)S(1)}, s32[32,2]{0,1:T(2,128)}, u32[]{:S(2)}) copy-start(s32[32,2]{0,1:T(2,128)} %param.4) | copy-start | bytes 772
  10.1 44.3 %all-to-all-start = ((bf16[8,1,128,768]{3,2,1,0:T(8,128)(2,1)}), bf16[8,1,128,768]{3,2,1,0:T(8,128)(2,1)S(1)}, u32[]{:S(2)}, u32[]{:S(2)}) async-start(bf16[8,1,128,768]{3,2,1,0:T(8,128)(2,1)} %broadcast_select_fusion), calls=%async_computation | async-start | bytes 3145728 | tf_op jit(solution)/shard_map/all_to_all | solution.py:129
  54.4 1.2 %copy-start = (bf16[8,1,128,768]{3,2,1,0:T(8,128)(2,1)}, bf16[8,1,128,768]{3,2,1,0:T(8,128)(2,1)S(1)}, u32[]{:S(2)}) copy-start(bf16[8,1,128,768]{3,2,1,0:T(8,128)(2,1)S(1)} %all-to-all-done.left_ref.right_ref) | copy-start | bytes 4718596
  55.5 14.6 %copy-start.3 = (s32[4]{0:T(128)S(1)}, s32[4]{0:T(128)}, u32[]{:S(2)}) copy-start(s32[4]{0:T(128)} %param.5) | copy-start | bytes 52
  64.2 2.7 %collective-permute-start = (bf16[16,64,512]{2,1,0:T(8,128)(2,1)S(1)}, bf16[16,64,512]{2,1,0:T(8,128)(2,1)S(1)}, u32[]{:S(2)}, u32[]{:S(2)}) collective-permute-start(bf16[16,64,512]{2,1,0:T(8,128)(2,1)S(1)} %dynamic-slice_bitcast_fusion), channel_id=1, source_target_pairs={{0,8},{8,0},{16,24},{24,16},{1,9},{9,1},{17,25},{25,17},{2,10},{10... | collective-permute-start | bytes 3145736 | tf_op jit(solution)/shard_map/ppermute | solution.py:147
  68.6 14.0 %collective-permute-start.1 = (bf16[16,32,512]{2,1,0:T(8,128)(2,1)S(1)}, bf16[16,32,512]{2,1,0:T(8,128)(2,1)S(1)}, u32[]{:S(2)}, u32[]{:S(2)}) collective-permute-start(bf16[16,32,512]{2,1,0:T(8,128)(2,1)S(1)} %fusion.10), channel_id=1, source_target_pairs={{0,16},{8,24},{16,0},{24,8},{1,17},{9,25},{17,1},{25,9},{2,18},{10... | collective-permute-start | bytes 1572872 | tf_op jit(solution)/shard_map/ppermute | solution.py:155

commit v8 on v7

--- a/solution.py
+++ b/solution.py
@@ -107,6 +107,44 @@
     )(slots, cc, sc, cf, sf, incoming, incoming)
 
 
+def block_choice(lists, group, b_dev):
+    return jnp.sum(jnp.where((lists // b_dev) == group, lists % b_dev, 0), axis=1)
+
+
+def pick_blocks(blocks, choice):
+    pick = choice[:, None, None, None]
+    out = jnp.broadcast_to(blocks[:, 0][None], choice.shape + blocks[:, 0].shape)
+    for k in range(1, blocks.shape[1]):
+        out = jnp.where(pick == k, blocks[:, k][None], out)
+    return out
+
+
+def exchange_by_halves(whitened, lists, groups, pair_here, b_dev):
+    n_pair = lists.shape[0]
+    half = n_pair // 2
+    base = (pair_here // half) * half
+    pos = pair_here % half
+    mirror_blocks = lax.ppermute(whitened, "pair", [(p, p ^ half) for p in range(n_pair)])
+    own_choice = block_choice(lists, pair_here, b_dev)
+    mirror_choice = block_choice(lists, pair_here ^ half, b_dev)
+    arrived_own = []
+    arrived_relay = []
+    for d in range(half):
+        dest = base + (pos + d) % half
+        own = pick_blocks(whitened, jnp.take(own_choice, dest[None], mode="clip"))[0]
+        relay = pick_blocks(mirror_blocks, jnp.take(mirror_choice, dest[None], mode="clip"))[0]
+        if d:
+            perm = [(p, (p // half) * half + (p % half + d) % half) for p in range(n_pair)]
+            own = lax.ppermute(own, "pair", perm)
+            relay = lax.ppermute(relay, "pair", perm)
+        arrived_own.append(own)
+        arrived_relay.append(relay)
+    incoming = jnp.stack(arrived_own + arrived_relay)
+    step = (pos - groups % half) % half
+    slots = jnp.where(groups // half == pair_here // half, step, half + step)
+    return incoming, slots
+
+
 def body(strain, pair_list, tile_live):
     window_count, local_rows, sample_count = strain.shape
     slot_count = tile_live.shape[0]
@@ -120,15 +158,15 @@
     whitened = whiten_rows(flat_rows, F).reshape(window_count, b_dev, C, 2 * F)
 
     lists = pair_list.reshape(n_pair, 2 * slot_count)
-    mine = (lists // b_dev) == pair_here
-    local_pick = jnp.sum(jnp.where(mine, lists % b_dev, 0), axis=1)
-    pick = local_pick[:, None, None, None]
-    outgoing = jnp.broadcast_to(whitened[:, 0][None], (n_pair,) + whitened[:, 0].shape)
-    for k in range(1, b_dev):
-        outgoing = jnp.where(pick == k, whitened[:, k][None], outgoing)
-    incoming = lax.all_to_all(outgoing, "pair", 0, 0, tiled=True)
     wanted = lax.dynamic_slice_in_dim(pair_list, pair_here * slot_count, slot_count, 0)
-    slots = jnp.clip(wanted.reshape(2 * slot_count) // b_dev, 0, n_pair - 1)
+    groups = wanted.reshape(2 * slot_count) // b_dev
+    if n_pair == 8:
+        incoming, slots = exchange_by_halves(whitened, lists, groups, pair_here, b_dev)
+    else:
+        outgoing = pick_blocks(whitened, block_choice(lists, pair_here, b_dev))
+        incoming = lax.all_to_all(outgoing, "pair", 0, 0, tiled=True)
+        slots = groups
+    slots = jnp.clip(slots, 0, n_pair - 1)
 
     sub = 4
     own_rows = C // n_win

time: 85.5 us -> 78.3 us (0.916)
  waiting for transfers between devices: 50.4 us -> 32.5 us
  between operations: 0.17 us -> 5.2 us
  starting transfers between devices: 8.91 us -> 13.2 us
  local copies, waits for them, and re-layouts: 4.84 us -> 6.82 us
    all_to_all x1 -> x0, waiting for transfers between devices: 35.4 us -> none  [body(): incoming = lax.all_to_all(outgoing, 'pair', 0, 0, tiled=True)]
    ppermute x0 -> x7, waiting for transfers between devices: none -> 17.1 us  [the longest x1 7.59 us: exchange_by_halves(): lax.ppermute(whitened, 'pair', [(p, p ^ half) for p in range(n_pair)])]
    ppermute x0 -> x7, starting transfers between devices: none -> 11.6 us  [the longest x3 6 us: exchange_by_halves(): own = lax.ppermute(own, 'pair', perm)]
    all_to_all x1 -> x0, starting transfers between devices: 7.25 us -> none  [body(): incoming = lax.all_to_all(outgoing, 'pair', 0, 0, tiled=True)]
    select_n x1 -> x0, other arithmetic: 1.35 us -> none  [body(): outgoing = jnp.where(pick == k, whitened[:, k][None], outgoing)]
    add x1, other arithmetic: 1.54 us -> 0.34 us  [body(): keep + got.astype(jnp.float32)]
    gather x1, local copies, waits for them, and re-layouts: 1.31 us -> 2.44 us  [body(): send = jnp.take(corr, 1 - core, axis=0, mode='clip')]
  transfers between devices with their start and end apart: 3 -> 9, of which waited for: 3 -> 8; matrix products, arithmetic and copies ran while one was open for 2% -> 4% of each run, Pallas kernels for 0% -> 0%
where the time goes in v8:
time: 78.3 us; the launch traced here: 78 us
  waiting for transfers between devices  32.5 us (42%)
  starting transfers between devices  13.2 us (17%)
  other arithmetic  9.87 us (13%)
  Pallas kernels  7.22 us (9%)
  local copies, waits for them, and re-layouts  6.82 us (9%)
  between operations  5.2 us (7%)
  matrix products  3.2 us (4%)
    ppermute x1, waiting for transfers between devices, body(): total = total + lax.ppermute(piece, 'win', perm).astype(jnp.float32)  12.4 us
    ppermute x1, waiting for transfers between devices, exchange_by_halves(): lax.ppermute(whitened, 'pair', [(p, p ^ half) for p in range(n_pair)])  7.59 us
    pallas_call x1, Pallas kernels, tile_correlation(): pl.pallas_call(functools.partial(correlation_kernel, sub, n_y, own_rows),...  7.22 us
    ppermute x3, starting transfers between devices, exchange_by_halves(): own = lax.ppermute(own, 'pair', perm)  6 us
    ppermute x3, waiting for transfers between devices, exchange_by_halves(): relay = lax.ppermute(relay, 'pair', perm)  5.11 us
    ppermute x3, waiting for transfers between devices, exchange_by_halves(): own = lax.ppermute(own, 'pair', perm)  4.44 us
    another operation x2, other arithmetic  3.7 us
    dot_general x1, matrix products, whiten_rows(): jnp.dot(strain_rows, dft_table(sample_count, bin_count), preferred_elemen...  3.2 us
  transfers between devices with their start and end apart: 9, of which 8 were waited for; matrix products, arithmetic and copies ran while one was open for 4% of the time, Pallas kernels for 0%

profile of v8, /device:TPU:0, one launch (start us, length us, event | category | flops | bytes accessed | tf_op | source)
XLA Modules:
  0.0 78.0 jit_solution(9099214552981290341)
XLA Ops:
  0.0 0.7 fusion.42
  0.7 0.1 reduce_sum.32
  0.8 0.1 reduce_sum.36
  0.9 0.1 reduce_sum.46
  1.0 0.1 reduce_sum.47
  1.1 0.8 %fusion.18 = (f32[128,384]{1,0:T(8,128)S(1)}, f32[128,384]{1,0:T(8,128)S(1)}) fusion(s32[384]{0:T(512)S(1)} %iota_add_fusion), kind=kLoop, calls=%fused_computation.45 | loop fusion | flops 442368 | bytes 394752 | tf_op jit(solution)/shard_map/cos | solution.py:20
  1.9 0.5 fusion.25
  2.4 0.0 copy-start.3
  2.4 3.5 %subtract_convert_fusion = (bf16[60,128,384]{2,1,0:T(8,128)(2,1)S(1)}, bf16[60,128,384]{2,1,0:T(8,128)(2,1)S(1)}) fusion(f32[128,384]{1,0:T(8,128)S(1)} %get-tuple-element.160, f32[60,384]{1,0:T(8,128)S(1)} %get-tuple-element.154, f32[128,384]{1,0:T(8,128)S(1)} %get-tuple-element.159, f32[60,384]{1,0:T(8,128)S(1)} %get-tuple-element.153), kind=kLoop, calls=%fused_computation.5 | loop fusion | flops 26542080 | bytes 12374016 | tf_op jit(solution)/shard_map/convert.7
  5.9 3.2 %fusion.5 = f32[256,768]{1,0:T(8,128)S(1)} fusion(bf16[7680,384]{1,0:T(8,128)(2,1)S(1)} %bitcast.62, bf16[7680,384]{1,0:T(8,128)(2,1)S(1)} %bitcast.61, bf16[1,256,7680]{2,1,0:T(8,128)(2,1)S(1)} %copy-done.3), kind=kOutput, calls=%fused_computation.8 | convolution fusion | flops 3043491840 | bytes 16515072 | tf_op jit(solution)/shard_map/dot_general | solution.py:37
  9.1 0.2 fusion.47
  9.4 0.0 copy-start.2
  9.4 0.2 divide_convert_fusion.1
  9.6 0.7 fusion.50
  12.7 0.1 select_bitcast_fusion.3
  12.8 0.1 select_bitcast_fusion.4
  12.9 3.0 %collective-permute-start = (bf16[1,128,768]{2,1,0:T(8,128)(2,1)S(1)}, bf16[1,128,768]{2,1,0:T(8,128)(2,1)S(1)}, u32[]{:S(2)}, u32[]{:S(2)}) collective-permute-start(bf16[1,128,768]{2,1,0:T(8,128)(2,1)S(1)} %get-tuple-element.151), channel_id=1, source_target_pairs={{0,1},{1,2},{2,3},{3,0},{4,5},{5,6},{6,7},{7,4},{8,9},{9,10},{10,1... | collective-permute-start | bytes 589832 | tf_op jit(solution)/shard_map/ppermute | solution.py:138
  15.9 1.6 %collective-permute-start.1 = (bf16[1,128,768]{2,1,0:T(8,128)(2,1)S(1)}, bf16[1,128,768]{2,1,0:T(8,128)(2,1)S(1)}, u32[]{:S(2)}, u32[]{:S(2)}) collective-permute-start(bf16[1,128,768]{2,1,0:T(8,128)(2,1)S(1)} %get-tuple-element.150), channel_id=1, source_target_pairs={{0,2},{1,3},{2,0},{3,1},{4,6},{5,7},{6,4},{7,5},{8,10},{9,11},{10,... | collective-permute-start | bytes 589832 | tf_op jit(solution)/shard_map/ppermute | solution.py:138
  17.5 1.4 %collective-permute-start.2 = (bf16[1,128,768]{2,1,0:T(8,128)(2,1)S(1)}, bf16[1,128,768]{2,1,0:T(8,128)(2,1)S(1)}, u32[]{:S(2)}, u32[]{:S(2)}) collective-permute-start(bf16[1,128,768]{2,1,0:T(8,128)(2,1)S(1)} %get-tuple-element.139), channel_id=1, source_target_pairs={{0,3},{1,0},{2,1},{3,2},{4,7},{5,4},{6,5},{7,6},{8,11},{9,8},{10,9... | collective-permute-start | bytes 589832 | tf_op jit(solution)/shard_map/ppermute | solution.py:138
  18.9 2.7 %collective-permute-start.3 = (bf16[1,2,128,768]{3,2,1,0:T(8,128)(2,1)S(1)}, bf16[1,2,128,768]{3,2,1,0:T(8,128)(2,1)S(1)}, u32[]{:S(2)}, u32[]{:S(2)}) collective-permute-start(bf16[1,2,128,768]{3,2,1,0:T(8,128)(2,1)S(1)} %pad_maximum_fusion), channel_id=1, source_target_pairs={{0,4},{1,5},{2,6},{3,7},{4,0},{5,1},{6,2},{7,3},{8,12},{9,13},{10,... | collective-permute-start | bytes 1179656 | tf_op jit(solution)/shard_map/ppermute | solution.py:127
  21.6 0.5 iota_multiply_fusion.1
  24.7 0.1 constant_dynamic-slice_fusion
  24.7 0.1 copy.5
  24.8 0.1 reshape.239
  24.9 1.4 %fusion.37 = (f32[4,384]{1,0:T(4,128)}, f32[4,384]{1,0:T(4,128)}, f32[4,384]{1,0:T(4,128)}, f32[4,384]{1,0:T(4,128)}) fusion(s32[384]{0:T(512)S(1)} %iota_add_fusion, s32[4]{0:T(128)S(1)} %get-tuple-element.175, s32[4]{0:T(128)} %get-tuple-element.176), kind=kLoop, calls=%fused_computation.70 | loop fusion | flops 27648 | bytes 26144 | tf_op jit(solution)/shard_map/sin | solution.py:20
  26.3 2.9 %collective-permute-done = bf16[1,128,768]{2,1,0:T(8,128)(2,1)S(1)} collective-permute-done((bf16[1,128,768]{2,1,0:T(8,128)(2,1)S(1)}, bf16[1,128,768]{2,1,0:T(8,128)(2,1)S(1)}, u32[]{:S(2)}, u32[]{:S(2)}) %collective-permute-start) | collective-permute-done | bytes 196640 | tf_op jit(solution)/shard_map/ppermute | solution.py:138
  29.2 1.6 %collective-permute-done.1 = bf16[1,128,768]{2,1,0:T(8,128)(2,1)S(1)} collective-permute-done((bf16[1,128,768]{2,1,0:T(8,128)(2,1)S(1)}, bf16[1,128,768]{2,1,0:T(8,128)(2,1)S(1)}, u32[]{:S(2)}, u32[]{:S(2)}) %collective-permute-start.1) | collective-permute-done | bytes 196640 | tf_op jit(solution)/shard_map/ppermute | solution.py:138
  30.8 7.6 %collective-permute-done.3 = bf16[1,2,128,768]{3,2,1,0:T(8,128)(2,1)S(1)} collective-permute-done((bf16[1,2,128,768]{3,2,1,0:T(8,128)(2,1)S(1)}, bf16[1,2,128,768]{3,2,1,0:T(8,128)(2,1)S(1)}, u32[]{:S(2)}, u32[]{:S(2)}) %collective-permute-start.3) | collective-permute-done | bytes 393248 | tf_op jit(solution)/shard_map/ppermute | solution.py:127
  38.4 0.1 select_bitcast_fusion
  38.5 0.7 collective-permute-start.4
  39.3 0.6 fusion.45.index_ref
  39.9 2.3 %collective-permute-start.6 = (bf16[1,128,768]{2,1,0:T(8,128)(2,1)S(1)}, bf16[1,128,768]{2,1,0:T(8,128)(2,1)S(1)}, u32[]{:S(2)}, u32[]{:S(2)}) collective-permute-start(bf16[1,128,768]{2,1,0:T(8,128)(2,1)S(1)} %get-tuple-element.146), channel_id=1, source_target_pairs={{0,3},{1,0},{2,1},{3,2},{4,7},{5,4},{6,5},{7,6},{8,11},{9,8},{10,9... | collective-permute-start | bytes 589832 | tf_op jit(solution)/shard_map/ppermute | solution.py:139
  42.1 3.1 %collective-permute-done.4 = bf16[1,128,768]{2,1,0:T(8,128)(2,1)S(1)} collective-permute-done((bf16[1,128,768]{2,1,0:T(8,128)(2,1)S(1)}, bf16[1,128,768]{2,1,0:T(8,128)(2,1)S(1)}, u32[]{:S(2)}, u32[]{:S(2)}) %collective-permute-start.4) | collective-permute-done | bytes 196640 | tf_op jit(solution)/shard_map/ppermute | solution.py:139
  45.3 0.2 collective-permute-done.5
  45.5 1.7 %collective-permute-done.6 = bf16[1,128,768]{2,1,0:T(8,128)(2,1)S(1)} collective-permute-done((bf16[1,128,768]{2,1,0:T(8,128)(2,1)S(1)}, bf16[1,128,768]{2,1,0:T(8,128)(2,1)S(1)}, u32[]{:S(2)}, u32[]{:S(2)}) %collective-permute-start.6) | collective-permute-done | bytes 196640 | tf_op jit(solution)/shard_map/ppermute | solution.py:139
  47.3 1.2 %copy-done.1 = bf16[8,1,128,768]{3,2,1,0:T(8,128)(2,1)} copy-done((bf16[8,1,128,768]{3,2,1,0:T(8,128)(2,1)}, bf16[8,1,128,768]{3,2,1,0:T(8,128)(2,1)S(1)}, u32[]{:S(2)}) %copy-start.1) | copy-done | bytes 1572888
  48.5 7.2 %shard_map.37 = bf16[2,16,64,512]{3,2,1,0:T(8,128)(2,1)} custom-call(s32[8]{0:T(128)} %fusion.45.index_ref, f32[4,384]{1,0:T(4,128)} %get-tuple-element.161.cc_ref, f32[4,384]{1,0:T(4,128)} %get-tuple-element.162.sc_ref, f32[4,384]{1,0:T(4,128)} %get-tuple-element.156.cf_ref, f32[4,384]{1,0:T(4,128)} %get-tuple-element.155.sf_ref, ...), custom_call_target="tpu_custom_call" | custom-call | flops 1610612736 | bytes 3670016 | tf_op jit(solution)/shard_map/pallas_call | solution.py:100
  55.7 2.4 %dynamic-slice_bitcast_fusion = bf16[16,64,512]{2,1,0:T(8,128)(2,1)} fusion(bf16[2,16,64,512]{3,2,1,0:T(8,128)(2,1)} %shard_map.37, s32[]{:T(128)S(6)} %sub.53), kind=kLoop, calls=%fused_computation.11 | loop fusion | bytes 2097156 | tf_op jit(solution)/shard_map/jit(_take)/gather | solution.py:183
  58.1 0.0 collective-permute-start.7
  58.1 2.9 %collective-permute-done.7 = bf16[16,64,512]{2,1,0:T(8,128)(2,1)S(1)} collective-permute-done((bf16[16,64,512]{2,1,0:T(8,128)(2,1)}, bf16[16,64,512]{2,1,0:T(8,128)(2,1)S(1)}, u32[]{:S(2)}, u32[]{:S(2)}) %collective-permute-start.7) | collective-permute-done | bytes 1048608 | tf_op jit(solution)/shard_map/ppermute | solution.py:185
  61.0 0.3 convert_add_fusion
  61.3 0.1 fusion.10
  61.4 1.6 %collective-permute-start.8 = (bf16[16,32,512]{2,1,0:T(8,128)(2,1)S(1)}, bf16[16,32,512]{2,1,0:T(8,128)(2,1)S(1)}, u32[]{:S(2)}, u32[]{:S(2)}) collective-permute-start(bf16[16,32,512]{2,1,0:T(8,128)(2,1)S(1)} %fusion.10), channel_id=1, source_target_pairs={{0,16},{8,24},{16,0},{24,8},{1,17},{9,25},{17,1},{25,9},{2,18},{10... | collective-permute-start | bytes 1572872 | tf_op jit(solution)/shard_map/ppermute | solution.py:193
  63.0 12.4 %collective-permute-done.8 = bf16[16,32,512]{2,1,0:T(8,128)(2,1)S(1)} collective-permute-done((bf16[16,32,512]{2,1,0:T(8,128)(2,1)S(1)}, bf16[16,32,512]{2,1,0:T(8,128)(2,1)S(1)}, u32[]{:S(2)}, u32[]{:S(2)}) %collective-permute-start.8) | collective-permute-done | bytes 524320 | tf_op jit(solution)/shard_map/ppermute | solution.py:193
  75.5 0.2 bitcast_add_fusion
  75.6 0.4 reshape.242
  76.0 0.4 multiply_bitcast_fusion
  76.4 1.6 %copy.7 = f32[32,4,16,128]{3,2,1,0:T(8,128)} copy(f32[32,4,16,128]{3,1,0,2:T(4,128)S(1)} %multiply_bitcast_fusion) | data formatting | bytes 2097152 | tf_op jit(solution)/shard_map/div | solution.py:197
  (20 shorter events, 0.1 us)
Async XLA Ops:
  2.4 3.5 %copy-start.3 = (bf16[1,256,7680]{2,1,0:T(8,128)(2,1)S(1)}, bf16[1,256,7680]{2,1,0:T(8,128)(2,1)}, u32[]{:S(2)}) copy-start(bf16[1,256,7680]{2,1,0:T(8,128)(2,1)} %param.3) | copy-start | bytes 11796484
  9.4 15.3 %copy-start.2 = (s32[32,2]{0,1:T(2,128)S(1)}, s32[32,2]{0,1:T(2,128)}, u32[]{:S(2)}) copy-start(s32[32,2]{0,1:T(2,128)} %param.4) | copy-start | bytes 772
  12.9 16.3 %collective-permute-start = (bf16[1,128,768]{2,1,0:T(8,128)(2,1)S(1)}, bf16[1,128,768]{2,1,0:T(8,128)(2,1)S(1)}, u32[]{:S(2)}, u32[]{:S(2)}) collective-permute-start(bf16[1,128,768]{2,1,0:T(8,128)(2,1)S(1)} %get-tuple-element.151), channel_id=1, source_target_pairs={{0,1},{1,2},{2,3},{3,0},{4,5},{5,6},{6,7},{7,4},{8,9},{9,10},{10,1... | collective-permute-start | bytes 589832 | tf_op jit(solution)/shard_map/ppermute | solution.py:138
  15.9 14.9 %collective-permute-start.1 = (bf16[1,128,768]{2,1,0:T(8,128)(2,1)S(1)}, bf16[1,128,768]{2,1,0:T(8,128)(2,1)S(1)}, u32[]{:S(2)}, u32[]{:S(2)}) collective-permute-start(bf16[1,128,768]{2,1,0:T(8,128)(2,1)S(1)} %get-tuple-element.150), channel_id=1, source_target_pairs={{0,2},{1,3},{2,0},{3,1},{4,6},{5,7},{6,4},{7,5},{8,10},{9,11},{10,... | collective-permute-start | bytes 589832 | tf_op jit(solution)/shard_map/ppermute | solution.py:138
  17.5 13.3 %collective-permute-start.2 = (bf16[1,128,768]{2,1,0:T(8,128)(2,1)S(1)}, bf16[1,128,768]{2,1,0:T(8,128)(2,1)S(1)}, u32[]{:S(2)}, u32[]{:S(2)}) collective-permute-start(bf16[1,128,768]{2,1,0:T(8,128)(2,1)S(1)} %get-tuple-element.139), channel_id=1, source_target_pairs={{0,3},{1,0},{2,1},{3,2},{4,7},{5,4},{6,5},{7,6},{8,11},{9,8},{10,9... | collective-permute-start | bytes 589832 | tf_op jit(solution)/shard_map/ppermute | solution.py:138
  18.9 19.5 %collective-permute-start.3 = (bf16[1,2,128,768]{3,2,1,0:T(8,128)(2,1)S(1)}, bf16[1,2,128,768]{3,2,1,0:T(8,128)(2,1)S(1)}, u32[]{:S(2)}, u32[]{:S(2)}) collective-permute-start(bf16[1,2,128,768]{3,2,1,0:T(8,128)(2,1)S(1)} %pad_maximum_fusion), channel_id=1, source_target_pairs={{0,4},{1,5},{2,6},{3,7},{4,0},{5,1},{6,2},{7,3},{8,12},{9,13},{10,... | collective-permute-start | bytes 1179656 | tf_op jit(solution)/shard_map/ppermute | solution.py:127
  38.5 6.7 %collective-permute-start.4 = (bf16[1,128,768]{2,1,0:T(8,128)(2,1)S(1)}, bf16[1,128,768]{2,1,0:T(8,128)(2,1)S(1)}, u32[]{:S(2)}, u32[]{:S(2)}) collective-permute-start(bf16[1,128,768]{2,1,0:T(8,128)(2,1)S(1)} %get-tuple-element.149), channel_id=1, source_target_pairs={{0,1},{1,2},{2,3},{3,0},{4,5},{5,6},{6,7},{7,4},{8,9},{9,10},{10,1... | collective-permute-start | bytes 589832 | tf_op jit(solution)/shard_map/ppermute | solution.py:139
  39.9 5.7 %collective-permute-start.5 = (bf16[1,128,768]{2,1,0:T(8,128)(2,1)S(1)}, bf16[1,128,768]{2,1,0:T(8,128)(2,1)S(1)}, u32[]{:S(2)}, u32[]{:S(2)}) collective-permute-start(bf16[1,128,768]{2,1,0:T(8,128)(2,1)S(1)} %get-tuple-element.147), channel_id=1, source_target_pairs={{0,2},{1,3},{2,0},{3,1},{4,6},{5,7},{6,4},{7,5},{8,10},{9,11},{10,... | collective-permute-start | bytes 589832 | tf_op jit(solution)/shard_map/ppermute | solution.py:139
  39.9 7.4 %collective-permute-start.6 = (bf16[1,128,768]{2,1,0:T(8,128)(2,1)S(1)}, bf16[1,128,768]{2,1,0:T(8,128)(2,1)S(1)}, u32[]{:S(2)}, u32[]{:S(2)}) collective-permute-start(bf16[1,128,768]{2,1,0:T(8,128)(2,1)S(1)} %get-tuple-element.146), channel_id=1, source_target_pairs={{0,3},{1,0},{2,1},{3,2},{4,7},{5,4},{6,5},{7,6},{8,11},{9,8},{10,9... | collective-permute-start | bytes 589832 | tf_op jit(solution)/shard_map/ppermute | solution.py:139
  47.3 1.2 %copy-start.1 = (bf16[8,1,128,768]{3,2,1,0:T(8,128)(2,1)}, bf16[8,1,128,768]{3,2,1,0:T(8,128)(2,1)S(1)}, u32[]{:S(2)}) copy-start(bf16[8,1,128,768]{3,2,1,0:T(8,128)(2,1)S(1)} %bitcast_dynamic-update-slice_fusion.left_ref.right_ref) | copy-start | bytes 4718596
  55.7 5.3 %copy-start = (bf16[2,16,64,512]{3,2,1,0:T(8,128)(2,1)S(1)}, bf16[2,16,64,512]{3,2,1,0:T(8,128)(2,1)}, u32[]{:S(2)}) copy-start(bf16[2,16,64,512]{3,2,1,0:T(8,128)(2,1)} %shard_map.37) | copy-start | bytes 6291460
  58.1 2.9 %collective-permute-start.7 = (bf16[16,64,512]{2,1,0:T(8,128)(2,1)}, bf16[16,64,512]{2,1,0:T(8,128)(2,1)S(1)}, u32[]{:S(2)}, u32[]{:S(2)}) collective-permute-start(bf16[16,64,512]{2,1,0:T(8,128)(2,1)} %dynamic-slice_bitcast_fusion), channel_id=1, source_target_pairs={{0,8},{8,0},{16,24},{24,16},{1,9},{9,1},{17,25},{25,17},{2,10},{10... | collective-permute-start | bytes 3145736 | tf_op jit(solution)/shard_map/ppermute | solution.py:185
  58.1 4.9 %copy-start.4 = (s32[4]{0:T(128)S(1)}, s32[4]{0:T(128)}, u32[]{:S(2)}) copy-start(s32[4]{0:T(128)} %param.5) | copy-start | bytes 52
  61.4 14.0 %collective-permute-start.8 = (bf16[16,32,512]{2,1,0:T(8,128)(2,1)S(1)}, bf16[16,32,512]{2,1,0:T(8,128)(2,1)S(1)}, u32[]{:S(2)}, u32[]{:S(2)}) collective-permute-start(bf16[16,32,512]{2,1,0:T(8,128)(2,1)S(1)} %fusion.10), channel_id=1, source_target_pairs={{0,16},{8,24},{16,0},{24,8},{1,17},{9,25},{17,1},{25,9},{2,18},{10... | collective-permute-start | bytes 1572872 | tf_op jit(solution)/shard_map/ppermute | solution.py:193

commit v9 on v8

--- a/solution.py
+++ b/solution.py
@@ -45,11 +45,13 @@
 
 def correlation_kernel(sub, n_y, own_rows, index_ref, cc_ref, sc_ref, cf_ref, sf_ref, left_ref, right_ref, out_ref):
     window_count = left_ref.shape[1]
-    order = [(y * 2 + c) * own_rows for c in range(2) for y in range(n_y)]
+    partner = 1 - lax.axis_index("win") % 2
+    orders = [[(y * 2 + c) * own_rows for c in (1 - first, first) for y in range(n_y)] for first in (1, 0)]
     acc = None
     for w in range(window_count):
         left = left_ref[0, w].astype(jnp.float32)
-        left = jnp.concatenate([left[r : r + own_rows] for r in order], axis=0)
+        by_order = [jnp.concatenate([left[r : r + own_rows] for r in order], axis=0) for order in orders]
+        left = jnp.where(partner == 0, by_order[0], by_order[1])
         lre = left[:, :F]
         lim = left[:, F:]
         rre = right_ref[0, w, :, :F].astype(jnp.float32)
@@ -180,8 +182,8 @@
 
     core = win_here % 2
     y_here = win_here // 2
-    send = jnp.take(corr, 1 - core, axis=0, mode="clip")
-    keep = jnp.take(corr, core, axis=0, mode="clip").astype(jnp.float32)
+    send = corr[0]
+    keep = corr[1].astype(jnp.float32)
     got = lax.ppermute(send, "win", [(w, w ^ 1) for w in range(n_win)])
     half = (keep + got.astype(jnp.float32)).reshape(LAGS, n_y, own_rows, slot_count * C)
     half = jnp.transpose(half, (1, 0, 2, 3))

time: 78.3 us -> 78.6 us (level)
  other arithmetic: 9.87 us -> 11.1 us
  local copies, waits for them, and re-layouts: 6.82 us -> 5.85 us
    gather x1 -> x0, local copies, waits for them, and re-layouts: 2.44 us -> none  [body(): send = jnp.take(corr, 1 - core, axis=0, mode='clip')]
    squeeze x0 -> x1, local copies, waits for them, and re-layouts: none -> 1.46 us  [body(): send = corr[0]]
    add x1, other arithmetic: 0.34 us -> 1.54 us  [body(): keep + got.astype(jnp.float32)]
where the time goes in v9:
time: 78.6 us; the launch traced here: 78.3 us
  waiting for transfers between devices  32.3 us (41%)
  starting transfers between devices  13.3 us (17%)
  other arithmetic  11.1 us (14%)
  Pallas kernels  7.3 us (9%)
  local copies, waits for them, and re-layouts  5.85 us (7%)
  between operations  5.25 us (7%)
  matrix products  3.2 us (4%)
    ppermute x1, waiting for transfers between devices, body(): total = total + lax.ppermute(piece, 'win', perm).astype(jnp.float32)  12.4 us
    ppermute x1, waiting for transfers between devices, exchange_by_halves(): lax.ppermute(whitened, 'pair', [(p, p ^ half) for p in range(n_pair)])  7.59 us
    pallas_call x1, Pallas kernels, tile_correlation(): pl.pallas_call(functools.partial(correlation_kernel, sub, n_y, own_rows),...  7.3 us
    ppermute x3, starting transfers between devices, exchange_by_halves(): own = lax.ppermute(own, 'pair', perm)  6 us
    ppermute x3, waiting for transfers between devices, exchange_by_halves(): relay = lax.ppermute(relay, 'pair', perm)  5.11 us
    ppermute x3, waiting for transfers between devices, exchange_by_halves(): own = lax.ppermute(own, 'pair', perm)  4.44 us
    another operation x2, other arithmetic  3.7 us
    dot_general x1, matrix products, whiten_rows(): jnp.dot(strain_rows, dft_table(sample_count, bin_count), preferred_elemen...  3.2 us
  transfers between devices with their start and end apart: 9, of which 8 were waited for; matrix products, arithmetic and copies ran while one was open for 4% of the time, Pallas kernels for 0%

profile of v9, /device:TPU:0, one launch (start us, length us, event | category | flops | bytes accessed | tf_op | source)
XLA Modules:
  0.0 78.3 jit_solution(6761073750405624303)
XLA Ops:
  0.0 0.7 fusion.42
  0.7 0.1 reduce_sum.32
  0.8 0.1 reduce_sum.36
  0.9 0.1 reduce_sum.46
  1.0 0.1 reduce_sum.47
  1.1 0.8 %fusion.18 = (f32[128,384]{1,0:T(8,128)S(1)}, f32[128,384]{1,0:T(8,128)S(1)}) fusion(s32[384]{0:T(512)S(1)} %iota_add_fusion), kind=kLoop, calls=%fused_computation.46 | loop fusion | flops 442368 | bytes 394752 | tf_op jit(solution)/shard_map/cos | solution.py:20
  1.9 0.5 fusion.25
  2.4 0.0 copy-start.3
  2.4 3.5 %subtract_convert_fusion = (bf16[60,128,384]{2,1,0:T(8,128)(2,1)S(1)}, bf16[60,128,384]{2,1,0:T(8,128)(2,1)S(1)}) fusion(f32[128,384]{1,0:T(8,128)S(1)} %get-tuple-element.138, f32[60,384]{1,0:T(8,128)S(1)} %get-tuple-element.132, f32[128,384]{1,0:T(8,128)S(1)} %get-tuple-element.137, f32[60,384]{1,0:T(8,128)S(1)} %get-tuple-element.131), kind=kLoop, calls=%fused_computation.5 | loop fusion | flops 26542080 | bytes 12374016 | tf_op jit(solution)/shard_map/convert.8
  5.9 3.2 %fusion.5 = f32[256,768]{1,0:T(8,128)S(1)} fusion(bf16[7680,384]{1,0:T(8,128)(2,1)S(1)} %bitcast.64, bf16[7680,384]{1,0:T(8,128)(2,1)S(1)} %bitcast.63, bf16[1,256,7680]{2,1,0:T(8,128)(2,1)S(1)} %copy-done.3), kind=kOutput, calls=%fused_computation.8 | convolution fusion | flops 3043491840 | bytes 16515072 | tf_op jit(solution)/shard_map/dot_general | solution.py:37
  9.1 0.2 fusion.47
  9.4 0.2 divide_convert_fusion.1
  9.6 0.7 fusion.50
  12.7 0.1 select_bitcast_fusion.3
  12.8 0.1 select_bitcast_fusion.4
  12.9 3.0 %collective-permute-start = (bf16[1,128,768]{2,1,0:T(8,128)(2,1)S(1)}, bf16[1,128,768]{2,1,0:T(8,128)(2,1)S(1)}, u32[]{:S(2)}, u32[]{:S(2)}) collective-permute-start(bf16[1,128,768]{2,1,0:T(8,128)(2,1)S(1)} %get-tuple-element.129), channel_id=1, source_target_pairs={{0,1},{1,2},{2,3},{3,0},{4,5},{5,6},{6,7},{7,4},{8,9},{9,10},{10,1... | collective-permute-start | bytes 589832 | tf_op jit(solution)/shard_map/ppermute | solution.py:140
  15.9 1.6 %collective-permute-start.1 = (bf16[1,128,768]{2,1,0:T(8,128)(2,1)S(1)}, bf16[1,128,768]{2,1,0:T(8,128)(2,1)S(1)}, u32[]{:S(2)}, u32[]{:S(2)}) collective-permute-start(bf16[1,128,768]{2,1,0:T(8,128)(2,1)S(1)} %get-tuple-element.128), channel_id=1, source_target_pairs={{0,2},{1,3},{2,0},{3,1},{4,6},{5,7},{6,4},{7,5},{8,10},{9,11},{10,... | collective-permute-start | bytes 589832 | tf_op jit(solution)/shard_map/ppermute | solution.py:140
  17.5 1.4 %collective-permute-start.2 = (bf16[1,128,768]{2,1,0:T(8,128)(2,1)S(1)}, bf16[1,128,768]{2,1,0:T(8,128)(2,1)S(1)}, u32[]{:S(2)}, u32[]{:S(2)}) collective-permute-start(bf16[1,128,768]{2,1,0:T(8,128)(2,1)S(1)} %get-tuple-element.117), channel_id=1, source_target_pairs={{0,3},{1,0},{2,1},{3,2},{4,7},{5,4},{6,5},{7,6},{8,11},{9,8},{10,9... | collective-permute-start | bytes 589832 | tf_op jit(solution)/shard_map/ppermute | solution.py:140
  18.9 2.7 %collective-permute-start.3 = (bf16[1,2,128,768]{3,2,1,0:T(8,128)(2,1)S(1)}, bf16[1,2,128,768]{3,2,1,0:T(8,128)(2,1)S(1)}, u32[]{:S(2)}, u32[]{:S(2)}) collective-permute-start(bf16[1,2,128,768]{3,2,1,0:T(8,128)(2,1)S(1)} %pad_maximum_fusion), channel_id=1, source_target_pairs={{0,4},{1,5},{2,6},{3,7},{4,0},{5,1},{6,2},{7,3},{8,12},{9,13},{10,... | collective-permute-start | bytes 1179656 | tf_op jit(solution)/shard_map/ppermute | solution.py:129
  21.6 0.5 iota_multiply_fusion.1
  24.7 0.1 constant_dynamic-slice_fusion
  24.7 0.1 copy.5
  24.8 0.1 reshape.241
  24.9 1.4 %fusion.37 = (f32[4,384]{1,0:T(4,128)}, f32[4,384]{1,0:T(4,128)}, f32[4,384]{1,0:T(4,128)}, f32[4,384]{1,0:T(4,128)}) fusion(s32[384]{0:T(512)S(1)} %iota_add_fusion, s32[4]{0:T(128)S(1)} %get-tuple-element.153, s32[4]{0:T(128)} %get-tuple-element.154), kind=kLoop, calls=%fused_computation.71 | loop fusion | flops 27648 | bytes 26144 | tf_op jit(solution)/shard_map/sin | solution.py:20
  26.3 2.9 %collective-permute-done = bf16[1,128,768]{2,1,0:T(8,128)(2,1)S(1)} collective-permute-done((bf16[1,128,768]{2,1,0:T(8,128)(2,1)S(1)}, bf16[1,128,768]{2,1,0:T(8,128)(2,1)S(1)}, u32[]{:S(2)}, u32[]{:S(2)}) %collective-permute-start) | collective-permute-done | bytes 196640 | tf_op jit(solution)/shard_map/ppermute | solution.py:140
  29.2 1.6 %collective-permute-done.1 = bf16[1,128,768]{2,1,0:T(8,128)(2,1)S(1)} collective-permute-done((bf16[1,128,768]{2,1,0:T(8,128)(2,1)S(1)}, bf16[1,128,768]{2,1,0:T(8,128)(2,1)S(1)}, u32[]{:S(2)}, u32[]{:S(2)}) %collective-permute-start.1) | collective-permute-done | bytes 196640 | tf_op jit(solution)/shard_map/ppermute | solution.py:140
  30.8 7.6 %collective-permute-done.3 = bf16[1,2,128,768]{3,2,1,0:T(8,128)(2,1)S(1)} collective-permute-done((bf16[1,2,128,768]{3,2,1,0:T(8,128)(2,1)S(1)}, bf16[1,2,128,768]{3,2,1,0:T(8,128)(2,1)S(1)}, u32[]{:S(2)}, u32[]{:S(2)}) %collective-permute-start.3) | collective-permute-done | bytes 393248 | tf_op jit(solution)/shard_map/ppermute | solution.py:129
  38.4 0.1 select_bitcast_fusion
  38.5 0.7 collective-permute-start.4
  39.3 0.6 fusion.45.index_ref
  39.9 2.3 %collective-permute-start.6 = (bf16[1,128,768]{2,1,0:T(8,128)(2,1)S(1)}, bf16[1,128,768]{2,1,0:T(8,128)(2,1)S(1)}, u32[]{:S(2)}, u32[]{:S(2)}) collective-permute-start(bf16[1,128,768]{2,1,0:T(8,128)(2,1)S(1)} %get-tuple-element.124), channel_id=1, source_target_pairs={{0,3},{1,0},{2,1},{3,2},{4,7},{5,4},{6,5},{7,6},{8,11},{9,8},{10,9... | collective-permute-start | bytes 589832 | tf_op jit(solution)/shard_map/ppermute | solution.py:141
  42.1 3.1 %collective-permute-done.4 = bf16[1,128,768]{2,1,0:T(8,128)(2,1)S(1)} collective-permute-done((bf16[1,128,768]{2,1,0:T(8,128)(2,1)S(1)}, bf16[1,128,768]{2,1,0:T(8,128)(2,1)S(1)}, u32[]{:S(2)}, u32[]{:S(2)}) %collective-permute-start.4) | collective-permute-done | bytes 196640 | tf_op jit(solution)/shard_map/ppermute | solution.py:141
  45.3 0.2 collective-permute-done.5
  45.5 1.7 %collective-permute-done.6 = bf16[1,128,768]{2,1,0:T(8,128)(2,1)S(1)} collective-permute-done((bf16[1,128,768]{2,1,0:T(8,128)(2,1)S(1)}, bf16[1,128,768]{2,1,0:T(8,128)(2,1)S(1)}, u32[]{:S(2)}, u32[]{:S(2)}) %collective-permute-start.6) | collective-permute-done | bytes 196640 | tf_op jit(solution)/shard_map/ppermute | solution.py:141
  47.3 1.2 %copy-done.1 = bf16[8,1,128,768]{3,2,1,0:T(8,128)(2,1)} copy-done((bf16[8,1,128,768]{3,2,1,0:T(8,128)(2,1)}, bf16[8,1,128,768]{3,2,1,0:T(8,128)(2,1)S(1)}, u32[]{:S(2)}) %copy-start.1) | copy-done | bytes 1572888
  48.5 7.3 %shard_map.37 = bf16[2,16,64,512]{3,2,1,0:T(8,128)(2,1)} custom-call(s32[8]{0:T(128)} %fusion.45.index_ref, f32[4,384]{1,0:T(4,128)} %get-tuple-element.139.cc_ref, f32[4,384]{1,0:T(4,128)} %get-tuple-element.140.sc_ref, f32[4,384]{1,0:T(4,128)} %get-tuple-element.134.cf_ref, f32[4,384]{1,0:T(4,128)} %get-tuple-element.133.sf_ref, ...), custom_call_target="tpu_custom_call" | custom-call | flops 1610612736 | bytes 3670016 | tf_op jit(solution)/shard_map/pallas_call | solution.py:102
  55.8 1.5 %slice_bitcast_fusion = bf16[16,64,512]{2,1,0:T(8,128)(2,1)S(1)} fusion(bf16[2,16,64,512]{3,2,1,0:T(8,128)(2,1)} %shard_map.37), kind=kLoop, calls=%fused_computation.9 | loop fusion | bytes 2097152 | tf_op jit(solution)/shard_map/squeeze | solution.py:185
  57.2 0.1 collective-permute-start.7
  57.3 0.0 copy-start.4
  57.4 2.7 %collective-permute-done.7 = bf16[16,64,512]{2,1,0:T(8,128)(2,1)} collective-permute-done((bf16[16,64,512]{2,1,0:T(8,128)(2,1)S(1)}, bf16[16,64,512]{2,1,0:T(8,128)(2,1)}, u32[]{:S(2)}, u32[]{:S(2)}) %collective-permute-start.7) | collective-permute-done | bytes 1048608 | tf_op jit(solution)/shard_map/ppermute | solution.py:187
  60.1 1.5 %convert_add_fusion = f32[16,64,512]{2,1,0:T(8,128)S(1)} fusion(bf16[16,64,512]{2,1,0:T(8,128)(2,1)} %collective-permute-done.7, bf16[2,16,64,512]{3,2,1,0:T(8,128)(2,1)S(1)} %copy-done), kind=kLoop, calls=%fused_computation.7 | loop fusion | flops 1572864 | bytes 4194304 | tf_op jit(solution)/shard_map/add | solution.py:188
  61.6 0.1 fusion.10
  61.7 1.6 %collective-permute-start.8 = (bf16[16,32,512]{2,1,0:T(8,128)(2,1)S(1)}, bf16[16,32,512]{2,1,0:T(8,128)(2,1)S(1)}, u32[]{:S(2)}, u32[]{:S(2)}) collective-permute-start(bf16[16,32,512]{2,1,0:T(8,128)(2,1)S(1)} %fusion.10), channel_id=1, source_target_pairs={{0,16},{8,24},{16,0},{24,8},{1,17},{9,25},{17,1},{25,9},{2,18},{10... | collective-permute-start | bytes 1572872 | tf_op jit(solution)/shard_map/ppermute | solution.py:195
  63.3 12.4 %collective-permute-done.8 = bf16[16,32,512]{2,1,0:T(8,128)(2,1)S(1)} collective-permute-done((bf16[16,32,512]{2,1,0:T(8,128)(2,1)S(1)}, bf16[16,32,512]{2,1,0:T(8,128)(2,1)S(1)}, u32[]{:S(2)}, u32[]{:S(2)}) %collective-permute-start.8) | collective-permute-done | bytes 524320 | tf_op jit(solution)/shard_map/ppermute | solution.py:195
  75.8 0.2 bitcast_add_fusion
  75.9 0.4 reshape.244
  76.3 0.4 multiply_bitcast_fusion
  76.7 1.6 %copy.7 = f32[32,4,16,128]{3,2,1,0:T(8,128)} copy(f32[32,4,16,128]{3,1,0,2:T(4,128)S(1)} %multiply_bitcast_fusion) | data formatting | bytes 2097152 | tf_op jit(solution)/shard_map/div | solution.py:199
  (20 shorter events, 0.1 us)
Async XLA Ops:
  2.4 3.5 %copy-start.3 = (bf16[1,256,7680]{2,1,0:T(8,128)(2,1)S(1)}, bf16[1,256,7680]{2,1,0:T(8,128)(2,1)}, u32[]{:S(2)}) copy-start(bf16[1,256,7680]{2,1,0:T(8,128)(2,1)} %param.3) | copy-start | bytes 11796484
  9.4 15.3 %copy-start.2 = (s32[32,2]{0,1:T(2,128)S(1)}, s32[32,2]{0,1:T(2,128)}, u32[]{:S(2)}) copy-start(s32[32,2]{0,1:T(2,128)} %param.4) | copy-start | bytes 772
  12.9 16.3 %collective-permute-start = (bf16[1,128,768]{2,1,0:T(8,128)(2,1)S(1)}, bf16[1,128,768]{2,1,0:T(8,128)(2,1)S(1)}, u32[]{:S(2)}, u32[]{:S(2)}) collective-permute-start(bf16[1,128,768]{2,1,0:T(8,128)(2,1)S(1)} %get-tuple-element.129), channel_id=1, source_target_pairs={{0,1},{1,2},{2,3},{3,0},{4,5},{5,6},{6,7},{7,4},{8,9},{9,10},{10,1... | collective-permute-start | bytes 589832 | tf_op jit(solution)/shard_map/ppermute | solution.py:140
  15.9 14.9 %collective-permute-start.1 = (bf16[1,128,768]{2,1,0:T(8,128)(2,1)S(1)}, bf16[1,128,768]{2,1,0:T(8,128)(2,1)S(1)}, u32[]{:S(2)}, u32[]{:S(2)}) collective-permute-start(bf16[1,128,768]{2,1,0:T(8,128)(2,1)S(1)} %get-tuple-element.128), channel_id=1, source_target_pairs={{0,2},{1,3},{2,0},{3,1},{4,6},{5,7},{6,4},{7,5},{8,10},{9,11},{10,... | collective-permute-start | bytes 589832 | tf_op jit(solution)/shard_map/ppermute | solution.py:140
  17.5 13.3 %collective-permute-start.2 = (bf16[1,128,768]{2,1,0:T(8,128)(2,1)S(1)}, bf16[1,128,768]{2,1,0:T(8,128)(2,1)S(1)}, u32[]{:S(2)}, u32[]{:S(2)}) collective-permute-start(bf16[1,128,768]{2,1,0:T(8,128)(2,1)S(1)} %get-tuple-element.117), channel_id=1, source_target_pairs={{0,3},{1,0},{2,1},{3,2},{4,7},{5,4},{6,5},{7,6},{8,11},{9,8},{10,9... | collective-permute-start | bytes 589832 | tf_op jit(solution)/shard_map/ppermute | solution.py:140
  18.9 19.5 %collective-permute-start.3 = (bf16[1,2,128,768]{3,2,1,0:T(8,128)(2,1)S(1)}, bf16[1,2,128,768]{3,2,1,0:T(8,128)(2,1)S(1)}, u32[]{:S(2)}, u32[]{:S(2)}) collective-permute-start(bf16[1,2,128,768]{3,2,1,0:T(8,128)(2,1)S(1)} %pad_maximum_fusion), channel_id=1, source_target_pairs={{0,4},{1,5},{2,6},{3,7},{4,0},{5,1},{6,2},{7,3},{8,12},{9,13},{10,... | collective-permute-start | bytes 1179656 | tf_op jit(solution)/shard_map/ppermute | solution.py:129
  38.5 6.7 %collective-permute-start.4 = (bf16[1,128,768]{2,1,0:T(8,128)(2,1)S(1)}, bf16[1,128,768]{2,1,0:T(8,128)(2,1)S(1)}, u32[]{:S(2)}, u32[]{:S(2)}) collective-permute-start(bf16[1,128,768]{2,1,0:T(8,128)(2,1)S(1)} %get-tuple-element.127), channel_id=1, source_target_pairs={{0,1},{1,2},{2,3},{3,0},{4,5},{5,6},{6,7},{7,4},{8,9},{9,10},{10,1... | collective-permute-start | bytes 589832 | tf_op jit(solution)/shard_map/ppermute | solution.py:141
  39.9 5.7 %collective-permute-start.5 = (bf16[1,128,768]{2,1,0:T(8,128)(2,1)S(1)}, bf16[1,128,768]{2,1,0:T(8,128)(2,1)S(1)}, u32[]{:S(2)}, u32[]{:S(2)}) collective-permute-start(bf16[1,128,768]{2,1,0:T(8,128)(2,1)S(1)} %get-tuple-element.125), channel_id=1, source_target_pairs={{0,2},{1,3},{2,0},{3,1},{4,6},{5,7},{6,4},{7,5},{8,10},{9,11},{10,... | collective-permute-start | bytes 589832 | tf_op jit(solution)/shard_map/ppermute | solution.py:141
  39.9 7.4 %collective-permute-start.6 = (bf16[1,128,768]{2,1,0:T(8,128)(2,1)S(1)}, bf16[1,128,768]{2,1,0:T(8,128)(2,1)S(1)}, u32[]{:S(2)}, u32[]{:S(2)}) collective-permute-start(bf16[1,128,768]{2,1,0:T(8,128)(2,1)S(1)} %get-tuple-element.124), channel_id=1, source_target_pairs={{0,3},{1,0},{2,1},{3,2},{4,7},{5,4},{6,5},{7,6},{8,11},{9,8},{10,9... | collective-permute-start | bytes 589832 | tf_op jit(solution)/shard_map/ppermute | solution.py:141
  47.3 1.2 %copy-start.1 = (bf16[8,1,128,768]{3,2,1,0:T(8,128)(2,1)}, bf16[8,1,128,768]{3,2,1,0:T(8,128)(2,1)S(1)}, u32[]{:S(2)}) copy-start(bf16[8,1,128,768]{3,2,1,0:T(8,128)(2,1)S(1)} %bitcast_dynamic-update-slice_fusion.left_ref.right_ref) | copy-start | bytes 4718596
  55.8 4.3 %copy-start = (bf16[2,16,64,512]{3,2,1,0:T(8,128)(2,1)S(1)}, bf16[2,16,64,512]{3,2,1,0:T(8,128)(2,1)}, u32[]{:S(2)}) copy-start(bf16[2,16,64,512]{3,2,1,0:T(8,128)(2,1)} %shard_map.37) | copy-start | bytes 6291460
  57.2 2.9 %collective-permute-start.7 = (bf16[16,64,512]{2,1,0:T(8,128)(2,1)S(1)}, bf16[16,64,512]{2,1,0:T(8,128)(2,1)}, u32[]{:S(2)}, u32[]{:S(2)}) collective-permute-start(bf16[16,64,512]{2,1,0:T(8,128)(2,1)S(1)} %slice_bitcast_fusion), channel_id=1, source_target_pairs={{0,8},{8,0},{16,24},{24,16},{1,9},{9,1},{17,25},{25,17},{2,10},{10... | collective-permute-start | bytes 3145736 | tf_op jit(solution)/shard_map/ppermute | solution.py:187
  57.3 6.0 %copy-start.4 = (s32[4]{0:T(128)S(1)}, s32[4]{0:T(128)}, u32[]{:S(2)}) copy-start(s32[4]{0:T(128)} %param.5) | copy-start | bytes 52
  61.7 14.0 %collective-permute-start.8 = (bf16[16,32,512]{2,1,0:T(8,128)(2,1)S(1)}, bf16[16,32,512]{2,1,0:T(8,128)(2,1)S(1)}, u32[]{:S(2)}, u32[]{:S(2)}) collective-permute-start(bf16[16,32,512]{2,1,0:T(8,128)(2,1)S(1)} %fusion.10), channel_id=1, source_target_pairs={{0,16},{8,24},{16,0},{24,8},{1,17},{9,25},{17,1},{25,9},{2,18},{10... | collective-permute-start | bytes 1572872 | tf_op jit(solution)/shard_map/ppermute | solution.py:195

commit v10 on v8

--- a/solution.py
+++ b/solution.py
@@ -32,9 +32,8 @@
     return table.reshape(sample_count, 2 * bin_count)
 
 
-def whiten_rows(strain_rows, bin_count):
-    sample_count = strain_rows.shape[1]
-    spectrum = jnp.dot(strain_rows, dft_table(sample_count, bin_count), preferred_element_type=jnp.float32)
+def whiten_rows(strain_rows, table, bin_count):
+    spectrum = jnp.dot(strain_rows, table, preferred_element_type=jnp.float32)
     real_part = spectrum[:, :bin_count]
     imag_part = spectrum[:, bin_count:]
     amplitude = jnp.sqrt(real_part * real_part + imag_part * imag_part)
@@ -119,12 +118,13 @@
     return out
 
 
-def exchange_by_halves(whitened, lists, groups, pair_here, b_dev):
+def exchange_by_halves(whitened, block_list, lists, groups, pair_here, b_dev):
     n_pair = lists.shape[0]
     half = n_pair // 2
     base = (pair_here // half) * half
     pos = pair_here % half
-    mirror_blocks = lax.ppermute(whitened, "pair", [(p, p ^ half) for p in range(n_pair)])
+    across = [(p, p ^ half) for p in range(n_pair)]
+    mirror_blocks = jnp.stack([lax.ppermute(block, "pair", across) for block in block_list], axis=1)
     own_choice = block_choice(lists, pair_here, b_dev)
     mirror_choice = block_choice(lists, pair_here ^ half, b_dev)
     arrived_own = []
@@ -154,14 +154,20 @@
     win_here = lax.axis_index("win")
     b_dev = local_rows // C
 
-    flat_rows = strain.reshape(window_count * local_rows, sample_count)
-    whitened = whiten_rows(flat_rows, F).reshape(window_count, b_dev, C, 2 * F)
+    table = dft_table(sample_count, F)
+    block_list = [
+        whiten_rows(strain[:, k * C : (k + 1) * C].reshape(window_count * C, sample_count), table, F).reshape(
+            window_count, C, 2 * F
+        )
+        for k in range(b_dev)
+    ]
+    whitened = jnp.stack(block_list, axis=1)
 
     lists = pair_list.reshape(n_pair, 2 * slot_count)
     wanted = lax.dynamic_slice_in_dim(pair_list, pair_here * slot_count, slot_count, 0)
     groups = wanted.reshape(2 * slot_count) // b_dev
     if n_pair == 8:
-        incoming, slots = exchange_by_halves(whitened, lists, groups, pair_here, b_dev)
+        incoming, slots = exchange_by_halves(whitened, block_list, lists, groups, pair_here, b_dev)
     else:
         outgoing = pick_blocks(whitened, block_choice(lists, pair_here, b_dev))
         incoming = lax.all_to_all(outgoing, "pair", 0, 0, tiled=True)

time: 78.3 us -> 75.8 us (0.968)
  waiting for transfers between devices: 32.5 us -> 30.6 us
  local copies, waits for them, and re-layouts: 6.82 us -> 5.68 us
  starting transfers between devices: 13.2 us -> 14 us
    ppermute x3, waiting for transfers between devices: 4.44 us -> 0.01 us  [exchange_by_halves(): own = lax.ppermute(own, 'pair', perm)]
    ppermute x3, waiting for transfers between devices: 5.11 us -> 7.37 us  [exchange_by_halves(): relay = lax.ppermute(relay, 'pair', perm)]
    ppermute x1 -> x2, starting transfers between devices: 2.65 us -> 4.18 us  [exchange_by_halves(): lax.ppermute(block, 'pair', across)]
    ppermute x3, starting transfers between devices: 6 us -> 4.76 us  [exchange_by_halves(): own = lax.ppermute(own, 'pair', perm)]
    add x1, other arithmetic: 0.34 us -> 1.54 us  [body(): keep + got.astype(jnp.float32)]
    gather x1, local copies, waits for them, and re-layouts: 2.44 us -> 1.33 us  [body(): send = jnp.take(corr, 1 - core, axis=0, mode='clip')]
    ppermute x1 -> x2, waiting for transfers between devices: 7.59 us -> 7.91 us  [exchange_by_halves(): lax.ppermute(block, 'pair', across)]
    dot_general x1 -> x2, matrix products: 3.2 us -> 3.38 us  [whiten_rows(): spectrum = jnp.dot(strain_rows, table, preferred_element_type=jnp.float32)]
  transfers between devices with their start and end apart: 9 -> 10, of which waited for: 8 -> 7; matrix products, arithmetic and copies ran while one was open for 4% -> 2% of each run, Pallas kernels for 0% -> 0%
where the time goes in v10:
time: 75.8 us; the launch traced here: 75.4 us
  waiting for transfers between devices  30.6 us (40%)
  starting transfers between devices  14 us (18%)
  other arithmetic  9.2 us (12%)
  Pallas kernels  7.22 us (10%)
  local copies, waits for them, and re-layouts  5.68 us (7%)
  between operations  5.38 us (7%)
  matrix products  3.38 us (4%)
    ppermute x1, waiting for transfers between devices, body(): total = total + lax.ppermute(piece, 'win', perm).astype(jnp.float32)  12.7 us
    ppermute x2, waiting for transfers between devices, exchange_by_halves(): lax.ppermute(block, 'pair', across)  7.91 us
    ppermute x3, waiting for transfers between devices, exchange_by_halves(): relay = lax.ppermute(relay, 'pair', perm)  7.37 us
    pallas_call x1, Pallas kernels, tile_correlation(): pl.pallas_call(functools.partial(correlation_kernel, sub, n_y, own_rows),...  7.22 us
    ppermute x3, starting transfers between devices, exchange_by_halves(): own = lax.ppermute(own, 'pair', perm)  4.76 us
    ppermute x2, starting transfers between devices, exchange_by_halves(): lax.ppermute(block, 'pair', across)  4.18 us
    another operation x3, other arithmetic  3.72 us
    ppermute x3, starting transfers between devices, exchange_by_halves(): relay = lax.ppermute(relay, 'pair', perm)  3.64 us
  transfers between devices with their start and end apart: 10, of which 7 were waited for; matrix products, arithmetic and copies ran while one was open for 2% of the time, Pallas kernels for 0%

profile of v10, /device:TPU:0, one launch (start us, length us, event | category | flops | bytes accessed | tf_op | source)
XLA Modules:
  0.0 75.4 jit_solution(12711338151294332255)
XLA Ops:
  0.0 0.8 %fusion.19 = (f32[128,384]{1,0:T(8,128)S(1)}, f32[128,384]{1,0:T(8,128)S(1)}) fusion(s32[384]{0:T(512)S(1)} %iota_add_fusion), kind=kLoop, calls=%fused_computation.41 | loop fusion | flops 442368 | bytes 394752 | tf_op jit(solution)/shard_map/cos | solution.py:20
  0.8 0.5 fusion.26
  1.3 0.0 copy-start.2
  1.3 3.5 %subtract_convert_fusion = (bf16[60,128,384]{2,1,0:T(8,128)(2,1)S(1)}, bf16[60,128,384]{2,1,0:T(8,128)(2,1)S(1)}) fusion(f32[128,384]{1,0:T(8,128)S(1)} %get-tuple-element.160, f32[60,384]{1,0:T(8,128)S(1)} %get-tuple-element.154, f32[128,384]{1,0:T(8,128)S(1)} %get-tuple-element.159, f32[60,384]{1,0:T(8,128)S(1)} %get-tuple-element.153), kind=kLoop, calls=%fused_computation.2 | loop fusion | flops 26542080 | bytes 12374016 | tf_op jit(solution)/shard_map/convert.19
  4.8 1.7 %fusion.6 = f32[128,768]{1,0:T(8,128)S(1)} fusion(bf16[7680,384]{1,0:T(8,128)(2,1)S(1)} %bitcast.66, bf16[7680,384]{1,0:T(8,128)(2,1)S(1)} %bitcast.64, bf16[1,256,7680]{2,1,0:T(8,128)(2,1)S(1)} %copy-done.2), kind=kOutput, calls=%fused_computation.10 | convolution fusion | flops 1533542400 | bytes 14155776 | tf_op jit(solution)/shard_map/dot_general | solution.py:36
  6.5 0.0 copy-start.1
  6.5 1.7 %fusion.9 = f32[128,768]{1,0:T(8,128)S(1)} fusion(bf16[7680,384]{1,0:T(8,128)(2,1)S(1)} %bitcast.67, bf16[7680,384]{1,0:T(8,128)(2,1)S(1)} %bitcast.65, bf16[1,256,7680]{2,1,0:T(8,128)(2,1)S(1)} %copy-done.2), kind=kOutput, calls=%fused_computation.11 | convolution fusion | flops 1533542400 | bytes 14155776 | tf_op jit(solution)/shard_map/dot_general | solution.py:36
  8.3 0.1 reduce_sum.43
  8.4 0.1 reduce_sum.52
  8.5 0.1 reduce_sum.56
  8.6 0.1 reduce_sum.57
  8.7 0.7 fusion.51
  11.2 0.2 fusion.49
  11.5 0.1 divide_convert_fusion.1
  11.6 0.1 divide_convert_fusion.3
  11.7 0.1 broadcast_select_fusion.3
  11.8 4.1 %collective-permute-start.3 = (bf16[1,128,768]{2,1,0:T(8,128)(2,1)S(1)}, bf16[1,128,768]{2,1,0:T(8,128)(2,1)S(1)}, u32[]{:S(2)}, u32[]{:S(2)}) collective-permute-start(bf16[1,128,768]{2,1,0:T(8,128)(2,1)S(1)} %get-tuple-element.152), channel_id=1, source_target_pairs={{0,4},{1,5},{2,6},{3,7},{4,0},{5,1},{6,2},{7,3},{8,12},{9,13},{10,... | collective-permute-start | bytes 589832 | tf_op jit(solution)/shard_map/ppermute | solution.py:127
  15.9 0.1 collective-permute-start.4
  16.0 1.7 %collective-permute-start = (bf16[1,128,768]{2,1,0:T(8,128)(2,1)S(1)}, bf16[1,128,768]{2,1,0:T(8,128)(2,1)S(1)}, u32[]{:S(2)}, u32[]{:S(2)}) collective-permute-start(bf16[1,128,768]{2,1,0:T(8,128)(2,1)S(1)} %get-tuple-element.149), channel_id=1, source_target_pairs={{0,1},{1,2},{2,3},{3,0},{4,5},{5,6},{6,7},{7,4},{8,9},{9,10},{10,1... | collective-permute-start | bytes 589832 | tf_op jit(solution)/shard_map/ppermute | solution.py:138
  17.8 1.6 %collective-permute-start.1 = (bf16[1,128,768]{2,1,0:T(8,128)(2,1)S(1)}, bf16[1,128,768]{2,1,0:T(8,128)(2,1)S(1)}, u32[]{:S(2)}, u32[]{:S(2)}) collective-permute-start(bf16[1,128,768]{2,1,0:T(8,128)(2,1)S(1)} %get-tuple-element.150), channel_id=1, source_target_pairs={{0,2},{1,3},{2,0},{3,1},{4,6},{5,7},{6,4},{7,5},{8,10},{9,11},{10,... | collective-permute-start | bytes 589832 | tf_op jit(solution)/shard_map/ppermute | solution.py:138
  19.3 1.4 %collective-permute-start.2 = (bf16[1,128,768]{2,1,0:T(8,128)(2,1)S(1)}, bf16[1,128,768]{2,1,0:T(8,128)(2,1)S(1)}, u32[]{:S(2)}, u32[]{:S(2)}) collective-permute-start(bf16[1,128,768]{2,1,0:T(8,128)(2,1)S(1)} %get-tuple-element.148), channel_id=1, source_target_pairs={{0,3},{1,0},{2,1},{3,2},{4,7},{5,4},{6,5},{7,6},{8,11},{9,8},{10,9... | collective-permute-start | bytes 589832 | tf_op jit(solution)/shard_map/ppermute | solution.py:138
  24.0 0.1 constant_dynamic-slice_fusion
  24.1 0.1 copy.7
  24.2 0.1 reshape.467
  24.3 0.8 %fusion.38 = (f32[4,384]{1,0:T(4,128)}, f32[4,384]{1,0:T(4,128)}, f32[4,384]{1,0:T(4,128)}, f32[4,384]{1,0:T(4,128)}) fusion(s32[384]{0:T(512)S(1)} %iota_add_fusion, s32[4]{0:T(128)S(1)} %get-tuple-element.175, s32[4]{0:T(128)S(1)} %get-tuple-element.176), kind=kLoop, calls=%fused_computation.72 | loop fusion | flops 27648 | bytes 26144 | tf_op jit(solution)/shard_map/sin | solution.py:20
  25.1 0.6 fusion.46.index_ref
  25.7 4.5 %collective-permute-done.3 = bf16[1,128,768]{2,1,0:T(8,128)(2,1)S(1)} collective-permute-done((bf16[1,128,768]{2,1,0:T(8,128)(2,1)S(1)}, bf16[1,128,768]{2,1,0:T(8,128)(2,1)S(1)}, u32[]{:S(2)}, u32[]{:S(2)}) %collective-permute-start.3) | collective-permute-done | bytes 196640 | tf_op jit(solution)/shard_map/ppermute | solution.py:127
  30.2 3.4 %collective-permute-done.4 = bf16[1,128,768]{2,1,0:T(8,128)(2,1)S(1)} collective-permute-done((bf16[1,128,768]{2,1,0:T(8,128)(2,1)S(1)}, bf16[1,128,768]{2,1,0:T(8,128)(2,1)S(1)}, u32[]{:S(2)}, u32[]{:S(2)}) %collective-permute-start.4) | collective-permute-done | bytes 196640 | tf_op jit(solution)/shard_map/ppermute | solution.py:127
  33.6 1.6 %collective-permute-start.5 = (bf16[1,128,768]{2,1,0:T(8,128)(2,1)S(1)}, bf16[1,128,768]{2,1,0:T(8,128)(2,1)S(1)}, u32[]{:S(2)}, u32[]{:S(2)}) collective-permute-start(bf16[1,128,768]{2,1,0:T(8,128)(2,1)S(1)} %get-tuple-element.147), channel_id=1, source_target_pairs={{0,1},{1,2},{2,3},{3,0},{4,5},{5,6},{6,7},{7,4},{8,9},{9,10},{10,1... | collective-permute-start | bytes 589832 | tf_op jit(solution)/shard_map/ppermute | solution.py:139
  35.2 0.6 collective-permute-start.6
  35.8 1.4 %collective-permute-start.7 = (bf16[1,128,768]{2,1,0:T(8,128)(2,1)S(1)}, bf16[1,128,768]{2,1,0:T(8,128)(2,1)S(1)}, u32[]{:S(2)}, u32[]{:S(2)}) collective-permute-start(bf16[1,128,768]{2,1,0:T(8,128)(2,1)S(1)} %get-tuple-element.145), channel_id=1, source_target_pairs={{0,3},{1,0},{2,1},{3,2},{4,7},{5,4},{6,5},{7,6},{8,11},{9,8},{10,9... | collective-permute-start | bytes 589832 | tf_op jit(solution)/shard_map/ppermute | solution.py:139
  37.3 0.1 bitcast_dynamic-update-slice_fusion.3
  37.4 5.0 %collective-permute-done.5 = bf16[1,128,768]{2,1,0:T(8,128)(2,1)S(1)} collective-permute-done((bf16[1,128,768]{2,1,0:T(8,128)(2,1)S(1)}, bf16[1,128,768]{2,1,0:T(8,128)(2,1)S(1)}, u32[]{:S(2)}, u32[]{:S(2)}) %collective-permute-start.5) | collective-permute-done | bytes 196640 | tf_op jit(solution)/shard_map/ppermute | solution.py:139
  42.4 0.3 collective-permute-done.6
  42.8 2.0 %collective-permute-done.7 = bf16[1,128,768]{2,1,0:T(8,128)(2,1)S(1)} collective-permute-done((bf16[1,128,768]{2,1,0:T(8,128)(2,1)S(1)}, bf16[1,128,768]{2,1,0:T(8,128)(2,1)S(1)}, u32[]{:S(2)}, u32[]{:S(2)}) %collective-permute-start.7) | collective-permute-done | bytes 196640 | tf_op jit(solution)/shard_map/ppermute | solution.py:139
  44.8 1.1 %copy-done = bf16[8,1,128,768]{3,2,1,0:T(8,128)(2,1)} copy-done((bf16[8,1,128,768]{3,2,1,0:T(8,128)(2,1)}, bf16[8,1,128,768]{3,2,1,0:T(8,128)(2,1)S(1)}, u32[]{:S(2)}) %copy-start) | copy-done | bytes 1572888
  46.0 7.2 %shard_map.37 = bf16[2,16,64,512]{3,2,1,0:T(8,128)(2,1)} custom-call(s32[8]{0:T(128)} %fusion.46.index_ref, f32[4,384]{1,0:T(4,128)} %get-tuple-element.161.cc_ref, f32[4,384]{1,0:T(4,128)} %get-tuple-element.162.sc_ref, f32[4,384]{1,0:T(4,128)} %get-tuple-element.156.cf_ref, f32[4,384]{1,0:T(4,128)} %get-tuple-element.155.sf_ref, ...), custom_call_target="tpu_custom_call" | custom-call | flops 1610612736 | bytes 3670016 | tf_op jit(solution)/shard_map/pallas_call | solution.py:99
  53.2 1.3 %dynamic-slice_bitcast_fusion = bf16[16,64,512]{2,1,0:T(8,128)(2,1)S(1)} fusion(bf16[2,16,64,512]{3,2,1,0:T(8,128)(2,1)} %shard_map.37, s32[]{:T(128)S(6)} %sub.53), kind=kLoop, calls=%fused_computation.14 | loop fusion | bytes 2097156 | tf_op jit(solution)/shard_map/jit(_take)/gather | solution.py:189
  54.5 0.1 collective-permute-start.8
  54.6 2.6 %collective-permute-done.8 = bf16[16,64,512]{2,1,0:T(8,128)(2,1)S(1)} collective-permute-done((bf16[16,64,512]{2,1,0:T(8,128)(2,1)S(1)}, bf16[16,64,512]{2,1,0:T(8,128)(2,1)S(1)}, u32[]{:S(2)}, u32[]{:S(2)}) %collective-permute-start.8) | collective-permute-done | bytes 1048608 | tf_op jit(solution)/shard_map/ppermute | solution.py:191
  57.2 1.5 %convert_add_fusion = f32[16,64,512]{2,1,0:T(8,128)S(1)} fusion(bf16[16,64,512]{2,1,0:T(8,128)(2,1)S(1)} %collective-permute-done.8, bf16[2,16,64,512]{3,2,1,0:T(8,128)(2,1)} %shard_map.37, s32[]{:T(128)S(6)} %select_n.243), kind=kLoop, calls=%fused_computation.5 | loop fusion | flops 1572864 | bytes 4194308 | tf_op jit(solution)/shard_map/add | solution.py:192
  58.8 0.1 fusion.12
  58.9 1.3 %collective-permute-start.9 = (bf16[16,32,512]{2,1,0:T(8,128)(2,1)S(1)}, bf16[16,32,512]{2,1,0:T(8,128)(2,1)S(1)}, u32[]{:S(2)}, u32[]{:S(2)}) collective-permute-start(bf16[16,32,512]{2,1,0:T(8,128)(2,1)S(1)} %fusion.12), channel_id=1, source_target_pairs={{0,16},{8,24},{16,0},{24,8},{1,17},{9,25},{17,1},{25,9},{2,18},{10... | collective-permute-start | bytes 1572872 | tf_op jit(solution)/shard_map/ppermute | solution.py:199
  60.2 12.7 %collective-permute-done.9 = bf16[16,32,512]{2,1,0:T(8,128)(2,1)S(1)} collective-permute-done((bf16[16,32,512]{2,1,0:T(8,128)(2,1)S(1)}, bf16[16,32,512]{2,1,0:T(8,128)(2,1)S(1)}, u32[]{:S(2)}, u32[]{:S(2)}) %collective-permute-start.9) | collective-permute-done | bytes 524320 | tf_op jit(solution)/shard_map/ppermute | solution.py:199
  72.9 0.2 bitcast_add_fusion
  73.1 0.4 reshape.471
  73.5 0.4 multiply_bitcast_fusion
  73.8 1.6 %copy.11 = f32[32,4,16,128]{3,2,1,0:T(8,128)} copy(f32[32,4,16,128]{3,1,0,2:T(4,128)S(1)} %multiply_bitcast_fusion) | data formatting | bytes 2097152 | tf_op jit(solution)/shard_map/div | solution.py:203
  (23 shorter events, 0.2 us)
Async XLA Ops:
  1.3 3.5 %copy-start.2 = (bf16[1,256,7680]{2,1,0:T(8,128)(2,1)S(1)}, bf16[1,256,7680]{2,1,0:T(8,128)(2,1)}, u32[]{:S(2)}) copy-start(bf16[1,256,7680]{2,1,0:T(8,128)(2,1)} %param.3) | copy-start | bytes 11796484
  6.5 1.8 %copy-start.1 = (s32[32,2]{0,1:T(2,128)S(1)}, s32[32,2]{0,1:T(2,128)}, u32[]{:S(2)}) copy-start(s32[32,2]{0,1:T(2,128)} %param.4) | copy-start | bytes 772
  11.8 18.4 %collective-permute-start.3 = (bf16[1,128,768]{2,1,0:T(8,128)(2,1)S(1)}, bf16[1,128,768]{2,1,0:T(8,128)(2,1)S(1)}, u32[]{:S(2)}, u32[]{:S(2)}) collective-permute-start(bf16[1,128,768]{2,1,0:T(8,128)(2,1)S(1)} %get-tuple-element.152), channel_id=1, source_target_pairs={{0,4},{1,5},{2,6},{3,7},{4,0},{5,1},{6,2},{7,3},{8,12},{9,13},{10,... | collective-permute-start | bytes 589832 | tf_op jit(solution)/shard_map/ppermute | solution.py:127
  15.9 17.6 %collective-permute-start.4 = (bf16[1,128,768]{2,1,0:T(8,128)(2,1)S(1)}, bf16[1,128,768]{2,1,0:T(8,128)(2,1)S(1)}, u32[]{:S(2)}, u32[]{:S(2)}) collective-permute-start(bf16[1,128,768]{2,1,0:T(8,128)(2,1)S(1)} %get-tuple-element.151), channel_id=1, source_target_pairs={{0,4},{1,5},{2,6},{3,7},{4,0},{5,1},{6,2},{7,3},{8,12},{9,13},{10,... | collective-permute-start | bytes 589832 | tf_op jit(solution)/shard_map/ppermute | solution.py:127
  16.0 19.8 %collective-permute-start = (bf16[1,128,768]{2,1,0:T(8,128)(2,1)S(1)}, bf16[1,128,768]{2,1,0:T(8,128)(2,1)S(1)}, u32[]{:S(2)}, u32[]{:S(2)}) collective-permute-start(bf16[1,128,768]{2,1,0:T(8,128)(2,1)S(1)} %get-tuple-element.149), channel_id=1, source_target_pairs={{0,1},{1,2},{2,3},{3,0},{4,5},{5,6},{6,7},{7,4},{8,9},{9,10},{10,1... | collective-permute-start | bytes 589832 | tf_op jit(solution)/shard_map/ppermute | solution.py:138
  17.8 19.5 %collective-permute-start.1 = (bf16[1,128,768]{2,1,0:T(8,128)(2,1)S(1)}, bf16[1,128,768]{2,1,0:T(8,128)(2,1)S(1)}, u32[]{:S(2)}, u32[]{:S(2)}) collective-permute-start(bf16[1,128,768]{2,1,0:T(8,128)(2,1)S(1)} %get-tuple-element.150), channel_id=1, source_target_pairs={{0,2},{1,3},{2,0},{3,1},{4,6},{5,7},{6,4},{7,5},{8,10},{9,11},{10,... | collective-permute-start | bytes 589832 | tf_op jit(solution)/shard_map/ppermute | solution.py:138
  19.3 18.0 %collective-permute-start.2 = (bf16[1,128,768]{2,1,0:T(8,128)(2,1)S(1)}, bf16[1,128,768]{2,1,0:T(8,128)(2,1)S(1)}, u32[]{:S(2)}, u32[]{:S(2)}) collective-permute-start(bf16[1,128,768]{2,1,0:T(8,128)(2,1)S(1)} %get-tuple-element.148), channel_id=1, source_target_pairs={{0,3},{1,0},{2,1},{3,2},{4,7},{5,4},{6,5},{7,6},{8,11},{9,8},{10,9... | collective-permute-start | bytes 589832 | tf_op jit(solution)/shard_map/ppermute | solution.py:138
  33.6 8.8 %collective-permute-start.5 = (bf16[1,128,768]{2,1,0:T(8,128)(2,1)S(1)}, bf16[1,128,768]{2,1,0:T(8,128)(2,1)S(1)}, u32[]{:S(2)}, u32[]{:S(2)}) collective-permute-start(bf16[1,128,768]{2,1,0:T(8,128)(2,1)S(1)} %get-tuple-element.147), channel_id=1, source_target_pairs={{0,1},{1,2},{2,3},{3,0},{4,5},{5,6},{6,7},{7,4},{8,9},{9,10},{10,1... | collective-permute-start | bytes 589832 | tf_op jit(solution)/shard_map/ppermute | solution.py:139
  35.2 7.6 %collective-permute-start.6 = (bf16[1,128,768]{2,1,0:T(8,128)(2,1)S(1)}, bf16[1,128,768]{2,1,0:T(8,128)(2,1)S(1)}, u32[]{:S(2)}, u32[]{:S(2)}) collective-permute-start(bf16[1,128,768]{2,1,0:T(8,128)(2,1)S(1)} %get-tuple-element.146), channel_id=1, source_target_pairs={{0,2},{1,3},{2,0},{3,1},{4,6},{5,7},{6,4},{7,5},{8,10},{9,11},{10,... | collective-permute-start | bytes 589832 | tf_op jit(solution)/shard_map/ppermute | solution.py:139
  35.8 9.0 %collective-permute-start.7 = (bf16[1,128,768]{2,1,0:T(8,128)(2,1)S(1)}, bf16[1,128,768]{2,1,0:T(8,128)(2,1)S(1)}, u32[]{:S(2)}, u32[]{:S(2)}) collective-permute-start(bf16[1,128,768]{2,1,0:T(8,128)(2,1)S(1)} %get-tuple-element.145), channel_id=1, source_target_pairs={{0,3},{1,0},{2,1},{3,2},{4,7},{5,4},{6,5},{7,6},{8,11},{9,8},{10,9... | collective-permute-start | bytes 589832 | tf_op jit(solution)/shard_map/ppermute | solution.py:139
  44.8 1.1 %copy-start = (bf16[8,1,128,768]{3,2,1,0:T(8,128)(2,1)}, bf16[8,1,128,768]{3,2,1,0:T(8,128)(2,1)S(1)}, u32[]{:S(2)}) copy-start(bf16[8,1,128,768]{3,2,1,0:T(8,128)(2,1)S(1)} %bitcast_dynamic-update-slice_fusion.left_ref.right_ref) | copy-start | bytes 4718596
  53.2 7.0 %copy-start.3 = (s32[4]{0:T(128)S(1)}, s32[4]{0:T(128)}, u32[]{:S(2)}) copy-start(s32[4]{0:T(128)} %param.5) | copy-start | bytes 52
  54.5 2.7 %collective-permute-start.8 = (bf16[16,64,512]{2,1,0:T(8,128)(2,1)S(1)}, bf16[16,64,512]{2,1,0:T(8,128)(2,1)S(1)}, u32[]{:S(2)}, u32[]{:S(2)}) collective-permute-start(bf16[16,64,512]{2,1,0:T(8,128)(2,1)S(1)} %dynamic-slice_bitcast_fusion), channel_id=1, source_target_pairs={{0,8},{8,0},{16,24},{24,16},{1,9},{9,1},{17,25},{25,17},{2,10},{10... | collective-permute-start | bytes 3145736 | tf_op jit(solution)/shard_map/ppermute | solution.py:191
  58.9 14.0 %collective-permute-start.9 = (bf16[16,32,512]{2,1,0:T(8,128)(2,1)S(1)}, bf16[16,32,512]{2,1,0:T(8,128)(2,1)S(1)}, u32[]{:S(2)}, u32[]{:S(2)}) collective-permute-start(bf16[16,32,512]{2,1,0:T(8,128)(2,1)S(1)} %fusion.12), channel_id=1, source_target_pairs={{0,16},{8,24},{16,0},{24,8},{1,17},{9,25},{17,1},{25,9},{2,18},{10... | collective-permute-start | bytes 1572872 | tf_op jit(solution)/shard_map/ppermute | solution.py:199

commit v11 on v10

--- a/solution.py
+++ b/solution.py
@@ -42,13 +42,21 @@
     return jnp.concatenate([real_part / divisor, imag_part / divisor], axis=1).astype(jnp.bfloat16)
 
 
-def correlation_kernel(sub, n_y, own_rows, index_ref, cc_ref, sc_ref, cf_ref, sf_ref, left_ref, right_ref, out_ref):
+def correlation_kernel(sub, n_y, own_rows, target, index_ref, cc_ref, sc_ref, cf_ref, sf_ref, left_ref, right_ref, out_ref):
     window_count = left_ref.shape[1]
-    order = [(y * 2 + c) * own_rows for c in range(2) for y in range(n_y)]
+    win = lax.axis_index("win")
+    core = win % 2
+    if target is None:
+        chips = list(range(n_y))
+    else:
+        chips = [(1 - win // 2) if target == 0 else win // 2]
+    starts = [(y * 2 + cc) * own_rows for cc in (1 - core, core) for y in chips]
+    part_rows = len(chips) * own_rows
     acc = None
     for w in range(window_count):
-        left = left_ref[0, w].astype(jnp.float32)
-        left = jnp.concatenate([left[r : r + own_rows] for r in order], axis=0)
+        left = jnp.concatenate(
+            [left_ref[0, w, pl.ds(pl.multiple_of(r, own_rows), own_rows), :] for r in starts], axis=0
+        ).astype(jnp.float32)
         lre = left[:, :F]
         lim = left[:, F:]
         rre = right_ref[0, w, :, :F].astype(jnp.float32)
@@ -74,34 +82,36 @@
                 lax.dot_general(left_t, right_all, (((1,), (1,)), ((), ())), preferred_element_type=jnp.float32)
             )
         acc = parts if acc is None else [a + p for a, p in zip(acc, parts)]
-    half_rows = C // 2
     for l2, res in enumerate(acc):
         for l1 in range(sub):
             for part in range(2):
-                out_ref[part, l2 * sub + l1] = res[part * half_rows : (part + 1) * half_rows, l1 * C : (l1 + 1) * C].astype(
+                out_ref[part, l2 * sub + l1] = res[part * part_rows : (part + 1) * part_rows, l1 * C : (l1 + 1) * C].astype(
                     out_ref.dtype
                 )
 
 
-def tile_correlation(cc, sc, cf, sf, incoming, slots, sub, n_y, own_rows):
+def tile_correlation(cc, sc, cf, sf, incoming, slots, sub, n_y, own_rows, target=None, weight=1.0):
     window_count = incoming.shape[1]
     slot_count = slots.shape[0] // 2
+    part_rows = own_rows * (n_y if target is None else 1)
     table_spec = pl.BlockSpec(cc.shape, lambda t, idx: (0, 0))
     left_spec = pl.BlockSpec((1, window_count, C, 2 * F), lambda t, idx: (idx[2 * t], 0, 0, 0))
     right_spec = pl.BlockSpec((1, window_count, C, 2 * F), lambda t, idx: (idx[2 * t + 1], 0, 0, 0))
-    flops = 2 * slot_count * window_count * C * 2 * F * LAGS * C
+    flops = int(weight * 2 * slot_count * window_count * 2 * part_rows * 2 * F * LAGS * C)
     grid_spec = pltpu.PrefetchScalarGridSpec(
         num_scalar_prefetch=1,
         grid=(slot_count,),
         in_specs=[table_spec] * 4 + [left_spec, right_spec],
-        out_specs=pl.BlockSpec((2, LAGS, C // 2, C), lambda t, idx: (0, 0, 0, t)),
+        out_specs=pl.BlockSpec((2, LAGS, part_rows, C), lambda t, idx: (0, 0, 0, t)),
     )
     return pl.pallas_call(
-        functools.partial(correlation_kernel, sub, n_y, own_rows),
+        functools.partial(correlation_kernel, sub, n_y, own_rows, target),
         grid_spec=grid_spec,
-        out_shape=jax.ShapeDtypeStruct((2, LAGS, C // 2, slot_count * C), jnp.bfloat16),
+        out_shape=jax.ShapeDtypeStruct((2, LAGS, part_rows, slot_count * C), jnp.bfloat16),
         cost_estimate=pl.CostEstimate(
-            flops=flops, transcendentals=0, bytes_accessed=slot_count * (4 * window_count * C * F * 2 + 2 * C * LAGS * C)
+            flops=max(flops, 1),
+            transcendentals=0,
+            bytes_accessed=int(weight * slot_count * (4 * window_count * C * F * 2 + 4 * part_rows * LAGS * C)),
         ),
     )(slots, cc, sc, cf, sf, incoming, incoming)
 
@@ -145,6 +155,21 @@
     return incoming, slots
 
 
+def window_sum(corr, win_here, n_win, own_rows, slot_count):
+    n_y = n_win // 2
+    y_here = win_here // 2
+    got = lax.ppermute(corr[0], "win", [(w, w ^ 1) for w in range(n_win)])
+    half = (corr[1].astype(jnp.float32) + got.astype(jnp.float32)).reshape(LAGS, n_y, own_rows, slot_count * C)
+    half = jnp.transpose(half, (1, 0, 2, 3))
+    total = jnp.take(half, y_here, axis=0, mode="clip")
+    for shift in range(1, n_y):
+        dest = (y_here + shift) % n_y
+        piece = jnp.take(half, dest, axis=0, mode="clip").astype(jnp.bfloat16)
+        perm = [(w, ((w // 2 + shift) % n_y) * 2 + w % 2) for w in range(n_win)]
+        total = total + lax.ppermute(piece, "win", perm).astype(jnp.float32)
+    return total
+
+
 def body(strain, pair_list, tile_live):
     window_count, local_rows, sample_count = strain.shape
     slot_count = tile_live.shape[0]
@@ -182,21 +207,19 @@
     coarse_lag = (lax.iota(jnp.int32, LAGS // sub) * sub - LAGS // 2) * DECIM
     cf, sf = cos_sin(fine_lag[:, None] * bins[None, :], sample_count)
     cc, sc = cos_sin(coarse_lag[:, None] * bins[None, :], sample_count)
-    corr = tile_correlation(cc, sc, cf, sf, incoming, slots, sub, n_y, own_rows)
-
-    core = win_here % 2
-    y_here = win_here // 2
-    send = jnp.take(corr, 1 - core, axis=0, mode="clip")
-    keep = jnp.take(corr, core, axis=0, mode="clip").astype(jnp.float32)
-    got = lax.ppermute(send, "win", [(w, w ^ 1) for w in range(n_win)])
-    half = (keep + got.astype(jnp.float32)).reshape(LAGS, n_y, own_rows, slot_count * C)
-    half = jnp.transpose(half, (1, 0, 2, 3))
-    total = jnp.take(half, y_here, axis=0, mode="clip")
-    for shift in range(1, n_y):
-        dest = (y_here + shift) % n_y
-        piece = jnp.take(half, dest, axis=0, mode="clip").astype(jnp.bfloat16)
-        perm = [(w, ((w // 2 + shift) % n_y) * 2 + w % 2) for w in range(n_win)]
-        total = total + lax.ppermute(piece, "win", perm).astype(jnp.float32)
+    core_pairs = [(w, w ^ 1) for w in range(n_win)]
+    if n_y == 2 and own_rows % 16 == 0:
+        far = tile_correlation(cc, sc, cf, sf, incoming, slots, sub, n_y, own_rows, target=0)
+        got = lax.ppermute(far[0], "win", core_pairs)
+        far_sum = (far[1].astype(jnp.float32) + got.astype(jnp.float32)).astype(jnp.bfloat16)
+        later, far_sum = lax.optimization_barrier((incoming, far_sum))
+        near = tile_correlation(cc, sc, cf, sf, later, slots, sub, n_y, own_rows, target=1, weight=0.01)
+        across = lax.ppermute(far_sum, "win", [(w, w ^ 2) for w in range(n_win)])
+        got = lax.ppermute(near[0], "win", core_pairs)
+        total = near[1].astype(jnp.float32) + got.astype(jnp.float32) + across.astype(jnp.float32)
+    else:
+        corr = tile_correlation(cc, sc, cf, sf, incoming, slots, sub, n_y, own_rows)
+        total = window_sum(corr, win_here, n_win, own_rows, slot_count)
     total = jnp.transpose(total.reshape(LAGS, own_rows, slot_count, C), (1, 2, 0, 3))
 
     live_local = tile_live.astype(jnp.float32)

time: 75.8 us -> 77.3 us (1.020)
  waiting for transfers between devices: 30.6 us -> 23.8 us
  Pallas kernels: 7.22 us -> 13.7 us
  other arithmetic: 9.2 us -> 12 us
  local copies, waits for them, and re-layouts: 5.68 us -> 4.86 us
    ppermute x2 -> x3, waiting for transfers between devices: 15.3 us -> 6.37 us  [the longest x1 4.47 us: body(): across = lax.ppermute(far_sum, 'win', [(w, w ^ 2) for w in range(n_win)])]
    pallas_call x1 -> x2, Pallas kernels: 7.22 us -> 13.7 us  [tile_correlation(): pl.pallas_call(functools.partial(correlation_kernel, sub, n_y, own_rows,...]
    ppermute x2, waiting for transfers between devices: 7.91 us -> 11.8 us  [exchange_by_halves(): lax.ppermute(block, 'pair', across)]
    squeeze x0 -> x2, local copies, waits for them, and re-layouts: none -> 2.15 us  [the longest x1 1.08 us: body(): got = lax.ppermute(far[0], 'win', core_pairs)]
    ppermute x3, waiting for transfers between devices: 7.37 us -> 5.55 us  [exchange_by_halves(): relay = lax.ppermute(relay, 'pair', perm)]
    div x1 -> x0, local copies, waits for them, and re-layouts: 1.58 us -> none  [body(): total * live_local[None, :, None, None]]
    gather x1 -> x0, local copies, waits for them, and re-layouts: 1.33 us -> none  [body(): send = jnp.take(corr, 1 - core, axis=0, mode='clip')]
    div x1, other arithmetic: 0.36 us -> 1.65 us  [body(): total * live_local[None, :, None, None]]
  transfers between devices with their start and end apart: 10 -> 11, of which waited for: 7 -> 6; matrix products, arithmetic and copies ran while one was open for 2% -> 4% of each run, Pallas kernels for 0% -> 9%
where the time goes in v11:
time: 77.3 us; the launch traced here: 76.8 us
  waiting for transfers between devices  23.8 us (31%)
  Pallas kernels  13.7 us (18%)
  starting transfers between devices  13.6 us (18%)
  other arithmetic  12 us (16%)
  between operations  5.47 us (7%)
  local copies, waits for them, and re-layouts  4.86 us (6%)
  matrix products  3.38 us (4%)
    pallas_call x2, Pallas kernels, tile_correlation(): pl.pallas_call(functools.partial(correlation_kernel, sub, n_y, own_rows,...  13.7 us
    ppermute x2, waiting for transfers between devices, exchange_by_halves(): lax.ppermute(block, 'pair', across)  11.8 us
    ppermute x3, starting transfers between devices, exchange_by_halves(): own = lax.ppermute(own, 'pair', perm)  5.95 us
    ppermute x3, waiting for transfers between devices, exchange_by_halves(): relay = lax.ppermute(relay, 'pair', perm)  5.55 us
    ppermute x1, waiting for transfers between devices, body(): across = lax.ppermute(far_sum, 'win', [(w, w ^ 2) for w in range(n_win)])  4.47 us
    another operation x3, other arithmetic  3.72 us
    dot_general x2, matrix products, whiten_rows(): spectrum = jnp.dot(strain_rows, table, preferred_element_type=jnp.float32)  3.38 us
    ppermute x3, starting transfers between devices, exchange_by_halves(): relay = lax.ppermute(relay, 'pair', perm)  2.98 us
  transfers between devices with their start and end apart: 11, of which 6 were waited for; matrix products, arithmetic and copies ran while one was open for 4% of the time, Pallas kernels for 9%

profile of v11, /device:TPU:0, one launch (start us, length us, event | category | flops | bytes accessed | tf_op | source)
XLA Modules:
  0.0 76.8 jit_solution(103065720834174381)
XLA Ops:
  0.0 0.8 %fusion.22 = (f32[128,384]{1,0:T(8,128)S(1)}, f32[128,384]{1,0:T(8,128)S(1)}) fusion(s32[384]{0:T(512)S(1)} %iota_add_fusion), kind=kLoop, calls=%fused_computation.46 | loop fusion | flops 442368 | bytes 394752 | tf_op jit(solution)/shard_map/cos | solution.py:20
  0.8 0.5 fusion.29
  1.3 0.0 copy-start.2
  1.3 3.5 %subtract_convert_fusion = (bf16[60,128,384]{2,1,0:T(8,128)(2,1)S(1)}, bf16[60,128,384]{2,1,0:T(8,128)(2,1)S(1)}) fusion(f32[128,384]{1,0:T(8,128)S(1)} %get-tuple-element.122, f32[60,384]{1,0:T(8,128)S(1)} %get-tuple-element.118, f32[128,384]{1,0:T(8,128)S(1)} %get-tuple-element.121, f32[60,384]{1,0:T(8,128)S(1)} %get-tuple-element.117), kind=kLoop, calls=%fused_computation.2 | loop fusion | flops 26542080 | bytes 12374016 | tf_op jit(solution)/shard_map/convert.21
  4.8 1.7 %fusion.9 = f32[128,768]{1,0:T(8,128)S(1)} fusion(bf16[7680,384]{1,0:T(8,128)(2,1)S(1)} %bitcast.64, bf16[7680,384]{1,0:T(8,128)(2,1)S(1)} %bitcast.62, bf16[1,256,7680]{2,1,0:T(8,128)(2,1)S(1)} %copy-done.2), kind=kOutput, calls=%fused_computation.10 | convolution fusion | flops 1533542400 | bytes 14155776 | tf_op jit(solution)/shard_map/dot_general | solution.py:36
  6.5 0.0 copy-start.1
  6.5 1.7 %fusion.6 = f32[128,768]{1,0:T(8,128)S(1)} fusion(bf16[7680,384]{1,0:T(8,128)(2,1)S(1)} %bitcast.65, bf16[7680,384]{1,0:T(8,128)(2,1)S(1)} %bitcast.63, bf16[1,256,7680]{2,1,0:T(8,128)(2,1)S(1)} %copy-done.2), kind=kOutput, calls=%fused_computation.9 | convolution fusion | flops 1533542400 | bytes 14155776 | tf_op jit(solution)/shard_map/dot_general | solution.py:36
  8.3 0.2 fusion.52
  8.5 0.1 divide_convert_fusion.3
  8.7 0.1 divide_convert_fusion.1
  8.8 0.1 reduce_sum.56
  8.9 0.1 reduce_sum.57
  9.1 0.1 reduce_sum.43
  9.1 0.1 reduce_sum.52
  9.3 0.7 fusion.54
  11.9 0.8 %broadcast_select_fusion.3 = (bf16[1,128,768]{2,1,0:T(8,128)(2,1)S(1)}, bf16[1,128,768]{2,1,0:T(8,128)(2,1)S(1)}, bf16[1,128,768]{2,1,0:T(8,128)(2,1)S(1)}, bf16[1,128,768]{2,1,0:T(8,128)(2,1)}, bf16[1,128,768]{2,1,0:T(8,128)(2,1)}) fusion(pred[]{:T(512)} %bitcast.19, bf16[1,128,384]{2,1,0:T(8,128)(2,1)S(1)} %bitcast.72, ...), kind=kLoop, calls=%fused_computation.51 | loop fusion | flops 1081344 | bytes 1376259 | tf_op jit(solution)/shard_map/jit(_where)/select_n | solution.py:127
  12.7 2.9 %collective-permute-start = (bf16[1,128,768]{2,1,0:T(8,128)(2,1)S(1)}, bf16[1,128,768]{2,1,0:T(8,128)(2,1)S(1)}, u32[]{:S(2)}, u32[]{:S(2)}) collective-permute-start(bf16[1,128,768]{2,1,0:T(8,128)(2,1)S(1)} %get-tuple-element.109), channel_id=1, source_target_pairs={{0,1},{1,2},{2,3},{3,0},{4,5},{5,6},{6,7},{7,4},{8,9},{9,10},{10,1... | collective-permute-start | bytes 589832 | tf_op jit(solution)/shard_map/ppermute | solution.py:148
  15.6 1.6 %collective-permute-start.1 = (bf16[1,128,768]{2,1,0:T(8,128)(2,1)S(1)}, bf16[1,128,768]{2,1,0:T(8,128)(2,1)S(1)}, u32[]{:S(2)}, u32[]{:S(2)}) collective-permute-start(bf16[1,128,768]{2,1,0:T(8,128)(2,1)S(1)} %get-tuple-element.110), channel_id=1, source_target_pairs={{0,2},{1,3},{2,0},{3,1},{4,6},{5,7},{6,4},{7,5},{8,10},{9,11},{10,... | collective-permute-start | bytes 589832 | tf_op jit(solution)/shard_map/ppermute | solution.py:148
  17.2 1.4 %collective-permute-start.2 = (bf16[1,128,768]{2,1,0:T(8,128)(2,1)S(1)}, bf16[1,128,768]{2,1,0:T(8,128)(2,1)S(1)}, u32[]{:S(2)}, u32[]{:S(2)}) collective-permute-start(bf16[1,128,768]{2,1,0:T(8,128)(2,1)S(1)} %get-tuple-element.108), channel_id=1, source_target_pairs={{0,3},{1,0},{2,1},{3,2},{4,7},{5,4},{6,5},{7,6},{8,11},{9,8},{10,9... | collective-permute-start | bytes 589832 | tf_op jit(solution)/shard_map/ppermute | solution.py:148
  18.7 2.6 %collective-permute-start.3 = (bf16[1,128,768]{2,1,0:T(8,128)(2,1)}, bf16[1,128,768]{2,1,0:T(8,128)(2,1)S(1)}, u32[]{:S(2)}, u32[]{:S(2)}) collective-permute-start(bf16[1,128,768]{2,1,0:T(8,128)(2,1)} %get-tuple-element.112), channel_id=1, source_target_pairs={{0,4},{1,5},{2,6},{3,7},{4,0},{5,1},{6,2},{7,3},{8,12},{9,13},{10,... | collective-permute-start | bytes 589832 | tf_op jit(solution)/shard_map/ppermute | solution.py:137
  21.2 0.3 collective-permute-start.4
  24.8 0.1 constant_dynamic-slice_fusion
  24.9 0.1 copy.8
  25.0 0.1 reshape.468
  25.0 0.8 %fusion.41 = (f32[4,384]{1,0:T(4,128)}, f32[4,384]{1,0:T(4,128)}, f32[4,384]{1,0:T(4,128)}, f32[4,384]{1,0:T(4,128)}) fusion(s32[384]{0:T(512)S(1)} %iota_add_fusion, s32[4]{0:T(128)S(1)} %get-tuple-element.137, s32[4]{0:T(128)S(1)} %get-tuple-element.138), kind=kLoop, calls=%fused_computation.77 | loop fusion | flops 27648 | bytes 26144 | tf_op jit(solution)/shard_map/sin | solution.py:20
  25.9 0.6 fusion.49.index_ref
  26.5 4.6 %collective-permute-done.3 = bf16[1,128,768]{2,1,0:T(8,128)(2,1)S(1)} collective-permute-done((bf16[1,128,768]{2,1,0:T(8,128)(2,1)}, bf16[1,128,768]{2,1,0:T(8,128)(2,1)S(1)}, u32[]{:S(2)}, u32[]{:S(2)}) %collective-permute-start.3) | collective-permute-done | bytes 196640 | tf_op jit(solution)/shard_map/ppermute | solution.py:137
  31.1 7.2 %collective-permute-done.4 = bf16[1,128,768]{2,1,0:T(8,128)(2,1)S(1)} collective-permute-done((bf16[1,128,768]{2,1,0:T(8,128)(2,1)}, bf16[1,128,768]{2,1,0:T(8,128)(2,1)S(1)}, u32[]{:S(2)}, u32[]{:S(2)}) %collective-permute-start.4) | collective-permute-done | bytes 196640 | tf_op jit(solution)/shard_map/ppermute | solution.py:137
  38.4 0.6 collective-permute-start.5
  39.0 0.0 collective-permute-start.6
  39.0 2.3 %collective-permute-start.7 = (bf16[1,128,768]{2,1,0:T(8,128)(2,1)S(1)}, bf16[1,128,768]{2,1,0:T(8,128)(2,1)S(1)}, u32[]{:S(2)}, u32[]{:S(2)}) collective-permute-start(bf16[1,128,768]{2,1,0:T(8,128)(2,1)S(1)} %get-tuple-element.105), channel_id=1, source_target_pairs={{0,3},{1,0},{2,1},{3,2},{4,7},{5,4},{6,5},{7,6},{8,11},{9,8},{10,9... | collective-permute-start | bytes 589832 | tf_op jit(solution)/shard_map/ppermute | solution.py:149
  41.5 0.1 bitcast_dynamic-update-slice_fusion.3
  41.5 3.6 %collective-permute-done.5 = bf16[1,128,768]{2,1,0:T(8,128)(2,1)S(1)} collective-permute-done((bf16[1,128,768]{2,1,0:T(8,128)(2,1)S(1)}, bf16[1,128,768]{2,1,0:T(8,128)(2,1)S(1)}, u32[]{:S(2)}, u32[]{:S(2)}) %collective-permute-start.5) | collective-permute-done | bytes 196640 | tf_op jit(solution)/shard_map/ppermute | solution.py:149
  45.2 2.0 %collective-permute-done.7 = bf16[1,128,768]{2,1,0:T(8,128)(2,1)S(1)} collective-permute-done((bf16[1,128,768]{2,1,0:T(8,128)(2,1)S(1)}, bf16[1,128,768]{2,1,0:T(8,128)(2,1)S(1)}, u32[]{:S(2)}, u32[]{:S(2)}) %collective-permute-start.7) | collective-permute-done | bytes 196640 | tf_op jit(solution)/shard_map/ppermute | solution.py:149
  47.1 1.1 %copy-done = bf16[8,1,128,768]{3,2,1,0:T(8,128)(2,1)} copy-done((bf16[8,1,128,768]{3,2,1,0:T(8,128)(2,1)}, bf16[8,1,128,768]{3,2,1,0:T(8,128)(2,1)S(1)}, u32[]{:S(2)}) %copy-start) | copy-done | bytes 1572888
  48.3 6.9 %shard_map.37 = bf16[2,16,32,512]{3,2,1,0:T(8,128)(2,1)} custom-call(s32[8]{0:T(128)} %fusion.49.index_ref, f32[4,384]{1,0:T(4,128)} %get-tuple-element.119.cc_ref, f32[4,384]{1,0:T(4,128)} %get-tuple-element.120.sc_ref, f32[4,384]{1,0:T(4,128)} %get-tuple-element.114.cf_ref, f32[4,384]{1,0:T(4,128)} %get-tuple-element.113.sf_ref, ...), custom_call_target="tpu_custom_call" | custom-call | flops 805306368 | bytes 2621440 | tf_op jit(solution)/shard_map/pallas_call | solution.py:107
  55.2 1.1 %slice_bitcast_fusion.2 = bf16[16,32,512]{2,1,0:T(8,128)(2,1)S(1)} fusion(bf16[2,16,32,512]{3,2,1,0:T(8,128)(2,1)} %shard_map.37), kind=kLoop, calls=%fused_computation.20 | loop fusion | bytes 1048576 | tf_op jit(solution)/shard_map/squeeze | solution.py:213
  56.3 0.1 collective-permute-start.8
  56.4 1.9 %collective-permute-done.8 = bf16[16,32,512]{2,1,0:T(8,128)(2,1)S(1)} collective-permute-done((bf16[16,32,512]{2,1,0:T(8,128)(2,1)S(1)}, bf16[16,32,512]{2,1,0:T(8,128)(2,1)S(1)}, u32[]{:S(2)}, u32[]{:S(2)}) %collective-permute-start.8) | collective-permute-done | bytes 524320 | tf_op jit(solution)/shard_map/ppermute | solution.py:213
  58.3 1.2 %fusion.13 = bf16[16,32,512]{2,1,0:T(8,128)(2,1)S(1)} fusion(bf16[16,32,512]{2,1,0:T(8,128)(2,1)S(1)} %collective-permute-done.8, bf16[2,16,32,512]{3,2,1,0:T(8,128)(2,1)} %shard_map.37), kind=kLoop, calls=%fused_computation.14 | loop fusion | flops 1048576 | bytes 1572864 | tf_op jit(solution)/shard_map/convert_element_type | solution.py:214
  59.5 1.6 %collective-permute-start.10 = (bf16[16,32,512]{2,1,0:T(8,128)(2,1)S(1)}, bf16[16,32,512]{2,1,0:T(8,128)(2,1)S(1)}, u32[]{:S(2)}, u32[]{:S(2)}) collective-permute-start(bf16[16,32,512]{2,1,0:T(8,128)(2,1)S(1)} %fusion.13), channel_id=1, source_target_pairs={{0,16},{8,24},{16,0},{24,8},{1,17},{9,25},{17,1},{25,9},{2,18},{10... | collective-permute-start | bytes 1572872 | tf_op jit(solution)/shard_map/ppermute | solution.py:217
  61.1 6.8 %shard_map.38 = bf16[2,16,32,512]{3,2,1,0:T(8,128)(2,1)} custom-call(s32[8]{0:T(128)} %fusion.49.index_ref, f32[4,384]{1,0:T(4,128)} %get-tuple-element.119.cc_ref, f32[4,384]{1,0:T(4,128)} %get-tuple-element.120.sc_ref, f32[4,384]{1,0:T(4,128)} %get-tuple-element.114.cf_ref, f32[4,384]{1,0:T(4,128)} %get-tuple-element.113.sf_ref, ...), custom_call_target="tpu_custom_call" | custom-call | flops 8053063 | bytes 26214 | tf_op jit(solution)/shard_map/pallas_call | solution.py:107
  67.9 1.1 %slice_bitcast_fusion = bf16[16,32,512]{2,1,0:T(8,128)(2,1)S(1)} fusion(bf16[2,16,32,512]{3,2,1,0:T(8,128)(2,1)} %shard_map.38), kind=kLoop, calls=%fused_computation.18 | loop fusion | bytes 1048576 | tf_op jit(solution)/shard_map/squeeze | solution.py:218
  68.9 0.1 collective-permute-start.9
  69.0 4.5 %collective-permute-done.10 = bf16[16,32,512]{2,1,0:T(8,128)(2,1)S(1)} collective-permute-done((bf16[16,32,512]{2,1,0:T(8,128)(2,1)S(1)}, bf16[16,32,512]{2,1,0:T(8,128)(2,1)S(1)}, u32[]{:S(2)}, u32[]{:S(2)}) %collective-permute-start.10) | collective-permute-done | bytes 524320 | tf_op jit(solution)/shard_map/ppermute | solution.py:217
  73.5 1.3 %fusion.12 = f32[16,32,512]{2,1,0:T(8,128)S(1)} fusion(bf16[16,32,512]{2,1,0:T(8,128)(2,1)S(1)} %collective-permute-done.10, bf16[16,32,512]{2,1,0:T(8,128)(2,1)S(1)} %collective-permute-done.9, bf16[2,16,32,512]{3,2,1,0:T(8,128)(2,1)} %shard_map.38), kind=kLoop, calls=%fused_computation.12 | loop fusion | flops 1310720 | bytes 2621440 | tf_op jit(solution)/shard_map/add | solution.py:219
  74.8 0.4 reshape.471
  75.2 1.7 %fusion.15 = f32[32,4,16,128]{3,2,1,0:T(8,128)} fusion(f32[16,32,4,128]{3,2,1,0:T(4,128)S(1)} %reshape.471, f32[4]{0:T(128)S(1)} %convert_element_type.143), kind=kLoop, calls=%fused_computation.17 | loop fusion | flops 524288 | bytes 2097168 | tf_op jit(solution)/shard_map/div | solution.py:226
  (25 shorter events, 0.3 us)
Async XLA Ops:
  1.3 3.5 %copy-start.2 = (bf16[1,256,7680]{2,1,0:T(8,128)(2,1)S(1)}, bf16[1,256,7680]{2,1,0:T(8,128)(2,1)}, u32[]{:S(2)}) copy-start(bf16[1,256,7680]{2,1,0:T(8,128)(2,1)} %param.3) | copy-start | bytes 11796484
  6.5 2.3 %copy-start.1 = (s32[32,2]{0,1:T(2,128)S(1)}, s32[32,2]{0,1:T(2,128)}, u32[]{:S(2)}) copy-start(s32[32,2]{0,1:T(2,128)} %param.4) | copy-start | bytes 772
  12.7 26.3 %collective-permute-start = (bf16[1,128,768]{2,1,0:T(8,128)(2,1)S(1)}, bf16[1,128,768]{2,1,0:T(8,128)(2,1)S(1)}, u32[]{:S(2)}, u32[]{:S(2)}) collective-permute-start(bf16[1,128,768]{2,1,0:T(8,128)(2,1)S(1)} %get-tuple-element.109), channel_id=1, source_target_pairs={{0,1},{1,2},{2,3},{3,0},{4,5},{5,6},{6,7},{7,4},{8,9},{9,10},{10,1... | collective-permute-start | bytes 589832 | tf_op jit(solution)/shard_map/ppermute | solution.py:148
  15.6 25.8 %collective-permute-start.1 = (bf16[1,128,768]{2,1,0:T(8,128)(2,1)S(1)}, bf16[1,128,768]{2,1,0:T(8,128)(2,1)S(1)}, u32[]{:S(2)}, u32[]{:S(2)}) collective-permute-start(bf16[1,128,768]{2,1,0:T(8,128)(2,1)S(1)} %get-tuple-element.110), channel_id=1, source_target_pairs={{0,2},{1,3},{2,0},{3,1},{4,6},{5,7},{6,4},{7,5},{8,10},{9,11},{10,... | collective-permute-start | bytes 589832 | tf_op jit(solution)/shard_map/ppermute | solution.py:148
  17.2 24.2 %collective-permute-start.2 = (bf16[1,128,768]{2,1,0:T(8,128)(2,1)S(1)}, bf16[1,128,768]{2,1,0:T(8,128)(2,1)S(1)}, u32[]{:S(2)}, u32[]{:S(2)}) collective-permute-start(bf16[1,128,768]{2,1,0:T(8,128)(2,1)S(1)} %get-tuple-element.108), channel_id=1, source_target_pairs={{0,3},{1,0},{2,1},{3,2},{4,7},{5,4},{6,5},{7,6},{8,11},{9,8},{10,9... | collective-permute-start | bytes 589832 | tf_op jit(solution)/shard_map/ppermute | solution.py:148
  18.7 12.5 %collective-permute-start.3 = (bf16[1,128,768]{2,1,0:T(8,128)(2,1)}, bf16[1,128,768]{2,1,0:T(8,128)(2,1)S(1)}, u32[]{:S(2)}, u32[]{:S(2)}) collective-permute-start(bf16[1,128,768]{2,1,0:T(8,128)(2,1)} %get-tuple-element.112), channel_id=1, source_target_pairs={{0,4},{1,5},{2,6},{3,7},{4,0},{5,1},{6,2},{7,3},{8,12},{9,13},{10,... | collective-permute-start | bytes 589832 | tf_op jit(solution)/shard_map/ppermute | solution.py:137
  21.2 17.1 %collective-permute-start.4 = (bf16[1,128,768]{2,1,0:T(8,128)(2,1)}, bf16[1,128,768]{2,1,0:T(8,128)(2,1)S(1)}, u32[]{:S(2)}, u32[]{:S(2)}) collective-permute-start(bf16[1,128,768]{2,1,0:T(8,128)(2,1)} %get-tuple-element.111), channel_id=1, source_target_pairs={{0,4},{1,5},{2,6},{3,7},{4,0},{5,1},{6,2},{7,3},{8,12},{9,13},{10,... | collective-permute-start | bytes 589832 | tf_op jit(solution)/shard_map/ppermute | solution.py:137
  38.4 6.7 %collective-permute-start.5 = (bf16[1,128,768]{2,1,0:T(8,128)(2,1)S(1)}, bf16[1,128,768]{2,1,0:T(8,128)(2,1)S(1)}, u32[]{:S(2)}, u32[]{:S(2)}) collective-permute-start(bf16[1,128,768]{2,1,0:T(8,128)(2,1)S(1)} %get-tuple-element.107), channel_id=1, source_target_pairs={{0,1},{1,2},{2,3},{3,0},{4,5},{5,6},{6,7},{7,4},{8,9},{9,10},{10,1... | collective-permute-start | bytes 589832 | tf_op jit(solution)/shard_map/ppermute | solution.py:149
  39.0 6.1 %collective-permute-start.6 = (bf16[1,128,768]{2,1,0:T(8,128)(2,1)S(1)}, bf16[1,128,768]{2,1,0:T(8,128)(2,1)S(1)}, u32[]{:S(2)}, u32[]{:S(2)}) collective-permute-start(bf16[1,128,768]{2,1,0:T(8,128)(2,1)S(1)} %get-tuple-element.106), channel_id=1, source_target_pairs={{0,2},{1,3},{2,0},{3,1},{4,6},{5,7},{6,4},{7,5},{8,10},{9,11},{10,... | collective-permute-start | bytes 589832 | tf_op jit(solution)/shard_map/ppermute | solution.py:149
  39.0 8.1 %collective-permute-start.7 = (bf16[1,128,768]{2,1,0:T(8,128)(2,1)S(1)}, bf16[1,128,768]{2,1,0:T(8,128)(2,1)S(1)}, u32[]{:S(2)}, u32[]{:S(2)}) collective-permute-start(bf16[1,128,768]{2,1,0:T(8,128)(2,1)S(1)} %get-tuple-element.105), channel_id=1, source_target_pairs={{0,3},{1,0},{2,1},{3,2},{4,7},{5,4},{6,5},{7,6},{8,11},{9,8},{10,9... | collective-permute-start | bytes 589832 | tf_op jit(solution)/shard_map/ppermute | solution.py:149
  47.1 1.1 %copy-start = (bf16[8,1,128,768]{3,2,1,0:T(8,128)(2,1)}, bf16[8,1,128,768]{3,2,1,0:T(8,128)(2,1)S(1)}, u32[]{:S(2)}) copy-start(bf16[8,1,128,768]{3,2,1,0:T(8,128)(2,1)S(1)} %bitcast_dynamic-update-slice_fusion.left_ref.right_ref) | copy-start | bytes 4718596
  48.3 20.7 %copy-start.3 = (s32[4]{0:T(128)S(1)}, s32[4]{0:T(128)}, u32[]{:S(2)}) copy-start(s32[4]{0:T(128)} %param.5) | copy-start | bytes 52
  56.3 2.0 %collective-permute-start.8 = (bf16[16,32,512]{2,1,0:T(8,128)(2,1)S(1)}, bf16[16,32,512]{2,1,0:T(8,128)(2,1)S(1)}, u32[]{:S(2)}, u32[]{:S(2)}) collective-permute-start(bf16[16,32,512]{2,1,0:T(8,128)(2,1)S(1)} %slice_bitcast_fusion.2), channel_id=1, source_target_pairs={{0,8},{8,0},{16,24},{24,16},{1,9},{9,1},{17,25},{25,17},{2,10},{10... | collective-permute-start | bytes 1572872 | tf_op jit(solution)/shard_map/ppermute | solution.py:213
  59.5 14.0 %collective-permute-start.10 = (bf16[16,32,512]{2,1,0:T(8,128)(2,1)S(1)}, bf16[16,32,512]{2,1,0:T(8,128)(2,1)S(1)}, u32[]{:S(2)}, u32[]{:S(2)}) collective-permute-start(bf16[16,32,512]{2,1,0:T(8,128)(2,1)S(1)} %fusion.13), channel_id=1, source_target_pairs={{0,16},{8,24},{16,0},{24,8},{1,17},{9,25},{17,1},{25,9},{2,18},{10... | collective-permute-start | bytes 1572872 | tf_op jit(solution)/shard_map/ppermute | solution.py:217
  68.9 4.6 %collective-permute-start.9 = (bf16[16,32,512]{2,1,0:T(8,128)(2,1)S(1)}, bf16[16,32,512]{2,1,0:T(8,128)(2,1)S(1)}, u32[]{:S(2)}, u32[]{:S(2)}) collective-permute-start(bf16[16,32,512]{2,1,0:T(8,128)(2,1)S(1)} %slice_bitcast_fusion), channel_id=1, source_target_pairs={{0,8},{8,0},{16,24},{24,16},{1,9},{9,1},{17,25},{25,17},{2,10},{10... | collective-permute-start | bytes 1572872 | tf_op jit(solution)/shard_map/ppermute | solution.py:218

commit v12 on v10

--- a/solution.py
+++ b/solution.py
@@ -62,25 +62,24 @@
             s = sf_ref[l1 : l1 + 1, :]
             turned.append(jnp.concatenate([rre * c + rim * s, rim * c - rre * s], axis=1).astype(jnp.bfloat16))
         right_all = jnp.concatenate(turned, axis=0)
-        parts = []
+        lefts = []
         for l2 in range(LAGS // sub):
             if l2 * sub == LAGS // 2:
-                left_t = left.astype(jnp.bfloat16)
+                lefts.append(left.astype(jnp.bfloat16))
             else:
                 c = cc_ref[l2 : l2 + 1, :]
                 s = sc_ref[l2 : l2 + 1, :]
-                left_t = jnp.concatenate([lre * c - lim * s, lre * s + lim * c], axis=1).astype(jnp.bfloat16)
-            parts.append(
-                lax.dot_general(left_t, right_all, (((1,), (1,)), ((), ())), preferred_element_type=jnp.float32)
-            )
-        acc = parts if acc is None else [a + p for a, p in zip(acc, parts)]
+                lefts.append(jnp.concatenate([lre * c - lim * s, lre * s + lim * c], axis=1).astype(jnp.bfloat16))
+        res = lax.dot_general(
+            jnp.concatenate(lefts, axis=0), right_all, (((1,), (1,)), ((), ())), preferred_element_type=jnp.float32
+        )
+        acc = res if acc is None else acc + res
     half_rows = C // 2
-    for l2, res in enumerate(acc):
+    for l2 in range(LAGS // sub):
         for l1 in range(sub):
             for part in range(2):
-                out_ref[part, l2 * sub + l1] = res[part * half_rows : (part + 1) * half_rows, l1 * C : (l1 + 1) * C].astype(
-                    out_ref.dtype
-                )
+                rows = l2 * C + part * half_rows
+                out_ref[part, l2 * sub + l1] = acc[rows : rows + half_rows, l1 * C : (l1 + 1) * C].astype(out_ref.dtype)
 
 
 def tile_correlation(cc, sc, cf, sf, incoming, slots, sub, n_y, own_rows):

time: 75.8 us -> 74.3 us (0.980)
  Pallas kernels: 7.22 us -> 5.73 us
    pallas_call x1, Pallas kernels: 7.22 us -> 5.73 us  [tile_correlation(): pl.pallas_call(functools.partial(correlation_kernel, sub, n_y, own_rows),...]
where the time goes in v12:
time: 74.3 us; the launch traced here: 73.9 us
  waiting for transfers between devices  30.6 us (41%)
  starting transfers between devices  14 us (19%)
  other arithmetic  9.2 us (12%)
  Pallas kernels  5.73 us (8%)
  local copies, waits for them, and re-layouts  5.68 us (8%)
  between operations  5.38 us (7%)
  matrix products  3.38 us (5%)
    ppermute x1, waiting for transfers between devices, body(): total = total + lax.ppermute(piece, 'win', perm).astype(jnp.float32)  12.7 us
    ppermute x2, waiting for transfers between devices, exchange_by_halves(): lax.ppermute(block, 'pair', across)  7.91 us
    ppermute x3, waiting for transfers between devices, exchange_by_halves(): relay = lax.ppermute(relay, 'pair', perm)  7.37 us
    pallas_call x1, Pallas kernels, tile_correlation(): pl.pallas_call(functools.partial(correlation_kernel, sub, n_y, own_rows),...  5.73 us
    ppermute x3, starting transfers between devices, exchange_by_halves(): own = lax.ppermute(own, 'pair', perm)  4.76 us
    ppermute x2, starting transfers between devices, exchange_by_halves(): lax.ppermute(block, 'pair', across)  4.18 us
    another operation x3, other arithmetic  3.72 us
    ppermute x3, starting transfers between devices, exchange_by_halves(): relay = lax.ppermute(relay, 'pair', perm)  3.64 us
  transfers between devices with their start and end apart: 10, of which 7 were waited for; matrix products, arithmetic and copies ran while one was open for 2% of the time, Pallas kernels for 0%

profile of v12, /device:TPU:0, one launch (start us, length us, event | category | flops | bytes accessed | tf_op | source)
XLA Modules:
  0.0 73.9 jit_solution(3015757346902084364)
XLA Ops:
  0.0 0.8 %fusion.19 = (f32[128,384]{1,0:T(8,128)S(1)}, f32[128,384]{1,0:T(8,128)S(1)}) fusion(s32[384]{0:T(512)S(1)} %iota_add_fusion), kind=kLoop, calls=%fused_computation.41 | loop fusion | flops 442368 | bytes 394752 | tf_op jit(solution)/shard_map/cos | solution.py:20
  0.8 0.5 fusion.26
  1.3 0.0 copy-start.2
  1.3 3.5 %subtract_convert_fusion = (bf16[60,128,384]{2,1,0:T(8,128)(2,1)S(1)}, bf16[60,128,384]{2,1,0:T(8,128)(2,1)S(1)}) fusion(f32[128,384]{1,0:T(8,128)S(1)} %get-tuple-element.160, f32[60,384]{1,0:T(8,128)S(1)} %get-tuple-element.154, f32[128,384]{1,0:T(8,128)S(1)} %get-tuple-element.159, f32[60,384]{1,0:T(8,128)S(1)} %get-tuple-element.153), kind=kLoop, calls=%fused_computation.2 | loop fusion | flops 26542080 | bytes 12374016 | tf_op jit(solution)/shard_map/convert.19
  4.8 1.7 %fusion.6 = f32[128,768]{1,0:T(8,128)S(1)} fusion(bf16[7680,384]{1,0:T(8,128)(2,1)S(1)} %bitcast.66, bf16[7680,384]{1,0:T(8,128)(2,1)S(1)} %bitcast.64, bf16[1,256,7680]{2,1,0:T(8,128)(2,1)S(1)} %copy-done.2), kind=kOutput, calls=%fused_computation.10 | convolution fusion | flops 1533542400 | bytes 14155776 | tf_op jit(solution)/shard_map/dot_general | solution.py:36
  6.5 0.0 copy-start.1
  6.5 1.7 %fusion.9 = f32[128,768]{1,0:T(8,128)S(1)} fusion(bf16[7680,384]{1,0:T(8,128)(2,1)S(1)} %bitcast.67, bf16[7680,384]{1,0:T(8,128)(2,1)S(1)} %bitcast.65, bf16[1,256,7680]{2,1,0:T(8,128)(2,1)S(1)} %copy-done.2), kind=kOutput, calls=%fused_computation.11 | convolution fusion | flops 1533542400 | bytes 14155776 | tf_op jit(solution)/shard_map/dot_general | solution.py:36
  8.3 0.1 reduce_sum.43
  8.4 0.1 reduce_sum.52
  8.5 0.1 reduce_sum.56
  8.6 0.1 reduce_sum.57
  8.7 0.7 fusion.51
  11.2 0.2 fusion.49
  11.5 0.1 divide_convert_fusion.1
  11.6 0.1 divide_convert_fusion.3
  11.7 0.1 broadcast_select_fusion.3
  11.8 4.1 %collective-permute-start.3 = (bf16[1,128,768]{2,1,0:T(8,128)(2,1)S(1)}, bf16[1,128,768]{2,1,0:T(8,128)(2,1)S(1)}, u32[]{:S(2)}, u32[]{:S(2)}) collective-permute-start(bf16[1,128,768]{2,1,0:T(8,128)(2,1)S(1)} %get-tuple-element.152), channel_id=1, source_target_pairs={{0,4},{1,5},{2,6},{3,7},{4,0},{5,1},{6,2},{7,3},{8,12},{9,13},{10,... | collective-permute-start | bytes 589832 | tf_op jit(solution)/shard_map/ppermute | solution.py:126
  15.9 0.1 collective-permute-start.4
  16.0 1.7 %collective-permute-start = (bf16[1,128,768]{2,1,0:T(8,128)(2,1)S(1)}, bf16[1,128,768]{2,1,0:T(8,128)(2,1)S(1)}, u32[]{:S(2)}, u32[]{:S(2)}) collective-permute-start(bf16[1,128,768]{2,1,0:T(8,128)(2,1)S(1)} %get-tuple-element.149), channel_id=1, source_target_pairs={{0,1},{1,2},{2,3},{3,0},{4,5},{5,6},{6,7},{7,4},{8,9},{9,10},{10,1... | collective-permute-start | bytes 589832 | tf_op jit(solution)/shard_map/ppermute | solution.py:137
  17.8 1.6 %collective-permute-start.1 = (bf16[1,128,768]{2,1,0:T(8,128)(2,1)S(1)}, bf16[1,128,768]{2,1,0:T(8,128)(2,1)S(1)}, u32[]{:S(2)}, u32[]{:S(2)}) collective-permute-start(bf16[1,128,768]{2,1,0:T(8,128)(2,1)S(1)} %get-tuple-element.150), channel_id=1, source_target_pairs={{0,2},{1,3},{2,0},{3,1},{4,6},{5,7},{6,4},{7,5},{8,10},{9,11},{10,... | collective-permute-start | bytes 589832 | tf_op jit(solution)/shard_map/ppermute | solution.py:137
  19.3 1.4 %collective-permute-start.2 = (bf16[1,128,768]{2,1,0:T(8,128)(2,1)S(1)}, bf16[1,128,768]{2,1,0:T(8,128)(2,1)S(1)}, u32[]{:S(2)}, u32[]{:S(2)}) collective-permute-start(bf16[1,128,768]{2,1,0:T(8,128)(2,1)S(1)} %get-tuple-element.148), channel_id=1, source_target_pairs={{0,3},{1,0},{2,1},{3,2},{4,7},{5,4},{6,5},{7,6},{8,11},{9,8},{10,9... | collective-permute-start | bytes 589832 | tf_op jit(solution)/shard_map/ppermute | solution.py:137
  24.0 0.1 constant_dynamic-slice_fusion
  24.1 0.1 copy.7
  24.2 0.1 reshape.467
  24.3 0.8 %fusion.38 = (f32[4,384]{1,0:T(4,128)}, f32[4,384]{1,0:T(4,128)}, f32[4,384]{1,0:T(4,128)}, f32[4,384]{1,0:T(4,128)}) fusion(s32[384]{0:T(512)S(1)} %iota_add_fusion, s32[4]{0:T(128)S(1)} %get-tuple-element.175, s32[4]{0:T(128)S(1)} %get-tuple-element.176), kind=kLoop, calls=%fused_computation.72 | loop fusion | flops 27648 | bytes 26144 | tf_op jit(solution)/shard_map/sin | solution.py:20
  25.1 0.6 fusion.46.index_ref
  25.7 4.5 %collective-permute-done.3 = bf16[1,128,768]{2,1,0:T(8,128)(2,1)S(1)} collective-permute-done((bf16[1,128,768]{2,1,0:T(8,128)(2,1)S(1)}, bf16[1,128,768]{2,1,0:T(8,128)(2,1)S(1)}, u32[]{:S(2)}, u32[]{:S(2)}) %collective-permute-start.3) | collective-permute-done | bytes 196640 | tf_op jit(solution)/shard_map/ppermute | solution.py:126
  30.2 3.4 %collective-permute-done.4 = bf16[1,128,768]{2,1,0:T(8,128)(2,1)S(1)} collective-permute-done((bf16[1,128,768]{2,1,0:T(8,128)(2,1)S(1)}, bf16[1,128,768]{2,1,0:T(8,128)(2,1)S(1)}, u32[]{:S(2)}, u32[]{:S(2)}) %collective-permute-start.4) | collective-permute-done | bytes 196640 | tf_op jit(solution)/shard_map/ppermute | solution.py:126
  33.6 1.6 %collective-permute-start.5 = (bf16[1,128,768]{2,1,0:T(8,128)(2,1)S(1)}, bf16[1,128,768]{2,1,0:T(8,128)(2,1)S(1)}, u32[]{:S(2)}, u32[]{:S(2)}) collective-permute-start(bf16[1,128,768]{2,1,0:T(8,128)(2,1)S(1)} %get-tuple-element.147), channel_id=1, source_target_pairs={{0,1},{1,2},{2,3},{3,0},{4,5},{5,6},{6,7},{7,4},{8,9},{9,10},{10,1... | collective-permute-start | bytes 589832 | tf_op jit(solution)/shard_map/ppermute | solution.py:138
  35.2 0.6 collective-permute-start.6
  35.8 1.4 %collective-permute-start.7 = (bf16[1,128,768]{2,1,0:T(8,128)(2,1)S(1)}, bf16[1,128,768]{2,1,0:T(8,128)(2,1)S(1)}, u32[]{:S(2)}, u32[]{:S(2)}) collective-permute-start(bf16[1,128,768]{2,1,0:T(8,128)(2,1)S(1)} %get-tuple-element.145), channel_id=1, source_target_pairs={{0,3},{1,0},{2,1},{3,2},{4,7},{5,4},{6,5},{7,6},{8,11},{9,8},{10,9... | collective-permute-start | bytes 589832 | tf_op jit(solution)/shard_map/ppermute | solution.py:138
  37.3 0.1 bitcast_dynamic-update-slice_fusion.3
  37.4 5.0 %collective-permute-done.5 = bf16[1,128,768]{2,1,0:T(8,128)(2,1)S(1)} collective-permute-done((bf16[1,128,768]{2,1,0:T(8,128)(2,1)S(1)}, bf16[1,128,768]{2,1,0:T(8,128)(2,1)S(1)}, u32[]{:S(2)}, u32[]{:S(2)}) %collective-permute-start.5) | collective-permute-done | bytes 196640 | tf_op jit(solution)/shard_map/ppermute | solution.py:138
  42.4 0.3 collective-permute-done.6
  42.8 2.0 %collective-permute-done.7 = bf16[1,128,768]{2,1,0:T(8,128)(2,1)S(1)} collective-permute-done((bf16[1,128,768]{2,1,0:T(8,128)(2,1)S(1)}, bf16[1,128,768]{2,1,0:T(8,128)(2,1)S(1)}, u32[]{:S(2)}, u32[]{:S(2)}) %collective-permute-start.7) | collective-permute-done | bytes 196640 | tf_op jit(solution)/shard_map/ppermute | solution.py:138
  44.8 1.1 %copy-done = bf16[8,1,128,768]{3,2,1,0:T(8,128)(2,1)} copy-done((bf16[8,1,128,768]{3,2,1,0:T(8,128)(2,1)}, bf16[8,1,128,768]{3,2,1,0:T(8,128)(2,1)S(1)}, u32[]{:S(2)}) %copy-start) | copy-done | bytes 1572888
  46.0 5.7 %shard_map.37 = bf16[2,16,64,512]{3,2,1,0:T(8,128)(2,1)} custom-call(s32[8]{0:T(128)} %fusion.46.index_ref, f32[4,384]{1,0:T(4,128)} %get-tuple-element.161.cc_ref, f32[4,384]{1,0:T(4,128)} %get-tuple-element.162.sc_ref, f32[4,384]{1,0:T(4,128)} %get-tuple-element.156.cf_ref, f32[4,384]{1,0:T(4,128)} %get-tuple-element.155.sf_ref, ...), custom_call_target="tpu_custom_call" | custom-call | flops 1610612736 | bytes 3670016 | tf_op jit(solution)/shard_map/pallas_call | solution.py:98
  51.7 1.3 %dynamic-slice_bitcast_fusion = bf16[16,64,512]{2,1,0:T(8,128)(2,1)S(1)} fusion(bf16[2,16,64,512]{3,2,1,0:T(8,128)(2,1)} %shard_map.37, s32[]{:T(128)S(6)} %sub.53), kind=kLoop, calls=%fused_computation.14 | loop fusion | bytes 2097156 | tf_op jit(solution)/shard_map/jit(_take)/gather | solution.py:188
  53.0 0.1 collective-permute-start.8
  53.1 2.6 %collective-permute-done.8 = bf16[16,64,512]{2,1,0:T(8,128)(2,1)S(1)} collective-permute-done((bf16[16,64,512]{2,1,0:T(8,128)(2,1)S(1)}, bf16[16,64,512]{2,1,0:T(8,128)(2,1)S(1)}, u32[]{:S(2)}, u32[]{:S(2)}) %collective-permute-start.8) | collective-permute-done | bytes 1048608 | tf_op jit(solution)/shard_map/ppermute | solution.py:190
  55.8 1.5 %convert_add_fusion = f32[16,64,512]{2,1,0:T(8,128)S(1)} fusion(bf16[16,64,512]{2,1,0:T(8,128)(2,1)S(1)} %collective-permute-done.8, bf16[2,16,64,512]{3,2,1,0:T(8,128)(2,1)} %shard_map.37, s32[]{:T(128)S(6)} %select_n.243), kind=kLoop, calls=%fused_computation.5 | loop fusion | flops 1572864 | bytes 4194308 | tf_op jit(solution)/shard_map/add | solution.py:191
  57.3 0.1 fusion.12
  57.4 1.3 %collective-permute-start.9 = (bf16[16,32,512]{2,1,0:T(8,128)(2,1)S(1)}, bf16[16,32,512]{2,1,0:T(8,128)(2,1)S(1)}, u32[]{:S(2)}, u32[]{:S(2)}) collective-permute-start(bf16[16,32,512]{2,1,0:T(8,128)(2,1)S(1)} %fusion.12), channel_id=1, source_target_pairs={{0,16},{8,24},{16,0},{24,8},{1,17},{9,25},{17,1},{25,9},{2,18},{10... | collective-permute-start | bytes 1572872 | tf_op jit(solution)/shard_map/ppermute | solution.py:198
  58.8 12.7 %collective-permute-done.9 = bf16[16,32,512]{2,1,0:T(8,128)(2,1)S(1)} collective-permute-done((bf16[16,32,512]{2,1,0:T(8,128)(2,1)S(1)}, bf16[16,32,512]{2,1,0:T(8,128)(2,1)S(1)}, u32[]{:S(2)}, u32[]{:S(2)}) %collective-permute-start.9) | collective-permute-done | bytes 524320 | tf_op jit(solution)/shard_map/ppermute | solution.py:198
  71.4 0.2 bitcast_add_fusion
  71.6 0.4 reshape.471
  72.0 0.4 multiply_bitcast_fusion
  72.4 1.6 %copy.11 = f32[32,4,16,128]{3,2,1,0:T(8,128)} copy(f32[32,4,16,128]{3,1,0,2:T(4,128)S(1)} %multiply_bitcast_fusion) | data formatting | bytes 2097152 | tf_op jit(solution)/shard_map/div | solution.py:202
  (23 shorter events, 0.2 us)
Async XLA Ops:
  1.3 3.5 %copy-start.2 = (bf16[1,256,7680]{2,1,0:T(8,128)(2,1)S(1)}, bf16[1,256,7680]{2,1,0:T(8,128)(2,1)}, u32[]{:S(2)}) copy-start(bf16[1,256,7680]{2,1,0:T(8,128)(2,1)} %param.3) | copy-start | bytes 11796484
  6.5 1.8 %copy-start.1 = (s32[32,2]{0,1:T(2,128)S(1)}, s32[32,2]{0,1:T(2,128)}, u32[]{:S(2)}) copy-start(s32[32,2]{0,1:T(2,128)} %param.4) | copy-start | bytes 772
  11.8 18.4 %collective-permute-start.3 = (bf16[1,128,768]{2,1,0:T(8,128)(2,1)S(1)}, bf16[1,128,768]{2,1,0:T(8,128)(2,1)S(1)}, u32[]{:S(2)}, u32[]{:S(2)}) collective-permute-start(bf16[1,128,768]{2,1,0:T(8,128)(2,1)S(1)} %get-tuple-element.152), channel_id=1, source_target_pairs={{0,4},{1,5},{2,6},{3,7},{4,0},{5,1},{6,2},{7,3},{8,12},{9,13},{10,... | collective-permute-start | bytes 589832 | tf_op jit(solution)/shard_map/ppermute | solution.py:126
  15.9 17.6 %collective-permute-start.4 = (bf16[1,128,768]{2,1,0:T(8,128)(2,1)S(1)}, bf16[1,128,768]{2,1,0:T(8,128)(2,1)S(1)}, u32[]{:S(2)}, u32[]{:S(2)}) collective-permute-start(bf16[1,128,768]{2,1,0:T(8,128)(2,1)S(1)} %get-tuple-element.151), channel_id=1, source_target_pairs={{0,4},{1,5},{2,6},{3,7},{4,0},{5,1},{6,2},{7,3},{8,12},{9,13},{10,... | collective-permute-start | bytes 589832 | tf_op jit(solution)/shard_map/ppermute | solution.py:126
  16.0 19.8 %collective-permute-start = (bf16[1,128,768]{2,1,0:T(8,128)(2,1)S(1)}, bf16[1,128,768]{2,1,0:T(8,128)(2,1)S(1)}, u32[]{:S(2)}, u32[]{:S(2)}) collective-permute-start(bf16[1,128,768]{2,1,0:T(8,128)(2,1)S(1)} %get-tuple-element.149), channel_id=1, source_target_pairs={{0,1},{1,2},{2,3},{3,0},{4,5},{5,6},{6,7},{7,4},{8,9},{9,10},{10,1... | collective-permute-start | bytes 589832 | tf_op jit(solution)/shard_map/ppermute | solution.py:137
  17.8 19.5 %collective-permute-start.1 = (bf16[1,128,768]{2,1,0:T(8,128)(2,1)S(1)}, bf16[1,128,768]{2,1,0:T(8,128)(2,1)S(1)}, u32[]{:S(2)}, u32[]{:S(2)}) collective-permute-start(bf16[1,128,768]{2,1,0:T(8,128)(2,1)S(1)} %get-tuple-element.150), channel_id=1, source_target_pairs={{0,2},{1,3},{2,0},{3,1},{4,6},{5,7},{6,4},{7,5},{8,10},{9,11},{10,... | collective-permute-start | bytes 589832 | tf_op jit(solution)/shard_map/ppermute | solution.py:137
  19.3 18.0 %collective-permute-start.2 = (bf16[1,128,768]{2,1,0:T(8,128)(2,1)S(1)}, bf16[1,128,768]{2,1,0:T(8,128)(2,1)S(1)}, u32[]{:S(2)}, u32[]{:S(2)}) collective-permute-start(bf16[1,128,768]{2,1,0:T(8,128)(2,1)S(1)} %get-tuple-element.148), channel_id=1, source_target_pairs={{0,3},{1,0},{2,1},{3,2},{4,7},{5,4},{6,5},{7,6},{8,11},{9,8},{10,9... | collective-permute-start | bytes 589832 | tf_op jit(solution)/shard_map/ppermute | solution.py:137
  33.6 8.8 %collective-permute-start.5 = (bf16[1,128,768]{2,1,0:T(8,128)(2,1)S(1)}, bf16[1,128,768]{2,1,0:T(8,128)(2,1)S(1)}, u32[]{:S(2)}, u32[]{:S(2)}) collective-permute-start(bf16[1,128,768]{2,1,0:T(8,128)(2,1)S(1)} %get-tuple-element.147), channel_id=1, source_target_pairs={{0,1},{1,2},{2,3},{3,0},{4,5},{5,6},{6,7},{7,4},{8,9},{9,10},{10,1... | collective-permute-start | bytes 589832 | tf_op jit(solution)/shard_map/ppermute | solution.py:138
  35.2 7.6 %collective-permute-start.6 = (bf16[1,128,768]{2,1,0:T(8,128)(2,1)S(1)}, bf16[1,128,768]{2,1,0:T(8,128)(2,1)S(1)}, u32[]{:S(2)}, u32[]{:S(2)}) collective-permute-start(bf16[1,128,768]{2,1,0:T(8,128)(2,1)S(1)} %get-tuple-element.146), channel_id=1, source_target_pairs={{0,2},{1,3},{2,0},{3,1},{4,6},{5,7},{6,4},{7,5},{8,10},{9,11},{10,... | collective-permute-start | bytes 589832 | tf_op jit(solution)/shard_map/ppermute | solution.py:138
  35.8 9.0 %collective-permute-start.7 = (bf16[1,128,768]{2,1,0:T(8,128)(2,1)S(1)}, bf16[1,128,768]{2,1,0:T(8,128)(2,1)S(1)}, u32[]{:S(2)}, u32[]{:S(2)}) collective-permute-start(bf16[1,128,768]{2,1,0:T(8,128)(2,1)S(1)} %get-tuple-element.145), channel_id=1, source_target_pairs={{0,3},{1,0},{2,1},{3,2},{4,7},{5,4},{6,5},{7,6},{8,11},{9,8},{10,9... | collective-permute-start | bytes 589832 | tf_op jit(solution)/shard_map/ppermute | solution.py:138
  44.8 1.1 %copy-start = (bf16[8,1,128,768]{3,2,1,0:T(8,128)(2,1)}, bf16[8,1,128,768]{3,2,1,0:T(8,128)(2,1)S(1)}, u32[]{:S(2)}) copy-start(bf16[8,1,128,768]{3,2,1,0:T(8,128)(2,1)S(1)} %bitcast_dynamic-update-slice_fusion.left_ref.right_ref) | copy-start | bytes 4718596
  51.7 7.0 %copy-start.3 = (s32[4]{0:T(128)S(1)}, s32[4]{0:T(128)}, u32[]{:S(2)}) copy-start(s32[4]{0:T(128)} %param.5) | copy-start | bytes 52
  53.0 2.7 %collective-permute-start.8 = (bf16[16,64,512]{2,1,0:T(8,128)(2,1)S(1)}, bf16[16,64,512]{2,1,0:T(8,128)(2,1)S(1)}, u32[]{:S(2)}, u32[]{:S(2)}) collective-permute-start(bf16[16,64,512]{2,1,0:T(8,128)(2,1)S(1)} %dynamic-slice_bitcast_fusion), channel_id=1, source_target_pairs={{0,8},{8,0},{16,24},{24,16},{1,9},{9,1},{17,25},{25,17},{2,10},{10... | collective-permute-start | bytes 3145736 | tf_op jit(solution)/shard_map/ppermute | solution.py:190
  57.4 14.0 %collective-permute-start.9 = (bf16[16,32,512]{2,1,0:T(8,128)(2,1)S(1)}, bf16[16,32,512]{2,1,0:T(8,128)(2,1)S(1)}, u32[]{:S(2)}, u32[]{:S(2)}) collective-permute-start(bf16[16,32,512]{2,1,0:T(8,128)(2,1)S(1)} %fusion.12), channel_id=1, source_target_pairs={{0,16},{8,24},{16,0},{24,8},{1,17},{9,25},{17,1},{25,9},{2,18},{10... | collective-permute-start | bytes 1572872 | tf_op jit(solution)/shard_map/ppermute | solution.py:198

commit v13 on v11

--- a/solution.py
+++ b/solution.py
@@ -70,24 +70,24 @@
             s = sf_ref[l1 : l1 + 1, :]
             turned.append(jnp.concatenate([rre * c + rim * s, rim * c - rre * s], axis=1).astype(jnp.bfloat16))
         right_all = jnp.concatenate(turned, axis=0)
-        parts = []
+        lefts = []
         for l2 in range(LAGS // sub):
             if l2 * sub == LAGS // 2:
-                left_t = left.astype(jnp.bfloat16)
+                lefts.append(left.astype(jnp.bfloat16))
             else:
                 c = cc_ref[l2 : l2 + 1, :]
                 s = sc_ref[l2 : l2 + 1, :]
-                left_t = jnp.concatenate([lre * c - lim * s, lre * s + lim * c], axis=1).astype(jnp.bfloat16)
-            parts.append(
-                lax.dot_general(left_t, right_all, (((1,), (1,)), ((), ())), preferred_element_type=jnp.float32)
-            )
-        acc = parts if acc is None else [a + p for a, p in zip(acc, parts)]
-    for l2, res in enumerate(acc):
+                lefts.append(jnp.concatenate([lre * c - lim * s, lre * s + lim * c], axis=1).astype(jnp.bfloat16))
+        res = lax.dot_general(
+            jnp.concatenate(lefts, axis=0), right_all, (((1,), (1,)), ((), ())), preferred_element_type=jnp.float32
+        )
+        acc = res if acc is None else acc + res
+    block_rows = 2 * part_rows
+    for l2 in range(LAGS // sub):
         for l1 in range(sub):
             for part in range(2):
-                out_ref[part, l2 * sub + l1] = res[part * part_rows : (part + 1) * part_rows, l1 * C : (l1 + 1) * C].astype(
-                    out_ref.dtype
-                )
+                rows = l2 * block_rows + part * part_rows
+                out_ref[part, l2 * sub + l1] = acc[rows : rows + part_rows, l1 * C : (l1 + 1) * C].astype(out_ref.dtype)
 
 
 def tile_correlation(cc, sc, cf, sf, incoming, slots, sub, n_y, own_rows, target=None, weight=1.0):

time: 77.3 us -> 75.6 us (0.978)
  Pallas kernels: 13.7 us -> 10.2 us
  waiting for transfers between devices: 23.8 us -> 25.5 us
    pallas_call x2, Pallas kernels: 13.7 us -> 10.2 us  [tile_correlation(): pl.pallas_call(functools.partial(correlation_kernel, sub, n_y, own_rows,...]
    ppermute x1, waiting for transfers between devices: 4.47 us -> 6.23 us  [body(): across = lax.ppermute(far_sum, 'win', [(w, w ^ 2) for w in range(n_win)])]
  transfers between devices with their start and end apart: 11 -> 11, of which waited for: 6 -> 6; matrix products, arithmetic and copies ran while one was open for 4% -> 4% of each run, Pallas kernels for 9% -> 7%
where the time goes in v13:
time: 75.6 us; the launch traced here: 75.1 us
  waiting for transfers between devices  25.5 us (34%)
  starting transfers between devices  13.6 us (18%)
  other arithmetic  12 us (16%)
  Pallas kernels  10.2 us (13%)
  between operations  5.47 us (7%)
  local copies, waits for them, and re-layouts  4.86 us (6%)
  matrix products  3.38 us (4%)
    ppermute x2, waiting for transfers between devices, exchange_by_halves(): lax.ppermute(block, 'pair', across)  11.8 us
    pallas_call x2, Pallas kernels, tile_correlation(): pl.pallas_call(functools.partial(correlation_kernel, sub, n_y, own_rows,...  10.2 us
    ppermute x1, waiting for transfers between devices, body(): across = lax.ppermute(far_sum, 'win', [(w, w ^ 2) for w in range(n_win)])  6.23 us
    ppermute x3, starting transfers between devices, exchange_by_halves(): own = lax.ppermute(own, 'pair', perm)  5.95 us
    ppermute x3, waiting for transfers between devices, exchange_by_halves(): relay = lax.ppermute(relay, 'pair', perm)  5.55 us
    another operation x3, other arithmetic  3.72 us
    dot_general x2, matrix products, whiten_rows(): spectrum = jnp.dot(strain_rows, table, preferred_element_type=jnp.float32)  3.38 us
    ppermute x3, starting transfers between devices, exchange_by_halves(): relay = lax.ppermute(relay, 'pair', perm)  2.98 us
  transfers between devices with their start and end apart: 11, of which 6 were waited for; matrix products, arithmetic and copies ran while one was open for 4% of the time, Pallas kernels for 7%

profile of v13, /device:TPU:0, one launch (start us, length us, event | category | flops | bytes accessed | tf_op | source)
XLA Modules:
  0.0 75.1 jit_solution(4629826070570231040)
XLA Ops:
  0.0 0.8 %fusion.22 = (f32[128,384]{1,0:T(8,128)S(1)}, f32[128,384]{1,0:T(8,128)S(1)}) fusion(s32[384]{0:T(512)S(1)} %iota_add_fusion), kind=kLoop, calls=%fused_computation.46 | loop fusion | flops 442368 | bytes 394752 | tf_op jit(solution)/shard_map/cos | solution.py:20
  0.8 0.5 fusion.29
  1.3 0.0 copy-start.2
  1.3 3.5 %subtract_convert_fusion = (bf16[60,128,384]{2,1,0:T(8,128)(2,1)S(1)}, bf16[60,128,384]{2,1,0:T(8,128)(2,1)S(1)}) fusion(f32[128,384]{1,0:T(8,128)S(1)} %get-tuple-element.122, f32[60,384]{1,0:T(8,128)S(1)} %get-tuple-element.118, f32[128,384]{1,0:T(8,128)S(1)} %get-tuple-element.121, f32[60,384]{1,0:T(8,128)S(1)} %get-tuple-element.117), kind=kLoop, calls=%fused_computation.2 | loop fusion | flops 26542080 | bytes 12374016 | tf_op jit(solution)/shard_map/convert.21
  4.8 1.7 %fusion.9 = f32[128,768]{1,0:T(8,128)S(1)} fusion(bf16[7680,384]{1,0:T(8,128)(2,1)S(1)} %bitcast.64, bf16[7680,384]{1,0:T(8,128)(2,1)S(1)} %bitcast.62, bf16[1,256,7680]{2,1,0:T(8,128)(2,1)S(1)} %copy-done.2), kind=kOutput, calls=%fused_computation.10 | convolution fusion | flops 1533542400 | bytes 14155776 | tf_op jit(solution)/shard_map/dot_general | solution.py:36
  6.5 0.0 copy-start.1
  6.5 1.7 %fusion.6 = f32[128,768]{1,0:T(8,128)S(1)} fusion(bf16[7680,384]{1,0:T(8,128)(2,1)S(1)} %bitcast.65, bf16[7680,384]{1,0:T(8,128)(2,1)S(1)} %bitcast.63, bf16[1,256,7680]{2,1,0:T(8,128)(2,1)S(1)} %copy-done.2), kind=kOutput, calls=%fused_computation.9 | convolution fusion | flops 1533542400 | bytes 14155776 | tf_op jit(solution)/shard_map/dot_general | solution.py:36
  8.3 0.2 fusion.52
  8.5 0.1 divide_convert_fusion.3
  8.7 0.1 divide_convert_fusion.1
  8.8 0.1 reduce_sum.56
  8.9 0.1 reduce_sum.57
  9.1 0.1 reduce_sum.43
  9.1 0.1 reduce_sum.52
  9.3 0.7 fusion.54
  11.9 0.8 %broadcast_select_fusion.3 = (bf16[1,128,768]{2,1,0:T(8,128)(2,1)S(1)}, bf16[1,128,768]{2,1,0:T(8,128)(2,1)S(1)}, bf16[1,128,768]{2,1,0:T(8,128)(2,1)S(1)}, bf16[1,128,768]{2,1,0:T(8,128)(2,1)}, bf16[1,128,768]{2,1,0:T(8,128)(2,1)}) fusion(pred[]{:T(512)} %bitcast.19, bf16[1,128,384]{2,1,0:T(8,128)(2,1)S(1)} %bitcast.72, ...), kind=kLoop, calls=%fused_computation.51 | loop fusion | flops 1081344 | bytes 1376259 | tf_op jit(solution)/shard_map/jit(_where)/select_n | solution.py:127
  12.7 2.9 %collective-permute-start = (bf16[1,128,768]{2,1,0:T(8,128)(2,1)S(1)}, bf16[1,128,768]{2,1,0:T(8,128)(2,1)S(1)}, u32[]{:S(2)}, u32[]{:S(2)}) collective-permute-start(bf16[1,128,768]{2,1,0:T(8,128)(2,1)S(1)} %get-tuple-element.109), channel_id=1, source_target_pairs={{0,1},{1,2},{2,3},{3,0},{4,5},{5,6},{6,7},{7,4},{8,9},{9,10},{10,1... | collective-permute-start | bytes 589832 | tf_op jit(solution)/shard_map/ppermute | solution.py:148
  15.6 1.6 %collective-permute-start.1 = (bf16[1,128,768]{2,1,0:T(8,128)(2,1)S(1)}, bf16[1,128,768]{2,1,0:T(8,128)(2,1)S(1)}, u32[]{:S(2)}, u32[]{:S(2)}) collective-permute-start(bf16[1,128,768]{2,1,0:T(8,128)(2,1)S(1)} %get-tuple-element.110), channel_id=1, source_target_pairs={{0,2},{1,3},{2,0},{3,1},{4,6},{5,7},{6,4},{7,5},{8,10},{9,11},{10,... | collective-permute-start | bytes 589832 | tf_op jit(solution)/shard_map/ppermute | solution.py:148
  17.2 1.4 %collective-permute-start.2 = (bf16[1,128,768]{2,1,0:T(8,128)(2,1)S(1)}, bf16[1,128,768]{2,1,0:T(8,128)(2,1)S(1)}, u32[]{:S(2)}, u32[]{:S(2)}) collective-permute-start(bf16[1,128,768]{2,1,0:T(8,128)(2,1)S(1)} %get-tuple-element.108), channel_id=1, source_target_pairs={{0,3},{1,0},{2,1},{3,2},{4,7},{5,4},{6,5},{7,6},{8,11},{9,8},{10,9... | collective-permute-start | bytes 589832 | tf_op jit(solution)/shard_map/ppermute | solution.py:148
  18.7 2.6 %collective-permute-start.3 = (bf16[1,128,768]{2,1,0:T(8,128)(2,1)}, bf16[1,128,768]{2,1,0:T(8,128)(2,1)S(1)}, u32[]{:S(2)}, u32[]{:S(2)}) collective-permute-start(bf16[1,128,768]{2,1,0:T(8,128)(2,1)} %get-tuple-element.112), channel_id=1, source_target_pairs={{0,4},{1,5},{2,6},{3,7},{4,0},{5,1},{6,2},{7,3},{8,12},{9,13},{10,... | collective-permute-start | bytes 589832 | tf_op jit(solution)/shard_map/ppermute | solution.py:137
  21.2 0.3 collective-permute-start.4
  24.8 0.1 constant_dynamic-slice_fusion
  24.9 0.1 copy.8
  25.0 0.1 reshape.468
  25.0 0.8 %fusion.41 = (f32[4,384]{1,0:T(4,128)}, f32[4,384]{1,0:T(4,128)}, f32[4,384]{1,0:T(4,128)}, f32[4,384]{1,0:T(4,128)}) fusion(s32[384]{0:T(512)S(1)} %iota_add_fusion, s32[4]{0:T(128)S(1)} %get-tuple-element.137, s32[4]{0:T(128)S(1)} %get-tuple-element.138), kind=kLoop, calls=%fused_computation.77 | loop fusion | flops 27648 | bytes 26144 | tf_op jit(solution)/shard_map/sin | solution.py:20
  25.9 0.6 fusion.49.index_ref
  26.5 4.6 %collective-permute-done.3 = bf16[1,128,768]{2,1,0:T(8,128)(2,1)S(1)} collective-permute-done((bf16[1,128,768]{2,1,0:T(8,128)(2,1)}, bf16[1,128,768]{2,1,0:T(8,128)(2,1)S(1)}, u32[]{:S(2)}, u32[]{:S(2)}) %collective-permute-start.3) | collective-permute-done | bytes 196640 | tf_op jit(solution)/shard_map/ppermute | solution.py:137
  31.1 7.2 %collective-permute-done.4 = bf16[1,128,768]{2,1,0:T(8,128)(2,1)S(1)} collective-permute-done((bf16[1,128,768]{2,1,0:T(8,128)(2,1)}, bf16[1,128,768]{2,1,0:T(8,128)(2,1)S(1)}, u32[]{:S(2)}, u32[]{:S(2)}) %collective-permute-start.4) | collective-permute-done | bytes 196640 | tf_op jit(solution)/shard_map/ppermute | solution.py:137
  38.4 0.6 collective-permute-start.5
  39.0 0.0 collective-permute-start.6
  39.0 2.3 %collective-permute-start.7 = (bf16[1,128,768]{2,1,0:T(8,128)(2,1)S(1)}, bf16[1,128,768]{2,1,0:T(8,128)(2,1)S(1)}, u32[]{:S(2)}, u32[]{:S(2)}) collective-permute-start(bf16[1,128,768]{2,1,0:T(8,128)(2,1)S(1)} %get-tuple-element.105), channel_id=1, source_target_pairs={{0,3},{1,0},{2,1},{3,2},{4,7},{5,4},{6,5},{7,6},{8,11},{9,8},{10,9... | collective-permute-start | bytes 589832 | tf_op jit(solution)/shard_map/ppermute | solution.py:149
  41.5 0.1 bitcast_dynamic-update-slice_fusion.3
  41.5 3.6 %collective-permute-done.5 = bf16[1,128,768]{2,1,0:T(8,128)(2,1)S(1)} collective-permute-done((bf16[1,128,768]{2,1,0:T(8,128)(2,1)S(1)}, bf16[1,128,768]{2,1,0:T(8,128)(2,1)S(1)}, u32[]{:S(2)}, u32[]{:S(2)}) %collective-permute-start.5) | collective-permute-done | bytes 196640 | tf_op jit(solution)/shard_map/ppermute | solution.py:149
  45.2 2.0 %collective-permute-done.7 = bf16[1,128,768]{2,1,0:T(8,128)(2,1)S(1)} collective-permute-done((bf16[1,128,768]{2,1,0:T(8,128)(2,1)S(1)}, bf16[1,128,768]{2,1,0:T(8,128)(2,1)S(1)}, u32[]{:S(2)}, u32[]{:S(2)}) %collective-permute-start.7) | collective-permute-done | bytes 196640 | tf_op jit(solution)/shard_map/ppermute | solution.py:149
  47.1 1.1 %copy-done = bf16[8,1,128,768]{3,2,1,0:T(8,128)(2,1)} copy-done((bf16[8,1,128,768]{3,2,1,0:T(8,128)(2,1)}, bf16[8,1,128,768]{3,2,1,0:T(8,128)(2,1)S(1)}, u32[]{:S(2)}) %copy-start) | copy-done | bytes 1572888
  48.3 5.2 %shard_map.37 = bf16[2,16,32,512]{3,2,1,0:T(8,128)(2,1)} custom-call(s32[8]{0:T(128)} %fusion.49.index_ref, f32[4,384]{1,0:T(4,128)} %get-tuple-element.119.cc_ref, f32[4,384]{1,0:T(4,128)} %get-tuple-element.120.sc_ref, f32[4,384]{1,0:T(4,128)} %get-tuple-element.114.cf_ref, f32[4,384]{1,0:T(4,128)} %get-tuple-element.113.sf_ref, ...), custom_call_target="tpu_custom_call" | custom-call | flops 805306368 | bytes 2621440 | tf_op jit(solution)/shard_map/pallas_call | solution.py:107
  53.5 1.1 %slice_bitcast_fusion.2 = bf16[16,32,512]{2,1,0:T(8,128)(2,1)S(1)} fusion(bf16[2,16,32,512]{3,2,1,0:T(8,128)(2,1)} %shard_map.37), kind=kLoop, calls=%fused_computation.20 | loop fusion | bytes 1048576 | tf_op jit(solution)/shard_map/squeeze | solution.py:213
  54.5 0.1 collective-permute-start.8
  54.6 1.9 %collective-permute-done.8 = bf16[16,32,512]{2,1,0:T(8,128)(2,1)S(1)} collective-permute-done((bf16[16,32,512]{2,1,0:T(8,128)(2,1)S(1)}, bf16[16,32,512]{2,1,0:T(8,128)(2,1)S(1)}, u32[]{:S(2)}, u32[]{:S(2)}) %collective-permute-start.8) | collective-permute-done | bytes 524320 | tf_op jit(solution)/shard_map/ppermute | solution.py:213
  56.5 1.2 %fusion.13 = bf16[16,32,512]{2,1,0:T(8,128)(2,1)S(1)} fusion(bf16[16,32,512]{2,1,0:T(8,128)(2,1)S(1)} %collective-permute-done.8, bf16[2,16,32,512]{3,2,1,0:T(8,128)(2,1)} %shard_map.37), kind=kLoop, calls=%fused_computation.14 | loop fusion | flops 1048576 | bytes 1572864 | tf_op jit(solution)/shard_map/convert_element_type | solution.py:214
  57.7 1.6 %collective-permute-start.10 = (bf16[16,32,512]{2,1,0:T(8,128)(2,1)S(1)}, bf16[16,32,512]{2,1,0:T(8,128)(2,1)S(1)}, u32[]{:S(2)}, u32[]{:S(2)}) collective-permute-start(bf16[16,32,512]{2,1,0:T(8,128)(2,1)S(1)} %fusion.13), channel_id=1, source_target_pairs={{0,16},{8,24},{16,0},{24,8},{1,17},{9,25},{17,1},{25,9},{2,18},{10... | collective-permute-start | bytes 1572872 | tf_op jit(solution)/shard_map/ppermute | solution.py:217
  59.3 5.0 %shard_map.38 = bf16[2,16,32,512]{3,2,1,0:T(8,128)(2,1)} custom-call(s32[8]{0:T(128)} %fusion.49.index_ref, f32[4,384]{1,0:T(4,128)} %get-tuple-element.119.cc_ref, f32[4,384]{1,0:T(4,128)} %get-tuple-element.120.sc_ref, f32[4,384]{1,0:T(4,128)} %get-tuple-element.114.cf_ref, f32[4,384]{1,0:T(4,128)} %get-tuple-element.113.sf_ref, ...), custom_call_target="tpu_custom_call" | custom-call | flops 8053063 | bytes 26214 | tf_op jit(solution)/shard_map/pallas_call | solution.py:107
  64.3 1.1 %slice_bitcast_fusion = bf16[16,32,512]{2,1,0:T(8,128)(2,1)S(1)} fusion(bf16[2,16,32,512]{3,2,1,0:T(8,128)(2,1)} %shard_map.38), kind=kLoop, calls=%fused_computation.18 | loop fusion | bytes 1048576 | tf_op jit(solution)/shard_map/squeeze | solution.py:218
  65.4 0.1 collective-permute-start.9
  65.5 6.2 %collective-permute-done.10 = bf16[16,32,512]{2,1,0:T(8,128)(2,1)S(1)} collective-permute-done((bf16[16,32,512]{2,1,0:T(8,128)(2,1)S(1)}, bf16[16,32,512]{2,1,0:T(8,128)(2,1)S(1)}, u32[]{:S(2)}, u32[]{:S(2)}) %collective-permute-start.10) | collective-permute-done | bytes 524320 | tf_op jit(solution)/shard_map/ppermute | solution.py:217
  71.8 1.3 %fusion.12 = f32[16,32,512]{2,1,0:T(8,128)S(1)} fusion(bf16[16,32,512]{2,1,0:T(8,128)(2,1)S(1)} %collective-permute-done.10, bf16[16,32,512]{2,1,0:T(8,128)(2,1)S(1)} %collective-permute-done.9, bf16[2,16,32,512]{3,2,1,0:T(8,128)(2,1)} %shard_map.38), kind=kLoop, calls=%fused_computation.12 | loop fusion | flops 1310720 | bytes 2621440 | tf_op jit(solution)/shard_map/add | solution.py:219
  73.0 0.4 reshape.471
  73.4 1.7 %fusion.15 = f32[32,4,16,128]{3,2,1,0:T(8,128)} fusion(f32[16,32,4,128]{3,2,1,0:T(4,128)S(1)} %reshape.471, f32[4]{0:T(128)S(1)} %convert_element_type.143), kind=kLoop, calls=%fused_computation.17 | loop fusion | flops 524288 | bytes 2097168 | tf_op jit(solution)/shard_map/div | solution.py:226
  (25 shorter events, 0.3 us)
Async XLA Ops:
  1.3 3.5 %copy-start.2 = (bf16[1,256,7680]{2,1,0:T(8,128)(2,1)S(1)}, bf16[1,256,7680]{2,1,0:T(8,128)(2,1)}, u32[]{:S(2)}) copy-start(bf16[1,256,7680]{2,1,0:T(8,128)(2,1)} %param.3) | copy-start | bytes 11796484
  6.5 2.3 %copy-start.1 = (s32[32,2]{0,1:T(2,128)S(1)}, s32[32,2]{0,1:T(2,128)}, u32[]{:S(2)}) copy-start(s32[32,2]{0,1:T(2,128)} %param.4) | copy-start | bytes 772
  12.7 26.3 %collective-permute-start = (bf16[1,128,768]{2,1,0:T(8,128)(2,1)S(1)}, bf16[1,128,768]{2,1,0:T(8,128)(2,1)S(1)}, u32[]{:S(2)}, u32[]{:S(2)}) collective-permute-start(bf16[1,128,768]{2,1,0:T(8,128)(2,1)S(1)} %get-tuple-element.109), channel_id=1, source_target_pairs={{0,1},{1,2},{2,3},{3,0},{4,5},{5,6},{6,7},{7,4},{8,9},{9,10},{10,1... | collective-permute-start | bytes 589832 | tf_op jit(solution)/shard_map/ppermute | solution.py:148
  15.6 25.8 %collective-permute-start.1 = (bf16[1,128,768]{2,1,0:T(8,128)(2,1)S(1)}, bf16[1,128,768]{2,1,0:T(8,128)(2,1)S(1)}, u32[]{:S(2)}, u32[]{:S(2)}) collective-permute-start(bf16[1,128,768]{2,1,0:T(8,128)(2,1)S(1)} %get-tuple-element.110), channel_id=1, source_target_pairs={{0,2},{1,3},{2,0},{3,1},{4,6},{5,7},{6,4},{7,5},{8,10},{9,11},{10,... | collective-permute-start | bytes 589832 | tf_op jit(solution)/shard_map/ppermute | solution.py:148
  17.2 24.2 %collective-permute-start.2 = (bf16[1,128,768]{2,1,0:T(8,128)(2,1)S(1)}, bf16[1,128,768]{2,1,0:T(8,128)(2,1)S(1)}, u32[]{:S(2)}, u32[]{:S(2)}) collective-permute-start(bf16[1,128,768]{2,1,0:T(8,128)(2,1)S(1)} %get-tuple-element.108), channel_id=1, source_target_pairs={{0,3},{1,0},{2,1},{3,2},{4,7},{5,4},{6,5},{7,6},{8,11},{9,8},{10,9... | collective-permute-start | bytes 589832 | tf_op jit(solution)/shard_map/ppermute | solution.py:148
  18.7 12.5 %collective-permute-start.3 = (bf16[1,128,768]{2,1,0:T(8,128)(2,1)}, bf16[1,128,768]{2,1,0:T(8,128)(2,1)S(1)}, u32[]{:S(2)}, u32[]{:S(2)}) collective-permute-start(bf16[1,128,768]{2,1,0:T(8,128)(2,1)} %get-tuple-element.112), channel_id=1, source_target_pairs={{0,4},{1,5},{2,6},{3,7},{4,0},{5,1},{6,2},{7,3},{8,12},{9,13},{10,... | collective-permute-start | bytes 589832 | tf_op jit(solution)/shard_map/ppermute | solution.py:137
  21.2 17.1 %collective-permute-start.4 = (bf16[1,128,768]{2,1,0:T(8,128)(2,1)}, bf16[1,128,768]{2,1,0:T(8,128)(2,1)S(1)}, u32[]{:S(2)}, u32[]{:S(2)}) collective-permute-start(bf16[1,128,768]{2,1,0:T(8,128)(2,1)} %get-tuple-element.111), channel_id=1, source_target_pairs={{0,4},{1,5},{2,6},{3,7},{4,0},{5,1},{6,2},{7,3},{8,12},{9,13},{10,... | collective-permute-start | bytes 589832 | tf_op jit(solution)/shard_map/ppermute | solution.py:137
  38.4 6.7 %collective-permute-start.5 = (bf16[1,128,768]{2,1,0:T(8,128)(2,1)S(1)}, bf16[1,128,768]{2,1,0:T(8,128)(2,1)S(1)}, u32[]{:S(2)}, u32[]{:S(2)}) collective-permute-start(bf16[1,128,768]{2,1,0:T(8,128)(2,1)S(1)} %get-tuple-element.107), channel_id=1, source_target_pairs={{0,1},{1,2},{2,3},{3,0},{4,5},{5,6},{6,7},{7,4},{8,9},{9,10},{10,1... | collective-permute-start | bytes 589832 | tf_op jit(solution)/shard_map/ppermute | solution.py:149
  39.0 6.1 %collective-permute-start.6 = (bf16[1,128,768]{2,1,0:T(8,128)(2,1)S(1)}, bf16[1,128,768]{2,1,0:T(8,128)(2,1)S(1)}, u32[]{:S(2)}, u32[]{:S(2)}) collective-permute-start(bf16[1,128,768]{2,1,0:T(8,128)(2,1)S(1)} %get-tuple-element.106), channel_id=1, source_target_pairs={{0,2},{1,3},{2,0},{3,1},{4,6},{5,7},{6,4},{7,5},{8,10},{9,11},{10,... | collective-permute-start | bytes 589832 | tf_op jit(solution)/shard_map/ppermute | solution.py:149
  39.0 8.1 %collective-permute-start.7 = (bf16[1,128,768]{2,1,0:T(8,128)(2,1)S(1)}, bf16[1,128,768]{2,1,0:T(8,128)(2,1)S(1)}, u32[]{:S(2)}, u32[]{:S(2)}) collective-permute-start(bf16[1,128,768]{2,1,0:T(8,128)(2,1)S(1)} %get-tuple-element.105), channel_id=1, source_target_pairs={{0,3},{1,0},{2,1},{3,2},{4,7},{5,4},{6,5},{7,6},{8,11},{9,8},{10,9... | collective-permute-start | bytes 589832 | tf_op jit(solution)/shard_map/ppermute | solution.py:149
  47.1 1.1 %copy-start = (bf16[8,1,128,768]{3,2,1,0:T(8,128)(2,1)}, bf16[8,1,128,768]{3,2,1,0:T(8,128)(2,1)S(1)}, u32[]{:S(2)}) copy-start(bf16[8,1,128,768]{3,2,1,0:T(8,128)(2,1)S(1)} %bitcast_dynamic-update-slice_fusion.left_ref.right_ref) | copy-start | bytes 4718596
  48.3 17.2 %copy-start.3 = (s32[4]{0:T(128)S(1)}, s32[4]{0:T(128)}, u32[]{:S(2)}) copy-start(s32[4]{0:T(128)} %param.5) | copy-start | bytes 52
  54.5 2.0 %collective-permute-start.8 = (bf16[16,32,512]{2,1,0:T(8,128)(2,1)S(1)}, bf16[16,32,512]{2,1,0:T(8,128)(2,1)S(1)}, u32[]{:S(2)}, u32[]{:S(2)}) collective-permute-start(bf16[16,32,512]{2,1,0:T(8,128)(2,1)S(1)} %slice_bitcast_fusion.2), channel_id=1, source_target_pairs={{0,8},{8,0},{16,24},{24,16},{1,9},{9,1},{17,25},{25,17},{2,10},{10... | collective-permute-start | bytes 1572872 | tf_op jit(solution)/shard_map/ppermute | solution.py:213
  57.7 14.0 %collective-permute-start.10 = (bf16[16,32,512]{2,1,0:T(8,128)(2,1)S(1)}, bf16[16,32,512]{2,1,0:T(8,128)(2,1)S(1)}, u32[]{:S(2)}, u32[]{:S(2)}) collective-permute-start(bf16[16,32,512]{2,1,0:T(8,128)(2,1)S(1)} %fusion.13), channel_id=1, source_target_pairs={{0,16},{8,24},{16,0},{24,8},{1,17},{9,25},{17,1},{25,9},{2,18},{10... | collective-permute-start | bytes 1572872 | tf_op jit(solution)/shard_map/ppermute | solution.py:217
  65.4 6.3 %collective-permute-start.9 = (bf16[16,32,512]{2,1,0:T(8,128)(2,1)S(1)}, bf16[16,32,512]{2,1,0:T(8,128)(2,1)S(1)}, u32[]{:S(2)}, u32[]{:S(2)}) collective-permute-start(bf16[16,32,512]{2,1,0:T(8,128)(2,1)S(1)} %slice_bitcast_fusion), channel_id=1, source_target_pairs={{0,8},{8,0},{16,24},{24,16},{1,9},{9,1},{17,25},{25,17},{2,10},{10... | collective-permute-start | bytes 1572872 | tf_op jit(solution)/shard_map/ppermute | solution.py:218

commit v14 on v12

--- a/solution.py
+++ b/solution.py
@@ -49,17 +49,17 @@
     for w in range(window_count):
         left = left_ref[0, w].astype(jnp.float32)
         left = jnp.concatenate([left[r : r + own_rows] for r in order], axis=0)
-        lre = left[:, :F]
-        lim = left[:, F:]
-        rre = right_ref[0, w, :, :F].astype(jnp.float32)
-        rim = right_ref[0, w, :, F:].astype(jnp.float32)
+        lre = left[:, :F].astype(jnp.bfloat16)
+        lim = left[:, F:].astype(jnp.bfloat16)
+        rre = right_ref[0, w, :, :F]
+        rim = right_ref[0, w, :, F:]
         turned = []
         for l1 in range(sub):
             if l1 == 0:
                 turned.append(right_ref[0, w])
                 continue
-            c = cf_ref[l1 : l1 + 1, :]
-            s = sf_ref[l1 : l1 + 1, :]
+            c = cf_ref[l1 : l1 + 1, :].astype(jnp.bfloat16)
+            s = sf_ref[l1 : l1 + 1, :].astype(jnp.bfloat16)
             turned.append(jnp.concatenate([rre * c + rim * s, rim * c - rre * s], axis=1).astype(jnp.bfloat16))
         right_all = jnp.concatenate(turned, axis=0)
         lefts = []
@@ -67,8 +67,8 @@
             if l2 * sub == LAGS // 2:
                 lefts.append(left.astype(jnp.bfloat16))
             else:
-                c = cc_ref[l2 : l2 + 1, :]
-                s = sc_ref[l2 : l2 + 1, :]
+                c = cc_ref[l2 : l2 + 1, :].astype(jnp.bfloat16)
+                s = sc_ref[l2 : l2 + 1, :].astype(jnp.bfloat16)
                 lefts.append(jnp.concatenate([lre * c - lim * s, lre * s + lim * c], axis=1).astype(jnp.bfloat16))
         res = lax.dot_general(
             jnp.concatenate(lefts, axis=0), right_all, (((1,), (1,)), ((), ())), preferred_element_type=jnp.float32

time: 74.3 us -> 74.3 us (level)
  no operation moved by 1% of the time
where the time goes in v14:
time: 74.3 us; the launch traced here: 73.9 us
  waiting for transfers between devices  30.6 us (41%)
  starting transfers between devices  14 us (19%)
  other arithmetic  9.2 us (12%)
  Pallas kernels  5.73 us (8%)
  local copies, waits for them, and re-layouts  5.68 us (8%)
  between operations  5.38 us (7%)
  matrix products  3.38 us (5%)
    ppermute x1, waiting for transfers between devices, body(): total = total + lax.ppermute(piece, 'win', perm).astype(jnp.float32)  12.7 us
    ppermute x2, waiting for transfers between devices, exchange_by_halves(): lax.ppermute(block, 'pair', across)  7.91 us
    ppermute x3, waiting for transfers between devices, exchange_by_halves(): relay = lax.ppermute(relay, 'pair', perm)  7.37 us
    pallas_call x1, Pallas kernels, tile_correlation(): pl.pallas_call(functools.partial(correlation_kernel, sub, n_y, own_rows),...  5.73 us
    ppermute x3, starting transfers between devices, exchange_by_halves(): own = lax.ppermute(own, 'pair', perm)  4.76 us
    ppermute x2, starting transfers between devices, exchange_by_halves(): lax.ppermute(block, 'pair', across)  4.18 us
    another operation x3, other arithmetic  3.72 us
    ppermute x3, starting transfers between devices, exchange_by_halves(): relay = lax.ppermute(relay, 'pair', perm)  3.64 us
  transfers between devices with their start and end apart: 10, of which 7 were waited for; matrix products, arithmetic and copies ran while one was open for 2% of the time, Pallas kernels for 0%

profile of v14, /device:TPU:0, one launch (start us, length us, event | category | flops | bytes accessed | tf_op | source)
XLA Modules:
  0.0 73.9 jit_solution(1583910625130328075)
XLA Ops:
  0.0 0.8 %fusion.19 = (f32[128,384]{1,0:T(8,128)S(1)}, f32[128,384]{1,0:T(8,128)S(1)}) fusion(s32[384]{0:T(512)S(1)} %iota_add_fusion), kind=kLoop, calls=%fused_computation.41 | loop fusion | flops 442368 | bytes 394752 | tf_op jit(solution)/shard_map/cos | solution.py:20
  0.8 0.5 fusion.26
  1.3 0.0 copy-start.2
  1.3 3.5 %subtract_convert_fusion = (bf16[60,128,384]{2,1,0:T(8,128)(2,1)S(1)}, bf16[60,128,384]{2,1,0:T(8,128)(2,1)S(1)}) fusion(f32[128,384]{1,0:T(8,128)S(1)} %get-tuple-element.160, f32[60,384]{1,0:T(8,128)S(1)} %get-tuple-element.154, f32[128,384]{1,0:T(8,128)S(1)} %get-tuple-element.159, f32[60,384]{1,0:T(8,128)S(1)} %get-tuple-element.153), kind=kLoop, calls=%fused_computation.2 | loop fusion | flops 26542080 | bytes 12374016 | tf_op jit(solution)/shard_map/convert.19
  4.8 1.7 %fusion.6 = f32[128,768]{1,0:T(8,128)S(1)} fusion(bf16[7680,384]{1,0:T(8,128)(2,1)S(1)} %bitcast.66, bf16[7680,384]{1,0:T(8,128)(2,1)S(1)} %bitcast.64, bf16[1,256,7680]{2,1,0:T(8,128)(2,1)S(1)} %copy-done.2), kind=kOutput, calls=%fused_computation.10 | convolution fusion | flops 1533542400 | bytes 14155776 | tf_op jit(solution)/shard_map/dot_general | solution.py:36
  6.5 0.0 copy-start.1
  6.5 1.7 %fusion.9 = f32[128,768]{1,0:T(8,128)S(1)} fusion(bf16[7680,384]{1,0:T(8,128)(2,1)S(1)} %bitcast.67, bf16[7680,384]{1,0:T(8,128)(2,1)S(1)} %bitcast.65, bf16[1,256,7680]{2,1,0:T(8,128)(2,1)S(1)} %copy-done.2), kind=kOutput, calls=%fused_computation.11 | convolution fusion | flops 1533542400 | bytes 14155776 | tf_op jit(solution)/shard_map/dot_general | solution.py:36
  8.3 0.1 reduce_sum.43
  8.4 0.1 reduce_sum.52
  8.5 0.1 reduce_sum.56
  8.6 0.1 reduce_sum.57
  8.7 0.7 fusion.51
  11.2 0.2 fusion.49
  11.5 0.1 divide_convert_fusion.1
  11.6 0.1 divide_convert_fusion.3
  11.7 0.1 broadcast_select_fusion.3
  11.8 4.1 %collective-permute-start.3 = (bf16[1,128,768]{2,1,0:T(8,128)(2,1)S(1)}, bf16[1,128,768]{2,1,0:T(8,128)(2,1)S(1)}, u32[]{:S(2)}, u32[]{:S(2)}) collective-permute-start(bf16[1,128,768]{2,1,0:T(8,128)(2,1)S(1)} %get-tuple-element.152), channel_id=1, source_target_pairs={{0,4},{1,5},{2,6},{3,7},{4,0},{5,1},{6,2},{7,3},{8,12},{9,13},{10,... | collective-permute-start | bytes 589832 | tf_op jit(solution)/shard_map/ppermute | solution.py:126
  15.9 0.1 collective-permute-start.4
  16.0 1.7 %collective-permute-start = (bf16[1,128,768]{2,1,0:T(8,128)(2,1)S(1)}, bf16[1,128,768]{2,1,0:T(8,128)(2,1)S(1)}, u32[]{:S(2)}, u32[]{:S(2)}) collective-permute-start(bf16[1,128,768]{2,1,0:T(8,128)(2,1)S(1)} %get-tuple-element.149), channel_id=1, source_target_pairs={{0,1},{1,2},{2,3},{3,0},{4,5},{5,6},{6,7},{7,4},{8,9},{9,10},{10,1... | collective-permute-start | bytes 589832 | tf_op jit(solution)/shard_map/ppermute | solution.py:137
  17.8 1.6 %collective-permute-start.1 = (bf16[1,128,768]{2,1,0:T(8,128)(2,1)S(1)}, bf16[1,128,768]{2,1,0:T(8,128)(2,1)S(1)}, u32[]{:S(2)}, u32[]{:S(2)}) collective-permute-start(bf16[1,128,768]{2,1,0:T(8,128)(2,1)S(1)} %get-tuple-element.150), channel_id=1, source_target_pairs={{0,2},{1,3},{2,0},{3,1},{4,6},{5,7},{6,4},{7,5},{8,10},{9,11},{10,... | collective-permute-start | bytes 589832 | tf_op jit(solution)/shard_map/ppermute | solution.py:137
  19.3 1.4 %collective-permute-start.2 = (bf16[1,128,768]{2,1,0:T(8,128)(2,1)S(1)}, bf16[1,128,768]{2,1,0:T(8,128)(2,1)S(1)}, u32[]{:S(2)}, u32[]{:S(2)}) collective-permute-start(bf16[1,128,768]{2,1,0:T(8,128)(2,1)S(1)} %get-tuple-element.148), channel_id=1, source_target_pairs={{0,3},{1,0},{2,1},{3,2},{4,7},{5,4},{6,5},{7,6},{8,11},{9,8},{10,9... | collective-permute-start | bytes 589832 | tf_op jit(solution)/shard_map/ppermute | solution.py:137
  24.0 0.1 constant_dynamic-slice_fusion
  24.1 0.1 copy.7
  24.2 0.1 reshape.467
  24.3 0.8 %fusion.38 = (f32[4,384]{1,0:T(4,128)}, f32[4,384]{1,0:T(4,128)}, f32[4,384]{1,0:T(4,128)}, f32[4,384]{1,0:T(4,128)}) fusion(s32[384]{0:T(512)S(1)} %iota_add_fusion, s32[4]{0:T(128)S(1)} %get-tuple-element.175, s32[4]{0:T(128)S(1)} %get-tuple-element.176), kind=kLoop, calls=%fused_computation.72 | loop fusion | flops 27648 | bytes 26144 | tf_op jit(solution)/shard_map/sin | solution.py:20
  25.1 0.6 fusion.46.index_ref
  25.7 4.5 %collective-permute-done.3 = bf16[1,128,768]{2,1,0:T(8,128)(2,1)S(1)} collective-permute-done((bf16[1,128,768]{2,1,0:T(8,128)(2,1)S(1)}, bf16[1,128,768]{2,1,0:T(8,128)(2,1)S(1)}, u32[]{:S(2)}, u32[]{:S(2)}) %collective-permute-start.3) | collective-permute-done | bytes 196640 | tf_op jit(solution)/shard_map/ppermute | solution.py:126
  30.2 3.4 %collective-permute-done.4 = bf16[1,128,768]{2,1,0:T(8,128)(2,1)S(1)} collective-permute-done((bf16[1,128,768]{2,1,0:T(8,128)(2,1)S(1)}, bf16[1,128,768]{2,1,0:T(8,128)(2,1)S(1)}, u32[]{:S(2)}, u32[]{:S(2)}) %collective-permute-start.4) | collective-permute-done | bytes 196640 | tf_op jit(solution)/shard_map/ppermute | solution.py:126
  33.6 1.6 %collective-permute-start.5 = (bf16[1,128,768]{2,1,0:T(8,128)(2,1)S(1)}, bf16[1,128,768]{2,1,0:T(8,128)(2,1)S(1)}, u32[]{:S(2)}, u32[]{:S(2)}) collective-permute-start(bf16[1,128,768]{2,1,0:T(8,128)(2,1)S(1)} %get-tuple-element.147), channel_id=1, source_target_pairs={{0,1},{1,2},{2,3},{3,0},{4,5},{5,6},{6,7},{7,4},{8,9},{9,10},{10,1... | collective-permute-start | bytes 589832 | tf_op jit(solution)/shard_map/ppermute | solution.py:138
  35.2 0.6 collective-permute-start.6
  35.8 1.4 %collective-permute-start.7 = (bf16[1,128,768]{2,1,0:T(8,128)(2,1)S(1)}, bf16[1,128,768]{2,1,0:T(8,128)(2,1)S(1)}, u32[]{:S(2)}, u32[]{:S(2)}) collective-permute-start(bf16[1,128,768]{2,1,0:T(8,128)(2,1)S(1)} %get-tuple-element.145), channel_id=1, source_target_pairs={{0,3},{1,0},{2,1},{3,2},{4,7},{5,4},{6,5},{7,6},{8,11},{9,8},{10,9... | collective-permute-start | bytes 589832 | tf_op jit(solution)/shard_map/ppermute | solution.py:138
  37.3 0.1 bitcast_dynamic-update-slice_fusion.3
  37.4 5.0 %collective-permute-done.5 = bf16[1,128,768]{2,1,0:T(8,128)(2,1)S(1)} collective-permute-done((bf16[1,128,768]{2,1,0:T(8,128)(2,1)S(1)}, bf16[1,128,768]{2,1,0:T(8,128)(2,1)S(1)}, u32[]{:S(2)}, u32[]{:S(2)}) %collective-permute-start.5) | collective-permute-done | bytes 196640 | tf_op jit(solution)/shard_map/ppermute | solution.py:138
  42.4 0.3 collective-permute-done.6
  42.8 2.0 %collective-permute-done.7 = bf16[1,128,768]{2,1,0:T(8,128)(2,1)S(1)} collective-permute-done((bf16[1,128,768]{2,1,0:T(8,128)(2,1)S(1)}, bf16[1,128,768]{2,1,0:T(8,128)(2,1)S(1)}, u32[]{:S(2)}, u32[]{:S(2)}) %collective-permute-start.7) | collective-permute-done | bytes 196640 | tf_op jit(solution)/shard_map/ppermute | solution.py:138
  44.8 1.1 %copy-done = bf16[8,1,128,768]{3,2,1,0:T(8,128)(2,1)} copy-done((bf16[8,1,128,768]{3,2,1,0:T(8,128)(2,1)}, bf16[8,1,128,768]{3,2,1,0:T(8,128)(2,1)S(1)}, u32[]{:S(2)}) %copy-start) | copy-done | bytes 1572888
  46.0 5.7 %shard_map.37 = bf16[2,16,64,512]{3,2,1,0:T(8,128)(2,1)} custom-call(s32[8]{0:T(128)} %fusion.46.index_ref, f32[4,384]{1,0:T(4,128)} %get-tuple-element.161.cc_ref, f32[4,384]{1,0:T(4,128)} %get-tuple-element.162.sc_ref, f32[4,384]{1,0:T(4,128)} %get-tuple-element.156.cf_ref, f32[4,384]{1,0:T(4,128)} %get-tuple-element.155.sf_ref, ...), custom_call_target="tpu_custom_call" | custom-call | flops 1610612736 | bytes 3670016 | tf_op jit(solution)/shard_map/pallas_call | solution.py:98
  51.7 1.3 %dynamic-slice_bitcast_fusion = bf16[16,64,512]{2,1,0:T(8,128)(2,1)S(1)} fusion(bf16[2,16,64,512]{3,2,1,0:T(8,128)(2,1)} %shard_map.37, s32[]{:T(128)S(6)} %sub.53), kind=kLoop, calls=%fused_computation.14 | loop fusion | bytes 2097156 | tf_op jit(solution)/shard_map/jit(_take)/gather | solution.py:188
  53.0 0.1 collective-permute-start.8
  53.1 2.6 %collective-permute-done.8 = bf16[16,64,512]{2,1,0:T(8,128)(2,1)S(1)} collective-permute-done((bf16[16,64,512]{2,1,0:T(8,128)(2,1)S(1)}, bf16[16,64,512]{2,1,0:T(8,128)(2,1)S(1)}, u32[]{:S(2)}, u32[]{:S(2)}) %collective-permute-start.8) | collective-permute-done | bytes 1048608 | tf_op jit(solution)/shard_map/ppermute | solution.py:190
  55.8 1.5 %convert_add_fusion = f32[16,64,512]{2,1,0:T(8,128)S(1)} fusion(bf16[16,64,512]{2,1,0:T(8,128)(2,1)S(1)} %collective-permute-done.8, bf16[2,16,64,512]{3,2,1,0:T(8,128)(2,1)} %shard_map.37, s32[]{:T(128)S(6)} %select_n.243), kind=kLoop, calls=%fused_computation.5 | loop fusion | flops 1572864 | bytes 4194308 | tf_op jit(solution)/shard_map/add | solution.py:191
  57.3 0.1 fusion.12
  57.4 1.3 %collective-permute-start.9 = (bf16[16,32,512]{2,1,0:T(8,128)(2,1)S(1)}, bf16[16,32,512]{2,1,0:T(8,128)(2,1)S(1)}, u32[]{:S(2)}, u32[]{:S(2)}) collective-permute-start(bf16[16,32,512]{2,1,0:T(8,128)(2,1)S(1)} %fusion.12), channel_id=1, source_target_pairs={{0,16},{8,24},{16,0},{24,8},{1,17},{9,25},{17,1},{25,9},{2,18},{10... | collective-permute-start | bytes 1572872 | tf_op jit(solution)/shard_map/ppermute | solution.py:198
  58.7 12.7 %collective-permute-done.9 = bf16[16,32,512]{2,1,0:T(8,128)(2,1)S(1)} collective-permute-done((bf16[16,32,512]{2,1,0:T(8,128)(2,1)S(1)}, bf16[16,32,512]{2,1,0:T(8,128)(2,1)S(1)}, u32[]{:S(2)}, u32[]{:S(2)}) %collective-permute-start.9) | collective-permute-done | bytes 524320 | tf_op jit(solution)/shard_map/ppermute | solution.py:198
  71.4 0.2 bitcast_add_fusion
  71.6 0.4 reshape.471
  72.0 0.4 multiply_bitcast_fusion
  72.4 1.6 %copy.11 = f32[32,4,16,128]{3,2,1,0:T(8,128)} copy(f32[32,4,16,128]{3,1,0,2:T(4,128)S(1)} %multiply_bitcast_fusion) | data formatting | bytes 2097152 | tf_op jit(solution)/shard_map/div | solution.py:202
  (23 shorter events, 0.2 us)
Async XLA Ops:
  1.3 3.5 %copy-start.2 = (bf16[1,256,7680]{2,1,0:T(8,128)(2,1)S(1)}, bf16[1,256,7680]{2,1,0:T(8,128)(2,1)}, u32[]{:S(2)}) copy-start(bf16[1,256,7680]{2,1,0:T(8,128)(2,1)} %param.3) | copy-start | bytes 11796484
  6.5 1.8 %copy-start.1 = (s32[32,2]{0,1:T(2,128)S(1)}, s32[32,2]{0,1:T(2,128)}, u32[]{:S(2)}) copy-start(s32[32,2]{0,1:T(2,128)} %param.4) | copy-start | bytes 772
  11.8 18.4 %collective-permute-start.3 = (bf16[1,128,768]{2,1,0:T(8,128)(2,1)S(1)}, bf16[1,128,768]{2,1,0:T(8,128)(2,1)S(1)}, u32[]{:S(2)}, u32[]{:S(2)}) collective-permute-start(bf16[1,128,768]{2,1,0:T(8,128)(2,1)S(1)} %get-tuple-element.152), channel_id=1, source_target_pairs={{0,4},{1,5},{2,6},{3,7},{4,0},{5,1},{6,2},{7,3},{8,12},{9,13},{10,... | collective-permute-start | bytes 589832 | tf_op jit(solution)/shard_map/ppermute | solution.py:126
  15.9 17.6 %collective-permute-start.4 = (bf16[1,128,768]{2,1,0:T(8,128)(2,1)S(1)}, bf16[1,128,768]{2,1,0:T(8,128)(2,1)S(1)}, u32[]{:S(2)}, u32[]{:S(2)}) collective-permute-start(bf16[1,128,768]{2,1,0:T(8,128)(2,1)S(1)} %get-tuple-element.151), channel_id=1, source_target_pairs={{0,4},{1,5},{2,6},{3,7},{4,0},{5,1},{6,2},{7,3},{8,12},{9,13},{10,... | collective-permute-start | bytes 589832 | tf_op jit(solution)/shard_map/ppermute | solution.py:126
  16.0 19.8 %collective-permute-start = (bf16[1,128,768]{2,1,0:T(8,128)(2,1)S(1)}, bf16[1,128,768]{2,1,0:T(8,128)(2,1)S(1)}, u32[]{:S(2)}, u32[]{:S(2)}) collective-permute-start(bf16[1,128,768]{2,1,0:T(8,128)(2,1)S(1)} %get-tuple-element.149), channel_id=1, source_target_pairs={{0,1},{1,2},{2,3},{3,0},{4,5},{5,6},{6,7},{7,4},{8,9},{9,10},{10,1... | collective-permute-start | bytes 589832 | tf_op jit(solution)/shard_map/ppermute | solution.py:137
  17.8 19.5 %collective-permute-start.1 = (bf16[1,128,768]{2,1,0:T(8,128)(2,1)S(1)}, bf16[1,128,768]{2,1,0:T(8,128)(2,1)S(1)}, u32[]{:S(2)}, u32[]{:S(2)}) collective-permute-start(bf16[1,128,768]{2,1,0:T(8,128)(2,1)S(1)} %get-tuple-element.150), channel_id=1, source_target_pairs={{0,2},{1,3},{2,0},{3,1},{4,6},{5,7},{6,4},{7,5},{8,10},{9,11},{10,... | collective-permute-start | bytes 589832 | tf_op jit(solution)/shard_map/ppermute | solution.py:137
  19.3 18.0 %collective-permute-start.2 = (bf16[1,128,768]{2,1,0:T(8,128)(2,1)S(1)}, bf16[1,128,768]{2,1,0:T(8,128)(2,1)S(1)}, u32[]{:S(2)}, u32[]{:S(2)}) collective-permute-start(bf16[1,128,768]{2,1,0:T(8,128)(2,1)S(1)} %get-tuple-element.148), channel_id=1, source_target_pairs={{0,3},{1,0},{2,1},{3,2},{4,7},{5,4},{6,5},{7,6},{8,11},{9,8},{10,9... | collective-permute-start | bytes 589832 | tf_op jit(solution)/shard_map/ppermute | solution.py:137
  33.6 8.8 %collective-permute-start.5 = (bf16[1,128,768]{2,1,0:T(8,128)(2,1)S(1)}, bf16[1,128,768]{2,1,0:T(8,128)(2,1)S(1)}, u32[]{:S(2)}, u32[]{:S(2)}) collective-permute-start(bf16[1,128,768]{2,1,0:T(8,128)(2,1)S(1)} %get-tuple-element.147), channel_id=1, source_target_pairs={{0,1},{1,2},{2,3},{3,0},{4,5},{5,6},{6,7},{7,4},{8,9},{9,10},{10,1... | collective-permute-start | bytes 589832 | tf_op jit(solution)/shard_map/ppermute | solution.py:138
  35.2 7.6 %collective-permute-start.6 = (bf16[1,128,768]{2,1,0:T(8,128)(2,1)S(1)}, bf16[1,128,768]{2,1,0:T(8,128)(2,1)S(1)}, u32[]{:S(2)}, u32[]{:S(2)}) collective-permute-start(bf16[1,128,768]{2,1,0:T(8,128)(2,1)S(1)} %get-tuple-element.146), channel_id=1, source_target_pairs={{0,2},{1,3},{2,0},{3,1},{4,6},{5,7},{6,4},{7,5},{8,10},{9,11},{10,... | collective-permute-start | bytes 589832 | tf_op jit(solution)/shard_map/ppermute | solution.py:138
  35.8 9.0 %collective-permute-start.7 = (bf16[1,128,768]{2,1,0:T(8,128)(2,1)S(1)}, bf16[1,128,768]{2,1,0:T(8,128)(2,1)S(1)}, u32[]{:S(2)}, u32[]{:S(2)}) collective-permute-start(bf16[1,128,768]{2,1,0:T(8,128)(2,1)S(1)} %get-tuple-element.145), channel_id=1, source_target_pairs={{0,3},{1,0},{2,1},{3,2},{4,7},{5,4},{6,5},{7,6},{8,11},{9,8},{10,9... | collective-permute-start | bytes 589832 | tf_op jit(solution)/shard_map/ppermute | solution.py:138
  44.8 1.1 %copy-start = (bf16[8,1,128,768]{3,2,1,0:T(8,128)(2,1)}, bf16[8,1,128,768]{3,2,1,0:T(8,128)(2,1)S(1)}, u32[]{:S(2)}) copy-start(bf16[8,1,128,768]{3,2,1,0:T(8,128)(2,1)S(1)} %bitcast_dynamic-update-slice_fusion.left_ref.right_ref) | copy-start | bytes 4718596
  51.7 7.0 %copy-start.3 = (s32[4]{0:T(128)S(1)}, s32[4]{0:T(128)}, u32[]{:S(2)}) copy-start(s32[4]{0:T(128)} %param.5) | copy-start | bytes 52
  53.0 2.7 %collective-permute-start.8 = (bf16[16,64,512]{2,1,0:T(8,128)(2,1)S(1)}, bf16[16,64,512]{2,1,0:T(8,128)(2,1)S(1)}, u32[]{:S(2)}, u32[]{:S(2)}) collective-permute-start(bf16[16,64,512]{2,1,0:T(8,128)(2,1)S(1)} %dynamic-slice_bitcast_fusion), channel_id=1, source_target_pairs={{0,8},{8,0},{16,24},{24,16},{1,9},{9,1},{17,25},{25,17},{2,10},{10... | collective-permute-start | bytes 3145736 | tf_op jit(solution)/shard_map/ppermute | solution.py:190
  57.4 14.0 %collective-permute-start.9 = (bf16[16,32,512]{2,1,0:T(8,128)(2,1)S(1)}, bf16[16,32,512]{2,1,0:T(8,128)(2,1)S(1)}, u32[]{:S(2)}, u32[]{:S(2)}) collective-permute-start(bf16[16,32,512]{2,1,0:T(8,128)(2,1)S(1)} %fusion.12), channel_id=1, source_target_pairs={{0,16},{8,24},{16,0},{24,8},{1,17},{9,25},{17,1},{25,9},{2,18},{10... | collective-permute-start | bytes 1572872 | tf_op jit(solution)/shard_map/ppermute | solution.py:198

commit v15 on v12

--- a/solution.py
+++ b/solution.py
@@ -154,12 +154,12 @@
     b_dev = local_rows // C
 
     table = dft_table(sample_count, F)
-    block_list = [
-        whiten_rows(strain[:, k * C : (k + 1) * C].reshape(window_count * C, sample_count), table, F).reshape(
-            window_count, C, 2 * F
-        )
-        for k in range(b_dev)
-    ]
+    block_list = []
+    for k in range(b_dev):
+        rows = strain[:, k * C : (k + 1) * C].reshape(window_count * C, sample_count)
+        if block_list:
+            rows, _ = lax.optimization_barrier((rows, block_list[-1]))
+        block_list.append(whiten_rows(rows, table, F).reshape(window_count, C, 2 * F))
     whitened = jnp.stack(block_list, axis=1)
 
     lists = pair_list.reshape(n_pair, 2 * slot_count)

time: 74.3 us -> 75.1 us (1.011)
  waiting for transfers between devices: 30.6 us -> 24.9 us
  matrix products: 3.38 us -> 7.16 us
  local copies, waits for them, and re-layouts: 5.68 us -> 8.4 us
    ppermute x2, waiting for transfers between devices: 7.91 us -> 1.95 us  [exchange_by_halves(): lax.ppermute(block, 'pair', across)]
    dot_general x2, matrix products: 3.38 us -> 7.16 us  [whiten_rows(): spectrum = jnp.dot(strain_rows, table, preferred_element_type=jnp.float32)]
    unnamed x13 -> x17, local copies, waits for them, and re-layouts: 1.22 us -> 3.82 us
  transfers between devices with their start and end apart: 10 -> 10, of which waited for: 7 -> 5; matrix products, arithmetic and copies ran while one was open for 2% -> 12% of each run, Pallas kernels for 0% -> 0%
where the time goes in v15:
time: 75.1 us; the launch traced here: 74.7 us
  waiting for transfers between devices  24.9 us (33%)
  starting transfers between devices  13.8 us (18%)
  other arithmetic  9.24 us (12%)
  local copies, waits for them, and re-layouts  8.4 us (11%)
  matrix products  7.16 us (10%)
  Pallas kernels  5.73 us (8%)
  between operations  5.41 us (7%)
    ppermute x1, waiting for transfers between devices, body(): total = total + lax.ppermute(piece, 'win', perm).astype(jnp.float32)  12.4 us
    ppermute x3, waiting for transfers between devices, exchange_by_halves(): relay = lax.ppermute(relay, 'pair', perm)  7.9 us
    dot_general x2, matrix products, whiten_rows(): spectrum = jnp.dot(strain_rows, table, preferred_element_type=jnp.float32)  7.16 us
    pallas_call x1, Pallas kernels, tile_correlation(): pl.pallas_call(functools.partial(correlation_kernel, sub, n_y, own_rows),...  5.73 us
    ppermute x3, starting transfers between devices, exchange_by_halves(): own = lax.ppermute(own, 'pair', perm)  4.81 us
    ppermute x2, starting transfers between devices, exchange_by_halves(): lax.ppermute(block, 'pair', across)  4.19 us
    unnamed x17, local copies, waits for them, and re-layouts  3.82 us
    another operation x3, other arithmetic  3.72 us
  transfers between devices with their start and end apart: 10, of which 5 were waited for; matrix products, arithmetic and copies ran while one was open for 12% of the time, Pallas kernels for 0%

profile of v15, /device:TPU:0, one launch (start us, length us, event | category | flops | bytes accessed | tf_op | source)
XLA Modules:
  0.0 74.7 jit_solution(3722542101399169441)
XLA Ops:
  0.0 0.8 %fusion.14 = (f32[128,384]{1,0:T(8,128)S(1)}, f32[128,384]{1,0:T(8,128)S(1)}) fusion(s32[384]{0:T(512)S(1)} %iota_add_fusion), kind=kLoop, calls=%fused_computation.39 | loop fusion | flops 442368 | bytes 394752 | tf_op jit(solution)/shard_map/cos | solution.py:20
  0.8 0.5 fusion.21
  1.3 3.5 %subtract_convert_fusion = (bf16[60,128,384]{2,1,0:T(8,128)(2,1)S(1)}, bf16[60,128,384]{2,1,0:T(8,128)(2,1)S(1)}) fusion(f32[128,384]{1,0:T(8,128)S(1)} %get-tuple-element.161, f32[60,384]{1,0:T(8,128)S(1)} %get-tuple-element.155, f32[128,384]{1,0:T(8,128)S(1)} %get-tuple-element.160, f32[60,384]{1,0:T(8,128)S(1)} %get-tuple-element.154), kind=kLoop, calls=%fused_computation.2 | loop fusion | flops 26542080 | bytes 12374016 | tf_op jit(solution)/shard_map/convert.19
  4.8 1.7 %fusion.4 = f32[128,768]{1,0:T(8,128)S(1)} fusion(bf16[7680,384]{1,0:T(8,128)(2,1)S(1)} %bitcast.62, bf16[7680,384]{1,0:T(8,128)(2,1)S(1)} %bitcast.60, bf16[1,256,7680]{2,1,0:T(8,128)(2,1)S(1)} %copy-done.2), kind=kOutput, calls=%fused_computation.9 | convolution fusion | flops 1533542400 | bytes 14155776 | tf_op jit(solution)/shard_map/dot_general | solution.py:36
  6.5 0.8 %copy-done = bf16[60,128,384]{2,1,0:T(8,128)(2,1)} copy-done((bf16[60,128,384]{2,1,0:T(8,128)(2,1)}, bf16[60,128,384]{2,1,0:T(8,128)(2,1)S(1)}, u32[]{:S(2)}) %copy-start) | copy-done | bytes 5898264
  7.4 1.7 %copy-done.1 = bf16[60,128,384]{2,1,0:T(8,128)(2,1)} copy-done((bf16[60,128,384]{2,1,0:T(8,128)(2,1)}, bf16[60,128,384]{2,1,0:T(8,128)(2,1)S(1)}, u32[]{:S(2)}) %copy-start.1) | copy-done | bytes 5898264
  9.1 0.2 fusion.44
  9.3 0.1 divide_convert_fusion.3
  9.4 4.1 %collective-permute-start.4 = (bf16[1,128,768]{2,1,0:T(8,128)(2,1)S(1)}, bf16[1,128,768]{2,1,0:T(8,128)(2,1)S(1)}, u32[]{:S(2)}, u32[]{:S(2)}) collective-permute-start(bf16[1,128,768]{2,1,0:T(8,128)(2,1)S(1)} %pad_maximum_fusion.5), channel_id=1, source_target_pairs={{0,4},{1,5},{2,6},{3,7},{4,0},{5,1},{6,2},{7,3},{8,12},{9,13},{10,... | collective-permute-start | bytes 589832 | tf_op jit(solution)/shard_map/ppermute | solution.py:126
  13.5 0.1 slice_bitcast_fusion
  13.7 5.5 %fusion = f32[128,768]{1,0:T(8,128)S(1)} fusion(bf16[128,7680]{1,0:T(8,128)(2,1)S(1)} %slice_bitcast_fusion, bf16[7680,384]{1,0:T(8,128)(2,1)} %bitcast.63, bf16[7680,384]{1,0:T(8,128)(2,1)} %bitcast.61), kind=kOutput, calls=%fused_computation.3 | convolution fusion | flops 1533542400 | bytes 14155776 | tf_op jit(solution)/shard_map/dot_general | solution.py:36
  19.2 0.2 fusion.45
  19.4 0.1 divide_convert_fusion.1
  19.6 0.1 reduce_sum.43
  19.7 0.1 reduce_sum.52
  19.8 0.1 reduce_sum.56
  19.9 0.1 reduce_sum.57
  20.0 0.7 fusion.46
  22.5 0.1 broadcast_select_fusion.3
  22.6 0.1 collective-permute-start.3
  22.7 1.8 %collective-permute-start = (bf16[1,128,768]{2,1,0:T(8,128)(2,1)S(1)}, bf16[1,128,768]{2,1,0:T(8,128)(2,1)S(1)}, u32[]{:S(2)}, u32[]{:S(2)}) collective-permute-start(bf16[1,128,768]{2,1,0:T(8,128)(2,1)S(1)} %get-tuple-element.151), channel_id=1, source_target_pairs={{0,1},{1,2},{2,3},{3,0},{4,5},{5,6},{6,7},{7,4},{8,9},{9,10},{10,1... | collective-permute-start | bytes 589832 | tf_op jit(solution)/shard_map/ppermute | solution.py:137
  24.5 1.6 %collective-permute-start.1 = (bf16[1,128,768]{2,1,0:T(8,128)(2,1)S(1)}, bf16[1,128,768]{2,1,0:T(8,128)(2,1)S(1)}, u32[]{:S(2)}, u32[]{:S(2)}) collective-permute-start(bf16[1,128,768]{2,1,0:T(8,128)(2,1)S(1)} %get-tuple-element.152), channel_id=1, source_target_pairs={{0,2},{1,3},{2,0},{3,1},{4,6},{5,7},{6,4},{7,5},{8,10},{9,11},{10,... | collective-permute-start | bytes 589832 | tf_op jit(solution)/shard_map/ppermute | solution.py:137
  26.1 1.4 %collective-permute-start.2 = (bf16[1,128,768]{2,1,0:T(8,128)(2,1)S(1)}, bf16[1,128,768]{2,1,0:T(8,128)(2,1)S(1)}, u32[]{:S(2)}, u32[]{:S(2)}) collective-permute-start(bf16[1,128,768]{2,1,0:T(8,128)(2,1)S(1)} %get-tuple-element.150), channel_id=1, source_target_pairs={{0,3},{1,0},{2,1},{3,2},{4,7},{5,4},{6,5},{7,6},{8,11},{9,8},{10,9... | collective-permute-start | bytes 589832 | tf_op jit(solution)/shard_map/ppermute | solution.py:137
  30.7 0.1 constant_dynamic-slice_fusion
  30.8 0.1 copy.6
  30.8 0.1 reshape.467
  30.9 0.8 %fusion.33 = (f32[4,384]{1,0:T(4,128)}, f32[4,384]{1,0:T(4,128)}, f32[4,384]{1,0:T(4,128)}, f32[4,384]{1,0:T(4,128)}) fusion(s32[384]{0:T(512)S(1)} %iota_add_fusion, s32[4]{0:T(128)S(1)} %get-tuple-element.176, s32[4]{0:T(128)S(1)} %get-tuple-element.177), kind=kLoop, calls=%fused_computation.70 | loop fusion | flops 27648 | bytes 26144 | tf_op jit(solution)/shard_map/sin | solution.py:20
  31.8 0.5 fusion.41.index_ref
  32.3 2.0 %collective-permute-done.3 = bf16[1,128,768]{2,1,0:T(8,128)(2,1)S(1)} collective-permute-done((bf16[1,128,768]{2,1,0:T(8,128)(2,1)S(1)}, bf16[1,128,768]{2,1,0:T(8,128)(2,1)S(1)}, u32[]{:S(2)}, u32[]{:S(2)}) %collective-permute-start.3) | collective-permute-done | bytes 196640 | tf_op jit(solution)/shard_map/ppermute | solution.py:126
  34.3 1.6 %collective-permute-start.5 = (bf16[1,128,768]{2,1,0:T(8,128)(2,1)S(1)}, bf16[1,128,768]{2,1,0:T(8,128)(2,1)S(1)}, u32[]{:S(2)}, u32[]{:S(2)}) collective-permute-start(bf16[1,128,768]{2,1,0:T(8,128)(2,1)S(1)} %get-tuple-element.149), channel_id=1, source_target_pairs={{0,1},{1,2},{2,3},{3,0},{4,5},{5,6},{6,7},{7,4},{8,9},{9,10},{10,1... | collective-permute-start | bytes 589832 | tf_op jit(solution)/shard_map/ppermute | solution.py:138
  35.9 1.5 %collective-permute-start.7 = (bf16[1,128,768]{2,1,0:T(8,128)(2,1)S(1)}, bf16[1,128,768]{2,1,0:T(8,128)(2,1)S(1)}, u32[]{:S(2)}, u32[]{:S(2)}) collective-permute-start(bf16[1,128,768]{2,1,0:T(8,128)(2,1)S(1)} %get-tuple-element.147), channel_id=1, source_target_pairs={{0,3},{1,0},{2,1},{3,2},{4,7},{5,4},{6,5},{7,6},{8,11},{9,8},{10,9... | collective-permute-start | bytes 589832 | tf_op jit(solution)/shard_map/ppermute | solution.py:138
  37.5 0.1 bitcast_dynamic-update-slice_fusion.3
  37.6 6.2 %collective-permute-done.5 = bf16[1,128,768]{2,1,0:T(8,128)(2,1)S(1)} collective-permute-done((bf16[1,128,768]{2,1,0:T(8,128)(2,1)S(1)}, bf16[1,128,768]{2,1,0:T(8,128)(2,1)S(1)}, u32[]{:S(2)}, u32[]{:S(2)}) %collective-permute-start.5) | collective-permute-done | bytes 196640 | tf_op jit(solution)/shard_map/ppermute | solution.py:138
  43.7 0.0 collective-permute-done.6
  43.8 1.7 %collective-permute-done.7 = bf16[1,128,768]{2,1,0:T(8,128)(2,1)S(1)} collective-permute-done((bf16[1,128,768]{2,1,0:T(8,128)(2,1)S(1)}, bf16[1,128,768]{2,1,0:T(8,128)(2,1)S(1)}, u32[]{:S(2)}, u32[]{:S(2)}) %collective-permute-start.7) | collective-permute-done | bytes 196640 | tf_op jit(solution)/shard_map/ppermute | solution.py:138
  45.5 1.1 %copy-done.3 = bf16[8,1,128,768]{3,2,1,0:T(8,128)(2,1)} copy-done((bf16[8,1,128,768]{3,2,1,0:T(8,128)(2,1)}, bf16[8,1,128,768]{3,2,1,0:T(8,128)(2,1)S(1)}, u32[]{:S(2)}) %copy-start.3) | copy-done | bytes 1572888
  46.7 5.7 %shard_map.37 = bf16[2,16,64,512]{3,2,1,0:T(8,128)(2,1)} custom-call(s32[8]{0:T(128)} %fusion.41.index_ref, f32[4,384]{1,0:T(4,128)} %get-tuple-element.162.cc_ref, f32[4,384]{1,0:T(4,128)} %get-tuple-element.163.sc_ref, f32[4,384]{1,0:T(4,128)} %get-tuple-element.157.cf_ref, f32[4,384]{1,0:T(4,128)} %get-tuple-element.156.sf_ref, ...), custom_call_target="tpu_custom_call" | custom-call | flops 1610612736 | bytes 3670016 | tf_op jit(solution)/shard_map/pallas_call | solution.py:98
  52.4 1.3 %dynamic-slice_bitcast_fusion = bf16[16,64,512]{2,1,0:T(8,128)(2,1)S(1)} fusion(bf16[2,16,64,512]{3,2,1,0:T(8,128)(2,1)} %shard_map.37, s32[]{:T(128)S(6)} %sub.53), kind=kLoop, calls=%fused_computation.12 | loop fusion | bytes 2097156 | tf_op jit(solution)/shard_map/jit(_take)/gather | solution.py:188
  53.7 0.1 collective-permute-start.8
  53.9 2.6 %collective-permute-done.8 = bf16[16,64,512]{2,1,0:T(8,128)(2,1)S(1)} collective-permute-done((bf16[16,64,512]{2,1,0:T(8,128)(2,1)S(1)}, bf16[16,64,512]{2,1,0:T(8,128)(2,1)S(1)}, u32[]{:S(2)}, u32[]{:S(2)}) %collective-permute-start.8) | collective-permute-done | bytes 1048608 | tf_op jit(solution)/shard_map/ppermute | solution.py:190
  56.5 1.5 %convert_add_fusion = f32[16,64,512]{2,1,0:T(8,128)S(1)} fusion(bf16[16,64,512]{2,1,0:T(8,128)(2,1)S(1)} %collective-permute-done.8, bf16[2,16,64,512]{3,2,1,0:T(8,128)(2,1)} %shard_map.37, s32[]{:T(128)S(6)} %select_n.243), kind=kLoop, calls=%fused_computation.5 | loop fusion | flops 1572864 | bytes 4194308 | tf_op jit(solution)/shard_map/add | solution.py:191
  58.0 0.1 fusion.7
  58.1 1.6 %collective-permute-start.9 = (bf16[16,32,512]{2,1,0:T(8,128)(2,1)S(1)}, bf16[16,32,512]{2,1,0:T(8,128)(2,1)S(1)}, u32[]{:S(2)}, u32[]{:S(2)}) collective-permute-start(bf16[16,32,512]{2,1,0:T(8,128)(2,1)S(1)} %fusion.7), channel_id=1, source_target_pairs={{0,16},{8,24},{16,0},{24,8},{1,17},{9,25},{17,1},{25,9},{2,18},{10... | collective-permute-start | bytes 1572872 | tf_op jit(solution)/shard_map/ppermute | solution.py:198
  59.7 12.4 %collective-permute-done.9 = bf16[16,32,512]{2,1,0:T(8,128)(2,1)S(1)} collective-permute-done((bf16[16,32,512]{2,1,0:T(8,128)(2,1)S(1)}, bf16[16,32,512]{2,1,0:T(8,128)(2,1)S(1)}, u32[]{:S(2)}, u32[]{:S(2)}) %collective-permute-start.9) | collective-permute-done | bytes 524320 | tf_op jit(solution)/shard_map/ppermute | solution.py:198
  72.1 0.2 bitcast_add_fusion
  72.3 0.4 reshape.471
  72.7 0.4 multiply_bitcast_fusion
  73.1 1.6 %copy.9 = f32[32,4,16,128]{3,2,1,0:T(8,128)} copy(f32[32,4,16,128]{3,1,0,2:T(4,128)S(1)} %multiply_bitcast_fusion) | data formatting | bytes 2097152 | tf_op jit(solution)/shard_map/div | solution.py:202
  (30 shorter events, 0.3 us)
Async XLA Ops:
  1.3 3.5 %copy-start.2 = (bf16[1,256,7680]{2,1,0:T(8,128)(2,1)S(1)}, bf16[1,256,7680]{2,1,0:T(8,128)(2,1)}, u32[]{:S(2)}) copy-start(bf16[1,256,7680]{2,1,0:T(8,128)(2,1)} %param.3) | copy-start | bytes 11796484
  4.8 2.6 %copy-start = (bf16[60,128,384]{2,1,0:T(8,128)(2,1)}, bf16[60,128,384]{2,1,0:T(8,128)(2,1)S(1)}, u32[]{:S(2)}) copy-start(bf16[60,128,384]{2,1,0:T(8,128)(2,1)S(1)} %get-tuple-element.141) | copy-start | bytes 17694724
  4.8 4.3 %copy-start.1 = (bf16[60,128,384]{2,1,0:T(8,128)(2,1)}, bf16[60,128,384]{2,1,0:T(8,128)(2,1)S(1)}, u32[]{:S(2)}) copy-start(bf16[60,128,384]{2,1,0:T(8,128)(2,1)S(1)} %get-tuple-element.142) | copy-start | bytes 17694724
  9.4 24.8 %collective-permute-start.4 = (bf16[1,128,768]{2,1,0:T(8,128)(2,1)S(1)}, bf16[1,128,768]{2,1,0:T(8,128)(2,1)S(1)}, u32[]{:S(2)}, u32[]{:S(2)}) collective-permute-start(bf16[1,128,768]{2,1,0:T(8,128)(2,1)S(1)} %pad_maximum_fusion.5), channel_id=1, source_target_pairs={{0,4},{1,5},{2,6},{3,7},{4,0},{5,1},{6,2},{7,3},{8,12},{9,13},{10,... | collective-permute-start | bytes 589832 | tf_op jit(solution)/shard_map/ppermute | solution.py:126
  13.7 5.8 %copy-start.4 = (s32[32,2]{0,1:T(2,128)S(1)}, s32[32,2]{0,1:T(2,128)}, u32[]{:S(2)}) copy-start(s32[32,2]{0,1:T(2,128)} %param.4) | copy-start | bytes 772
  22.6 11.6 %collective-permute-start.3 = (bf16[1,128,768]{2,1,0:T(8,128)(2,1)S(1)}, bf16[1,128,768]{2,1,0:T(8,128)(2,1)S(1)}, u32[]{:S(2)}, u32[]{:S(2)}) collective-permute-start(bf16[1,128,768]{2,1,0:T(8,128)(2,1)S(1)} %get-tuple-element.153), channel_id=1, source_target_pairs={{0,4},{1,5},{2,6},{3,7},{4,0},{5,1},{6,2},{7,3},{8,12},{9,13},{10,... | collective-permute-start | bytes 589832 | tf_op jit(solution)/shard_map/ppermute | solution.py:126
  22.7 13.2 %collective-permute-start = (bf16[1,128,768]{2,1,0:T(8,128)(2,1)S(1)}, bf16[1,128,768]{2,1,0:T(8,128)(2,1)S(1)}, u32[]{:S(2)}, u32[]{:S(2)}) collective-permute-start(bf16[1,128,768]{2,1,0:T(8,128)(2,1)S(1)} %get-tuple-element.151), channel_id=1, source_target_pairs={{0,1},{1,2},{2,3},{3,0},{4,5},{5,6},{6,7},{7,4},{8,9},{9,10},{10,1... | collective-permute-start | bytes 589832 | tf_op jit(solution)/shard_map/ppermute | solution.py:137
  24.5 13.0 %collective-permute-start.1 = (bf16[1,128,768]{2,1,0:T(8,128)(2,1)S(1)}, bf16[1,128,768]{2,1,0:T(8,128)(2,1)S(1)}, u32[]{:S(2)}, u32[]{:S(2)}) collective-permute-start(bf16[1,128,768]{2,1,0:T(8,128)(2,1)S(1)} %get-tuple-element.152), channel_id=1, source_target_pairs={{0,2},{1,3},{2,0},{3,1},{4,6},{5,7},{6,4},{7,5},{8,10},{9,11},{10,... | collective-permute-start | bytes 589832 | tf_op jit(solution)/shard_map/ppermute | solution.py:137
  26.1 11.4 %collective-permute-start.2 = (bf16[1,128,768]{2,1,0:T(8,128)(2,1)S(1)}, bf16[1,128,768]{2,1,0:T(8,128)(2,1)S(1)}, u32[]{:S(2)}, u32[]{:S(2)}) collective-permute-start(bf16[1,128,768]{2,1,0:T(8,128)(2,1)S(1)} %get-tuple-element.150), channel_id=1, source_target_pairs={{0,3},{1,0},{2,1},{3,2},{4,7},{5,4},{6,5},{7,6},{8,11},{9,8},{10,9... | collective-permute-start | bytes 589832 | tf_op jit(solution)/shard_map/ppermute | solution.py:137
  34.3 9.4 %collective-permute-start.5 = (bf16[1,128,768]{2,1,0:T(8,128)(2,1)S(1)}, bf16[1,128,768]{2,1,0:T(8,128)(2,1)S(1)}, u32[]{:S(2)}, u32[]{:S(2)}) collective-permute-start(bf16[1,128,768]{2,1,0:T(8,128)(2,1)S(1)} %get-tuple-element.149), channel_id=1, source_target_pairs={{0,1},{1,2},{2,3},{3,0},{4,5},{5,6},{6,7},{7,4},{8,9},{9,10},{10,1... | collective-permute-start | bytes 589832 | tf_op jit(solution)/shard_map/ppermute | solution.py:138
  35.9 7.9 %collective-permute-start.6 = (bf16[1,128,768]{2,1,0:T(8,128)(2,1)S(1)}, bf16[1,128,768]{2,1,0:T(8,128)(2,1)S(1)}, u32[]{:S(2)}, u32[]{:S(2)}) collective-permute-start(bf16[1,128,768]{2,1,0:T(8,128)(2,1)S(1)} %get-tuple-element.148), channel_id=1, source_target_pairs={{0,2},{1,3},{2,0},{3,1},{4,6},{5,7},{6,4},{7,5},{8,10},{9,11},{10,... | collective-permute-start | bytes 589832 | tf_op jit(solution)/shard_map/ppermute | solution.py:138
  35.9 9.6 %collective-permute-start.7 = (bf16[1,128,768]{2,1,0:T(8,128)(2,1)S(1)}, bf16[1,128,768]{2,1,0:T(8,128)(2,1)S(1)}, u32[]{:S(2)}, u32[]{:S(2)}) collective-permute-start(bf16[1,128,768]{2,1,0:T(8,128)(2,1)S(1)} %get-tuple-element.147), channel_id=1, source_target_pairs={{0,3},{1,0},{2,1},{3,2},{4,7},{5,4},{6,5},{7,6},{8,11},{9,8},{10,9... | collective-permute-start | bytes 589832 | tf_op jit(solution)/shard_map/ppermute | solution.py:138
  45.5 1.2 %copy-start.3 = (bf16[8,1,128,768]{3,2,1,0:T(8,128)(2,1)}, bf16[8,1,128,768]{3,2,1,0:T(8,128)(2,1)S(1)}, u32[]{:S(2)}) copy-start(bf16[8,1,128,768]{3,2,1,0:T(8,128)(2,1)S(1)} %bitcast_dynamic-update-slice_fusion.left_ref.right_ref) | copy-start | bytes 4718596
  52.4 7.3 %copy-start.5 = (s32[4]{0:T(128)S(1)}, s32[4]{0:T(128)}, u32[]{:S(2)}) copy-start(s32[4]{0:T(128)} %param.5) | copy-start | bytes 52
  53.7 2.7 %collective-permute-start.8 = (bf16[16,64,512]{2,1,0:T(8,128)(2,1)S(1)}, bf16[16,64,512]{2,1,0:T(8,128)(2,1)S(1)}, u32[]{:S(2)}, u32[]{:S(2)}) collective-permute-start(bf16[16,64,512]{2,1,0:T(8,128)(2,1)S(1)} %dynamic-slice_bitcast_fusion), channel_id=1, source_target_pairs={{0,8},{8,0},{16,24},{24,16},{1,9},{9,1},{17,25},{25,17},{2,10},{10... | collective-permute-start | bytes 3145736 | tf_op jit(solution)/shard_map/ppermute | solution.py:190
  58.1 14.0 %collective-permute-start.9 = (bf16[16,32,512]{2,1,0:T(8,128)(2,1)S(1)}, bf16[16,32,512]{2,1,0:T(8,128)(2,1)S(1)}, u32[]{:S(2)}, u32[]{:S(2)}) collective-permute-start(bf16[16,32,512]{2,1,0:T(8,128)(2,1)S(1)} %fusion.7), channel_id=1, source_target_pairs={{0,16},{8,24},{16,0},{24,8},{1,17},{9,25},{17,1},{25,9},{2,18},{10... | collective-permute-start | bytes 1572872 | tf_op jit(solution)/shard_map/ppermute | solution.py:198

commit v16 on v12

--- a/solution.py
+++ b/solution.py
@@ -42,13 +42,15 @@
     return jnp.concatenate([real_part / divisor, imag_part / divisor], axis=1).astype(jnp.bfloat16)
 
 
-def correlation_kernel(sub, n_y, own_rows, index_ref, cc_ref, sc_ref, cf_ref, sf_ref, left_ref, right_ref, out_ref):
+def correlation_kernel(sub, n_y, own_rows, index_ref, cc_ref, sc_ref, cf_ref, sf_ref, left_ref, right_ref, send_ref, keep_ref):
     window_count = left_ref.shape[1]
-    order = [(y * 2 + c) * own_rows for c in range(2) for y in range(n_y)]
+    partner = 1 - lax.axis_index("win") % 2
+    orders = [[(y * 2 + c) * own_rows for c in (1 - first, first) for y in range(n_y)] for first in (1, 0)]
     acc = None
     for w in range(window_count):
         left = left_ref[0, w].astype(jnp.float32)
-        left = jnp.concatenate([left[r : r + own_rows] for r in order], axis=0)
+        by_order = [jnp.concatenate([left[r : r + own_rows] for r in order], axis=0) for order in orders]
+        left = jnp.where(partner == 0, by_order[0], by_order[1])
         lre = left[:, :F]
         lim = left[:, F:]
         rre = right_ref[0, w, :, :F].astype(jnp.float32)
@@ -79,7 +81,8 @@
         for l1 in range(sub):
             for part in range(2):
                 rows = l2 * C + part * half_rows
-                out_ref[part, l2 * sub + l1] = acc[rows : rows + half_rows, l1 * C : (l1 + 1) * C].astype(out_ref.dtype)
+                out_ref = (send_ref, keep_ref)[part]
+                out_ref[l2 * sub + l1] = acc[rows : rows + half_rows, l1 * C : (l1 + 1) * C].astype(out_ref.dtype)
 
 
 def tile_correlation(cc, sc, cf, sf, incoming, slots, sub, n_y, own_rows):
@@ -93,12 +96,12 @@
         num_scalar_prefetch=1,
         grid=(slot_count,),
         in_specs=[table_spec] * 4 + [left_spec, right_spec],
-        out_specs=pl.BlockSpec((2, LAGS, C // 2, C), lambda t, idx: (0, 0, 0, t)),
+        out_specs=[pl.BlockSpec((LAGS, C // 2, C), lambda t, idx: (0, 0, t))] * 2,
     )
     return pl.pallas_call(
         functools.partial(correlation_kernel, sub, n_y, own_rows),
         grid_spec=grid_spec,
-        out_shape=jax.ShapeDtypeStruct((2, LAGS, C // 2, slot_count * C), jnp.bfloat16),
+        out_shape=[jax.ShapeDtypeStruct((LAGS, C // 2, slot_count * C), jnp.bfloat16)] * 2,
         cost_estimate=pl.CostEstimate(
             flops=flops, transcendentals=0, bytes_accessed=slot_count * (4 * window_count * C * F * 2 + 2 * C * LAGS * C)
         ),
@@ -185,8 +188,8 @@
 
     core = win_here % 2
     y_here = win_here // 2
-    send = jnp.take(corr, 1 - core, axis=0, mode="clip")
-    keep = jnp.take(corr, core, axis=0, mode="clip").astype(jnp.float32)
+    send, keep = corr
+    keep = keep.astype(jnp.float32)
     got = lax.ppermute(send, "win", [(w, w ^ 1) for w in range(n_win)])
     half = (keep + got.astype(jnp.float32)).reshape(LAGS, n_y, own_rows, slot_count * C)
     half = jnp.transpose(half, (1, 0, 2, 3))

time: 74.3 us -> 73.1 us (0.984)
  local copies, waits for them, and re-layouts: 5.68 us -> 4.35 us
    gather x1 -> x0, local copies, waits for them, and re-layouts: 1.33 us -> none  [body(): send = jnp.take(corr, 1 - core, axis=0, mode='clip')]
where the time goes in v16:
time: 73.1 us; the launch traced here: 72.8 us
  waiting for transfers between devices  30.9 us (42%)
  starting transfers between devices  14 us (19%)
  other arithmetic  9.14 us (13%)
  Pallas kernels  5.74 us (8%)
  between operations  5.31 us (7%)
  local copies, waits for them, and re-layouts  4.35 us (6%)
  matrix products  3.38 us (5%)
    ppermute x1, waiting for transfers between devices, body(): total = total + lax.ppermute(piece, 'win', perm).astype(jnp.float32)  12.7 us
    ppermute x2, waiting for transfers between devices, exchange_by_halves(): lax.ppermute(block, 'pair', across)  8.02 us
    ppermute x3, waiting for transfers between devices, exchange_by_halves(): relay = lax.ppermute(relay, 'pair', perm)  7.37 us
    pallas_call x1, Pallas kernels, tile_correlation(): pl.pallas_call(functools.partial(correlation_kernel, sub, n_y, own_rows),...  5.74 us
    ppermute x3, starting transfers between devices, exchange_by_halves(): own = lax.ppermute(own, 'pair', perm)  4.76 us
    ppermute x2, starting transfers between devices, exchange_by_halves(): lax.ppermute(block, 'pair', across)  4.18 us
    another operation x3, other arithmetic  3.72 us
    ppermute x3, starting transfers between devices, exchange_by_halves(): relay = lax.ppermute(relay, 'pair', perm)  3.64 us
  transfers between devices with their start and end apart: 10, of which 7 were waited for; matrix products, arithmetic and copies ran while one was open for 2% of the time, Pallas kernels for 0%

profile of v16, /device:TPU:0, one launch (start us, length us, event | category | flops | bytes accessed | tf_op | source)
XLA Modules:
  0.0 72.8 jit_solution(12611812807126906000)
XLA Ops:
  0.0 0.8 %fusion.19 = (f32[128,384]{1,0:T(8,128)S(1)}, f32[128,384]{1,0:T(8,128)S(1)}) fusion(s32[384]{0:T(512)S(1)} %iota_add_fusion), kind=kLoop, calls=%fused_computation.40 | loop fusion | flops 442368 | bytes 394752 | tf_op jit(solution)/shard_map/cos | solution.py:20
  0.8 0.5 fusion.26
  1.3 0.0 copy-start.2
  1.3 3.5 %subtract_convert_fusion = (bf16[60,128,384]{2,1,0:T(8,128)(2,1)S(1)}, bf16[60,128,384]{2,1,0:T(8,128)(2,1)S(1)}) fusion(f32[128,384]{1,0:T(8,128)S(1)} %get-tuple-element.142, f32[60,384]{1,0:T(8,128)S(1)} %get-tuple-element.136, f32[128,384]{1,0:T(8,128)S(1)} %get-tuple-element.141, f32[60,384]{1,0:T(8,128)S(1)} %get-tuple-element.135), kind=kLoop, calls=%fused_computation.2 | loop fusion | flops 26542080 | bytes 12374016 | tf_op jit(solution)/shard_map/convert.19
  4.8 1.7 %fusion.6 = f32[128,768]{1,0:T(8,128)S(1)} fusion(bf16[7680,384]{1,0:T(8,128)(2,1)S(1)} %bitcast.61, bf16[7680,384]{1,0:T(8,128)(2,1)S(1)} %bitcast.59, bf16[1,256,7680]{2,1,0:T(8,128)(2,1)S(1)} %copy-done.2), kind=kOutput, calls=%fused_computation.10 | convolution fusion | flops 1533542400 | bytes 14155776 | tf_op jit(solution)/shard_map/dot_general | solution.py:36
  6.5 0.0 copy-start.1
  6.5 1.7 %fusion.9 = f32[128,768]{1,0:T(8,128)S(1)} fusion(bf16[7680,384]{1,0:T(8,128)(2,1)S(1)} %bitcast.62, bf16[7680,384]{1,0:T(8,128)(2,1)S(1)} %bitcast.60, bf16[1,256,7680]{2,1,0:T(8,128)(2,1)S(1)} %copy-done.2), kind=kOutput, calls=%fused_computation.11 | convolution fusion | flops 1533542400 | bytes 14155776 | tf_op jit(solution)/shard_map/dot_general | solution.py:36
  8.3 0.1 reduce_sum.43
  8.4 0.1 reduce_sum.52
  8.5 0.1 reduce_sum.56
  8.6 0.1 reduce_sum.57
  8.7 0.7 fusion.51
  11.2 0.2 fusion.49
  11.4 0.1 divide_convert_fusion.1
  11.6 0.1 divide_convert_fusion.3
  11.7 0.1 broadcast_select_fusion.3
  11.8 4.1 %collective-permute-start.3 = (bf16[1,128,768]{2,1,0:T(8,128)(2,1)S(1)}, bf16[1,128,768]{2,1,0:T(8,128)(2,1)S(1)}, u32[]{:S(2)}, u32[]{:S(2)}) collective-permute-start(bf16[1,128,768]{2,1,0:T(8,128)(2,1)S(1)} %get-tuple-element.134), channel_id=1, source_target_pairs={{0,4},{1,5},{2,6},{3,7},{4,0},{5,1},{6,2},{7,3},{8,12},{9,13},{10,... | collective-permute-start | bytes 589832 | tf_op jit(solution)/shard_map/ppermute | solution.py:129
  15.9 0.1 collective-permute-start.4
  16.0 1.7 %collective-permute-start = (bf16[1,128,768]{2,1,0:T(8,128)(2,1)S(1)}, bf16[1,128,768]{2,1,0:T(8,128)(2,1)S(1)}, u32[]{:S(2)}, u32[]{:S(2)}) collective-permute-start(bf16[1,128,768]{2,1,0:T(8,128)(2,1)S(1)} %get-tuple-element.131), channel_id=1, source_target_pairs={{0,1},{1,2},{2,3},{3,0},{4,5},{5,6},{6,7},{7,4},{8,9},{9,10},{10,1... | collective-permute-start | bytes 589832 | tf_op jit(solution)/shard_map/ppermute | solution.py:140
  17.7 1.6 %collective-permute-start.1 = (bf16[1,128,768]{2,1,0:T(8,128)(2,1)S(1)}, bf16[1,128,768]{2,1,0:T(8,128)(2,1)S(1)}, u32[]{:S(2)}, u32[]{:S(2)}) collective-permute-start(bf16[1,128,768]{2,1,0:T(8,128)(2,1)S(1)} %get-tuple-element.132), channel_id=1, source_target_pairs={{0,2},{1,3},{2,0},{3,1},{4,6},{5,7},{6,4},{7,5},{8,10},{9,11},{10,... | collective-permute-start | bytes 589832 | tf_op jit(solution)/shard_map/ppermute | solution.py:140
  19.3 1.4 %collective-permute-start.2 = (bf16[1,128,768]{2,1,0:T(8,128)(2,1)S(1)}, bf16[1,128,768]{2,1,0:T(8,128)(2,1)S(1)}, u32[]{:S(2)}, u32[]{:S(2)}) collective-permute-start(bf16[1,128,768]{2,1,0:T(8,128)(2,1)S(1)} %get-tuple-element.130), channel_id=1, source_target_pairs={{0,3},{1,0},{2,1},{3,2},{4,7},{5,4},{6,5},{7,6},{8,11},{9,8},{10,9... | collective-permute-start | bytes 589832 | tf_op jit(solution)/shard_map/ppermute | solution.py:140
  23.9 0.1 constant_dynamic-slice_fusion
  24.0 0.1 copy.7
  24.1 0.1 reshape.467
  24.2 0.8 %fusion.38 = (f32[4,384]{1,0:T(4,128)}, f32[4,384]{1,0:T(4,128)}, f32[4,384]{1,0:T(4,128)}, f32[4,384]{1,0:T(4,128)}) fusion(s32[384]{0:T(512)S(1)} %iota_add_fusion, s32[4]{0:T(128)S(1)} %get-tuple-element.157, s32[4]{0:T(128)S(1)} %get-tuple-element.158), kind=kLoop, calls=%fused_computation.71 | loop fusion | flops 27648 | bytes 26144 | tf_op jit(solution)/shard_map/sin | solution.py:20
  25.0 0.5 fusion.46.index_ref
  25.5 4.6 %collective-permute-done.3 = bf16[1,128,768]{2,1,0:T(8,128)(2,1)S(1)} collective-permute-done((bf16[1,128,768]{2,1,0:T(8,128)(2,1)S(1)}, bf16[1,128,768]{2,1,0:T(8,128)(2,1)S(1)}, u32[]{:S(2)}, u32[]{:S(2)}) %collective-permute-start.3) | collective-permute-done | bytes 196640 | tf_op jit(solution)/shard_map/ppermute | solution.py:129
  30.2 3.4 %collective-permute-done.4 = bf16[1,128,768]{2,1,0:T(8,128)(2,1)S(1)} collective-permute-done((bf16[1,128,768]{2,1,0:T(8,128)(2,1)S(1)}, bf16[1,128,768]{2,1,0:T(8,128)(2,1)S(1)}, u32[]{:S(2)}, u32[]{:S(2)}) %collective-permute-start.4) | collective-permute-done | bytes 196640 | tf_op jit(solution)/shard_map/ppermute | solution.py:129
  33.6 1.6 %collective-permute-start.5 = (bf16[1,128,768]{2,1,0:T(8,128)(2,1)S(1)}, bf16[1,128,768]{2,1,0:T(8,128)(2,1)S(1)}, u32[]{:S(2)}, u32[]{:S(2)}) collective-permute-start(bf16[1,128,768]{2,1,0:T(8,128)(2,1)S(1)} %get-tuple-element.129), channel_id=1, source_target_pairs={{0,1},{1,2},{2,3},{3,0},{4,5},{5,6},{6,7},{7,4},{8,9},{9,10},{10,1... | collective-permute-start | bytes 589832 | tf_op jit(solution)/shard_map/ppermute | solution.py:141
  35.2 0.6 collective-permute-start.6
  35.8 0.0 collective-permute-done
  35.8 1.4 %collective-permute-start.7 = (bf16[1,128,768]{2,1,0:T(8,128)(2,1)S(1)}, bf16[1,128,768]{2,1,0:T(8,128)(2,1)S(1)}, u32[]{:S(2)}, u32[]{:S(2)}) collective-permute-start(bf16[1,128,768]{2,1,0:T(8,128)(2,1)S(1)} %get-tuple-element.127), channel_id=1, source_target_pairs={{0,3},{1,0},{2,1},{3,2},{4,7},{5,4},{6,5},{7,6},{8,11},{9,8},{10,9... | collective-permute-start | bytes 589832 | tf_op jit(solution)/shard_map/ppermute | solution.py:141
  37.3 0.1 bitcast_dynamic-update-slice_fusion.3
  37.4 5.0 %collective-permute-done.5 = bf16[1,128,768]{2,1,0:T(8,128)(2,1)S(1)} collective-permute-done((bf16[1,128,768]{2,1,0:T(8,128)(2,1)S(1)}, bf16[1,128,768]{2,1,0:T(8,128)(2,1)S(1)}, u32[]{:S(2)}, u32[]{:S(2)}) %collective-permute-start.5) | collective-permute-done | bytes 196640 | tf_op jit(solution)/shard_map/ppermute | solution.py:141
  42.4 0.3 collective-permute-done.6
  42.8 2.0 %collective-permute-done.7 = bf16[1,128,768]{2,1,0:T(8,128)(2,1)S(1)} collective-permute-done((bf16[1,128,768]{2,1,0:T(8,128)(2,1)S(1)}, bf16[1,128,768]{2,1,0:T(8,128)(2,1)S(1)}, u32[]{:S(2)}, u32[]{:S(2)}) %collective-permute-start.7) | collective-permute-done | bytes 196640 | tf_op jit(solution)/shard_map/ppermute | solution.py:141
  44.8 1.1 %copy-done = bf16[8,1,128,768]{3,2,1,0:T(8,128)(2,1)} copy-done((bf16[8,1,128,768]{3,2,1,0:T(8,128)(2,1)}, bf16[8,1,128,768]{3,2,1,0:T(8,128)(2,1)S(1)}, u32[]{:S(2)}) %copy-start) | copy-done | bytes 1572888
  45.9 5.7 %shard_map.37 = (bf16[16,64,512]{2,1,0:T(8,128)(2,1)}, bf16[16,64,512]{2,1,0:T(8,128)(2,1)}) custom-call(s32[8]{0:T(128)} %fusion.46.index_ref, f32[4,384]{1,0:T(4,128)} %get-tuple-element.143.cc_ref, f32[4,384]{1,0:T(4,128)} %get-tuple-element.144.sc_ref, f32[4,384]{1,0:T(4,128)} %get-tuple-element.138.cf_ref, f32[4,384]{1,0:T(4,128)} %get-tuple-element.137.sf_ref, ...), custom_call_target="tpu_custom_call" | custom-call | flops 1610612736 | bytes 3670016 | tf_op jit(solution)/shard_map/pallas_call | solution.py:101
  51.7 0.0 collective-permute-start.8
  51.8 2.8 %collective-permute-done.8 = bf16[16,64,512]{2,1,0:T(8,128)(2,1)S(1)} collective-permute-done((bf16[16,64,512]{2,1,0:T(8,128)(2,1)}, bf16[16,64,512]{2,1,0:T(8,128)(2,1)S(1)}, u32[]{:S(2)}, u32[]{:S(2)}) %collective-permute-start.8) | collective-permute-done | bytes 1048608 | tf_op jit(solution)/shard_map/ppermute | solution.py:193
  54.6 1.5 %convert_add_fusion = f32[16,64,512]{2,1,0:T(8,128)S(1)} fusion(bf16[16,64,512]{2,1,0:T(8,128)(2,1)S(1)} %collective-permute-done.8, bf16[16,64,512]{2,1,0:T(8,128)(2,1)} %get-tuple-element.7), kind=kLoop, calls=%fused_computation.5 | loop fusion | flops 1572864 | bytes 4194304 | tf_op jit(solution)/shard_map/add | solution.py:194
  56.1 0.1 fusion.12
  56.2 1.3 %collective-permute-start.9 = (bf16[16,32,512]{2,1,0:T(8,128)(2,1)S(1)}, bf16[16,32,512]{2,1,0:T(8,128)(2,1)S(1)}, u32[]{:S(2)}, u32[]{:S(2)}) collective-permute-start(bf16[16,32,512]{2,1,0:T(8,128)(2,1)S(1)} %fusion.12), channel_id=1, source_target_pairs={{0,16},{8,24},{16,0},{24,8},{1,17},{9,25},{17,1},{25,9},{2,18},{10... | collective-permute-start | bytes 1572872 | tf_op jit(solution)/shard_map/ppermute | solution.py:201
  57.6 12.7 %collective-permute-done.9 = bf16[16,32,512]{2,1,0:T(8,128)(2,1)S(1)} collective-permute-done((bf16[16,32,512]{2,1,0:T(8,128)(2,1)S(1)}, bf16[16,32,512]{2,1,0:T(8,128)(2,1)S(1)}, u32[]{:S(2)}, u32[]{:S(2)}) %collective-permute-start.9) | collective-permute-done | bytes 524320 | tf_op jit(solution)/shard_map/ppermute | solution.py:201
  70.3 0.2 bitcast_add_fusion
  70.4 0.4 reshape.471
  70.8 0.4 multiply_bitcast_fusion
  71.2 1.6 %copy.11 = f32[32,4,16,128]{3,2,1,0:T(8,128)} copy(f32[32,4,16,128]{3,1,0,2:T(4,128)S(1)} %multiply_bitcast_fusion) | data formatting | bytes 2097152 | tf_op jit(solution)/shard_map/div | solution.py:205
  (22 shorter events, 0.2 us)
Async XLA Ops:
  1.3 3.5 %copy-start.2 = (bf16[1,256,7680]{2,1,0:T(8,128)(2,1)S(1)}, bf16[1,256,7680]{2,1,0:T(8,128)(2,1)}, u32[]{:S(2)}) copy-start(bf16[1,256,7680]{2,1,0:T(8,128)(2,1)} %param.3) | copy-start | bytes 11796484
  6.5 1.8 %copy-start.1 = (s32[32,2]{0,1:T(2,128)S(1)}, s32[32,2]{0,1:T(2,128)}, u32[]{:S(2)}) copy-start(s32[32,2]{0,1:T(2,128)} %param.4) | copy-start | bytes 772
  11.8 18.4 %collective-permute-start.3 = (bf16[1,128,768]{2,1,0:T(8,128)(2,1)S(1)}, bf16[1,128,768]{2,1,0:T(8,128)(2,1)S(1)}, u32[]{:S(2)}, u32[]{:S(2)}) collective-permute-start(bf16[1,128,768]{2,1,0:T(8,128)(2,1)S(1)} %get-tuple-element.134), channel_id=1, source_target_pairs={{0,4},{1,5},{2,6},{3,7},{4,0},{5,1},{6,2},{7,3},{8,12},{9,13},{10,... | collective-permute-start | bytes 589832 | tf_op jit(solution)/shard_map/ppermute | solution.py:129
  15.9 17.6 %collective-permute-start.4 = (bf16[1,128,768]{2,1,0:T(8,128)(2,1)S(1)}, bf16[1,128,768]{2,1,0:T(8,128)(2,1)S(1)}, u32[]{:S(2)}, u32[]{:S(2)}) collective-permute-start(bf16[1,128,768]{2,1,0:T(8,128)(2,1)S(1)} %get-tuple-element.133), channel_id=1, source_target_pairs={{0,4},{1,5},{2,6},{3,7},{4,0},{5,1},{6,2},{7,3},{8,12},{9,13},{10,... | collective-permute-start | bytes 589832 | tf_op jit(solution)/shard_map/ppermute | solution.py:129
  16.0 19.8 %collective-permute-start = (bf16[1,128,768]{2,1,0:T(8,128)(2,1)S(1)}, bf16[1,128,768]{2,1,0:T(8,128)(2,1)S(1)}, u32[]{:S(2)}, u32[]{:S(2)}) collective-permute-start(bf16[1,128,768]{2,1,0:T(8,128)(2,1)S(1)} %get-tuple-element.131), channel_id=1, source_target_pairs={{0,1},{1,2},{2,3},{3,0},{4,5},{5,6},{6,7},{7,4},{8,9},{9,10},{10,1... | collective-permute-start | bytes 589832 | tf_op jit(solution)/shard_map/ppermute | solution.py:140
  17.7 19.5 %collective-permute-start.1 = (bf16[1,128,768]{2,1,0:T(8,128)(2,1)S(1)}, bf16[1,128,768]{2,1,0:T(8,128)(2,1)S(1)}, u32[]{:S(2)}, u32[]{:S(2)}) collective-permute-start(bf16[1,128,768]{2,1,0:T(8,128)(2,1)S(1)} %get-tuple-element.132), channel_id=1, source_target_pairs={{0,2},{1,3},{2,0},{3,1},{4,6},{5,7},{6,4},{7,5},{8,10},{9,11},{10,... | collective-permute-start | bytes 589832 | tf_op jit(solution)/shard_map/ppermute | solution.py:140
  19.3 18.0 %collective-permute-start.2 = (bf16[1,128,768]{2,1,0:T(8,128)(2,1)S(1)}, bf16[1,128,768]{2,1,0:T(8,128)(2,1)S(1)}, u32[]{:S(2)}, u32[]{:S(2)}) collective-permute-start(bf16[1,128,768]{2,1,0:T(8,128)(2,1)S(1)} %get-tuple-element.130), channel_id=1, source_target_pairs={{0,3},{1,0},{2,1},{3,2},{4,7},{5,4},{6,5},{7,6},{8,11},{9,8},{10,9... | collective-permute-start | bytes 589832 | tf_op jit(solution)/shard_map/ppermute | solution.py:140
  33.6 8.8 %collective-permute-start.5 = (bf16[1,128,768]{2,1,0:T(8,128)(2,1)S(1)}, bf16[1,128,768]{2,1,0:T(8,128)(2,1)S(1)}, u32[]{:S(2)}, u32[]{:S(2)}) collective-permute-start(bf16[1,128,768]{2,1,0:T(8,128)(2,1)S(1)} %get-tuple-element.129), channel_id=1, source_target_pairs={{0,1},{1,2},{2,3},{3,0},{4,5},{5,6},{6,7},{7,4},{8,9},{9,10},{10,1... | collective-permute-start | bytes 589832 | tf_op jit(solution)/shard_map/ppermute | solution.py:141
  35.2 7.6 %collective-permute-start.6 = (bf16[1,128,768]{2,1,0:T(8,128)(2,1)S(1)}, bf16[1,128,768]{2,1,0:T(8,128)(2,1)S(1)}, u32[]{:S(2)}, u32[]{:S(2)}) collective-permute-start(bf16[1,128,768]{2,1,0:T(8,128)(2,1)S(1)} %get-tuple-element.128), channel_id=1, source_target_pairs={{0,2},{1,3},{2,0},{3,1},{4,6},{5,7},{6,4},{7,5},{8,10},{9,11},{10,... | collective-permute-start | bytes 589832 | tf_op jit(solution)/shard_map/ppermute | solution.py:141
  35.8 9.0 %collective-permute-start.7 = (bf16[1,128,768]{2,1,0:T(8,128)(2,1)S(1)}, bf16[1,128,768]{2,1,0:T(8,128)(2,1)S(1)}, u32[]{:S(2)}, u32[]{:S(2)}) collective-permute-start(bf16[1,128,768]{2,1,0:T(8,128)(2,1)S(1)} %get-tuple-element.127), channel_id=1, source_target_pairs={{0,3},{1,0},{2,1},{3,2},{4,7},{5,4},{6,5},{7,6},{8,11},{9,8},{10,9... | collective-permute-start | bytes 589832 | tf_op jit(solution)/shard_map/ppermute | solution.py:141
  44.8 1.1 %copy-start = (bf16[8,1,128,768]{3,2,1,0:T(8,128)(2,1)}, bf16[8,1,128,768]{3,2,1,0:T(8,128)(2,1)S(1)}, u32[]{:S(2)}) copy-start(bf16[8,1,128,768]{3,2,1,0:T(8,128)(2,1)S(1)} %bitcast_dynamic-update-slice_fusion.left_ref.right_ref) | copy-start | bytes 4718596
  51.7 5.9 %copy-start.3 = (s32[4]{0:T(128)S(1)}, s32[4]{0:T(128)}, u32[]{:S(2)}) copy-start(s32[4]{0:T(128)} %param.5) | copy-start | bytes 52
  51.7 2.9 %collective-permute-start.8 = (bf16[16,64,512]{2,1,0:T(8,128)(2,1)}, bf16[16,64,512]{2,1,0:T(8,128)(2,1)S(1)}, u32[]{:S(2)}, u32[]{:S(2)}) collective-permute-start(bf16[16,64,512]{2,1,0:T(8,128)(2,1)} %get-tuple-element.8), channel_id=1, source_target_pairs={{0,8},{8,0},{16,24},{24,16},{1,9},{9,1},{17,25},{25,17},{2,10},{10... | collective-permute-start | bytes 3145736 | tf_op jit(solution)/shard_map/ppermute | solution.py:193
  56.2 14.0 %collective-permute-start.9 = (bf16[16,32,512]{2,1,0:T(8,128)(2,1)S(1)}, bf16[16,32,512]{2,1,0:T(8,128)(2,1)S(1)}, u32[]{:S(2)}, u32[]{:S(2)}) collective-permute-start(bf16[16,32,512]{2,1,0:T(8,128)(2,1)S(1)} %fusion.12), channel_id=1, source_target_pairs={{0,16},{8,24},{16,0},{24,8},{1,17},{9,25},{17,1},{25,9},{2,18},{10... | collective-permute-start | bytes 1572872 | tf_op jit(solution)/shard_map/ppermute | solution.py:201

commit v17 on v16

--- a/solution.py
+++ b/solution.py
@@ -191,14 +191,21 @@
     send, keep = corr
     keep = keep.astype(jnp.float32)
     got = lax.ppermute(send, "win", [(w, w ^ 1) for w in range(n_win)])
-    half = (keep + got.astype(jnp.float32)).reshape(LAGS, n_y, own_rows, slot_count * C)
-    half = jnp.transpose(half, (1, 0, 2, 3))
-    total = jnp.take(half, y_here, axis=0, mode="clip")
+    keep = keep.reshape(LAGS, n_y, own_rows, slot_count * C)
+    got = got.reshape(LAGS, n_y, own_rows, slot_count * C)
+
+    def chip_sum(y):
+        pick = lambda a: jnp.take(a, y, axis=1, mode="clip")
+        return pick(keep) + pick(got).astype(jnp.float32)
+
+    pieces = []
     for shift in range(1, n_y):
         dest = (y_here + shift) % n_y
-        piece = jnp.take(half, dest, axis=0, mode="clip").astype(jnp.bfloat16)
         perm = [(w, ((w // 2 + shift) % n_y) * 2 + w % 2) for w in range(n_win)]
-        total = total + lax.ppermute(piece, "win", perm).astype(jnp.float32)
+        pieces.append(lax.ppermute(chip_sum(dest).astype(jnp.bfloat16), "win", perm))
+    total = chip_sum(y_here)
+    for piece in pieces:
+        total = total + piece.astype(jnp.float32)
     total = jnp.transpose(total.reshape(LAGS, own_rows, slot_count, C), (1, 2, 0, 3))
 
     live_local = tile_live.astype(jnp.float32)

time: 73.1 us -> 71.6 us (0.979)
  waiting for transfers between devices: 30.9 us -> 29.4 us
    ppermute x1, waiting for transfers between devices: 2.83 us -> 1.33 us  [body(): got = lax.ppermute(send, 'win', [(w, w ^ 1) for w in range(n_win)])]
    reshape x0 -> x1, other arithmetic: none -> 1.49 us  [body(): keep = keep.reshape(LAGS, n_y, own_rows, slot_count * C)]
    add x2 -> x1, other arithmetic: 1.72 us -> 0.23 us  [body(): total = total + piece.astype(jnp.float32)]
  transfers between devices with their start and end apart: 10 -> 10, of which waited for: 7 -> 7; matrix products, arithmetic and copies ran while one was open for 2% -> 5% of each run, Pallas kernels for 0% -> 0%
where the time goes in v17:
time: 71.6 us; the launch traced here: 71.3 us
  waiting for transfers between devices  29.4 us (41%)
  starting transfers between devices  13.9 us (19%)
  other arithmetic  9.3 us (13%)
  Pallas kernels  5.74 us (8%)
  between operations  5.31 us (7%)
  local copies, waits for them, and re-layouts  4.27 us (6%)
  matrix products  3.38 us (5%)
    ppermute x1, waiting for transfers between devices, body(): lax.ppermute(chip_sum(dest).astype(jnp.bfloat16), 'win', perm)  12.7 us
    ppermute x2, waiting for transfers between devices, exchange_by_halves(): lax.ppermute(block, 'pair', across)  8.02 us
    ppermute x3, waiting for transfers between devices, exchange_by_halves(): relay = lax.ppermute(relay, 'pair', perm)  7.36 us
    pallas_call x1, Pallas kernels, tile_correlation(): pl.pallas_call(functools.partial(correlation_kernel, sub, n_y, own_rows),...  5.74 us
    ppermute x3, starting transfers between devices, exchange_by_halves(): own = lax.ppermute(own, 'pair', perm)  4.76 us
    ppermute x2, starting transfers between devices, exchange_by_halves(): lax.ppermute(block, 'pair', across)  4.18 us
    another operation x3, other arithmetic  3.72 us
    ppermute x3, starting transfers between devices, exchange_by_halves(): relay = lax.ppermute(relay, 'pair', perm)  3.64 us
  transfers between devices with their start and end apart: 10, of which 7 were waited for; matrix products, arithmetic and copies ran while one was open for 5% of the time, Pallas kernels for 0%

profile of v17, /device:TPU:0, one launch (start us, length us, event | category | flops | bytes accessed | tf_op | source)
XLA Modules:
  0.0 71.3 jit_solution(9585295248255038059)
XLA Ops:
  0.0 0.8 %fusion.22 = (f32[128,384]{1,0:T(8,128)S(1)}, f32[128,384]{1,0:T(8,128)S(1)}) fusion(s32[384]{0:T(512)S(1)} %iota_add_fusion), kind=kLoop, calls=%fused_computation.42 | loop fusion | flops 442368 | bytes 394752 | tf_op jit(solution)/shard_map/cos | solution.py:20
  0.8 0.5 fusion.29
  1.3 0.0 copy-start.2
  1.3 3.5 %subtract_convert_fusion = (bf16[60,128,384]{2,1,0:T(8,128)(2,1)S(1)}, bf16[60,128,384]{2,1,0:T(8,128)(2,1)S(1)}) fusion(f32[128,384]{1,0:T(8,128)S(1)} %get-tuple-element.164, f32[60,384]{1,0:T(8,128)S(1)} %get-tuple-element.158, f32[128,384]{1,0:T(8,128)S(1)} %get-tuple-element.163, f32[60,384]{1,0:T(8,128)S(1)} %get-tuple-element.157), kind=kLoop, calls=%fused_computation.2 | loop fusion | flops 26542080 | bytes 12374016 | tf_op jit(solution)/shard_map/convert.20
  4.8 1.7 %fusion.6 = f32[128,768]{1,0:T(8,128)S(1)} fusion(bf16[7680,384]{1,0:T(8,128)(2,1)S(1)} %bitcast.75, bf16[7680,384]{1,0:T(8,128)(2,1)S(1)} %bitcast.73, bf16[1,256,7680]{2,1,0:T(8,128)(2,1)S(1)} %copy-done.2), kind=kOutput, calls=%fused_computation.9 | convolution fusion | flops 1533542400 | bytes 14155776 | tf_op jit(solution)/shard_map/dot_general | solution.py:36
  6.5 0.0 copy-start.1
  6.5 1.7 %fusion.9 = f32[128,768]{1,0:T(8,128)S(1)} fusion(bf16[7680,384]{1,0:T(8,128)(2,1)S(1)} %bitcast.76, bf16[7680,384]{1,0:T(8,128)(2,1)S(1)} %bitcast.74, bf16[1,256,7680]{2,1,0:T(8,128)(2,1)S(1)} %copy-done.2), kind=kOutput, calls=%fused_computation.10 | convolution fusion | flops 1533542400 | bytes 14155776 | tf_op jit(solution)/shard_map/dot_general | solution.py:36
  8.3 0.1 reduce_sum.43
  8.4 0.1 reduce_sum.52
  8.5 0.1 reduce_sum.56
  8.6 0.1 reduce_sum.57
  8.7 0.7 fusion.54
  11.2 0.2 fusion.52
  11.4 0.1 divide_convert_fusion.1
  11.6 0.1 divide_convert_fusion.3
  11.7 0.1 broadcast_select_fusion.3
  11.8 4.1 %collective-permute-start.3 = (bf16[1,128,768]{2,1,0:T(8,128)(2,1)S(1)}, bf16[1,128,768]{2,1,0:T(8,128)(2,1)S(1)}, u32[]{:S(2)}, u32[]{:S(2)}) collective-permute-start(bf16[1,128,768]{2,1,0:T(8,128)(2,1)S(1)} %get-tuple-element.156), channel_id=1, source_target_pairs={{0,4},{1,5},{2,6},{3,7},{4,0},{5,1},{6,2},{7,3},{8,12},{9,13},{10,... | collective-permute-start | bytes 589832 | tf_op jit(solution)/shard_map/ppermute | solution.py:129
  15.9 0.1 collective-permute-start.4
  16.0 1.7 %collective-permute-start = (bf16[1,128,768]{2,1,0:T(8,128)(2,1)S(1)}, bf16[1,128,768]{2,1,0:T(8,128)(2,1)S(1)}, u32[]{:S(2)}, u32[]{:S(2)}) collective-permute-start(bf16[1,128,768]{2,1,0:T(8,128)(2,1)S(1)} %get-tuple-element.153), channel_id=1, source_target_pairs={{0,1},{1,2},{2,3},{3,0},{4,5},{5,6},{6,7},{7,4},{8,9},{9,10},{10,1... | collective-permute-start | bytes 589832 | tf_op jit(solution)/shard_map/ppermute | solution.py:140
  17.7 1.6 %collective-permute-start.1 = (bf16[1,128,768]{2,1,0:T(8,128)(2,1)S(1)}, bf16[1,128,768]{2,1,0:T(8,128)(2,1)S(1)}, u32[]{:S(2)}, u32[]{:S(2)}) collective-permute-start(bf16[1,128,768]{2,1,0:T(8,128)(2,1)S(1)} %get-tuple-element.154), channel_id=1, source_target_pairs={{0,2},{1,3},{2,0},{3,1},{4,6},{5,7},{6,4},{7,5},{8,10},{9,11},{10,... | collective-permute-start | bytes 589832 | tf_op jit(solution)/shard_map/ppermute | solution.py:140
  19.3 1.4 %collective-permute-start.2 = (bf16[1,128,768]{2,1,0:T(8,128)(2,1)S(1)}, bf16[1,128,768]{2,1,0:T(8,128)(2,1)S(1)}, u32[]{:S(2)}, u32[]{:S(2)}) collective-permute-start(bf16[1,128,768]{2,1,0:T(8,128)(2,1)S(1)} %get-tuple-element.152), channel_id=1, source_target_pairs={{0,3},{1,0},{2,1},{3,2},{4,7},{5,4},{6,5},{7,6},{8,11},{9,8},{10,9... | collective-permute-start | bytes 589832 | tf_op jit(solution)/shard_map/ppermute | solution.py:140
  23.9 0.1 constant_dynamic-slice_fusion
  24.0 0.1 copy.9
  24.1 0.1 reshape.473
  24.2 0.8 %fusion.41 = (f32[4,384]{1,0:T(4,128)}, f32[4,384]{1,0:T(4,128)}, f32[4,384]{1,0:T(4,128)}, f32[4,384]{1,0:T(4,128)}) fusion(s32[384]{0:T(512)S(1)} %iota_add_fusion, s32[4]{0:T(128)S(1)} %get-tuple-element.179, s32[4]{0:T(128)S(1)} %get-tuple-element.180), kind=kLoop, calls=%fused_computation.73 | loop fusion | flops 27648 | bytes 26144 | tf_op jit(solution)/shard_map/sin | solution.py:20
  25.0 0.5 fusion.49.index_ref
  25.5 4.6 %collective-permute-done.3 = bf16[1,128,768]{2,1,0:T(8,128)(2,1)S(1)} collective-permute-done((bf16[1,128,768]{2,1,0:T(8,128)(2,1)S(1)}, bf16[1,128,768]{2,1,0:T(8,128)(2,1)S(1)}, u32[]{:S(2)}, u32[]{:S(2)}) %collective-permute-start.3) | collective-permute-done | bytes 196640 | tf_op jit(solution)/shard_map/ppermute | solution.py:129
  30.2 3.4 %collective-permute-done.4 = bf16[1,128,768]{2,1,0:T(8,128)(2,1)S(1)} collective-permute-done((bf16[1,128,768]{2,1,0:T(8,128)(2,1)S(1)}, bf16[1,128,768]{2,1,0:T(8,128)(2,1)S(1)}, u32[]{:S(2)}, u32[]{:S(2)}) %collective-permute-start.4) | collective-permute-done | bytes 196640 | tf_op jit(solution)/shard_map/ppermute | solution.py:129
  33.6 1.6 %collective-permute-start.5 = (bf16[1,128,768]{2,1,0:T(8,128)(2,1)S(1)}, bf16[1,128,768]{2,1,0:T(8,128)(2,1)S(1)}, u32[]{:S(2)}, u32[]{:S(2)}) collective-permute-start(bf16[1,128,768]{2,1,0:T(8,128)(2,1)S(1)} %get-tuple-element.151), channel_id=1, source_target_pairs={{0,1},{1,2},{2,3},{3,0},{4,5},{5,6},{6,7},{7,4},{8,9},{9,10},{10,1... | collective-permute-start | bytes 589832 | tf_op jit(solution)/shard_map/ppermute | solution.py:141
  35.2 0.6 collective-permute-start.6
  35.8 0.0 collective-permute-done
  35.8 1.4 %collective-permute-start.7 = (bf16[1,128,768]{2,1,0:T(8,128)(2,1)S(1)}, bf16[1,128,768]{2,1,0:T(8,128)(2,1)S(1)}, u32[]{:S(2)}, u32[]{:S(2)}) collective-permute-start(bf16[1,128,768]{2,1,0:T(8,128)(2,1)S(1)} %get-tuple-element.149), channel_id=1, source_target_pairs={{0,3},{1,0},{2,1},{3,2},{4,7},{5,4},{6,5},{7,6},{8,11},{9,8},{10,9... | collective-permute-start | bytes 589832 | tf_op jit(solution)/shard_map/ppermute | solution.py:141
  37.3 0.1 bitcast_dynamic-update-slice_fusion.3
  37.4 5.0 %collective-permute-done.5 = bf16[1,128,768]{2,1,0:T(8,128)(2,1)S(1)} collective-permute-done((bf16[1,128,768]{2,1,0:T(8,128)(2,1)S(1)}, bf16[1,128,768]{2,1,0:T(8,128)(2,1)S(1)}, u32[]{:S(2)}, u32[]{:S(2)}) %collective-permute-start.5) | collective-permute-done | bytes 196640 | tf_op jit(solution)/shard_map/ppermute | solution.py:141
  42.4 0.3 collective-permute-done.6
  42.8 0.0 copy-start.3
  42.8 2.0 %collective-permute-done.7 = bf16[1,128,768]{2,1,0:T(8,128)(2,1)S(1)} collective-permute-done((bf16[1,128,768]{2,1,0:T(8,128)(2,1)S(1)}, bf16[1,128,768]{2,1,0:T(8,128)(2,1)S(1)}, u32[]{:S(2)}, u32[]{:S(2)}) %collective-permute-start.7) | collective-permute-done | bytes 196640 | tf_op jit(solution)/shard_map/ppermute | solution.py:141
  44.8 1.1 %copy-done = bf16[8,1,128,768]{3,2,1,0:T(8,128)(2,1)} copy-done((bf16[8,1,128,768]{3,2,1,0:T(8,128)(2,1)}, bf16[8,1,128,768]{3,2,1,0:T(8,128)(2,1)S(1)}, u32[]{:S(2)}) %copy-start) | copy-done | bytes 1572888
  45.9 5.7 %shard_map.37 = (bf16[16,64,512]{2,1,0:T(8,128)(2,1)}, bf16[16,64,512]{2,1,0:T(8,128)(2,1)}) custom-call(s32[8]{0:T(128)} %fusion.49.index_ref, f32[4,384]{1,0:T(4,128)} %get-tuple-element.165.cc_ref, f32[4,384]{1,0:T(4,128)} %get-tuple-element.166.sc_ref, f32[4,384]{1,0:T(4,128)} %get-tuple-element.160.cf_ref, f32[4,384]{1,0:T(4,128)} %get-tuple-element.159.sf_ref, ...), custom_call_target="tpu_custom_call" | custom-call | flops 1610612736 | bytes 3670016 | tf_op jit(solution)/shard_map/pallas_call | solution.py:101
  51.7 1.5 %convert.39 = f32[16,2,32,512]{3,2,1,0:T(8,128)S(1)} convert(bf16[16,2,32,512]{3,2,1,0:T(8,128)(2,1)} %bitcast.77) | non-fusion elementwise | flops 524288 | bytes 3145728 | tf_op jit(solution)/shard_map/reshape | solution.py:194
  53.2 1.3 %collective-permute-done.8 = bf16[16,64,512]{2,1,0:T(8,128)(2,1)S(1)} collective-permute-done((bf16[16,64,512]{2,1,0:T(8,128)(2,1)}, bf16[16,64,512]{2,1,0:T(8,128)(2,1)S(1)}, u32[]{:S(2)}, u32[]{:S(2)}) %collective-permute-start.8) | collective-permute-done | bytes 1048608 | tf_op jit(solution)/shard_map/ppermute | solution.py:193
  54.6 0.2 fusion.15
  54.7 1.3 %collective-permute-start.9 = (bf16[16,32,512]{2,1,0:T(8,128)(2,1)S(1)}, bf16[16,32,512]{2,1,0:T(8,128)(2,1)S(1)}, u32[]{:S(2)}, u32[]{:S(2)}) collective-permute-start(bf16[16,32,512]{2,1,0:T(8,128)(2,1)S(1)} %fusion.15), channel_id=1, source_target_pairs={{0,16},{8,24},{16,0},{24,8},{1,17},{9,25},{17,1},{25,9},{2,18},{10... | collective-permute-start | bytes 1572872 | tf_op jit(solution)/shard_map/ppermute | solution.py:205
  56.1 12.7 %collective-permute-done.9 = bf16[16,32,512]{2,1,0:T(8,128)(2,1)S(1)} collective-permute-done((bf16[16,32,512]{2,1,0:T(8,128)(2,1)S(1)}, bf16[16,32,512]{2,1,0:T(8,128)(2,1)S(1)}, u32[]{:S(2)}, u32[]{:S(2)}) %collective-permute-start.9) | collective-permute-done | bytes 524320 | tf_op jit(solution)/shard_map/ppermute | solution.py:205
  68.8 0.2 fusion.14
  69.0 0.4 reshape.479
  69.4 0.4 multiply_bitcast_fusion
  69.7 1.6 %copy.16 = f32[32,4,16,128]{3,2,1,0:T(8,128)} copy(f32[32,4,16,128]{3,1,0,2:T(4,128)S(1)} %multiply_bitcast_fusion) | data formatting | bytes 2097152 | tf_op jit(solution)/shard_map/div | solution.py:212
  (22 shorter events, 0.2 us)
Async XLA Ops:
  1.3 3.5 %copy-start.2 = (bf16[1,256,7680]{2,1,0:T(8,128)(2,1)S(1)}, bf16[1,256,7680]{2,1,0:T(8,128)(2,1)}, u32[]{:S(2)}) copy-start(bf16[1,256,7680]{2,1,0:T(8,128)(2,1)} %param.3) | copy-start | bytes 11796484
  6.5 1.8 %copy-start.1 = (s32[32,2]{0,1:T(2,128)S(1)}, s32[32,2]{0,1:T(2,128)}, u32[]{:S(2)}) copy-start(s32[32,2]{0,1:T(2,128)} %param.4) | copy-start | bytes 772
  11.8 18.4 %collective-permute-start.3 = (bf16[1,128,768]{2,1,0:T(8,128)(2,1)S(1)}, bf16[1,128,768]{2,1,0:T(8,128)(2,1)S(1)}, u32[]{:S(2)}, u32[]{:S(2)}) collective-permute-start(bf16[1,128,768]{2,1,0:T(8,128)(2,1)S(1)} %get-tuple-element.156), channel_id=1, source_target_pairs={{0,4},{1,5},{2,6},{3,7},{4,0},{5,1},{6,2},{7,3},{8,12},{9,13},{10,... | collective-permute-start | bytes 589832 | tf_op jit(solution)/shard_map/ppermute | solution.py:129
  15.9 17.6 %collective-permute-start.4 = (bf16[1,128,768]{2,1,0:T(8,128)(2,1)S(1)}, bf16[1,128,768]{2,1,0:T(8,128)(2,1)S(1)}, u32[]{:S(2)}, u32[]{:S(2)}) collective-permute-start(bf16[1,128,768]{2,1,0:T(8,128)(2,1)S(1)} %get-tuple-element.155), channel_id=1, source_target_pairs={{0,4},{1,5},{2,6},{3,7},{4,0},{5,1},{6,2},{7,3},{8,12},{9,13},{10,... | collective-permute-start | bytes 589832 | tf_op jit(solution)/shard_map/ppermute | solution.py:129
  16.0 19.8 %collective-permute-start = (bf16[1,128,768]{2,1,0:T(8,128)(2,1)S(1)}, bf16[1,128,768]{2,1,0:T(8,128)(2,1)S(1)}, u32[]{:S(2)}, u32[]{:S(2)}) collective-permute-start(bf16[1,128,768]{2,1,0:T(8,128)(2,1)S(1)} %get-tuple-element.153), channel_id=1, source_target_pairs={{0,1},{1,2},{2,3},{3,0},{4,5},{5,6},{6,7},{7,4},{8,9},{9,10},{10,1... | collective-permute-start | bytes 589832 | tf_op jit(solution)/shard_map/ppermute | solution.py:140
  17.7 19.5 %collective-permute-start.1 = (bf16[1,128,768]{2,1,0:T(8,128)(2,1)S(1)}, bf16[1,128,768]{2,1,0:T(8,128)(2,1)S(1)}, u32[]{:S(2)}, u32[]{:S(2)}) collective-permute-start(bf16[1,128,768]{2,1,0:T(8,128)(2,1)S(1)} %get-tuple-element.154), channel_id=1, source_target_pairs={{0,2},{1,3},{2,0},{3,1},{4,6},{5,7},{6,4},{7,5},{8,10},{9,11},{10,... | collective-permute-start | bytes 589832 | tf_op jit(solution)/shard_map/ppermute | solution.py:140
  19.3 18.0 %collective-permute-start.2 = (bf16[1,128,768]{2,1,0:T(8,128)(2,1)S(1)}, bf16[1,128,768]{2,1,0:T(8,128)(2,1)S(1)}, u32[]{:S(2)}, u32[]{:S(2)}) collective-permute-start(bf16[1,128,768]{2,1,0:T(8,128)(2,1)S(1)} %get-tuple-element.152), channel_id=1, source_target_pairs={{0,3},{1,0},{2,1},{3,2},{4,7},{5,4},{6,5},{7,6},{8,11},{9,8},{10,9... | collective-permute-start | bytes 589832 | tf_op jit(solution)/shard_map/ppermute | solution.py:140
  33.6 8.8 %collective-permute-start.5 = (bf16[1,128,768]{2,1,0:T(8,128)(2,1)S(1)}, bf16[1,128,768]{2,1,0:T(8,128)(2,1)S(1)}, u32[]{:S(2)}, u32[]{:S(2)}) collective-permute-start(bf16[1,128,768]{2,1,0:T(8,128)(2,1)S(1)} %get-tuple-element.151), channel_id=1, source_target_pairs={{0,1},{1,2},{2,3},{3,0},{4,5},{5,6},{6,7},{7,4},{8,9},{9,10},{10,1... | collective-permute-start | bytes 589832 | tf_op jit(solution)/shard_map/ppermute | solution.py:141
  35.2 7.6 %collective-permute-start.6 = (bf16[1,128,768]{2,1,0:T(8,128)(2,1)S(1)}, bf16[1,128,768]{2,1,0:T(8,128)(2,1)S(1)}, u32[]{:S(2)}, u32[]{:S(2)}) collective-permute-start(bf16[1,128,768]{2,1,0:T(8,128)(2,1)S(1)} %get-tuple-element.150), channel_id=1, source_target_pairs={{0,2},{1,3},{2,0},{3,1},{4,6},{5,7},{6,4},{7,5},{8,10},{9,11},{10,... | collective-permute-start | bytes 589832 | tf_op jit(solution)/shard_map/ppermute | solution.py:141
  35.8 9.0 %collective-permute-start.7 = (bf16[1,128,768]{2,1,0:T(8,128)(2,1)S(1)}, bf16[1,128,768]{2,1,0:T(8,128)(2,1)S(1)}, u32[]{:S(2)}, u32[]{:S(2)}) collective-permute-start(bf16[1,128,768]{2,1,0:T(8,128)(2,1)S(1)} %get-tuple-element.149), channel_id=1, source_target_pairs={{0,3},{1,0},{2,1},{3,2},{4,7},{5,4},{6,5},{7,6},{8,11},{9,8},{10,9... | collective-permute-start | bytes 589832 | tf_op jit(solution)/shard_map/ppermute | solution.py:141
  42.8 13.3 %copy-start.3 = (s32[4]{0:T(128)S(1)}, s32[4]{0:T(128)}, u32[]{:S(2)}) copy-start(s32[4]{0:T(128)} %param.5) | copy-start | bytes 52
  44.8 1.1 %copy-start = (bf16[8,1,128,768]{3,2,1,0:T(8,128)(2,1)}, bf16[8,1,128,768]{3,2,1,0:T(8,128)(2,1)S(1)}, u32[]{:S(2)}) copy-start(bf16[8,1,128,768]{3,2,1,0:T(8,128)(2,1)S(1)} %bitcast_dynamic-update-slice_fusion.left_ref.right_ref) | copy-start | bytes 4718596
  51.7 2.9 %collective-permute-start.8 = (bf16[16,64,512]{2,1,0:T(8,128)(2,1)}, bf16[16,64,512]{2,1,0:T(8,128)(2,1)S(1)}, u32[]{:S(2)}, u32[]{:S(2)}) collective-permute-start(bf16[16,64,512]{2,1,0:T(8,128)(2,1)} %get-tuple-element.8), channel_id=1, source_target_pairs={{0,8},{8,0},{16,24},{24,16},{1,9},{9,1},{17,25},{25,17},{2,10},{10... | collective-permute-start | bytes 3145736 | tf_op jit(solution)/shard_map/ppermute | solution.py:193
  54.7 14.0 %collective-permute-start.9 = (bf16[16,32,512]{2,1,0:T(8,128)(2,1)S(1)}, bf16[16,32,512]{2,1,0:T(8,128)(2,1)S(1)}, u32[]{:S(2)}, u32[]{:S(2)}) collective-permute-start(bf16[16,32,512]{2,1,0:T(8,128)(2,1)S(1)} %fusion.15), channel_id=1, source_target_pairs={{0,16},{8,24},{16,0},{24,8},{1,17},{9,25},{17,1},{25,9},{2,18},{10... | collective-permute-start | bytes 1572872 | tf_op jit(solution)/shard_map/ppermute | solution.py:205

commit v18 on v17

--- a/solution.py
+++ b/solution.py
@@ -82,7 +82,7 @@
             for part in range(2):
                 rows = l2 * C + part * half_rows
                 out_ref = (send_ref, keep_ref)[part]
-                out_ref[l2 * sub + l1] = acc[rows : rows + half_rows, l1 * C : (l1 + 1) * C].astype(out_ref.dtype)
+                out_ref[l2 * sub + l1, 0] = acc[rows : rows + half_rows, l1 * C : (l1 + 1) * C].astype(out_ref.dtype)
 
 
 def tile_correlation(cc, sc, cf, sf, incoming, slots, sub, n_y, own_rows):
@@ -96,12 +96,12 @@
         num_scalar_prefetch=1,
         grid=(slot_count,),
         in_specs=[table_spec] * 4 + [left_spec, right_spec],
-        out_specs=[pl.BlockSpec((LAGS, C // 2, C), lambda t, idx: (0, 0, t))] * 2,
+        out_specs=[pl.BlockSpec((LAGS, 1, C // 2, C), lambda t, idx: (0, t, 0, 0))] * 2,
     )
     return pl.pallas_call(
         functools.partial(correlation_kernel, sub, n_y, own_rows),
         grid_spec=grid_spec,
-        out_shape=[jax.ShapeDtypeStruct((LAGS, C // 2, slot_count * C), jnp.bfloat16)] * 2,
+        out_shape=[jax.ShapeDtypeStruct((LAGS, slot_count, C // 2, C), jnp.bfloat16)] * 2,
         cost_estimate=pl.CostEstimate(
             flops=flops, transcendentals=0, bytes_accessed=slot_count * (4 * window_count * C * F * 2 + 2 * C * LAGS * C)
         ),
@@ -191,11 +191,11 @@
     send, keep = corr
     keep = keep.astype(jnp.float32)
     got = lax.ppermute(send, "win", [(w, w ^ 1) for w in range(n_win)])
-    keep = keep.reshape(LAGS, n_y, own_rows, slot_count * C)
-    got = got.reshape(LAGS, n_y, own_rows, slot_count * C)
+    keep = keep.reshape(LAGS, slot_count, n_y, own_rows, C)
+    got = got.reshape(LAGS, slot_count, n_y, own_rows, C)
 
     def chip_sum(y):
-        pick = lambda a: jnp.take(a, y, axis=1, mode="clip")
+        pick = lambda a: jnp.take(a, y, axis=2, mode="clip")
         return pick(keep) + pick(got).astype(jnp.float32)
 
     pieces = []
@@ -206,7 +206,7 @@
     total = chip_sum(y_here)
     for piece in pieces:
         total = total + piece.astype(jnp.float32)
-    total = jnp.transpose(total.reshape(LAGS, own_rows, slot_count, C), (1, 2, 0, 3))
+    total = jnp.transpose(total, (2, 1, 0, 3))
 
     live_local = tile_live.astype(jnp.float32)
     return total * live_local[None, :, None, None] / math.sqrt(F * window_count * n_win)

time: 71.6 us -> 71.9 us (level)
  other arithmetic: 9.3 us -> 11.5 us
  local copies, waits for them, and re-layouts: 4.27 us -> 2.71 us
    div x1, other arithmetic: 0.36 us -> 1.96 us  [body(): total * live_local[None, :, None, None]]
    div x1 -> x0, local copies, waits for them, and re-layouts: 1.58 us -> none  [body(): total * live_local[None, :, None, None]]
    convert_element_type x1, other arithmetic: 0.16 us -> 0.9 us  [body(): chip_sum(dest).astype(jnp.bfloat16)]
where the time goes in v18:
time: 71.9 us; the launch traced here: 71.6 us
  waiting for transfers between devices  29.1 us (40%)
  starting transfers between devices  14 us (19%)
  other arithmetic  11.5 us (16%)
  Pallas kernels  5.76 us (8%)
  between operations  5.21 us (7%)
  matrix products  3.38 us (5%)
  local copies, waits for them, and re-layouts  2.71 us (4%)
    ppermute x1, waiting for transfers between devices, body(): lax.ppermute(chip_sum(dest).astype(jnp.bfloat16), 'win', perm)  12.7 us
    ppermute x2, waiting for transfers between devices, exchange_by_halves(): lax.ppermute(block, 'pair', across)  7.99 us
    ppermute x3, waiting for transfers between devices, exchange_by_halves(): relay = lax.ppermute(relay, 'pair', perm)  7.37 us
    pallas_call x1, Pallas kernels, tile_correlation(): pl.pallas_call(functools.partial(correlation_kernel, sub, n_y, own_rows),...  5.76 us
    ppermute x3, starting transfers between devices, exchange_by_halves(): own = lax.ppermute(own, 'pair', perm)  4.76 us
    ppermute x2, starting transfers between devices, exchange_by_halves(): lax.ppermute(block, 'pair', across)  4.18 us
    another operation x3, other arithmetic  3.72 us
    ppermute x3, starting transfers between devices, exchange_by_halves(): relay = lax.ppermute(relay, 'pair', perm)  3.64 us
  transfers between devices with their start and end apart: 10, of which 7 were waited for; matrix products, arithmetic and copies ran while one was open for 5% of the time, Pallas kernels for 0%

profile of v18, /device:TPU:0, one launch (start us, length us, event | category | flops | bytes accessed | tf_op | source)
XLA Modules:
  0.0 71.6 jit_solution(17585507701768545991)
XLA Ops:
  0.0 0.8 %fusion.25 = (f32[128,384]{1,0:T(8,128)S(1)}, f32[128,384]{1,0:T(8,128)S(1)}) fusion(s32[384]{0:T(512)S(1)} %iota_add_fusion), kind=kLoop, calls=%fused_computation.44 | loop fusion | flops 442368 | bytes 394752 | tf_op jit(solution)/shard_map/cos | solution.py:20
  0.8 0.5 fusion.32
  1.3 0.0 copy-start.2
  1.3 3.5 %subtract_convert_fusion = (bf16[60,128,384]{2,1,0:T(8,128)(2,1)S(1)}, bf16[60,128,384]{2,1,0:T(8,128)(2,1)S(1)}) fusion(f32[128,384]{1,0:T(8,128)S(1)} %get-tuple-element.168, f32[60,384]{1,0:T(8,128)S(1)} %get-tuple-element.162, f32[128,384]{1,0:T(8,128)S(1)} %get-tuple-element.167, f32[60,384]{1,0:T(8,128)S(1)} %get-tuple-element.161), kind=kLoop, calls=%fused_computation.2 | loop fusion | flops 26542080 | bytes 12374016 | tf_op jit(solution)/shard_map/convert.20
  4.8 1.7 %fusion.6 = f32[128,768]{1,0:T(8,128)S(1)} fusion(bf16[7680,384]{1,0:T(8,128)(2,1)S(1)} %bitcast.65, bf16[7680,384]{1,0:T(8,128)(2,1)S(1)} %bitcast.63, bf16[1,256,7680]{2,1,0:T(8,128)(2,1)S(1)} %copy-done.2), kind=kOutput, calls=%fused_computation.9 | convolution fusion | flops 1533542400 | bytes 14155776 | tf_op jit(solution)/shard_map/dot_general | solution.py:36
  6.5 0.0 copy-start.1
  6.5 1.7 %fusion.9 = f32[128,768]{1,0:T(8,128)S(1)} fusion(bf16[7680,384]{1,0:T(8,128)(2,1)S(1)} %bitcast.66, bf16[7680,384]{1,0:T(8,128)(2,1)S(1)} %bitcast.64, bf16[1,256,7680]{2,1,0:T(8,128)(2,1)S(1)} %copy-done.2), kind=kOutput, calls=%fused_computation.10 | convolution fusion | flops 1533542400 | bytes 14155776 | tf_op jit(solution)/shard_map/dot_general | solution.py:36
  8.3 0.1 reduce_sum.43
  8.4 0.1 reduce_sum.52
  8.5 0.1 reduce_sum.56
  8.6 0.1 reduce_sum.57
  8.7 0.7 fusion.57
  11.2 0.2 fusion.55
  11.4 0.1 divide_convert_fusion.1
  11.6 0.1 divide_convert_fusion.3
  11.7 0.1 broadcast_select_fusion.3
  11.8 4.1 %collective-permute-start.3 = (bf16[1,128,768]{2,1,0:T(8,128)(2,1)S(1)}, bf16[1,128,768]{2,1,0:T(8,128)(2,1)S(1)}, u32[]{:S(2)}, u32[]{:S(2)}) collective-permute-start(bf16[1,128,768]{2,1,0:T(8,128)(2,1)S(1)} %get-tuple-element.160), channel_id=1, source_target_pairs={{0,4},{1,5},{2,6},{3,7},{4,0},{5,1},{6,2},{7,3},{8,12},{9,13},{10,... | collective-permute-start | bytes 589832 | tf_op jit(solution)/shard_map/ppermute | solution.py:129
  15.9 0.1 collective-permute-start.4
  16.0 1.7 %collective-permute-start = (bf16[1,128,768]{2,1,0:T(8,128)(2,1)S(1)}, bf16[1,128,768]{2,1,0:T(8,128)(2,1)S(1)}, u32[]{:S(2)}, u32[]{:S(2)}) collective-permute-start(bf16[1,128,768]{2,1,0:T(8,128)(2,1)S(1)} %get-tuple-element.157), channel_id=1, source_target_pairs={{0,1},{1,2},{2,3},{3,0},{4,5},{5,6},{6,7},{7,4},{8,9},{9,10},{10,1... | collective-permute-start | bytes 589832 | tf_op jit(solution)/shard_map/ppermute | solution.py:140
  17.7 1.6 %collective-permute-start.1 = (bf16[1,128,768]{2,1,0:T(8,128)(2,1)S(1)}, bf16[1,128,768]{2,1,0:T(8,128)(2,1)S(1)}, u32[]{:S(2)}, u32[]{:S(2)}) collective-permute-start(bf16[1,128,768]{2,1,0:T(8,128)(2,1)S(1)} %get-tuple-element.158), channel_id=1, source_target_pairs={{0,2},{1,3},{2,0},{3,1},{4,6},{5,7},{6,4},{7,5},{8,10},{9,11},{10,... | collective-permute-start | bytes 589832 | tf_op jit(solution)/shard_map/ppermute | solution.py:140
  19.3 1.4 %collective-permute-start.2 = (bf16[1,128,768]{2,1,0:T(8,128)(2,1)S(1)}, bf16[1,128,768]{2,1,0:T(8,128)(2,1)S(1)}, u32[]{:S(2)}, u32[]{:S(2)}) collective-permute-start(bf16[1,128,768]{2,1,0:T(8,128)(2,1)S(1)} %get-tuple-element.156), channel_id=1, source_target_pairs={{0,3},{1,0},{2,1},{3,2},{4,7},{5,4},{6,5},{7,6},{8,11},{9,8},{10,9... | collective-permute-start | bytes 589832 | tf_op jit(solution)/shard_map/ppermute | solution.py:140
  23.9 0.1 constant_dynamic-slice_fusion.4
  23.9 0.1 copy.11
  24.0 0.1 reshape.470
  24.1 0.8 %fusion.44 = (f32[4,384]{1,0:T(4,128)}, f32[4,384]{1,0:T(4,128)}, f32[4,384]{1,0:T(4,128)}, f32[4,384]{1,0:T(4,128)}) fusion(s32[384]{0:T(512)S(1)} %iota_add_fusion, s32[4]{0:T(128)S(1)} %get-tuple-element.183, s32[4]{0:T(128)S(1)} %get-tuple-element.184), kind=kLoop, calls=%fused_computation.75 | loop fusion | flops 27648 | bytes 26144 | tf_op jit(solution)/shard_map/sin | solution.py:20
  25.0 0.6 fusion.52.index_ref
  25.6 4.6 %collective-permute-done.3 = bf16[1,128,768]{2,1,0:T(8,128)(2,1)S(1)} collective-permute-done((bf16[1,128,768]{2,1,0:T(8,128)(2,1)S(1)}, bf16[1,128,768]{2,1,0:T(8,128)(2,1)S(1)}, u32[]{:S(2)}, u32[]{:S(2)}) %collective-permute-start.3) | collective-permute-done | bytes 196640 | tf_op jit(solution)/shard_map/ppermute | solution.py:129
  30.2 3.4 %collective-permute-done.4 = bf16[1,128,768]{2,1,0:T(8,128)(2,1)S(1)} collective-permute-done((bf16[1,128,768]{2,1,0:T(8,128)(2,1)S(1)}, bf16[1,128,768]{2,1,0:T(8,128)(2,1)S(1)}, u32[]{:S(2)}, u32[]{:S(2)}) %collective-permute-start.4) | collective-permute-done | bytes 196640 | tf_op jit(solution)/shard_map/ppermute | solution.py:129
  33.6 1.6 %collective-permute-start.5 = (bf16[1,128,768]{2,1,0:T(8,128)(2,1)S(1)}, bf16[1,128,768]{2,1,0:T(8,128)(2,1)S(1)}, u32[]{:S(2)}, u32[]{:S(2)}) collective-permute-start(bf16[1,128,768]{2,1,0:T(8,128)(2,1)S(1)} %get-tuple-element.155), channel_id=1, source_target_pairs={{0,1},{1,2},{2,3},{3,0},{4,5},{5,6},{6,7},{7,4},{8,9},{9,10},{10,1... | collective-permute-start | bytes 589832 | tf_op jit(solution)/shard_map/ppermute | solution.py:141
  35.2 0.6 collective-permute-start.6
  35.8 0.0 collective-permute-done
  35.8 1.4 %collective-permute-start.7 = (bf16[1,128,768]{2,1,0:T(8,128)(2,1)S(1)}, bf16[1,128,768]{2,1,0:T(8,128)(2,1)S(1)}, u32[]{:S(2)}, u32[]{:S(2)}) collective-permute-start(bf16[1,128,768]{2,1,0:T(8,128)(2,1)S(1)} %get-tuple-element.153), channel_id=1, source_target_pairs={{0,3},{1,0},{2,1},{3,2},{4,7},{5,4},{6,5},{7,6},{8,11},{9,8},{10,9... | collective-permute-start | bytes 589832 | tf_op jit(solution)/shard_map/ppermute | solution.py:141
  37.3 0.0 collective-permute-done.1
  37.3 0.1 bitcast_dynamic-update-slice_fusion.3
  37.4 5.0 %collective-permute-done.5 = bf16[1,128,768]{2,1,0:T(8,128)(2,1)S(1)} collective-permute-done((bf16[1,128,768]{2,1,0:T(8,128)(2,1)S(1)}, bf16[1,128,768]{2,1,0:T(8,128)(2,1)S(1)}, u32[]{:S(2)}, u32[]{:S(2)}) %collective-permute-start.5) | collective-permute-done | bytes 196640 | tf_op jit(solution)/shard_map/ppermute | solution.py:141
  42.4 0.3 collective-permute-done.6
  42.8 2.0 %collective-permute-done.7 = bf16[1,128,768]{2,1,0:T(8,128)(2,1)S(1)} collective-permute-done((bf16[1,128,768]{2,1,0:T(8,128)(2,1)S(1)}, bf16[1,128,768]{2,1,0:T(8,128)(2,1)S(1)}, u32[]{:S(2)}, u32[]{:S(2)}) %collective-permute-start.7) | collective-permute-done | bytes 196640 | tf_op jit(solution)/shard_map/ppermute | solution.py:141
  44.8 1.1 %copy-done = bf16[8,1,128,768]{3,2,1,0:T(8,128)(2,1)} copy-done((bf16[8,1,128,768]{3,2,1,0:T(8,128)(2,1)}, bf16[8,1,128,768]{3,2,1,0:T(8,128)(2,1)S(1)}, u32[]{:S(2)}) %copy-start) | copy-done | bytes 1572888
  46.0 5.8 %shard_map.37 = (bf16[16,4,64,128]{3,2,1,0:T(8,128)(2,1)}, bf16[16,4,64,128]{3,2,1,0:T(8,128)(2,1)}) custom-call(s32[8]{0:T(128)} %fusion.52.index_ref, f32[4,384]{1,0:T(4,128)} %get-tuple-element.169.cc_ref, f32[4,384]{1,0:T(4,128)} %get-tuple-element.170.sc_ref, f32[4,384]{1,0:T(4,128)} %get-tuple-element.164.cf_ref, f32[4,384]{1,0:T(4,128)} %get-tuple-element.163.sf_ref, ...), custom_call_target="tpu_custom_call" | custom-call | flops 1610612736 | bytes 3670016 | tf_op jit(solution)/shard_map/pallas_call | solution.py:101
  51.7 0.0 collective-permute-start.8
  51.8 1.5 %convert.39 = f32[16,4,2,32,128]{4,3,2,1,0:T(8,128)S(1)} convert(bf16[16,4,2,32,128]{4,3,2,1,0:T(8,128)(2,1)} %bitcast.67) | non-fusion elementwise | flops 524288 | bytes 3145728 | tf_op jit(solution)/shard_map/reshape | solution.py:194
  53.3 0.2 constant_dynamic-slice_fusion.1
  53.6 1.1 %collective-permute-done.8 = bf16[16,4,64,128]{3,2,1,0:T(8,128)(2,1)S(1)} collective-permute-done((bf16[16,4,64,128]{3,2,1,0:T(8,128)(2,1)}, bf16[16,4,64,128]{3,2,1,0:T(8,128)(2,1)S(1)}, u32[]{:S(2)}, u32[]{:S(2)}) %collective-permute-start.8) | collective-permute-done | bytes 1048608 | tf_op jit(solution)/shard_map/ppermute | solution.py:193
  54.6 0.1 constant_dynamic-slice_fusion.2
  54.7 0.9 %fusion.18 = bf16[16,4,32,128]{3,0,1,2:T(8,128)(2,1)S(1)} fusion(f32[16,4,1,32,128]{4,3,2,1,0:T(8,128)S(1)} %get-tuple-element.143, bf16[16,4,1,32,128]{4,3,2,1,0:T(8,128)(2,1)S(1)} %get-tuple-element.146), kind=kLoop, calls=%fused_computation.19 | loop fusion | flops 786432 | bytes 2097152 | tf_op jit(solution)/shard_map/convert_element_type | solution.py:205
  55.6 1.3 %collective-permute-start.9 = (bf16[16,4,32,128]{3,0,1,2:T(8,128)(2,1)S(1)}, bf16[16,4,32,128]{3,0,1,2:T(8,128)(2,1)S(1)}, u32[]{:S(2)}, u32[]{:S(2)}) collective-permute-start(bf16[16,4,32,128]{3,0,1,2:T(8,128)(2,1)S(1)} %fusion.18), channel_id=1, source_target_pairs={{0,16},{8,24},{16,0},{24,8},{1,17},{9,25},{17,1},{25,9},{2,18},{10... | collective-permute-start | bytes 1572872 | tf_op jit(solution)/shard_map/ppermute | solution.py:205
  57.0 12.7 %collective-permute-done.9 = bf16[16,4,32,128]{3,0,1,2:T(8,128)(2,1)S(1)} collective-permute-done((bf16[16,4,32,128]{3,0,1,2:T(8,128)(2,1)S(1)}, bf16[16,4,32,128]{3,0,1,2:T(8,128)(2,1)S(1)}, u32[]{:S(2)}, u32[]{:S(2)}) %collective-permute-start.9) | collective-permute-done | bytes 524320 | tf_op jit(solution)/shard_map/ppermute | solution.py:205
  69.7 2.0 %fusion.17 = f32[32,4,16,128]{3,2,1,0:T(8,128)} fusion(f32[16,4,1,32,128]{4,3,2,1,0:T(8,128)S(1)} %get-tuple-element.144, bf16[16,4,32,128]{3,0,1,2:T(8,128)(2,1)S(1)} %collective-permute-done.9, bf16[16,4,1,32,128]{4,3,2,1,0:T(8,128)(2,1)S(1)} %get-tuple-element.145, f32[4]{0:T(128)S(1)} %convert_element_type.120), kind=kLoop, calls=%fused_computation.18 | loop fusion | flops 1572864 | bytes 3145744 | tf_op jit(solution)/shard_map/div | solution.py:212
  (21 shorter events, 0.2 us)
Async XLA Ops:
  1.3 3.5 %copy-start.2 = (bf16[1,256,7680]{2,1,0:T(8,128)(2,1)S(1)}, bf16[1,256,7680]{2,1,0:T(8,128)(2,1)}, u32[]{:S(2)}) copy-start(bf16[1,256,7680]{2,1,0:T(8,128)(2,1)} %param.3) | copy-start | bytes 11796484
  6.5 1.8 %copy-start.1 = (s32[32,2]{0,1:T(2,128)S(1)}, s32[32,2]{0,1:T(2,128)}, u32[]{:S(2)}) copy-start(s32[32,2]{0,1:T(2,128)} %param.4) | copy-start | bytes 772
  11.8 18.4 %collective-permute-start.3 = (bf16[1,128,768]{2,1,0:T(8,128)(2,1)S(1)}, bf16[1,128,768]{2,1,0:T(8,128)(2,1)S(1)}, u32[]{:S(2)}, u32[]{:S(2)}) collective-permute-start(bf16[1,128,768]{2,1,0:T(8,128)(2,1)S(1)} %get-tuple-element.160), channel_id=1, source_target_pairs={{0,4},{1,5},{2,6},{3,7},{4,0},{5,1},{6,2},{7,3},{8,12},{9,13},{10,... | collective-permute-start | bytes 589832 | tf_op jit(solution)/shard_map/ppermute | solution.py:129
  15.9 17.6 %collective-permute-start.4 = (bf16[1,128,768]{2,1,0:T(8,128)(2,1)S(1)}, bf16[1,128,768]{2,1,0:T(8,128)(2,1)S(1)}, u32[]{:S(2)}, u32[]{:S(2)}) collective-permute-start(bf16[1,128,768]{2,1,0:T(8,128)(2,1)S(1)} %get-tuple-element.159), channel_id=1, source_target_pairs={{0,4},{1,5},{2,6},{3,7},{4,0},{5,1},{6,2},{7,3},{8,12},{9,13},{10,... | collective-permute-start | bytes 589832 | tf_op jit(solution)/shard_map/ppermute | solution.py:129
  16.0 19.8 %collective-permute-start = (bf16[1,128,768]{2,1,0:T(8,128)(2,1)S(1)}, bf16[1,128,768]{2,1,0:T(8,128)(2,1)S(1)}, u32[]{:S(2)}, u32[]{:S(2)}) collective-permute-start(bf16[1,128,768]{2,1,0:T(8,128)(2,1)S(1)} %get-tuple-element.157), channel_id=1, source_target_pairs={{0,1},{1,2},{2,3},{3,0},{4,5},{5,6},{6,7},{7,4},{8,9},{9,10},{10,1... | collective-permute-start | bytes 589832 | tf_op jit(solution)/shard_map/ppermute | solution.py:140
  17.7 19.5 %collective-permute-start.1 = (bf16[1,128,768]{2,1,0:T(8,128)(2,1)S(1)}, bf16[1,128,768]{2,1,0:T(8,128)(2,1)S(1)}, u32[]{:S(2)}, u32[]{:S(2)}) collective-permute-start(bf16[1,128,768]{2,1,0:T(8,128)(2,1)S(1)} %get-tuple-element.158), channel_id=1, source_target_pairs={{0,2},{1,3},{2,0},{3,1},{4,6},{5,7},{6,4},{7,5},{8,10},{9,11},{10,... | collective-permute-start | bytes 589832 | tf_op jit(solution)/shard_map/ppermute | solution.py:140
  19.3 18.0 %collective-permute-start.2 = (bf16[1,128,768]{2,1,0:T(8,128)(2,1)S(1)}, bf16[1,128,768]{2,1,0:T(8,128)(2,1)S(1)}, u32[]{:S(2)}, u32[]{:S(2)}) collective-permute-start(bf16[1,128,768]{2,1,0:T(8,128)(2,1)S(1)} %get-tuple-element.156), channel_id=1, source_target_pairs={{0,3},{1,0},{2,1},{3,2},{4,7},{5,4},{6,5},{7,6},{8,11},{9,8},{10,9... | collective-permute-start | bytes 589832 | tf_op jit(solution)/shard_map/ppermute | solution.py:140
  33.6 8.8 %collective-permute-start.5 = (bf16[1,128,768]{2,1,0:T(8,128)(2,1)S(1)}, bf16[1,128,768]{2,1,0:T(8,128)(2,1)S(1)}, u32[]{:S(2)}, u32[]{:S(2)}) collective-permute-start(bf16[1,128,768]{2,1,0:T(8,128)(2,1)S(1)} %get-tuple-element.155), channel_id=1, source_target_pairs={{0,1},{1,2},{2,3},{3,0},{4,5},{5,6},{6,7},{7,4},{8,9},{9,10},{10,1... | collective-permute-start | bytes 589832 | tf_op jit(solution)/shard_map/ppermute | solution.py:141
  35.2 7.6 %collective-permute-start.6 = (bf16[1,128,768]{2,1,0:T(8,128)(2,1)S(1)}, bf16[1,128,768]{2,1,0:T(8,128)(2,1)S(1)}, u32[]{:S(2)}, u32[]{:S(2)}) collective-permute-start(bf16[1,128,768]{2,1,0:T(8,128)(2,1)S(1)} %get-tuple-element.154), channel_id=1, source_target_pairs={{0,2},{1,3},{2,0},{3,1},{4,6},{5,7},{6,4},{7,5},{8,10},{9,11},{10,... | collective-permute-start | bytes 589832 | tf_op jit(solution)/shard_map/ppermute | solution.py:141
  35.8 9.0 %collective-permute-start.7 = (bf16[1,128,768]{2,1,0:T(8,128)(2,1)S(1)}, bf16[1,128,768]{2,1,0:T(8,128)(2,1)S(1)}, u32[]{:S(2)}, u32[]{:S(2)}) collective-permute-start(bf16[1,128,768]{2,1,0:T(8,128)(2,1)S(1)} %get-tuple-element.153), channel_id=1, source_target_pairs={{0,3},{1,0},{2,1},{3,2},{4,7},{5,4},{6,5},{7,6},{8,11},{9,8},{10,9... | collective-permute-start | bytes 589832 | tf_op jit(solution)/shard_map/ppermute | solution.py:141
  44.8 1.2 %copy-start = (bf16[8,1,128,768]{3,2,1,0:T(8,128)(2,1)}, bf16[8,1,128,768]{3,2,1,0:T(8,128)(2,1)S(1)}, u32[]{:S(2)}) copy-start(bf16[8,1,128,768]{3,2,1,0:T(8,128)(2,1)S(1)} %bitcast_dynamic-update-slice_fusion.left_ref.right_ref) | copy-start | bytes 4718596
  51.7 5.3 %copy-start.3 = (s32[4]{0:T(128)S(1)}, s32[4]{0:T(128)}, u32[]{:S(2)}) copy-start(s32[4]{0:T(128)} %param.5) | copy-start | bytes 52
  51.7 2.9 %collective-permute-start.8 = (bf16[16,4,64,128]{3,2,1,0:T(8,128)(2,1)}, bf16[16,4,64,128]{3,2,1,0:T(8,128)(2,1)S(1)}, u32[]{:S(2)}, u32[]{:S(2)}) collective-permute-start(bf16[16,4,64,128]{3,2,1,0:T(8,128)(2,1)} %get-tuple-element.8), channel_id=1, source_target_pairs={{0,8},{8,0},{16,24},{24,16},{1,9},{9,1},{17,25},{25,17},{2,10},{10... | collective-permute-start | bytes 3145736 | tf_op jit(solution)/shard_map/ppermute | solution.py:193
  55.6 14.0 %collective-permute-start.9 = (bf16[16,4,32,128]{3,0,1,2:T(8,128)(2,1)S(1)}, bf16[16,4,32,128]{3,0,1,2:T(8,128)(2,1)S(1)}, u32[]{:S(2)}, u32[]{:S(2)}) collective-permute-start(bf16[16,4,32,128]{3,0,1,2:T(8,128)(2,1)S(1)} %fusion.18), channel_id=1, source_target_pairs={{0,16},{8,24},{16,0},{24,8},{1,17},{9,25},{17,1},{25,9},{2,18},{10... | collective-permute-start | bytes 1572872 | tf_op jit(solution)/shard_map/ppermute | solution.py:205

commit v19 on v12

--- a/solution.py
+++ b/solution.py
@@ -42,13 +42,20 @@
     return jnp.concatenate([real_part / divisor, imag_part / divisor], axis=1).astype(jnp.bfloat16)
 
 
-def correlation_kernel(sub, n_y, own_rows, index_ref, cc_ref, sc_ref, cf_ref, sf_ref, left_ref, right_ref, out_ref):
+def correlation_kernel(sub, n_y, own_rows, index_ref, cc_ref, sc_ref, cf_ref, sf_ref, left_ref, right_ref, far_ref, near_ref, keep_ref):
     window_count = left_ref.shape[1]
-    order = [(y * 2 + c) * own_rows for c in range(2) for y in range(n_y)]
+    win = lax.axis_index("win")
+    variants = [(c, y) for c in range(2) for y in range(n_y)]
     acc = None
     for w in range(window_count):
         left = left_ref[0, w].astype(jnp.float32)
-        left = jnp.concatenate([left[r : r + own_rows] for r in order], axis=0)
+        picked = None
+        for c, y in variants:
+            chips = [(y + shift) % n_y for shift in range(1, n_y)] + [y]
+            order = [(yy * 2 + cc) * own_rows for cc in (1 - c, c) for yy in chips]
+            this = jnp.concatenate([left[r : r + own_rows] for r in order], axis=0)
+            picked = this if picked is None else jnp.where(win == y * 2 + c, this, picked)
+        left = picked
         lre = left[:, :F]
         lim = left[:, F:]
         rre = right_ref[0, w, :, :F].astype(jnp.float32)
@@ -79,7 +86,12 @@
         for l1 in range(sub):
             for part in range(2):
                 rows = l2 * C + part * half_rows
-                out_ref[part, l2 * sub + l1] = acc[rows : rows + half_rows, l1 * C : (l1 + 1) * C].astype(out_ref.dtype)
+                block = acc[rows : rows + half_rows, l1 * C : (l1 + 1) * C].astype(keep_ref.dtype)
+                if part:
+                    keep_ref[l2 * sub + l1] = block
+                else:
+                    far_ref[l2 * sub + l1] = block[: half_rows - own_rows]
+                    near_ref[l2 * sub + l1] = block[half_rows - own_rows :]
 
 
 def tile_correlation(cc, sc, cf, sf, incoming, slots, sub, n_y, own_rows):
@@ -93,12 +105,20 @@
         num_scalar_prefetch=1,
         grid=(slot_count,),
         in_specs=[table_spec] * 4 + [left_spec, right_spec],
-        out_specs=pl.BlockSpec((2, LAGS, C // 2, C), lambda t, idx: (0, 0, 0, t)),
+        out_specs=[
+            pl.BlockSpec((LAGS, C // 2 - own_rows, C), lambda t, idx: (0, 0, t)),
+            pl.BlockSpec((LAGS, own_rows, C), lambda t, idx: (0, 0, t)),
+            pl.BlockSpec((LAGS, C // 2, C), lambda t, idx: (0, 0, t)),
+        ],
     )
     return pl.pallas_call(
         functools.partial(correlation_kernel, sub, n_y, own_rows),
         grid_spec=grid_spec,
-        out_shape=jax.ShapeDtypeStruct((2, LAGS, C // 2, slot_count * C), jnp.bfloat16),
+        out_shape=[
+            jax.ShapeDtypeStruct((LAGS, C // 2 - own_rows, slot_count * C), jnp.bfloat16),
+            jax.ShapeDtypeStruct((LAGS, own_rows, slot_count * C), jnp.bfloat16),
+            jax.ShapeDtypeStruct((LAGS, C // 2, slot_count * C), jnp.bfloat16),
+        ],
         cost_estimate=pl.CostEstimate(
             flops=flops, transcendentals=0, bytes_accessed=slot_count * (4 * window_count * C * F * 2 + 2 * C * LAGS * C)
         ),
@@ -185,17 +205,19 @@
 
     core = win_here % 2
     y_here = win_here // 2
-    send = jnp.take(corr, 1 - core, axis=0, mode="clip")
-    keep = jnp.take(corr, core, axis=0, mode="clip").astype(jnp.float32)
-    got = lax.ppermute(send, "win", [(w, w ^ 1) for w in range(n_win)])
-    half = (keep + got.astype(jnp.float32)).reshape(LAGS, n_y, own_rows, slot_count * C)
-    half = jnp.transpose(half, (1, 0, 2, 3))
-    total = jnp.take(half, y_here, axis=0, mode="clip")
+    far, near, keep = corr
+    core_pairs = [(w, w ^ 1) for w in range(n_win)]
+    got_far = lax.ppermute(far, "win", core_pairs)
+    pieces = []
     for shift in range(1, n_y):
-        dest = (y_here + shift) % n_y
-        piece = jnp.take(half, dest, axis=0, mode="clip").astype(jnp.bfloat16)
+        rows = slice((shift - 1) * own_rows, shift * own_rows)
+        piece = keep[:, rows].astype(jnp.float32) + got_far[:, rows].astype(jnp.float32)
         perm = [(w, ((w // 2 + shift) % n_y) * 2 + w % 2) for w in range(n_win)]
-        total = total + lax.ppermute(piece, "win", perm).astype(jnp.float32)
+        pieces.append(lax.ppermute(piece.astype(jnp.bfloat16), "win", perm))
+    got_near = lax.ppermute(near, "win", core_pairs)
+    total = keep[:, (n_y - 1) * own_rows :].astype(jnp.float32) + got_near.astype(jnp.float32)
+    for piece in pieces:
+        total = total + piece.astype(jnp.float32)
     total = jnp.transpose(total.reshape(LAGS, own_rows, slot_count, C), (1, 2, 0, 3))
 
     live_local = tile_live.astype(jnp.float32)

time: 74.3 us -> 72.8 us (0.980)
  local copies, waits for them, and re-layouts: 5.68 us -> 2.71 us
  other arithmetic: 9.2 us -> 11.2 us
  waiting for transfers between devices: 30.6 us -> 29.7 us
    div x1 -> x0, local copies, waits for them, and re-layouts: 1.58 us -> none  [body(): total * live_local[None, :, None, None]]
    gather x1 -> x0, local copies, waits for them, and re-layouts: 1.33 us -> none  [body(): send = jnp.take(corr, 1 - core, axis=0, mode='clip')]
    div x1, other arithmetic: 0.36 us -> 1.65 us  [body(): total * live_local[None, :, None, None]]
    convert_element_type x0 -> x1, other arithmetic: none -> 1.2 us  [body(): pieces.append(lax.ppermute(piece.astype(jnp.bfloat16), 'win', perm))]
    ppermute x2 -> x3, waiting for transfers between devices: 15.3 us -> 14.3 us  [the longest x1 12.7 us: body(): pieces.append(lax.ppermute(piece.astype(jnp.bfloat16), 'win', perm))]
    add x2 -> x1, other arithmetic: 1.72 us -> 1.27 us  [body(): total = total + piece.astype(jnp.float32)]
    ppermute x2 -> x3, starting transfers between devices: 1.42 us -> 1.84 us  [the longest x1 1.33 us: body(): pieces.append(lax.ppermute(piece.astype(jnp.bfloat16), 'win', perm))]
  transfers between devices with their start and end apart: 10 -> 11, of which waited for: 7 -> 7; matrix products, arithmetic and copies ran while one was open for 2% -> 4% of each run, Pallas kernels for 0% -> 0%
where the time goes in v19:
time: 72.8 us; the launch traced here: 72.5 us
  waiting for transfers between devices  29.7 us (41%)
  starting transfers between devices  14.4 us (20%)
  other arithmetic  11.2 us (15%)
  Pallas kernels  5.76 us (8%)
  between operations  5.27 us (7%)
  matrix products  3.38 us (5%)
  local copies, waits for them, and re-layouts  2.71 us (4%)
    ppermute x1, waiting for transfers between devices, body(): pieces.append(lax.ppermute(piece.astype(jnp.bfloat16), 'win', perm))  12.7 us
    ppermute x2, waiting for transfers between devices, exchange_by_halves(): lax.ppermute(block, 'pair', across)  8.03 us
    ppermute x3, waiting for transfers between devices, exchange_by_halves(): relay = lax.ppermute(relay, 'pair', perm)  7.37 us
    pallas_call x1, Pallas kernels, tile_correlation(): pl.pallas_call(functools.partial(correlation_kernel, sub, n_y, own_rows),...  5.76 us
    ppermute x3, starting transfers between devices, exchange_by_halves(): own = lax.ppermute(own, 'pair', perm)  4.76 us
    ppermute x2, starting transfers between devices, exchange_by_halves(): lax.ppermute(block, 'pair', across)  4.18 us
    another operation x3, other arithmetic  3.72 us
    ppermute x3, starting transfers between devices, exchange_by_halves(): relay = lax.ppermute(relay, 'pair', perm)  3.64 us
  transfers between devices with their start and end apart: 11, of which 7 were waited for; matrix products, arithmetic and copies ran while one was open for 4% of the time, Pallas kernels for 0%

profile of v19, /device:TPU:0, one launch (start us, length us, event | category | flops | bytes accessed | tf_op | source)
XLA Modules:
  0.0 72.5 jit_solution(3711707098240253492)
XLA Ops:
  0.0 0.8 %fusion.20 = (f32[128,384]{1,0:T(8,128)S(1)}, f32[128,384]{1,0:T(8,128)S(1)}) fusion(s32[384]{0:T(512)S(1)} %iota_add_fusion), kind=kLoop, calls=%fused_computation.40 | loop fusion | flops 442368 | bytes 394752 | tf_op jit(solution)/shard_map/cos | solution.py:20
  0.8 0.5 fusion.27
  1.3 0.0 copy-start.2
  1.3 3.5 %subtract_convert_fusion = (bf16[60,128,384]{2,1,0:T(8,128)(2,1)S(1)}, bf16[60,128,384]{2,1,0:T(8,128)(2,1)S(1)}) fusion(f32[128,384]{1,0:T(8,128)S(1)} %get-tuple-element.122, f32[60,384]{1,0:T(8,128)S(1)} %get-tuple-element.116, f32[128,384]{1,0:T(8,128)S(1)} %get-tuple-element.121, f32[60,384]{1,0:T(8,128)S(1)} %get-tuple-element.115), kind=kLoop, calls=%fused_computation.2 | loop fusion | flops 26542080 | bytes 12374016 | tf_op jit(solution)/shard_map/convert.19
  4.8 1.7 %fusion.6 = f32[128,768]{1,0:T(8,128)S(1)} fusion(bf16[7680,384]{1,0:T(8,128)(2,1)S(1)} %bitcast.50, bf16[7680,384]{1,0:T(8,128)(2,1)S(1)} %bitcast.48, bf16[1,256,7680]{2,1,0:T(8,128)(2,1)S(1)} %copy-done.2), kind=kOutput, calls=%fused_computation.9 | convolution fusion | flops 1533542400 | bytes 14155776 | tf_op jit(solution)/shard_map/dot_general | solution.py:36
  6.5 0.0 copy-start.1
  6.5 1.7 %fusion.9 = f32[128,768]{1,0:T(8,128)S(1)} fusion(bf16[7680,384]{1,0:T(8,128)(2,1)S(1)} %bitcast.51, bf16[7680,384]{1,0:T(8,128)(2,1)S(1)} %bitcast.49, bf16[1,256,7680]{2,1,0:T(8,128)(2,1)S(1)} %copy-done.2), kind=kOutput, calls=%fused_computation.10 | convolution fusion | flops 1533542400 | bytes 14155776 | tf_op jit(solution)/shard_map/dot_general | solution.py:36
  8.3 0.1 reduce_sum.43
  8.4 0.1 reduce_sum.52
  8.5 0.1 reduce_sum.56
  8.6 0.1 reduce_sum.57
  8.7 0.7 fusion.52
  11.3 0.2 fusion.50
  11.5 0.1 divide_convert_fusion.1
  11.7 0.1 divide_convert_fusion.3
  11.8 0.1 broadcast_select_fusion.3
  11.9 4.1 %collective-permute-start.3 = (bf16[1,128,768]{2,1,0:T(8,128)(2,1)S(1)}, bf16[1,128,768]{2,1,0:T(8,128)(2,1)S(1)}, u32[]{:S(2)}, u32[]{:S(2)}) collective-permute-start(bf16[1,128,768]{2,1,0:T(8,128)(2,1)S(1)} %get-tuple-element.114), channel_id=1, source_target_pairs={{0,4},{1,5},{2,6},{3,7},{4,0},{5,1},{6,2},{7,3},{8,12},{9,13},{10,... | collective-permute-start | bytes 589832 | tf_op jit(solution)/shard_map/ppermute | solution.py:146
  16.0 0.1 collective-permute-start.4
  16.1 1.7 %collective-permute-start = (bf16[1,128,768]{2,1,0:T(8,128)(2,1)S(1)}, bf16[1,128,768]{2,1,0:T(8,128)(2,1)S(1)}, u32[]{:S(2)}, u32[]{:S(2)}) collective-permute-start(bf16[1,128,768]{2,1,0:T(8,128)(2,1)S(1)} %get-tuple-element.111), channel_id=1, source_target_pairs={{0,1},{1,2},{2,3},{3,0},{4,5},{5,6},{6,7},{7,4},{8,9},{9,10},{10,1... | collective-permute-start | bytes 589832 | tf_op jit(solution)/shard_map/ppermute | solution.py:157
  17.8 1.6 %collective-permute-start.1 = (bf16[1,128,768]{2,1,0:T(8,128)(2,1)S(1)}, bf16[1,128,768]{2,1,0:T(8,128)(2,1)S(1)}, u32[]{:S(2)}, u32[]{:S(2)}) collective-permute-start(bf16[1,128,768]{2,1,0:T(8,128)(2,1)S(1)} %get-tuple-element.112), channel_id=1, source_target_pairs={{0,2},{1,3},{2,0},{3,1},{4,6},{5,7},{6,4},{7,5},{8,10},{9,11},{10,... | collective-permute-start | bytes 589832 | tf_op jit(solution)/shard_map/ppermute | solution.py:157
  19.4 1.4 %collective-permute-start.2 = (bf16[1,128,768]{2,1,0:T(8,128)(2,1)S(1)}, bf16[1,128,768]{2,1,0:T(8,128)(2,1)S(1)}, u32[]{:S(2)}, u32[]{:S(2)}) collective-permute-start(bf16[1,128,768]{2,1,0:T(8,128)(2,1)S(1)} %get-tuple-element.110), channel_id=1, source_target_pairs={{0,3},{1,0},{2,1},{3,2},{4,7},{5,4},{6,5},{7,6},{8,11},{9,8},{10,9... | collective-permute-start | bytes 589832 | tf_op jit(solution)/shard_map/ppermute | solution.py:157
  23.9 0.1 constant_dynamic-slice_fusion
  24.0 0.1 copy.8
  24.1 0.1 reshape.464
  24.2 0.8 %fusion.39 = (f32[4,384]{1,0:T(4,128)}, f32[4,384]{1,0:T(4,128)}, f32[4,384]{1,0:T(4,128)}, f32[4,384]{1,0:T(4,128)}) fusion(s32[384]{0:T(512)S(1)} %iota_add_fusion, s32[4]{0:T(128)S(1)} %get-tuple-element.137, s32[4]{0:T(128)S(1)} %get-tuple-element.138), kind=kLoop, calls=%fused_computation.71 | loop fusion | flops 27648 | bytes 26144 | tf_op jit(solution)/shard_map/sin | solution.py:20
  25.0 0.5 fusion.47.index_ref
  25.6 4.7 %collective-permute-done.3 = bf16[1,128,768]{2,1,0:T(8,128)(2,1)S(1)} collective-permute-done((bf16[1,128,768]{2,1,0:T(8,128)(2,1)S(1)}, bf16[1,128,768]{2,1,0:T(8,128)(2,1)S(1)}, u32[]{:S(2)}, u32[]{:S(2)}) %collective-permute-start.3) | collective-permute-done | bytes 196640 | tf_op jit(solution)/shard_map/ppermute | solution.py:146
  30.3 3.4 %collective-permute-done.4 = bf16[1,128,768]{2,1,0:T(8,128)(2,1)S(1)} collective-permute-done((bf16[1,128,768]{2,1,0:T(8,128)(2,1)S(1)}, bf16[1,128,768]{2,1,0:T(8,128)(2,1)S(1)}, u32[]{:S(2)}, u32[]{:S(2)}) %collective-permute-start.4) | collective-permute-done | bytes 196640 | tf_op jit(solution)/shard_map/ppermute | solution.py:146
  33.7 1.6 %collective-permute-start.5 = (bf16[1,128,768]{2,1,0:T(8,128)(2,1)S(1)}, bf16[1,128,768]{2,1,0:T(8,128)(2,1)S(1)}, u32[]{:S(2)}, u32[]{:S(2)}) collective-permute-start(bf16[1,128,768]{2,1,0:T(8,128)(2,1)S(1)} %get-tuple-element.109), channel_id=1, source_target_pairs={{0,1},{1,2},{2,3},{3,0},{4,5},{5,6},{6,7},{7,4},{8,9},{9,10},{10,1... | collective-permute-start | bytes 589832 | tf_op jit(solution)/shard_map/ppermute | solution.py:158
  35.3 0.6 collective-permute-start.6
  35.9 0.0 collective-permute-done
  35.9 1.4 %collective-permute-start.7 = (bf16[1,128,768]{2,1,0:T(8,128)(2,1)S(1)}, bf16[1,128,768]{2,1,0:T(8,128)(2,1)S(1)}, u32[]{:S(2)}, u32[]{:S(2)}) collective-permute-start(bf16[1,128,768]{2,1,0:T(8,128)(2,1)S(1)} %get-tuple-element.107), channel_id=1, source_target_pairs={{0,3},{1,0},{2,1},{3,2},{4,7},{5,4},{6,5},{7,6},{8,11},{9,8},{10,9... | collective-permute-start | bytes 589832 | tf_op jit(solution)/shard_map/ppermute | solution.py:158
  37.3 0.0 collective-permute-done.1
  37.4 0.0 collective-permute-done.2
  37.4 0.1 bitcast_dynamic-update-slice_fusion.3
  37.5 5.0 %collective-permute-done.5 = bf16[1,128,768]{2,1,0:T(8,128)(2,1)S(1)} collective-permute-done((bf16[1,128,768]{2,1,0:T(8,128)(2,1)S(1)}, bf16[1,128,768]{2,1,0:T(8,128)(2,1)S(1)}, u32[]{:S(2)}, u32[]{:S(2)}) %collective-permute-start.5) | collective-permute-done | bytes 196640 | tf_op jit(solution)/shard_map/ppermute | solution.py:158
  42.5 0.3 collective-permute-done.6
  42.8 2.0 %collective-permute-done.7 = bf16[1,128,768]{2,1,0:T(8,128)(2,1)S(1)} collective-permute-done((bf16[1,128,768]{2,1,0:T(8,128)(2,1)S(1)}, bf16[1,128,768]{2,1,0:T(8,128)(2,1)S(1)}, u32[]{:S(2)}, u32[]{:S(2)}) %collective-permute-start.7) | collective-permute-done | bytes 196640 | tf_op jit(solution)/shard_map/ppermute | solution.py:158
  44.9 1.1 %copy-done = bf16[8,1,128,768]{3,2,1,0:T(8,128)(2,1)} copy-done((bf16[8,1,128,768]{3,2,1,0:T(8,128)(2,1)}, bf16[8,1,128,768]{3,2,1,0:T(8,128)(2,1)S(1)}, u32[]{:S(2)}) %copy-start) | copy-done | bytes 1572888
  46.0 5.8 %shard_map.37 = (bf16[16,32,512]{2,1,0:T(8,128)(2,1)}, bf16[16,32,512]{2,1,0:T(8,128)(2,1)}, bf16[16,64,512]{2,1,0:T(8,128)(2,1)}) custom-call(s32[8]{0:T(128)} %fusion.47.index_ref, f32[4,384]{1,0:T(4,128)} %get-tuple-element.123.cc_ref, f32[4,384]{1,0:T(4,128)} %get-tuple-element.124.sc_ref, f32[4,384]{1,0:T(4,128)} %get-tuple-element.118.cf_ref, ...), custom_call_target="tpu_custom_call" | custom-call | flops 1610612736 | bytes 3670016 | tf_op jit(solution)/shard_map/pallas_call | solution.py:114
  51.8 0.5 collective-permute-start.8
  52.3 1.6 %collective-permute-done.9 = bf16[16,32,512]{2,1,0:T(8,128)(2,1)S(1)} collective-permute-done((bf16[16,32,512]{2,1,0:T(8,128)(2,1)}, bf16[16,32,512]{2,1,0:T(8,128)(2,1)S(1)}, u32[]{:S(2)}, u32[]{:S(2)}) %collective-permute-start.9) | collective-permute-done | bytes 524320 | tf_op jit(solution)/shard_map/ppermute | solution.py:210
  53.9 1.2 %add_convert_fusion = bf16[16,32,512]{2,1,0:T(8,128)(2,1)S(1)} fusion(bf16[16,32,512]{2,1,0:T(8,128)(2,1)S(1)} %collective-permute-done.9, bf16[16,64,512]{2,1,0:T(8,128)(2,1)} %get-tuple-element.8), kind=kLoop, calls=%fused_computation.15 | loop fusion | flops 1048576 | bytes 1572864 | tf_op jit(solution)/shard_map/convert_element_type | solution.py:216
  55.1 1.3 %collective-permute-start.10 = (bf16[16,32,512]{2,1,0:T(8,128)(2,1)S(1)}, bf16[16,32,512]{2,1,0:T(8,128)(2,1)S(1)}, u32[]{:S(2)}, u32[]{:S(2)}) collective-permute-start(bf16[16,32,512]{2,1,0:T(8,128)(2,1)S(1)} %add_convert_fusion), channel_id=1, source_target_pairs={{0,16},{8,24},{16,0},{24,8},{1,17},{9,25},{17,1},{25,9},{2,18},{10... | collective-permute-start | bytes 1572872 | tf_op jit(solution)/shard_map/ppermute | solution.py:216
  56.5 12.7 %collective-permute-done.10 = bf16[16,32,512]{2,1,0:T(8,128)(2,1)S(1)} collective-permute-done((bf16[16,32,512]{2,1,0:T(8,128)(2,1)S(1)}, bf16[16,32,512]{2,1,0:T(8,128)(2,1)S(1)}, u32[]{:S(2)}, u32[]{:S(2)}) %collective-permute-start.10) | collective-permute-done | bytes 524320 | tf_op jit(solution)/shard_map/ppermute | solution.py:216
  69.2 1.3 %convert_add_fusion = f32[16,32,512]{2,1,0:T(8,128)S(1)} fusion(bf16[16,32,512]{2,1,0:T(8,128)(2,1)S(1)} %collective-permute-done.10, bf16[16,32,512]{2,1,0:T(8,128)(2,1)S(1)} %collective-permute-done.8, bf16[16,64,512]{2,1,0:T(8,128)(2,1)} %get-tuple-element.8), kind=kLoop, calls=%fused_computation.14 | loop fusion | flops 1310720 | bytes 2621440 | tf_op jit(solution)/shard_map/add | solution.py:220
  70.4 0.4 reshape.467
  70.8 1.7 %fusion.13 = f32[32,4,16,128]{3,2,1,0:T(8,128)} fusion(f32[16,32,4,128]{3,2,1,0:T(4,128)S(1)} %reshape.467, f32[4]{0:T(128)S(1)} %convert_element_type.127), kind=kLoop, calls=%fused_computation.13 | loop fusion | flops 524288 | bytes 2097168 | tf_op jit(solution)/shard_map/div | solution.py:224
  (22 shorter events, 0.2 us)
Async XLA Ops:
  1.3 3.5 %copy-start.2 = (bf16[1,256,7680]{2,1,0:T(8,128)(2,1)S(1)}, bf16[1,256,7680]{2,1,0:T(8,128)(2,1)}, u32[]{:S(2)}) copy-start(bf16[1,256,7680]{2,1,0:T(8,128)(2,1)} %param.3) | copy-start | bytes 11796484
  6.5 1.8 %copy-start.1 = (s32[32,2]{0,1:T(2,128)S(1)}, s32[32,2]{0,1:T(2,128)}, u32[]{:S(2)}) copy-start(s32[32,2]{0,1:T(2,128)} %param.4) | copy-start | bytes 772
  11.9 18.4 %collective-permute-start.3 = (bf16[1,128,768]{2,1,0:T(8,128)(2,1)S(1)}, bf16[1,128,768]{2,1,0:T(8,128)(2,1)S(1)}, u32[]{:S(2)}, u32[]{:S(2)}) collective-permute-start(bf16[1,128,768]{2,1,0:T(8,128)(2,1)S(1)} %get-tuple-element.114), channel_id=1, source_target_pairs={{0,4},{1,5},{2,6},{3,7},{4,0},{5,1},{6,2},{7,3},{8,12},{9,13},{10,... | collective-permute-start | bytes 589832 | tf_op jit(solution)/shard_map/ppermute | solution.py:146
  16.0 17.6 %collective-permute-start.4 = (bf16[1,128,768]{2,1,0:T(8,128)(2,1)S(1)}, bf16[1,128,768]{2,1,0:T(8,128)(2,1)S(1)}, u32[]{:S(2)}, u32[]{:S(2)}) collective-permute-start(bf16[1,128,768]{2,1,0:T(8,128)(2,1)S(1)} %get-tuple-element.113), channel_id=1, source_target_pairs={{0,4},{1,5},{2,6},{3,7},{4,0},{5,1},{6,2},{7,3},{8,12},{9,13},{10,... | collective-permute-start | bytes 589832 | tf_op jit(solution)/shard_map/ppermute | solution.py:146
  16.1 19.8 %collective-permute-start = (bf16[1,128,768]{2,1,0:T(8,128)(2,1)S(1)}, bf16[1,128,768]{2,1,0:T(8,128)(2,1)S(1)}, u32[]{:S(2)}, u32[]{:S(2)}) collective-permute-start(bf16[1,128,768]{2,1,0:T(8,128)(2,1)S(1)} %get-tuple-element.111), channel_id=1, source_target_pairs={{0,1},{1,2},{2,3},{3,0},{4,5},{5,6},{6,7},{7,4},{8,9},{9,10},{10,1... | collective-permute-start | bytes 589832 | tf_op jit(solution)/shard_map/ppermute | solution.py:157
  17.8 19.5 %collective-permute-start.1 = (bf16[1,128,768]{2,1,0:T(8,128)(2,1)S(1)}, bf16[1,128,768]{2,1,0:T(8,128)(2,1)S(1)}, u32[]{:S(2)}, u32[]{:S(2)}) collective-permute-start(bf16[1,128,768]{2,1,0:T(8,128)(2,1)S(1)} %get-tuple-element.112), channel_id=1, source_target_pairs={{0,2},{1,3},{2,0},{3,1},{4,6},{5,7},{6,4},{7,5},{8,10},{9,11},{10,... | collective-permute-start | bytes 589832 | tf_op jit(solution)/shard_map/ppermute | solution.py:157
  19.4 18.0 %collective-permute-start.2 = (bf16[1,128,768]{2,1,0:T(8,128)(2,1)S(1)}, bf16[1,128,768]{2,1,0:T(8,128)(2,1)S(1)}, u32[]{:S(2)}, u32[]{:S(2)}) collective-permute-start(bf16[1,128,768]{2,1,0:T(8,128)(2,1)S(1)} %get-tuple-element.110), channel_id=1, source_target_pairs={{0,3},{1,0},{2,1},{3,2},{4,7},{5,4},{6,5},{7,6},{8,11},{9,8},{10,9... | collective-permute-start | bytes 589832 | tf_op jit(solution)/shard_map/ppermute | solution.py:157
  25.0 31.5 %copy-start.3 = (s32[4]{0:T(128)S(1)}, s32[4]{0:T(128)}, u32[]{:S(2)}) copy-start(s32[4]{0:T(128)} %param.5) | copy-start | bytes 52
  33.7 8.8 %collective-permute-start.5 = (bf16[1,128,768]{2,1,0:T(8,128)(2,1)S(1)}, bf16[1,128,768]{2,1,0:T(8,128)(2,1)S(1)}, u32[]{:S(2)}, u32[]{:S(2)}) collective-permute-start(bf16[1,128,768]{2,1,0:T(8,128)(2,1)S(1)} %get-tuple-element.109), channel_id=1, source_target_pairs={{0,1},{1,2},{2,3},{3,0},{4,5},{5,6},{6,7},{7,4},{8,9},{9,10},{10,1... | collective-permute-start | bytes 589832 | tf_op jit(solution)/shard_map/ppermute | solution.py:158
  35.3 7.6 %collective-permute-start.6 = (bf16[1,128,768]{2,1,0:T(8,128)(2,1)S(1)}, bf16[1,128,768]{2,1,0:T(8,128)(2,1)S(1)}, u32[]{:S(2)}, u32[]{:S(2)}) collective-permute-start(bf16[1,128,768]{2,1,0:T(8,128)(2,1)S(1)} %get-tuple-element.108), channel_id=1, source_target_pairs={{0,2},{1,3},{2,0},{3,1},{4,6},{5,7},{6,4},{7,5},{8,10},{9,11},{10,... | collective-permute-start | bytes 589832 | tf_op jit(solution)/shard_map/ppermute | solution.py:158
  35.9 9.0 %collective-permute-start.7 = (bf16[1,128,768]{2,1,0:T(8,128)(2,1)S(1)}, bf16[1,128,768]{2,1,0:T(8,128)(2,1)S(1)}, u32[]{:S(2)}, u32[]{:S(2)}) collective-permute-start(bf16[1,128,768]{2,1,0:T(8,128)(2,1)S(1)} %get-tuple-element.107), channel_id=1, source_target_pairs={{0,3},{1,0},{2,1},{3,2},{4,7},{5,4},{6,5},{7,6},{8,11},{9,8},{10,9... | collective-permute-start | bytes 589832 | tf_op jit(solution)/shard_map/ppermute | solution.py:158
  44.9 1.2 %copy-start = (bf16[8,1,128,768]{3,2,1,0:T(8,128)(2,1)}, bf16[8,1,128,768]{3,2,1,0:T(8,128)(2,1)S(1)}, u32[]{:S(2)}) copy-start(bf16[8,1,128,768]{3,2,1,0:T(8,128)(2,1)S(1)} %bitcast_dynamic-update-slice_fusion.left_ref.right_ref) | copy-start | bytes 4718596
  51.8 2.1 %collective-permute-start.9 = (bf16[16,32,512]{2,1,0:T(8,128)(2,1)}, bf16[16,32,512]{2,1,0:T(8,128)(2,1)S(1)}, u32[]{:S(2)}, u32[]{:S(2)}) collective-permute-start(bf16[16,32,512]{2,1,0:T(8,128)(2,1)} %get-tuple-element.10), channel_id=1, source_target_pairs={{0,8},{8,0},{16,24},{24,16},{1,9},{9,1},{17,25},{25,17},{2,10},{10... | collective-permute-start | bytes 1572872 | tf_op jit(solution)/shard_map/ppermute | solution.py:210
  51.8 4.7 %collective-permute-start.8 = (bf16[16,32,512]{2,1,0:T(8,128)(2,1)}, bf16[16,32,512]{2,1,0:T(8,128)(2,1)S(1)}, u32[]{:S(2)}, u32[]{:S(2)}) collective-permute-start(bf16[16,32,512]{2,1,0:T(8,128)(2,1)} %get-tuple-element.9), channel_id=1, source_target_pairs={{0,8},{8,0},{16,24},{24,16},{1,9},{9,1},{17,25},{25,17},{2,10},{10... | collective-permute-start | bytes 1572872 | tf_op jit(solution)/shard_map/ppermute | solution.py:217
  55.1 14.0 %collective-permute-start.10 = (bf16[16,32,512]{2,1,0:T(8,128)(2,1)S(1)}, bf16[16,32,512]{2,1,0:T(8,128)(2,1)S(1)}, u32[]{:S(2)}, u32[]{:S(2)}) collective-permute-start(bf16[16,32,512]{2,1,0:T(8,128)(2,1)S(1)} %add_convert_fusion), channel_id=1, source_target_pairs={{0,16},{8,24},{16,0},{24,8},{1,17},{9,25},{17,1},{25,9},{2,18},{10... | collective-permute-start | bytes 1572872 | tf_op jit(solution)/shard_map/ppermute | solution.py:216

commit v20 on v17

--- a/solution.py
+++ b/solution.py
@@ -23,9 +23,11 @@
 def dft_table(sample_count, bin_count):
     bin_index = lax.iota(jnp.int32, bin_count) + 1
     coarse = lax.iota(jnp.int32, sample_count // SPLIT) * SPLIT
-    fine = lax.iota(jnp.int32, SPLIT)
     ca, sa = cos_sin(coarse[:, None] * bin_index[None, :], sample_count)
-    cb, sb = cos_sin(fine[:, None] * bin_index[None, :], sample_count)
+    c1, s1 = cos_sin((lax.iota(jnp.int32, SPLIT // 16) * 16)[:, None] * bin_index[None, :], sample_count)
+    c0, s0 = cos_sin(lax.iota(jnp.int32, 16)[:, None] * bin_index[None, :], sample_count)
+    cb = (c1[:, None, :] * c0[None, :, :] - s1[:, None, :] * s0[None, :, :]).reshape(SPLIT, bin_count)
+    sb = (s1[:, None, :] * c0[None, :, :] + c1[:, None, :] * s0[None, :, :]).reshape(SPLIT, bin_count)
     cos_t = ca[:, None, :] * cb[None, :, :] - sa[:, None, :] * sb[None, :, :]
     sin_t = sa[:, None, :] * cb[None, :, :] + ca[:, None, :] * sb[None, :, :]
     table = jnp.concatenate([cos_t, -sin_t], axis=2).astype(jnp.bfloat16)

time: 71.6 us -> 71.2 us (level)
  no operation moved by 1% of the time
where the time goes in v20:
time: 71.2 us; the launch traced here: 70.9 us
  waiting for transfers between devices  29.4 us (41%)
  starting transfers between devices  13.9 us (20%)
  other arithmetic  8.91 us (13%)
  Pallas kernels  5.76 us (8%)
  between operations  5.3 us (7%)
  local copies, waits for them, and re-layouts  4.29 us (6%)
  matrix products  3.38 us (5%)
    ppermute x1, waiting for transfers between devices, body(): lax.ppermute(chip_sum(dest).astype(jnp.bfloat16), 'win', perm)  12.7 us
    ppermute x2, waiting for transfers between devices, exchange_by_halves(): lax.ppermute(block, 'pair', across)  7.99 us
    ppermute x3, waiting for transfers between devices, exchange_by_halves(): relay = lax.ppermute(relay, 'pair', perm)  7.36 us
    pallas_call x1, Pallas kernels, tile_correlation(): pl.pallas_call(functools.partial(correlation_kernel, sub, n_y, own_rows),...  5.76 us
    ppermute x3, starting transfers between devices, exchange_by_halves(): own = lax.ppermute(own, 'pair', perm)  4.76 us
    ppermute x2, starting transfers between devices, exchange_by_halves(): lax.ppermute(block, 'pair', across)  4.18 us
    another operation x3, other arithmetic  3.72 us
    ppermute x3, starting transfers between devices, exchange_by_halves(): relay = lax.ppermute(relay, 'pair', perm)  3.64 us
  transfers between devices with their start and end apart: 10, of which 7 were waited for; matrix products, arithmetic and copies ran while one was open for 5% of the time, Pallas kernels for 0%

profile of v20, /device:TPU:0, one launch (start us, length us, event | category | flops | bytes accessed | tf_op | source)
XLA Modules:
  0.0 70.9 jit_solution(12427180711837953603)
XLA Ops:
  0.0 0.1 fusion.29
  0.1 0.1 fusion.36
  0.3 0.5 fusion.22
  0.8 0.0 copy-start.2
  0.8 3.5 %subtract_convert_fusion = (bf16[60,128,384]{2,1,0:T(8,128)(2,1)S(1)}, bf16[60,128,384]{2,1,0:T(8,128)(2,1)S(1)}) fusion(f32[128,384]{1,0:T(8,128)S(1)} %bitcast.91, f32[60,384]{1,0:T(8,128)S(1)} %get-tuple-element.160, f32[128,384]{1,0:T(8,128)S(1)} %bitcast.90, f32[60,384]{1,0:T(8,128)S(1)} %get-tuple-element.159), kind=kLoop, calls=%fused_computation.2 | loop fusion | flops 26542080 | bytes 12374016 | tf_op jit(solution)/shard_map/convert.20
  4.3 1.7 %fusion.6 = f32[128,768]{1,0:T(8,128)S(1)} fusion(bf16[7680,384]{1,0:T(8,128)(2,1)S(1)} %bitcast.77, bf16[7680,384]{1,0:T(8,128)(2,1)S(1)} %bitcast.75, bf16[1,256,7680]{2,1,0:T(8,128)(2,1)S(1)} %copy-done.2), kind=kOutput, calls=%fused_computation.9 | convolution fusion | flops 1533542400 | bytes 14155776 | tf_op jit(solution)/shard_map/dot_general | solution.py:38
  6.0 0.0 copy-start.1
  6.0 1.7 %fusion.9 = f32[128,768]{1,0:T(8,128)S(1)} fusion(bf16[7680,384]{1,0:T(8,128)(2,1)S(1)} %bitcast.78, bf16[7680,384]{1,0:T(8,128)(2,1)S(1)} %bitcast.76, bf16[1,256,7680]{2,1,0:T(8,128)(2,1)S(1)} %copy-done.2), kind=kOutput, calls=%fused_computation.10 | convolution fusion | flops 1533542400 | bytes 14155776 | tf_op jit(solution)/shard_map/dot_general | solution.py:38
  7.8 0.2 fusion.59
  8.0 0.1 divide_convert_fusion.1
  8.2 0.1 divide_convert_fusion.3
  8.4 0.1 reduce_sum.43
  8.5 0.1 reduce_sum.52
  8.6 0.1 reduce_sum.56
  8.7 0.1 reduce_sum.57
  8.8 0.7 fusion.61
  11.3 0.1 broadcast_select_fusion.3
  11.4 4.1 %collective-permute-start.3 = (bf16[1,128,768]{2,1,0:T(8,128)(2,1)S(1)}, bf16[1,128,768]{2,1,0:T(8,128)(2,1)S(1)}, u32[]{:S(2)}, u32[]{:S(2)}) collective-permute-start(bf16[1,128,768]{2,1,0:T(8,128)(2,1)S(1)} %get-tuple-element.156), channel_id=1, source_target_pairs={{0,4},{1,5},{2,6},{3,7},{4,0},{5,1},{6,2},{7,3},{8,12},{9,13},{10,... | collective-permute-start | bytes 589832 | tf_op jit(solution)/shard_map/ppermute | solution.py:131
  15.5 0.1 collective-permute-start.4
  15.6 1.7 %collective-permute-start = (bf16[1,128,768]{2,1,0:T(8,128)(2,1)S(1)}, bf16[1,128,768]{2,1,0:T(8,128)(2,1)S(1)}, u32[]{:S(2)}, u32[]{:S(2)}) collective-permute-start(bf16[1,128,768]{2,1,0:T(8,128)(2,1)S(1)} %get-tuple-element.153), channel_id=1, source_target_pairs={{0,1},{1,2},{2,3},{3,0},{4,5},{5,6},{6,7},{7,4},{8,9},{9,10},{10,1... | collective-permute-start | bytes 589832 | tf_op jit(solution)/shard_map/ppermute | solution.py:142
  17.3 1.6 %collective-permute-start.1 = (bf16[1,128,768]{2,1,0:T(8,128)(2,1)S(1)}, bf16[1,128,768]{2,1,0:T(8,128)(2,1)S(1)}, u32[]{:S(2)}, u32[]{:S(2)}) collective-permute-start(bf16[1,128,768]{2,1,0:T(8,128)(2,1)S(1)} %get-tuple-element.154), channel_id=1, source_target_pairs={{0,2},{1,3},{2,0},{3,1},{4,6},{5,7},{6,4},{7,5},{8,10},{9,11},{10,... | collective-permute-start | bytes 589832 | tf_op jit(solution)/shard_map/ppermute | solution.py:142
  18.9 1.4 %collective-permute-start.2 = (bf16[1,128,768]{2,1,0:T(8,128)(2,1)S(1)}, bf16[1,128,768]{2,1,0:T(8,128)(2,1)S(1)}, u32[]{:S(2)}, u32[]{:S(2)}) collective-permute-start(bf16[1,128,768]{2,1,0:T(8,128)(2,1)S(1)} %get-tuple-element.152), channel_id=1, source_target_pairs={{0,3},{1,0},{2,1},{3,2},{4,7},{5,4},{6,5},{7,6},{8,11},{9,8},{10,9... | collective-permute-start | bytes 589832 | tf_op jit(solution)/shard_map/ppermute | solution.py:142
  23.4 0.1 constant_dynamic-slice_fusion
  23.5 0.1 copy.9
  23.6 0.1 reshape.592
  23.7 0.8 %fusion.48 = (f32[4,384]{1,0:T(4,128)}, f32[4,384]{1,0:T(4,128)}, f32[4,384]{1,0:T(4,128)}, f32[4,384]{1,0:T(4,128)}) fusion(s32[384]{0:T(512)S(1)} %iota_add_fusion, s32[4]{0:T(128)S(1)} %get-tuple-element.183, s32[4]{0:T(128)S(1)} %get-tuple-element.184), kind=kLoop, calls=%fused_computation.84 | loop fusion | flops 27648 | bytes 26144 | tf_op jit(solution)/shard_map/sin | solution.py:20
  24.5 0.6 fusion.56.index_ref
  25.1 4.6 %collective-permute-done.3 = bf16[1,128,768]{2,1,0:T(8,128)(2,1)S(1)} collective-permute-done((bf16[1,128,768]{2,1,0:T(8,128)(2,1)S(1)}, bf16[1,128,768]{2,1,0:T(8,128)(2,1)S(1)}, u32[]{:S(2)}, u32[]{:S(2)}) %collective-permute-start.3) | collective-permute-done | bytes 196640 | tf_op jit(solution)/shard_map/ppermute | solution.py:131
  29.8 3.4 %collective-permute-done.4 = bf16[1,128,768]{2,1,0:T(8,128)(2,1)S(1)} collective-permute-done((bf16[1,128,768]{2,1,0:T(8,128)(2,1)S(1)}, bf16[1,128,768]{2,1,0:T(8,128)(2,1)S(1)}, u32[]{:S(2)}, u32[]{:S(2)}) %collective-permute-start.4) | collective-permute-done | bytes 196640 | tf_op jit(solution)/shard_map/ppermute | solution.py:131
  33.2 1.6 %collective-permute-start.5 = (bf16[1,128,768]{2,1,0:T(8,128)(2,1)S(1)}, bf16[1,128,768]{2,1,0:T(8,128)(2,1)S(1)}, u32[]{:S(2)}, u32[]{:S(2)}) collective-permute-start(bf16[1,128,768]{2,1,0:T(8,128)(2,1)S(1)} %get-tuple-element.151), channel_id=1, source_target_pairs={{0,1},{1,2},{2,3},{3,0},{4,5},{5,6},{6,7},{7,4},{8,9},{9,10},{10,1... | collective-permute-start | bytes 589832 | tf_op jit(solution)/shard_map/ppermute | solution.py:143
  34.8 0.6 collective-permute-start.6
  35.4 1.4 %collective-permute-start.7 = (bf16[1,128,768]{2,1,0:T(8,128)(2,1)S(1)}, bf16[1,128,768]{2,1,0:T(8,128)(2,1)S(1)}, u32[]{:S(2)}, u32[]{:S(2)}) collective-permute-start(bf16[1,128,768]{2,1,0:T(8,128)(2,1)S(1)} %get-tuple-element.149), channel_id=1, source_target_pairs={{0,3},{1,0},{2,1},{3,2},{4,7},{5,4},{6,5},{7,6},{8,11},{9,8},{10,9... | collective-permute-start | bytes 589832 | tf_op jit(solution)/shard_map/ppermute | solution.py:143
  36.9 0.1 bitcast_dynamic-update-slice_fusion.3
  37.0 5.0 %collective-permute-done.5 = bf16[1,128,768]{2,1,0:T(8,128)(2,1)S(1)} collective-permute-done((bf16[1,128,768]{2,1,0:T(8,128)(2,1)S(1)}, bf16[1,128,768]{2,1,0:T(8,128)(2,1)S(1)}, u32[]{:S(2)}, u32[]{:S(2)}) %collective-permute-start.5) | collective-permute-done | bytes 196640 | tf_op jit(solution)/shard_map/ppermute | solution.py:143
  42.0 0.3 collective-permute-done.6
  42.4 0.0 copy-start.3
  42.4 2.0 %collective-permute-done.7 = bf16[1,128,768]{2,1,0:T(8,128)(2,1)S(1)} collective-permute-done((bf16[1,128,768]{2,1,0:T(8,128)(2,1)S(1)}, bf16[1,128,768]{2,1,0:T(8,128)(2,1)S(1)}, u32[]{:S(2)}, u32[]{:S(2)}) %collective-permute-start.7) | collective-permute-done | bytes 196640 | tf_op jit(solution)/shard_map/ppermute | solution.py:143
  44.4 1.1 %copy-done = bf16[8,1,128,768]{3,2,1,0:T(8,128)(2,1)} copy-done((bf16[8,1,128,768]{3,2,1,0:T(8,128)(2,1)}, bf16[8,1,128,768]{3,2,1,0:T(8,128)(2,1)S(1)}, u32[]{:S(2)}) %copy-start) | copy-done | bytes 1572888
  45.5 5.8 %shard_map.37 = (bf16[16,64,512]{2,1,0:T(8,128)(2,1)}, bf16[16,64,512]{2,1,0:T(8,128)(2,1)}) custom-call(s32[8]{0:T(128)} %fusion.56.index_ref, f32[4,384]{1,0:T(4,128)} %get-tuple-element.169.cc_ref, f32[4,384]{1,0:T(4,128)} %get-tuple-element.170.sc_ref, f32[4,384]{1,0:T(4,128)} %get-tuple-element.164.cf_ref, f32[4,384]{1,0:T(4,128)} %get-tuple-element.163.sf_ref, ...), custom_call_target="tpu_custom_call" | custom-call | flops 1610612736 | bytes 3670016 | tf_op jit(solution)/shard_map/pallas_call | solution.py:103
  51.3 1.5 %convert.39 = f32[16,2,32,512]{3,2,1,0:T(8,128)S(1)} convert(bf16[16,2,32,512]{3,2,1,0:T(8,128)(2,1)} %bitcast.79) | non-fusion elementwise | flops 524288 | bytes 3145728 | tf_op jit(solution)/shard_map/reshape | solution.py:196
  52.8 1.3 %collective-permute-done.8 = bf16[16,64,512]{2,1,0:T(8,128)(2,1)S(1)} collective-permute-done((bf16[16,64,512]{2,1,0:T(8,128)(2,1)}, bf16[16,64,512]{2,1,0:T(8,128)(2,1)S(1)}, u32[]{:S(2)}, u32[]{:S(2)}) %collective-permute-start.8) | collective-permute-done | bytes 1048608 | tf_op jit(solution)/shard_map/ppermute | solution.py:195
  54.2 0.2 fusion.15
  54.3 1.3 %collective-permute-start.9 = (bf16[16,32,512]{2,1,0:T(8,128)(2,1)S(1)}, bf16[16,32,512]{2,1,0:T(8,128)(2,1)S(1)}, u32[]{:S(2)}, u32[]{:S(2)}) collective-permute-start(bf16[16,32,512]{2,1,0:T(8,128)(2,1)S(1)} %fusion.15), channel_id=1, source_target_pairs={{0,16},{8,24},{16,0},{24,8},{1,17},{9,25},{17,1},{25,9},{2,18},{10... | collective-permute-start | bytes 1572872 | tf_op jit(solution)/shard_map/ppermute | solution.py:207
  55.7 12.7 %collective-permute-done.9 = bf16[16,32,512]{2,1,0:T(8,128)(2,1)S(1)} collective-permute-done((bf16[16,32,512]{2,1,0:T(8,128)(2,1)S(1)}, bf16[16,32,512]{2,1,0:T(8,128)(2,1)S(1)}, u32[]{:S(2)}, u32[]{:S(2)}) %collective-permute-start.9) | collective-permute-done | bytes 524320 | tf_op jit(solution)/shard_map/ppermute | solution.py:207
  68.4 0.2 fusion.14
  68.6 0.4 reshape.598
  69.0 0.4 multiply_bitcast_fusion
  69.4 1.6 %copy.16 = f32[32,4,16,128]{3,2,1,0:T(8,128)} copy(f32[32,4,16,128]{3,1,0,2:T(4,128)S(1)} %multiply_bitcast_fusion) | data formatting | bytes 2097152 | tf_op jit(solution)/shard_map/div | solution.py:214
  (25 shorter events, 0.3 us)
Async XLA Ops:
  0.8 3.5 %copy-start.2 = (bf16[1,256,7680]{2,1,0:T(8,128)(2,1)S(1)}, bf16[1,256,7680]{2,1,0:T(8,128)(2,1)}, u32[]{:S(2)}) copy-start(bf16[1,256,7680]{2,1,0:T(8,128)(2,1)} %param.3) | copy-start | bytes 11796484
  6.0 2.3 %copy-start.1 = (s32[32,2]{0,1:T(2,128)S(1)}, s32[32,2]{0,1:T(2,128)}, u32[]{:S(2)}) copy-start(s32[32,2]{0,1:T(2,128)} %param.4) | copy-start | bytes 772
  11.4 18.4 %collective-permute-start.3 = (bf16[1,128,768]{2,1,0:T(8,128)(2,1)S(1)}, bf16[1,128,768]{2,1,0:T(8,128)(2,1)S(1)}, u32[]{:S(2)}, u32[]{:S(2)}) collective-permute-start(bf16[1,128,768]{2,1,0:T(8,128)(2,1)S(1)} %get-tuple-element.156), channel_id=1, source_target_pairs={{0,4},{1,5},{2,6},{3,7},{4,0},{5,1},{6,2},{7,3},{8,12},{9,13},{10,... | collective-permute-start | bytes 589832 | tf_op jit(solution)/shard_map/ppermute | solution.py:131
  15.5 17.6 %collective-permute-start.4 = (bf16[1,128,768]{2,1,0:T(8,128)(2,1)S(1)}, bf16[1,128,768]{2,1,0:T(8,128)(2,1)S(1)}, u32[]{:S(2)}, u32[]{:S(2)}) collective-permute-start(bf16[1,128,768]{2,1,0:T(8,128)(2,1)S(1)} %get-tuple-element.155), channel_id=1, source_target_pairs={{0,4},{1,5},{2,6},{3,7},{4,0},{5,1},{6,2},{7,3},{8,12},{9,13},{10,... | collective-permute-start | bytes 589832 | tf_op jit(solution)/shard_map/ppermute | solution.py:131
  15.6 19.8 %collective-permute-start = (bf16[1,128,768]{2,1,0:T(8,128)(2,1)S(1)}, bf16[1,128,768]{2,1,0:T(8,128)(2,1)S(1)}, u32[]{:S(2)}, u32[]{:S(2)}) collective-permute-start(bf16[1,128,768]{2,1,0:T(8,128)(2,1)S(1)} %get-tuple-element.153), channel_id=1, source_target_pairs={{0,1},{1,2},{2,3},{3,0},{4,5},{5,6},{6,7},{7,4},{8,9},{9,10},{10,1... | collective-permute-start | bytes 589832 | tf_op jit(solution)/shard_map/ppermute | solution.py:142
  17.3 19.5 %collective-permute-start.1 = (bf16[1,128,768]{2,1,0:T(8,128)(2,1)S(1)}, bf16[1,128,768]{2,1,0:T(8,128)(2,1)S(1)}, u32[]{:S(2)}, u32[]{:S(2)}) collective-permute-start(bf16[1,128,768]{2,1,0:T(8,128)(2,1)S(1)} %get-tuple-element.154), channel_id=1, source_target_pairs={{0,2},{1,3},{2,0},{3,1},{4,6},{5,7},{6,4},{7,5},{8,10},{9,11},{10,... | collective-permute-start | bytes 589832 | tf_op jit(solution)/shard_map/ppermute | solution.py:142
  18.9 18.0 %collective-permute-start.2 = (bf16[1,128,768]{2,1,0:T(8,128)(2,1)S(1)}, bf16[1,128,768]{2,1,0:T(8,128)(2,1)S(1)}, u32[]{:S(2)}, u32[]{:S(2)}) collective-permute-start(bf16[1,128,768]{2,1,0:T(8,128)(2,1)S(1)} %get-tuple-element.152), channel_id=1, source_target_pairs={{0,3},{1,0},{2,1},{3,2},{4,7},{5,4},{6,5},{7,6},{8,11},{9,8},{10,9... | collective-permute-start | bytes 589832 | tf_op jit(solution)/shard_map/ppermute | solution.py:142
  33.2 8.8 %collective-permute-start.5 = (bf16[1,128,768]{2,1,0:T(8,128)(2,1)S(1)}, bf16[1,128,768]{2,1,0:T(8,128)(2,1)S(1)}, u32[]{:S(2)}, u32[]{:S(2)}) collective-permute-start(bf16[1,128,768]{2,1,0:T(8,128)(2,1)S(1)} %get-tuple-element.151), channel_id=1, source_target_pairs={{0,1},{1,2},{2,3},{3,0},{4,5},{5,6},{6,7},{7,4},{8,9},{9,10},{10,1... | collective-permute-start | bytes 589832 | tf_op jit(solution)/shard_map/ppermute | solution.py:143
  34.8 7.6 %collective-permute-start.6 = (bf16[1,128,768]{2,1,0:T(8,128)(2,1)S(1)}, bf16[1,128,768]{2,1,0:T(8,128)(2,1)S(1)}, u32[]{:S(2)}, u32[]{:S(2)}) collective-permute-start(bf16[1,128,768]{2,1,0:T(8,128)(2,1)S(1)} %get-tuple-element.150), channel_id=1, source_target_pairs={{0,2},{1,3},{2,0},{3,1},{4,6},{5,7},{6,4},{7,5},{8,10},{9,11},{10,... | collective-permute-start | bytes 589832 | tf_op jit(solution)/shard_map/ppermute | solution.py:143
  35.4 9.0 %collective-permute-start.7 = (bf16[1,128,768]{2,1,0:T(8,128)(2,1)S(1)}, bf16[1,128,768]{2,1,0:T(8,128)(2,1)S(1)}, u32[]{:S(2)}, u32[]{:S(2)}) collective-permute-start(bf16[1,128,768]{2,1,0:T(8,128)(2,1)S(1)} %get-tuple-element.149), channel_id=1, source_target_pairs={{0,3},{1,0},{2,1},{3,2},{4,7},{5,4},{6,5},{7,6},{8,11},{9,8},{10,9... | collective-permute-start | bytes 589832 | tf_op jit(solution)/shard_map/ppermute | solution.py:143
  42.4 13.3 %copy-start.3 = (s32[4]{0:T(128)S(1)}, s32[4]{0:T(128)}, u32[]{:S(2)}) copy-start(s32[4]{0:T(128)} %param.5) | copy-start | bytes 52
  44.4 1.2 %copy-start = (bf16[8,1,128,768]{3,2,1,0:T(8,128)(2,1)}, bf16[8,1,128,768]{3,2,1,0:T(8,128)(2,1)S(1)}, u32[]{:S(2)}) copy-start(bf16[8,1,128,768]{3,2,1,0:T(8,128)(2,1)S(1)} %bitcast_dynamic-update-slice_fusion.left_ref.right_ref) | copy-start | bytes 4718596
  51.3 2.9 %collective-permute-start.8 = (bf16[16,64,512]{2,1,0:T(8,128)(2,1)}, bf16[16,64,512]{2,1,0:T(8,128)(2,1)S(1)}, u32[]{:S(2)}, u32[]{:S(2)}) collective-permute-start(bf16[16,64,512]{2,1,0:T(8,128)(2,1)} %get-tuple-element.8), channel_id=1, source_target_pairs={{0,8},{8,0},{16,24},{24,16},{1,9},{9,1},{17,25},{25,17},{2,10},{10... | collective-permute-start | bytes 3145736 | tf_op jit(solution)/shard_map/ppermute | solution.py:195
  54.3 14.0 %collective-permute-start.9 = (bf16[16,32,512]{2,1,0:T(8,128)(2,1)S(1)}, bf16[16,32,512]{2,1,0:T(8,128)(2,1)S(1)}, u32[]{:S(2)}, u32[]{:S(2)}) collective-permute-start(bf16[16,32,512]{2,1,0:T(8,128)(2,1)S(1)} %fusion.15), channel_id=1, source_target_pairs={{0,16},{8,24},{16,0},{24,8},{1,17},{9,25},{17,1},{25,9},{2,18},{10... | collective-permute-start | bytes 1572872 | tf_op jit(solution)/shard_map/ppermute | solution.py:207

commit v21 on v20

--- a/solution.py
+++ b/solution.py
@@ -22,8 +22,12 @@
 
 def dft_table(sample_count, bin_count):
     bin_index = lax.iota(jnp.int32, bin_count) + 1
-    coarse = lax.iota(jnp.int32, sample_count // SPLIT) * SPLIT
-    ca, sa = cos_sin(coarse[:, None] * bin_index[None, :], sample_count)
+    coarse_count = sample_count // SPLIT
+    step = max(g for g in range(1, 11) if coarse_count % g == 0)
+    c3, s3 = cos_sin((lax.iota(jnp.int32, coarse_count // step) * step * SPLIT)[:, None] * bin_index[None, :], sample_count)
+    c2, s2 = cos_sin((lax.iota(jnp.int32, step) * SPLIT)[:, None] * bin_index[None, :], sample_count)
+    ca = (c3[:, None, :] * c2[None, :, :] - s3[:, None, :] * s2[None, :, :]).reshape(coarse_count, bin_count)
+    sa = (s3[:, None, :] * c2[None, :, :] + c3[:, None, :] * s2[None, :, :]).reshape(coarse_count, bin_count)
     c1, s1 = cos_sin((lax.iota(jnp.int32, SPLIT // 16) * 16)[:, None] * bin_index[None, :], sample_count)
     c0, s0 = cos_sin(lax.iota(jnp.int32, 16)[:, None] * bin_index[None, :], sample_count)
     cb = (c1[:, None, :] * c0[None, :, :] - s1[:, None, :] * s0[None, :, :]).reshape(SPLIT, bin_count)

time: 71.2 us -> 71.3 us (level)
  no operation moved by 1% of the time
where the time goes in v21:
time: 71.3 us; the launch traced here: 71 us
  waiting for transfers between devices  29.4 us (41%)
  starting transfers between devices  13.9 us (19%)
  other arithmetic  8.78 us (12%)
  Pallas kernels  5.75 us (8%)
  between operations  5.45 us (8%)
  local copies, waits for them, and re-layouts  4.35 us (6%)
  matrix products  3.38 us (5%)
    ppermute x1, waiting for transfers between devices, body(): lax.ppermute(chip_sum(dest).astype(jnp.bfloat16), 'win', perm)  12.7 us
    ppermute x2, waiting for transfers between devices, exchange_by_halves(): lax.ppermute(block, 'pair', across)  8 us
    ppermute x3, waiting for transfers between devices, exchange_by_halves(): relay = lax.ppermute(relay, 'pair', perm)  7.36 us
    pallas_call x1, Pallas kernels, tile_correlation(): pl.pallas_call(functools.partial(correlation_kernel, sub, n_y, own_rows),...  5.75 us
    ppermute x3, starting transfers between devices, exchange_by_halves(): own = lax.ppermute(own, 'pair', perm)  4.76 us
    ppermute x2, starting transfers between devices, exchange_by_halves(): lax.ppermute(block, 'pair', across)  4.19 us
    another operation x3, other arithmetic  3.71 us
    ppermute x3, starting transfers between devices, exchange_by_halves(): relay = lax.ppermute(relay, 'pair', perm)  3.65 us
  transfers between devices with their start and end apart: 10, of which 7 were waited for; matrix products, arithmetic and copies ran while one was open for 5% of the time, Pallas kernels for 0%

profile of v21, /device:TPU:0, one launch (start us, length us, event | category | flops | bytes accessed | tf_op | source)
XLA Modules:
  0.0 71.0 jit_solution(7842323639479508709)
XLA Ops:
  0.0 0.1 fusion.24
  0.1 0.2 fusion.28
  0.3 0.1 fusion.42
  0.6 0.1 fusion.38
  0.8 0.0 copy-start.2
  0.8 3.5 %subtract_convert_fusion = (bf16[60,128,384]{2,1,0:T(8,128)(2,1)S(1)}, bf16[60,128,384]{2,1,0:T(8,128)(2,1)S(1)}) fusion(f32[128,384]{1,0:T(8,128)S(1)} %bitcast.91, f32[60,384]{1,0:T(8,128)S(1)} %add.253, f32[128,384]{1,0:T(8,128)S(1)} %bitcast.90, f32[60,384]{1,0:T(8,128)S(1)} %sub.77), kind=kLoop, calls=%fused_computation.2 | loop fusion | flops 26542080 | bytes 12374016 | tf_op jit(solution)/shard_map/convert.20
  4.3 1.7 %fusion.6 = f32[128,768]{1,0:T(8,128)S(1)} fusion(bf16[7680,384]{1,0:T(8,128)(2,1)S(1)} %bitcast.77, bf16[7680,384]{1,0:T(8,128)(2,1)S(1)} %bitcast.75, bf16[1,256,7680]{2,1,0:T(8,128)(2,1)S(1)} %copy-done.2), kind=kOutput, calls=%fused_computation.9 | convolution fusion | flops 1533542400 | bytes 14155776 | tf_op jit(solution)/shard_map/dot_general | solution.py:42
  6.0 0.0 copy-start.1
  6.0 1.7 %fusion.9 = f32[128,768]{1,0:T(8,128)S(1)} fusion(bf16[7680,384]{1,0:T(8,128)(2,1)S(1)} %bitcast.78, bf16[7680,384]{1,0:T(8,128)(2,1)S(1)} %bitcast.76, bf16[1,256,7680]{2,1,0:T(8,128)(2,1)S(1)} %copy-done.2), kind=kOutput, calls=%fused_computation.10 | convolution fusion | flops 1533542400 | bytes 14155776 | tf_op jit(solution)/shard_map/dot_general | solution.py:42
  7.8 0.2 fusion.66
  8.0 0.1 divide_convert_fusion.1
  8.1 0.1 divide_convert_fusion.3
  8.3 0.1 reduce_sum.43
  8.4 0.1 reduce_sum.52
  8.5 0.1 reduce_sum.56
  8.6 0.1 reduce_sum.57
  8.7 0.7 fusion.68
  11.4 0.1 broadcast_select_fusion.3
  11.5 4.1 %collective-permute-start.3 = (bf16[1,128,768]{2,1,0:T(8,128)(2,1)S(1)}, bf16[1,128,768]{2,1,0:T(8,128)(2,1)S(1)}, u32[]{:S(2)}, u32[]{:S(2)}) collective-permute-start(bf16[1,128,768]{2,1,0:T(8,128)(2,1)S(1)} %get-tuple-element.156), channel_id=1, source_target_pairs={{0,4},{1,5},{2,6},{3,7},{4,0},{5,1},{6,2},{7,3},{8,12},{9,13},{10,... | collective-permute-start | bytes 589832 | tf_op jit(solution)/shard_map/ppermute | solution.py:135
  15.6 0.1 collective-permute-start.4
  15.7 1.8 %collective-permute-start = (bf16[1,128,768]{2,1,0:T(8,128)(2,1)S(1)}, bf16[1,128,768]{2,1,0:T(8,128)(2,1)S(1)}, u32[]{:S(2)}, u32[]{:S(2)}) collective-permute-start(bf16[1,128,768]{2,1,0:T(8,128)(2,1)S(1)} %get-tuple-element.153), channel_id=1, source_target_pairs={{0,1},{1,2},{2,3},{3,0},{4,5},{5,6},{6,7},{7,4},{8,9},{9,10},{10,1... | collective-permute-start | bytes 589832 | tf_op jit(solution)/shard_map/ppermute | solution.py:146
  17.4 1.6 %collective-permute-start.1 = (bf16[1,128,768]{2,1,0:T(8,128)(2,1)S(1)}, bf16[1,128,768]{2,1,0:T(8,128)(2,1)S(1)}, u32[]{:S(2)}, u32[]{:S(2)}) collective-permute-start(bf16[1,128,768]{2,1,0:T(8,128)(2,1)S(1)} %get-tuple-element.154), channel_id=1, source_target_pairs={{0,2},{1,3},{2,0},{3,1},{4,6},{5,7},{6,4},{7,5},{8,10},{9,11},{10,... | collective-permute-start | bytes 589832 | tf_op jit(solution)/shard_map/ppermute | solution.py:146
  19.0 1.4 %collective-permute-start.2 = (bf16[1,128,768]{2,1,0:T(8,128)(2,1)S(1)}, bf16[1,128,768]{2,1,0:T(8,128)(2,1)S(1)}, u32[]{:S(2)}, u32[]{:S(2)}) collective-permute-start(bf16[1,128,768]{2,1,0:T(8,128)(2,1)S(1)} %get-tuple-element.152), channel_id=1, source_target_pairs={{0,3},{1,0},{2,1},{3,2},{4,7},{5,4},{6,5},{7,6},{8,11},{9,8},{10,9... | collective-permute-start | bytes 589832 | tf_op jit(solution)/shard_map/ppermute | solution.py:146
  23.5 0.1 constant_dynamic-slice_fusion
  23.6 0.1 copy.9
  23.7 0.1 reshape.719
  23.8 0.8 %fusion.55 = (f32[4,384]{1,0:T(4,128)}, f32[4,384]{1,0:T(4,128)}, f32[4,384]{1,0:T(4,128)}, f32[4,384]{1,0:T(4,128)}) fusion(s32[384]{0:T(512)S(1)} %iota_add_fusion, s32[4]{0:T(128)S(1)} %get-tuple-element.187, s32[4]{0:T(128)S(1)} %get-tuple-element.188), kind=kLoop, calls=%fused_computation.95 | loop fusion | flops 27648 | bytes 26144 | tf_op jit(solution)/shard_map/sin | solution.py:20
  24.6 0.6 fusion.63.index_ref
  25.2 4.6 %collective-permute-done.3 = bf16[1,128,768]{2,1,0:T(8,128)(2,1)S(1)} collective-permute-done((bf16[1,128,768]{2,1,0:T(8,128)(2,1)S(1)}, bf16[1,128,768]{2,1,0:T(8,128)(2,1)S(1)}, u32[]{:S(2)}, u32[]{:S(2)}) %collective-permute-start.3) | collective-permute-done | bytes 196640 | tf_op jit(solution)/shard_map/ppermute | solution.py:135
  29.8 3.4 %collective-permute-done.4 = bf16[1,128,768]{2,1,0:T(8,128)(2,1)S(1)} collective-permute-done((bf16[1,128,768]{2,1,0:T(8,128)(2,1)S(1)}, bf16[1,128,768]{2,1,0:T(8,128)(2,1)S(1)}, u32[]{:S(2)}, u32[]{:S(2)}) %collective-permute-start.4) | collective-permute-done | bytes 196640 | tf_op jit(solution)/shard_map/ppermute | solution.py:135
  33.3 1.6 %collective-permute-start.5 = (bf16[1,128,768]{2,1,0:T(8,128)(2,1)S(1)}, bf16[1,128,768]{2,1,0:T(8,128)(2,1)S(1)}, u32[]{:S(2)}, u32[]{:S(2)}) collective-permute-start(bf16[1,128,768]{2,1,0:T(8,128)(2,1)S(1)} %get-tuple-element.151), channel_id=1, source_target_pairs={{0,1},{1,2},{2,3},{3,0},{4,5},{5,6},{6,7},{7,4},{8,9},{9,10},{10,1... | collective-permute-start | bytes 589832 | tf_op jit(solution)/shard_map/ppermute | solution.py:147
  34.9 0.6 collective-permute-start.6
  35.5 1.4 %collective-permute-start.7 = (bf16[1,128,768]{2,1,0:T(8,128)(2,1)S(1)}, bf16[1,128,768]{2,1,0:T(8,128)(2,1)S(1)}, u32[]{:S(2)}, u32[]{:S(2)}) collective-permute-start(bf16[1,128,768]{2,1,0:T(8,128)(2,1)S(1)} %get-tuple-element.149), channel_id=1, source_target_pairs={{0,3},{1,0},{2,1},{3,2},{4,7},{5,4},{6,5},{7,6},{8,11},{9,8},{10,9... | collective-permute-start | bytes 589832 | tf_op jit(solution)/shard_map/ppermute | solution.py:147
  37.0 0.1 bitcast_dynamic-update-slice_fusion.3
  37.1 5.0 %collective-permute-done.5 = bf16[1,128,768]{2,1,0:T(8,128)(2,1)S(1)} collective-permute-done((bf16[1,128,768]{2,1,0:T(8,128)(2,1)S(1)}, bf16[1,128,768]{2,1,0:T(8,128)(2,1)S(1)}, u32[]{:S(2)}, u32[]{:S(2)}) %collective-permute-start.5) | collective-permute-done | bytes 196640 | tf_op jit(solution)/shard_map/ppermute | solution.py:147
  42.1 0.4 collective-permute-done.6
  42.4 2.0 %collective-permute-done.7 = bf16[1,128,768]{2,1,0:T(8,128)(2,1)S(1)} collective-permute-done((bf16[1,128,768]{2,1,0:T(8,128)(2,1)S(1)}, bf16[1,128,768]{2,1,0:T(8,128)(2,1)S(1)}, u32[]{:S(2)}, u32[]{:S(2)}) %collective-permute-start.7) | collective-permute-done | bytes 196640 | tf_op jit(solution)/shard_map/ppermute | solution.py:147
  44.5 1.2 %copy-done = bf16[8,1,128,768]{3,2,1,0:T(8,128)(2,1)} copy-done((bf16[8,1,128,768]{3,2,1,0:T(8,128)(2,1)}, bf16[8,1,128,768]{3,2,1,0:T(8,128)(2,1)S(1)}, u32[]{:S(2)}) %copy-start) | copy-done | bytes 1572888
  45.6 5.8 %shard_map.37 = (bf16[16,64,512]{2,1,0:T(8,128)(2,1)}, bf16[16,64,512]{2,1,0:T(8,128)(2,1)}) custom-call(s32[8]{0:T(128)} %fusion.63.index_ref, f32[4,384]{1,0:T(4,128)} %get-tuple-element.173.cc_ref, f32[4,384]{1,0:T(4,128)} %get-tuple-element.174.sc_ref, f32[4,384]{1,0:T(4,128)} %get-tuple-element.168.cf_ref, f32[4,384]{1,0:T(4,128)} %get-tuple-element.167.sf_ref, ...), custom_call_target="tpu_custom_call" | custom-call | flops 1610612736 | bytes 3670016 | tf_op jit(solution)/shard_map/pallas_call | solution.py:107
  51.4 1.5 %convert.39 = f32[16,2,32,512]{3,2,1,0:T(8,128)S(1)} convert(bf16[16,2,32,512]{3,2,1,0:T(8,128)(2,1)} %bitcast.79) | non-fusion elementwise | flops 524288 | bytes 3145728 | tf_op jit(solution)/shard_map/reshape | solution.py:200
  52.9 1.3 %collective-permute-done.8 = bf16[16,64,512]{2,1,0:T(8,128)(2,1)S(1)} collective-permute-done((bf16[16,64,512]{2,1,0:T(8,128)(2,1)}, bf16[16,64,512]{2,1,0:T(8,128)(2,1)S(1)}, u32[]{:S(2)}, u32[]{:S(2)}) %collective-permute-start.8) | collective-permute-done | bytes 1048608 | tf_op jit(solution)/shard_map/ppermute | solution.py:199
  54.3 0.2 fusion.15
  54.4 1.3 %collective-permute-start.9 = (bf16[16,32,512]{2,1,0:T(8,128)(2,1)S(1)}, bf16[16,32,512]{2,1,0:T(8,128)(2,1)S(1)}, u32[]{:S(2)}, u32[]{:S(2)}) collective-permute-start(bf16[16,32,512]{2,1,0:T(8,128)(2,1)S(1)} %fusion.15), channel_id=1, source_target_pairs={{0,16},{8,24},{16,0},{24,8},{1,17},{9,25},{17,1},{25,9},{2,18},{10... | collective-permute-start | bytes 1572872 | tf_op jit(solution)/shard_map/ppermute | solution.py:211
  55.8 12.7 %collective-permute-done.9 = bf16[16,32,512]{2,1,0:T(8,128)(2,1)S(1)} collective-permute-done((bf16[16,32,512]{2,1,0:T(8,128)(2,1)S(1)}, bf16[16,32,512]{2,1,0:T(8,128)(2,1)S(1)}, u32[]{:S(2)}, u32[]{:S(2)}) %collective-permute-start.9) | collective-permute-done | bytes 524320 | tf_op jit(solution)/shard_map/ppermute | solution.py:211
  68.5 0.2 fusion.14
  68.7 0.4 reshape.725
  69.1 0.4 multiply_bitcast_fusion
  69.4 1.6 %copy.16 = f32[32,4,16,128]{3,2,1,0:T(8,128)} copy(f32[32,4,16,128]{3,1,0,2:T(4,128)S(1)} %multiply_bitcast_fusion) | data formatting | bytes 2097152 | tf_op jit(solution)/shard_map/div | solution.py:218
  (30 shorter events, 0.4 us)
Async XLA Ops:
  0.8 3.5 %copy-start.2 = (bf16[1,256,7680]{2,1,0:T(8,128)(2,1)S(1)}, bf16[1,256,7680]{2,1,0:T(8,128)(2,1)}, u32[]{:S(2)}) copy-start(bf16[1,256,7680]{2,1,0:T(8,128)(2,1)} %param.3) | copy-start | bytes 11796484
  6.0 2.3 %copy-start.1 = (s32[32,2]{0,1:T(2,128)S(1)}, s32[32,2]{0,1:T(2,128)}, u32[]{:S(2)}) copy-start(s32[32,2]{0,1:T(2,128)} %param.4) | copy-start | bytes 772
  11.5 18.4 %collective-permute-start.3 = (bf16[1,128,768]{2,1,0:T(8,128)(2,1)S(1)}, bf16[1,128,768]{2,1,0:T(8,128)(2,1)S(1)}, u32[]{:S(2)}, u32[]{:S(2)}) collective-permute-start(bf16[1,128,768]{2,1,0:T(8,128)(2,1)S(1)} %get-tuple-element.156), channel_id=1, source_target_pairs={{0,4},{1,5},{2,6},{3,7},{4,0},{5,1},{6,2},{7,3},{8,12},{9,13},{10,... | collective-permute-start | bytes 589832 | tf_op jit(solution)/shard_map/ppermute | solution.py:135
  15.6 17.6 %collective-permute-start.4 = (bf16[1,128,768]{2,1,0:T(8,128)(2,1)S(1)}, bf16[1,128,768]{2,1,0:T(8,128)(2,1)S(1)}, u32[]{:S(2)}, u32[]{:S(2)}) collective-permute-start(bf16[1,128,768]{2,1,0:T(8,128)(2,1)S(1)} %get-tuple-element.155), channel_id=1, source_target_pairs={{0,4},{1,5},{2,6},{3,7},{4,0},{5,1},{6,2},{7,3},{8,12},{9,13},{10,... | collective-permute-start | bytes 589832 | tf_op jit(solution)/shard_map/ppermute | solution.py:135
  15.7 19.8 %collective-permute-start = (bf16[1,128,768]{2,1,0:T(8,128)(2,1)S(1)}, bf16[1,128,768]{2,1,0:T(8,128)(2,1)S(1)}, u32[]{:S(2)}, u32[]{:S(2)}) collective-permute-start(bf16[1,128,768]{2,1,0:T(8,128)(2,1)S(1)} %get-tuple-element.153), channel_id=1, source_target_pairs={{0,1},{1,2},{2,3},{3,0},{4,5},{5,6},{6,7},{7,4},{8,9},{9,10},{10,1... | collective-permute-start | bytes 589832 | tf_op jit(solution)/shard_map/ppermute | solution.py:146
  17.4 19.5 %collective-permute-start.1 = (bf16[1,128,768]{2,1,0:T(8,128)(2,1)S(1)}, bf16[1,128,768]{2,1,0:T(8,128)(2,1)S(1)}, u32[]{:S(2)}, u32[]{:S(2)}) collective-permute-start(bf16[1,128,768]{2,1,0:T(8,128)(2,1)S(1)} %get-tuple-element.154), channel_id=1, source_target_pairs={{0,2},{1,3},{2,0},{3,1},{4,6},{5,7},{6,4},{7,5},{8,10},{9,11},{10,... | collective-permute-start | bytes 589832 | tf_op jit(solution)/shard_map/ppermute | solution.py:146
  19.0 18.0 %collective-permute-start.2 = (bf16[1,128,768]{2,1,0:T(8,128)(2,1)S(1)}, bf16[1,128,768]{2,1,0:T(8,128)(2,1)S(1)}, u32[]{:S(2)}, u32[]{:S(2)}) collective-permute-start(bf16[1,128,768]{2,1,0:T(8,128)(2,1)S(1)} %get-tuple-element.152), channel_id=1, source_target_pairs={{0,3},{1,0},{2,1},{3,2},{4,7},{5,4},{6,5},{7,6},{8,11},{9,8},{10,9... | collective-permute-start | bytes 589832 | tf_op jit(solution)/shard_map/ppermute | solution.py:146
  33.3 8.8 %collective-permute-start.5 = (bf16[1,128,768]{2,1,0:T(8,128)(2,1)S(1)}, bf16[1,128,768]{2,1,0:T(8,128)(2,1)S(1)}, u32[]{:S(2)}, u32[]{:S(2)}) collective-permute-start(bf16[1,128,768]{2,1,0:T(8,128)(2,1)S(1)} %get-tuple-element.151), channel_id=1, source_target_pairs={{0,1},{1,2},{2,3},{3,0},{4,5},{5,6},{6,7},{7,4},{8,9},{9,10},{10,1... | collective-permute-start | bytes 589832 | tf_op jit(solution)/shard_map/ppermute | solution.py:147
  34.9 7.6 %collective-permute-start.6 = (bf16[1,128,768]{2,1,0:T(8,128)(2,1)S(1)}, bf16[1,128,768]{2,1,0:T(8,128)(2,1)S(1)}, u32[]{:S(2)}, u32[]{:S(2)}) collective-permute-start(bf16[1,128,768]{2,1,0:T(8,128)(2,1)S(1)} %get-tuple-element.150), channel_id=1, source_target_pairs={{0,2},{1,3},{2,0},{3,1},{4,6},{5,7},{6,4},{7,5},{8,10},{9,11},{10,... | collective-permute-start | bytes 589832 | tf_op jit(solution)/shard_map/ppermute | solution.py:147
  35.5 9.0 %collective-permute-start.7 = (bf16[1,128,768]{2,1,0:T(8,128)(2,1)S(1)}, bf16[1,128,768]{2,1,0:T(8,128)(2,1)S(1)}, u32[]{:S(2)}, u32[]{:S(2)}) collective-permute-start(bf16[1,128,768]{2,1,0:T(8,128)(2,1)S(1)} %get-tuple-element.149), channel_id=1, source_target_pairs={{0,3},{1,0},{2,1},{3,2},{4,7},{5,4},{6,5},{7,6},{8,11},{9,8},{10,9... | collective-permute-start | bytes 589832 | tf_op jit(solution)/shard_map/ppermute | solution.py:147
  42.4 13.3 %copy-start.3 = (s32[4]{0:T(128)S(1)}, s32[4]{0:T(128)}, u32[]{:S(2)}) copy-start(s32[4]{0:T(128)} %param.5) | copy-start | bytes 52
  44.5 1.2 %copy-start = (bf16[8,1,128,768]{3,2,1,0:T(8,128)(2,1)}, bf16[8,1,128,768]{3,2,1,0:T(8,128)(2,1)S(1)}, u32[]{:S(2)}) copy-start(bf16[8,1,128,768]{3,2,1,0:T(8,128)(2,1)S(1)} %bitcast_dynamic-update-slice_fusion.left_ref.right_ref) | copy-start | bytes 4718596
  51.4 2.9 %collective-permute-start.8 = (bf16[16,64,512]{2,1,0:T(8,128)(2,1)}, bf16[16,64,512]{2,1,0:T(8,128)(2,1)S(1)}, u32[]{:S(2)}, u32[]{:S(2)}) collective-permute-start(bf16[16,64,512]{2,1,0:T(8,128)(2,1)} %get-tuple-element.8), channel_id=1, source_target_pairs={{0,8},{8,0},{16,24},{24,16},{1,9},{9,1},{17,25},{25,17},{2,10},{10... | collective-permute-start | bytes 3145736 | tf_op jit(solution)/shard_map/ppermute | solution.py:199
  54.4 14.0 %collective-permute-start.9 = (bf16[16,32,512]{2,1,0:T(8,128)(2,1)S(1)}, bf16[16,32,512]{2,1,0:T(8,128)(2,1)S(1)}, u32[]{:S(2)}, u32[]{:S(2)}) collective-permute-start(bf16[16,32,512]{2,1,0:T(8,128)(2,1)S(1)} %fusion.15), channel_id=1, source_target_pairs={{0,16},{8,24},{16,0},{24,8},{1,17},{9,25},{17,1},{25,9},{2,18},{10... | collective-permute-start | bytes 1572872 | tf_op jit(solution)/shard_map/ppermute | solution.py:211
